TPU v7x, 256 devices: a whole 4x4x8 slice. The times are simulated.
256 devices in a mesh: blk: 128 (over z, x_hi, y, core), rows: 2 (over x_lo).
Axes of the slice: x: 4 (x_hi: 2, x_lo: 2; x = x_hi * 2 + x_lo), y: 4, z: 8, core: 2. Of those that a mesh axis runs over, the one named last changes fastest.
Arguments:
- tokens: bfloat16 [512, 8192], P(('blk', 'rows')), may hold values from -60 to 60
- norm_gain: float32 [8192], replicated, may hold values from 0.1 to 1.9
- gate_weight: bfloat16 [8192, 32768], P(None, 'blk'), may hold values from -0.09375 to 0.09375
- up_weight: bfloat16 [8192, 32768], P(None, 'blk'), may hold values from -0.09375 to 0.09375
- down_weight: bfloat16 [32768, 8192], P('blk'), may hold values from -0.046875 to 0.046875
- gate_mask: int32 [64, 256], P(None, 'blk'), may hold values from 0 to 1, as said below
- up_mask: int32 [64, 256], P(None, 'blk'), may hold values from 0 to 1, as said below
- down_mask: int32 [256, 64], P('blk'), may hold values 0 or 1
Outputs:
- ffn_out: bfloat16 [512, 8192], P(('blk', 'rows'))
Inputs may be any that keep to these rules, and one draw needn't show every extreme that they name: Each column of gate_mask (64 block flags) has between 16 and 48 ones, and some column has exactly 48. Each column of up_mask (64 block flags) has between 16 and 48 ones, and some column has exactly 48.
All inputs are finite; a program needn't handle non-finite values. No bound on the sum of `down_mask` on one device may be relied on, other than what follows from the above.
Results may differ from a plain program's by a relative error of at most 0.0065.
Values may be sent and summed in bfloat16 or wider, within the bound.
No kernel may reach another device: no remote copies, remote signals or barrier semaphores. Data moves between devices by JAX's collectives and lax.ppermute only.
A program may use at most 128 MiB of HBM per device.

v0:
```python
import jax
import jax.numpy as jnp
from jax import lax
from jax.sharding import PartitionSpec as P

BLK_AXES = {"z": (16, 8), "xh": (8, 2), "y": (2, 4), "c": (1, 2)}
AG_ORDER = ("xh", "y", "z", "c")
PARTS = (
    (32, ("c", "z", "y", "xh")),
    (32, ("c", "y", "z", "xh")),
)


def mask_blocks(weight, flags):
    height, width = weight.shape
    down_n = flags.shape[0]
    across_n = flags.shape[1]
    cols = jnp.repeat(flags.astype(weight.dtype), width // across_n, axis=1)
    shaped = weight.reshape(down_n, height // down_n, width)
    return (shaped * cols[:, None, :]).reshape(height, width)


def _perm(axis, k, size):
    stride, n = BLK_AXES[axis]
    pairs = []
    for i in range(size):
        coord = (i // stride) % n
        pairs.append((i, i + ((coord + k) % n - coord) * stride))
    return pairs


def _ag_stage(block, axis, size):
    _, n = BLK_AXES[axis]
    m_plus = n // 2
    m_minus = n - 1 - m_plus
    got = [None] * n
    got[0] = block
    cur = block
    for s in range(m_plus):
        cur = lax.ppermute(cur, "blk", _perm(axis, 1, size))
        got[n - s - 1] = cur
    cur = block
    for s in range(m_minus):
        cur = lax.ppermute(cur, "blk", _perm(axis, -1, size))
        got[s + 1] = cur
    return jnp.concatenate(got, axis=0)


def _rs_stage(x, axis, size):
    _, n = BLK_AXES[axis]
    r = x.shape[0] // n
    m_plus = n // 2
    m_minus = n - 1 - m_plus

    def take(j):
        return lax.slice_in_dim(x, (j % n) * r, (j % n + 1) * r, axis=0)

    total = take(0)
    buf = take(m_plus)
    for s in range(m_plus):
        recv = lax.ppermute(buf, "blk", _perm(axis, 1, size))
        if s < m_plus - 1:
            buf = recv + take(m_plus - s - 1)
        else:
            total = total + recv
    if m_minus:
        buf = take(n - m_minus)
        for s in range(m_minus):
            recv = lax.ppermute(buf, "blk", _perm(axis, -1, size))
            if s < m_minus - 1:
                buf = recv + take(n - m_minus + s + 1)
            else:
                total = total + recv
    return total


def _reorder_rows(x, src, dst, t):
    sizes = tuple(BLK_AXES[a][1] for a in src) + (t,)
    y = x.reshape(sizes + x.shape[1:])
    perm = [src.index(a) for a in dst] + [len(src)] + [len(src) + 1 + i for i in range(x.ndim - 1)]
    return jnp.transpose(y, perm).reshape(x.shape)


def local(tokens, norm_gain, gate_weight, up_weight, down_weight, gate_mask, up_mask, down_mask):
    size = 1
    for a in BLK_AXES:
        size *= BLK_AXES[a][1]
    t = tokens.shape[0]
    wide_tok = tokens.astype(jnp.float32)
    scale_inv = lax.rsqrt(jnp.mean(wide_tok * wide_tok, axis=-1, keepdims=True) + 1e-05)
    normed = (wide_tok * scale_inv * norm_gain).astype(jnp.bfloat16)
    gate_kept = mask_blocks(gate_weight, gate_mask)
    up_kept = mask_blocks(up_weight, up_mask)
    down_kept = mask_blocks(down_weight, down_mask)

    base = tuple(reversed(AG_ORDER))
    piece = normed
    for axis in AG_ORDER:
        piece = _ag_stage(piece, axis, size)
    gate = jnp.dot(piece, gate_kept, preferred_element_type=jnp.float32)
    up_val = jnp.dot(piece, up_kept, preferred_element_type=jnp.float32)
    hidden = (jax.nn.silu(gate) * up_val).astype(jnp.bfloat16)

    outs = []
    lo = 0
    for groups, rs_order in PARTS:
        hi = lo + groups * 128
        h = hidden if rs_order == base else _reorder_rows(hidden, base, rs_order, t)
        x = jnp.dot(h, down_kept[:, lo:hi], preferred_element_type=jnp.float32)
        for axis in rs_order:
            x = _rs_stage(x, axis, size)
        outs.append(x)
        lo = hi
    summed = jnp.concatenate(outs, axis=1) if len(outs) > 1 else outs[0]
    return summed.astype(jnp.bfloat16)


def solution(mesh):
    assert mesh.shape["blk"] == 128
    return jax.shard_map(
        local,
        mesh=mesh,
        in_specs=(
            P(("blk", "rows"), None),
            P(),
            P(None, "blk"),
            P(None, "blk"),
            P("blk", None),
            P(None, "blk"),
            P(None, "blk"),
            P("blk", None),
        ),
        out_specs=P(("blk", "rows"), None),
        check_vma=False,
    )
```

profile of v0, /device:TPU:2, one launch (start us, length us, event | category | flops | bytes accessed | tf_op | source)
XLA Modules:
  0.0 178.9 jit_solution(13852768237559503771)
XLA Ops:
  4.1 3.3 %collective-permute-done = bf16[2,8192]{1,0:T(2,128)(2,1)S(1)} collective-permute-done((bf16[2,8192]{1,0:T(2,128)(2,1)S(1)}, bf16[2,8192]{1,0:T(2,128)(2,1)S(1)}, u32[]{:S(2)}, u32[]{:S(2)}) %collective-permute-start) | collective-permute-done | bytes 32800 | tf_op jit(solution)/shard_map/ppermute | solution.py:40
  13.4 5.1 %collective-permute-done.3 = bf16[4,8192]{1,0:T(4,128)(2,1)S(1)} collective-permute-done((bf16[4,8192]{1,0:T(4,128)(2,1)S(1)}, bf16[4,8192]{1,0:T(4,128)(2,1)S(1)}, u32[]{:S(2)}, u32[]{:S(2)}) %collective-permute-start.3) | collective-permute-done | bytes 65568 | tf_op jit(solution)/shard_map/ppermute | solution.py:40
  20.7 4.0 %collective-permute-start.4 = (bf16[16,8192]{1,0:T(8,128)(2,1)S(1)}, bf16[16,8192]{1,0:T(8,128)(2,1)S(1)}, u32[]{:S(2)}, u32[]{:S(2)}) collective-permute-start(bf16[16,8192]{1,0:T(8,128)(2,1)S(1)} %concatenate.20), channel_id=1, source_target_pairs={{0,224},{2,226},{4,228},{6,230},{8,232},{10,234},{12,236},{14,238}... | collective-permute-start | bytes 786440 | tf_op jit(solution)/shard_map/ppermute | solution.py:44
  24.7 4.8 %collective-permute-done.7 = bf16[16,8192]{1,0:T(8,128)(2,1)S(1)} collective-permute-done((bf16[16,8192]{1,0:T(8,128)(2,1)S(1)}, bf16[16,8192]{1,0:T(8,128)(2,1)S(1)}, u32[]{:S(2)}, u32[]{:S(2)}) %collective-permute-start.7) | collective-permute-done | bytes 262176 | tf_op jit(solution)/shard_map/ppermute | solution.py:40
  29.5 3.6 %collective-permute-start.5 = (bf16[16,8192]{1,0:T(8,128)(2,1)S(1)}, bf16[16,8192]{1,0:T(8,128)(2,1)S(1)}, u32[]{:S(2)}, u32[]{:S(2)}) collective-permute-start(bf16[16,8192]{1,0:T(8,128)(2,1)S(1)} %collective-permute-done.4), channel_id=1, source_target_pairs={{0,224},{2,226},{4,228},{6,230},{8,232},{10,234},{12,236},{14,238}... | collective-permute-start | bytes 786440 | tf_op jit(solution)/shard_map/ppermute | solution.py:44
  33.1 6.5 %collective-permute-done.8 = bf16[16,8192]{1,0:T(8,128)(2,1)S(1)} collective-permute-done((bf16[16,8192]{1,0:T(8,128)(2,1)S(1)}, bf16[16,8192]{1,0:T(8,128)(2,1)S(1)}, u32[]{:S(2)}, u32[]{:S(2)}) %collective-permute-start.8) | collective-permute-done | bytes 262176 | tf_op jit(solution)/shard_map/ppermute | solution.py:40
  39.6 3.2 %collective-permute-start.6 = (bf16[16,8192]{1,0:T(8,128)(2,1)S(1)}, bf16[16,8192]{1,0:T(8,128)(2,1)S(1)}, u32[]{:S(2)}, u32[]{:S(2)}) collective-permute-start(bf16[16,8192]{1,0:T(8,128)(2,1)S(1)} %collective-permute-done.5), channel_id=1, source_target_pairs={{0,224},{2,226},{4,228},{6,230},{8,232},{10,234},{12,236},{14,238}... | collective-permute-start | bytes 786440 | tf_op jit(solution)/shard_map/ppermute | solution.py:44
  42.8 6.7 %collective-permute-done.9 = bf16[16,8192]{1,0:T(8,128)(2,1)S(1)} collective-permute-done((bf16[16,8192]{1,0:T(8,128)(2,1)S(1)}, bf16[16,8192]{1,0:T(8,128)(2,1)S(1)}, u32[]{:S(2)}, u32[]{:S(2)}) %collective-permute-start.9) | collective-permute-done | bytes 262176 | tf_op jit(solution)/shard_map/ppermute | solution.py:40
  50.3 6.9 %collective-permute-done.10 = bf16[16,8192]{1,0:T(8,128)(2,1)} collective-permute-done((bf16[16,8192]{1,0:T(8,128)(2,1)S(1)}, bf16[16,8192]{1,0:T(8,128)(2,1)}, u32[]{:S(2)}, u32[]{:S(2)}) %collective-permute-start.10) | collective-permute-done | bytes 262176 | tf_op jit(solution)/shard_map/ppermute | solution.py:40
  57.2 4.3 %concatenate.21 = bf16[128,8192]{1,0:T(8,128)(2,1)S(1)} concatenate(bf16[2,8192]{1,0:T(2,128)(2,1)S(1)} %fusion.8, bf16[2,8192]{1,0:T(2,128)(2,1)S(1)} %collective-permute-done, bf16[4,8192]{1,0:T(4,128)(2,1)} %copy-done.8, bf16[4,8192]{1,0:T(4,128)(2,1)} %copy-done.9, bf16[4,8192]{1,0:T(4,128)(2,1)S(1)} %collective-permute-done.2, bf16[16,8192]{1,0:T(8,128)(2,1)S(1)} %collective-permute-done.4, ...), dimensions={0} | concatenate | bytes 4194304 | tf_op jit(solution)/shard_map/concatenate | solution.py:46
  66.9 4.6 %bitcast_multiply_fusion.2 = bf16[8192,256]{1,0:T(8,128)(2,1)} fusion(bf16[8192,256]{1,0:T(8,128)(2,1)} %param.10, bf16[64,256]{1,0:T(8,128)(2,1)} %bitcast.29), kind=kLoop, calls=%fused_computation.2 | loop fusion | flops 2097152 | bytes 8421376 | tf_op jit(solution)/shard_map/mul | solution.py:20
  77.5 19.7 %concatenate.22 = bf16[256,8192]{1,0:T(8,128)(2,1)} concatenate(bf16[2,8192]{1,0:T(2,128)(2,1)S(1)} %fusion.8, bf16[2,8192]{1,0:T(2,128)(2,1)S(1)} %collective-permute-done, bf16[4,8192]{1,0:T(4,128)(2,1)} %copy-done.8, bf16[4,8192]{1,0:T(4,128)(2,1)} %copy-done.9, bf16[4,8192]{1,0:T(4,128)(2,1)S(1)} %collective-permute-done.2, bf16[16,8192]{1,0:T(8,128)(2,1)S(1)} %collective-permute-done.4, ...), dimensions={0} | concatenate | bytes 8388608 | tf_op jit(solution)/shard_map/concatenate | solution.py:46
  97.2 4.8 %fusion.13 = f32[256,256]{1,0:T(8,128)S(1)} fusion(bf16[256,8192]{1,0:T(8,128)(2,1)} %concatenate.22, bf16[8192,256]{1,0:T(8,128)(2,1)} %bitcast_multiply_fusion.2), kind=kOutput, calls=%fused_computation.47 | convolution fusion | flops 1073741824 | bytes 8650752 | tf_op jit(solution)/shard_map/dot_general | solution.py:100
  117.5 6.6 %collective-permute-done.13 = f32[16,4096]{1,0:T(8,128)S(1)} collective-permute-done((f32[16,4096]{1,0:T(8,128)S(1)}, f32[16,4096]{1,0:T(8,128)S(1)}, u32[]{:S(2)}, u32[]{:S(2)}) %collective-permute-start.13) | collective-permute-done | bytes 262176 | tf_op jit(solution)/shard_map/ppermute | solution.py:61
  124.3 3.2 %collective-permute-start.17 = (f32[16,4096]{1,0:T(8,128)S(1)}, f32[16,4096]{1,0:T(8,128)S(1)}, u32[]{:S(2)}, u32[]{:S(2)}) collective-permute-start(f32[16,4096]{1,0:T(8,128)S(1)} %get-tuple-element.10), channel_id=1, source_target_pairs={{0,224},{2,226},{4,228},{6,230},{8,232},{10,234},{12,236},{14,238}... | collective-permute-start | bytes 786440 | tf_op jit(solution)/shard_map/ppermute | solution.py:69
  127.5 5.2 %collective-permute-done.25 = f32[32,4096]{1,0:T(8,128)S(1)} collective-permute-done((f32[32,4096]{1,0:T(8,128)S(1)}, f32[32,4096]{1,0:T(8,128)S(1)}, u32[]{:S(2)}, u32[]{:S(2)}) %collective-permute-start.25) | collective-permute-done | bytes 524320 | tf_op jit(solution)/shard_map/ppermute | solution.py:61
  132.8 3.2 %collective-permute-start.27 = (f32[32,4096]{1,0:T(8,128)S(1)}, f32[32,4096]{1,0:T(8,128)S(1)}, u32[]{:S(2)}, u32[]{:S(2)}) collective-permute-start(f32[32,4096]{1,0:T(8,128)S(1)} %get-tuple-element.12), channel_id=1, source_target_pairs={{0,12},{2,14},{4,0},{6,2},{8,4},{10,6},{12,8},{14,10},{16,28},{18,... | collective-permute-start | bytes 1572872 | tf_op jit(solution)/shard_map/ppermute | solution.py:69
  136.5 3.2 %collective-permute-start.18 = (f32[16,4096]{1,0:T(8,128)S(1)}, f32[16,4096]{1,0:T(8,128)S(1)}, u32[]{:S(2)}, u32[]{:S(2)}) collective-permute-start(f32[16,4096]{1,0:T(8,128)S(1)} %get-tuple-element.8), channel_id=1, source_target_pairs={{0,224},{2,226},{4,228},{6,230},{8,232},{10,234},{12,236},{14,238}... | collective-permute-start | bytes 786440 | tf_op jit(solution)/shard_map/ppermute | solution.py:69
  139.7 7.5 %collective-permute-done.26 = f32[32,4096]{1,0:T(8,128)S(1)} collective-permute-done((f32[32,4096]{1,0:T(8,128)S(1)}, f32[32,4096]{1,0:T(8,128)S(1)}, u32[]{:S(2)}, u32[]{:S(2)}) %collective-permute-start.26) | collective-permute-done | bytes 524320 | tf_op jit(solution)/shard_map/ppermute | solution.py:61
  147.6 3.3 %collective-permute-start.19 = (f32[16,4096]{1,0:T(8,128)S(1)}, f32[16,4096]{1,0:T(8,128)S(1)}, u32[]{:S(2)}, u32[]{:S(2)}) collective-permute-start(f32[16,4096]{1,0:T(8,128)S(1)} %get-tuple-element.6), channel_id=1, source_target_pairs={{0,224},{2,226},{4,228},{6,230},{8,232},{10,234},{12,236},{14,238}... | collective-permute-start | bytes 786440 | tf_op jit(solution)/shard_map/ppermute | solution.py:69
  153.8 3.2 %collective-permute-start.32 = (f32[4,4096]{1,0:T(4,128)S(1)}, f32[4,4096]{1,0:T(4,128)S(1)}, u32[]{:S(2)}, u32[]{:S(2)}) collective-permute-start(f32[4,4096]{1,0:T(4,128)S(1)} %get-tuple-element.18), channel_id=1, source_target_pairs={{0,224},{2,226},{4,228},{6,230},{8,232},{10,234},{12,236},{14,238}... | collective-permute-start | bytes 196616 | tf_op jit(solution)/shard_map/ppermute | solution.py:69
  159.5 3.1 %collective-permute-start.33 = (f32[4,4096]{1,0:T(4,128)S(1)}, f32[4,4096]{1,0:T(4,128)S(1)}, u32[]{:S(2)}, u32[]{:S(2)}) collective-permute-start(f32[4,4096]{1,0:T(4,128)S(1)} %get-tuple-element.16), channel_id=1, source_target_pairs={{0,224},{2,226},{4,228},{6,230},{8,232},{10,234},{12,236},{14,238}... | collective-permute-start | bytes 196616 | tf_op jit(solution)/shard_map/ppermute | solution.py:69
  163.3 3.2 %collective-permute-start.22 = (f32[4,4096]{1,0:T(4,128)S(1)}, f32[4,4096]{1,0:T(4,128)S(1)}, u32[]{:S(2)}, u32[]{:S(2)}) collective-permute-start(f32[4,4096]{1,0:T(4,128)S(1)} %get-tuple-element.20), channel_id=1, source_target_pairs={{0,12},{2,14},{4,0},{6,2},{8,4},{10,6},{12,8},{14,10},{16,28},{18,... | collective-permute-start | bytes 196616 | tf_op jit(solution)/shard_map/ppermute | solution.py:69
  175.5 2.8 %collective-permute-done.35 = f32[2,4096]{1,0:T(2,128)S(1)} collective-permute-done((f32[2,4096]{1,0:T(2,128)S(1)}, f32[2,4096]{1,0:T(2,128)S(1)}, u32[]{:S(2)}, u32[]{:S(2)}) %collective-permute-start.35) | collective-permute-done | bytes 32800 | tf_op jit(solution)/shard_map/ppermute | solution.py:61
  (123 shorter events, 56.2 us)
Async XLA Ops:
  18.7 10.8 %collective-permute-start.7 = (bf16[16,8192]{1,0:T(8,128)(2,1)S(1)}, bf16[16,8192]{1,0:T(8,128)(2,1)S(1)}, u32[]{:S(2)}, u32[]{:S(2)}) collective-permute-start(bf16[16,8192]{1,0:T(8,128)(2,1)S(1)} %concatenate.20), channel_id=1, source_target_pairs={{0,32},{2,34},{4,36},{6,38},{8,40},{10,42},{12,44},{14,46},{16,48}... | collective-permute-start | bytes 786440 | tf_op jit(solution)/shard_map/ppermute | solution.py:40
  20.7 8.8 %collective-permute-start.4 = (bf16[16,8192]{1,0:T(8,128)(2,1)S(1)}, bf16[16,8192]{1,0:T(8,128)(2,1)S(1)}, u32[]{:S(2)}, u32[]{:S(2)}) collective-permute-start(bf16[16,8192]{1,0:T(8,128)(2,1)S(1)} %concatenate.20), channel_id=1, source_target_pairs={{0,224},{2,226},{4,228},{6,230},{8,232},{10,234},{12,236},{14,238}... | collective-permute-start | bytes 786440 | tf_op jit(solution)/shard_map/ppermute | solution.py:44
  29.5 10.1 %collective-permute-start.8 = (bf16[16,8192]{1,0:T(8,128)(2,1)S(1)}, bf16[16,8192]{1,0:T(8,128)(2,1)S(1)}, u32[]{:S(2)}, u32[]{:S(2)}) collective-permute-start(bf16[16,8192]{1,0:T(8,128)(2,1)S(1)} %collective-permute-done.7), channel_id=1, source_target_pairs={{0,32},{2,34},{4,36},{6,38},{8,40},{10,42},{12,44},{14,46},{16,48}... | collective-permute-start | bytes 786440 | tf_op jit(solution)/shard_map/ppermute | solution.py:40
  29.5 10.1 %collective-permute-start.5 = (bf16[16,8192]{1,0:T(8,128)(2,1)S(1)}, bf16[16,8192]{1,0:T(8,128)(2,1)S(1)}, u32[]{:S(2)}, u32[]{:S(2)}) collective-permute-start(bf16[16,8192]{1,0:T(8,128)(2,1)S(1)} %collective-permute-done.4), channel_id=1, source_target_pairs={{0,224},{2,226},{4,228},{6,230},{8,232},{10,234},{12,236},{14,238}... | collective-permute-start | bytes 786440 | tf_op jit(solution)/shard_map/ppermute | solution.py:44
  39.6 9.9 %collective-permute-start.9 = (bf16[16,8192]{1,0:T(8,128)(2,1)S(1)}, bf16[16,8192]{1,0:T(8,128)(2,1)S(1)}, u32[]{:S(2)}, u32[]{:S(2)}) collective-permute-start(bf16[16,8192]{1,0:T(8,128)(2,1)S(1)} %collective-permute-done.8), channel_id=1, source_target_pairs={{0,32},{2,34},{4,36},{6,38},{8,40},{10,42},{12,44},{14,46},{16,48}... | collective-permute-start | bytes 786440 | tf_op jit(solution)/shard_map/ppermute | solution.py:40
  39.6 9.9 %collective-permute-start.6 = (bf16[16,8192]{1,0:T(8,128)(2,1)S(1)}, bf16[16,8192]{1,0:T(8,128)(2,1)S(1)}, u32[]{:S(2)}, u32[]{:S(2)}) collective-permute-start(bf16[16,8192]{1,0:T(8,128)(2,1)S(1)} %collective-permute-done.5), channel_id=1, source_target_pairs={{0,224},{2,226},{4,228},{6,230},{8,232},{10,234},{12,236},{14,238}... | collective-permute-start | bytes 786440 | tf_op jit(solution)/shard_map/ppermute | solution.py:44
  49.5 7.7 %collective-permute-start.10 = (bf16[16,8192]{1,0:T(8,128)(2,1)S(1)}, bf16[16,8192]{1,0:T(8,128)(2,1)}, u32[]{:S(2)}, u32[]{:S(2)}) collective-permute-start(bf16[16,8192]{1,0:T(8,128)(2,1)S(1)} %collective-permute-done.9), channel_id=1, source_target_pairs={{0,32},{2,34},{4,36},{6,38},{8,40},{10,42},{12,44},{14,46},{16,48}... | collective-permute-start | bytes 786440 | tf_op jit(solution)/shard_map/ppermute | solution.py:40
  61.6 15.9 %collective-permute-start.11 = (bf16[128,8192]{1,0:T(8,128)(2,1)S(1)}, bf16[128,8192]{1,0:T(8,128)(2,1)}, u32[]{:S(2)}, u32[]{:S(2)}) collective-permute-start(bf16[128,8192]{1,0:T(8,128)(2,1)S(1)} %concatenate.21), channel_id=1, source_target_pairs={{0,2},{2,0},{4,6},{6,4},{8,10},{10,8},{12,14},{14,12},{16,18},{18,... | collective-permute-start | bytes 6291464 | tf_op jit(solution)/shard_map/ppermute | solution.py:40
  114.3 9.9 %collective-permute-start.13 = (f32[16,4096]{1,0:T(8,128)S(1)}, f32[16,4096]{1,0:T(8,128)S(1)}, u32[]{:S(2)}, u32[]{:S(2)}) collective-permute-start(f32[16,4096]{1,0:T(8,128)S(1)} %slice.140), channel_id=1, source_target_pairs={{0,32},{2,34},{4,36},{6,38},{8,40},{10,42},{12,44},{14,46},{16,48}... | collective-permute-start | bytes 786440 | tf_op jit(solution)/shard_map/ppermute | solution.py:61
  117.4 15.3 %collective-permute-start.25 = (f32[32,4096]{1,0:T(8,128)S(1)}, f32[32,4096]{1,0:T(8,128)S(1)}, u32[]{:S(2)}, u32[]{:S(2)}) collective-permute-start(f32[32,4096]{1,0:T(8,128)S(1)} %slice.157), channel_id=1, source_target_pairs={{0,4},{2,6},{4,8},{6,10},{8,12},{10,14},{12,0},{14,2},{16,20},{18,... | collective-permute-start | bytes 1572872 | tf_op jit(solution)/shard_map/ppermute | solution.py:61
  124.2 11.9 %collective-permute-start.14 = (f32[16,4096]{1,0:T(8,128)S(1)}, f32[16,4096]{1,0:T(8,128)S(1)}, u32[]{:S(2)}, u32[]{:S(2)}) collective-permute-start(f32[16,4096]{1,0:T(8,128)S(1)} %get-tuple-element.9), channel_id=1, source_target_pairs={{0,32},{2,34},{4,36},{6,38},{8,40},{10,42},{12,44},{14,46},{16,48}... | collective-permute-start | bytes 786440 | tf_op jit(solution)/shard_map/ppermute | solution.py:61
  124.3 11.8 %collective-permute-start.17 = (f32[16,4096]{1,0:T(8,128)S(1)}, f32[16,4096]{1,0:T(8,128)S(1)}, u32[]{:S(2)}, u32[]{:S(2)}) collective-permute-start(f32[16,4096]{1,0:T(8,128)S(1)} %get-tuple-element.10), channel_id=1, source_target_pairs={{0,224},{2,226},{4,228},{6,230},{8,232},{10,234},{12,236},{14,238}... | collective-permute-start | bytes 786440 | tf_op jit(solution)/shard_map/ppermute | solution.py:69
  132.8 14.4 %collective-permute-start.26 = (f32[32,4096]{1,0:T(8,128)S(1)}, f32[32,4096]{1,0:T(8,128)S(1)}, u32[]{:S(2)}, u32[]{:S(2)}) collective-permute-start(f32[32,4096]{1,0:T(8,128)S(1)} %get-tuple-element.11), channel_id=1, source_target_pairs={{0,4},{2,6},{4,8},{6,10},{8,12},{10,14},{12,0},{14,2},{16,20},{18,... | collective-permute-start | bytes 1572872 | tf_op jit(solution)/shard_map/ppermute | solution.py:61
  132.8 14.3 %collective-permute-start.27 = (f32[32,4096]{1,0:T(8,128)S(1)}, f32[32,4096]{1,0:T(8,128)S(1)}, u32[]{:S(2)}, u32[]{:S(2)}) collective-permute-start(f32[32,4096]{1,0:T(8,128)S(1)} %get-tuple-element.12), channel_id=1, source_target_pairs={{0,12},{2,14},{4,0},{6,2},{8,4},{10,6},{12,8},{14,10},{16,28},{18,... | collective-permute-start | bytes 1572872 | tf_op jit(solution)/shard_map/ppermute | solution.py:69
  136.1 11.3 %collective-permute-start.15 = (f32[16,4096]{1,0:T(8,128)S(1)}, f32[16,4096]{1,0:T(8,128)S(1)}, u32[]{:S(2)}, u32[]{:S(2)}) collective-permute-start(f32[16,4096]{1,0:T(8,128)S(1)} %get-tuple-element.7), channel_id=1, source_target_pairs={{0,32},{2,34},{4,36},{6,38},{8,40},{10,42},{12,44},{14,46},{16,48}... | collective-permute-start | bytes 786440 | tf_op jit(solution)/shard_map/ppermute | solution.py:61
  136.5 11.0 %collective-permute-start.18 = (f32[16,4096]{1,0:T(8,128)S(1)}, f32[16,4096]{1,0:T(8,128)S(1)}, u32[]{:S(2)}, u32[]{:S(2)}) collective-permute-start(f32[16,4096]{1,0:T(8,128)S(1)} %get-tuple-element.8), channel_id=1, source_target_pairs={{0,224},{2,226},{4,228},{6,230},{8,232},{10,234},{12,236},{14,238}... | collective-permute-start | bytes 786440 | tf_op jit(solution)/shard_map/ppermute | solution.py:69
  147.3 6.3 %collective-permute-start.28 = (f32[4,4096]{1,0:T(4,128)S(1)}, f32[4,4096]{1,0:T(4,128)S(1)}, u32[]{:S(2)}, u32[]{:S(2)}) collective-permute-start(f32[4,4096]{1,0:T(4,128)S(1)} %slice.161), channel_id=1, source_target_pairs={{0,32},{2,34},{4,36},{6,38},{8,40},{10,42},{12,44},{14,46},{16,48}... | collective-permute-start | bytes 196616 | tf_op jit(solution)/shard_map/ppermute | solution.py:61
  147.5 9.8 %collective-permute-start.16 = (f32[16,4096]{1,0:T(8,128)S(1)}, f32[16,4096]{1,0:T(8,128)S(1)}, u32[]{:S(2)}, u32[]{:S(2)}) collective-permute-start(f32[16,4096]{1,0:T(8,128)S(1)} %get-tuple-element.5), channel_id=1, source_target_pairs={{0,32},{2,34},{4,36},{6,38},{8,40},{10,42},{12,44},{14,46},{16,48}... | collective-permute-start | bytes 786440 | tf_op jit(solution)/shard_map/ppermute | solution.py:61
  147.6 9.7 %collective-permute-start.19 = (f32[16,4096]{1,0:T(8,128)S(1)}, f32[16,4096]{1,0:T(8,128)S(1)}, u32[]{:S(2)}, u32[]{:S(2)}) collective-permute-start(f32[16,4096]{1,0:T(8,128)S(1)} %get-tuple-element.6), channel_id=1, source_target_pairs={{0,224},{2,226},{4,228},{6,230},{8,232},{10,234},{12,236},{14,238}... | collective-permute-start | bytes 786440 | tf_op jit(solution)/shard_map/ppermute | solution.py:69
  157.4 5.8 %collective-permute-start.20 = (f32[4,4096]{1,0:T(4,128)S(1)}, f32[4,4096]{1,0:T(4,128)S(1)}, u32[]{:S(2)}, u32[]{:S(2)}) collective-permute-start(f32[4,4096]{1,0:T(4,128)S(1)} %slice.148), channel_id=1, source_target_pairs={{0,4},{2,6},{4,8},{6,10},{8,12},{10,14},{12,0},{14,2},{16,20},{18,... | collective-permute-start | bytes 196616 | tf_op jit(solution)/shard_map/ppermute | solution.py:61
  159.3 7.3 %collective-permute-start.30 = (f32[4,4096]{1,0:T(4,128)S(1)}, f32[4,4096]{1,0:T(4,128)S(1)}, u32[]{:S(2)}, u32[]{:S(2)}) collective-permute-start(f32[4,4096]{1,0:T(4,128)S(1)} %get-tuple-element.15), channel_id=1, source_target_pairs={{0,32},{2,34},{4,36},{6,38},{8,40},{10,42},{12,44},{14,46},{16,48}... | collective-permute-start | bytes 196616 | tf_op jit(solution)/shard_map/ppermute | solution.py:61
  159.5 7.0 %collective-permute-start.33 = (f32[4,4096]{1,0:T(4,128)S(1)}, f32[4,4096]{1,0:T(4,128)S(1)}, u32[]{:S(2)}, u32[]{:S(2)}) collective-permute-start(f32[4,4096]{1,0:T(4,128)S(1)} %get-tuple-element.16), channel_id=1, source_target_pairs={{0,224},{2,226},{4,228},{6,230},{8,232},{10,234},{12,236},{14,238}... | collective-permute-start | bytes 196616 | tf_op jit(solution)/shard_map/ppermute | solution.py:69
  163.2 6.7 %collective-permute-start.21 = (f32[4,4096]{1,0:T(4,128)S(1)}, f32[4,4096]{1,0:T(4,128)S(1)}, u32[]{:S(2)}, u32[]{:S(2)}) collective-permute-start(f32[4,4096]{1,0:T(4,128)S(1)} %get-tuple-element.19), channel_id=1, source_target_pairs={{0,4},{2,6},{4,8},{6,10},{8,12},{10,14},{12,0},{14,2},{16,20},{18,... | collective-permute-start | bytes 196616 | tf_op jit(solution)/shard_map/ppermute | solution.py:61
  163.3 6.6 %collective-permute-start.22 = (f32[4,4096]{1,0:T(4,128)S(1)}, f32[4,4096]{1,0:T(4,128)S(1)}, u32[]{:S(2)}, u32[]{:S(2)}) collective-permute-start(f32[4,4096]{1,0:T(4,128)S(1)} %get-tuple-element.20), channel_id=1, source_target_pairs={{0,12},{2,14},{4,0},{6,2},{8,4},{10,6},{12,8},{14,10},{16,28},{18,... | collective-permute-start | bytes 196616 | tf_op jit(solution)/shard_map/ppermute | solution.py:69
  (23 other events, 218.4 us)
where the time goes:
time: 180 us; the launch traced here: 179 us
  waiting for transfers between devices  67.7 us (38%)
  starting transfers between devices  51.2 us (28%)
  local copies, waits for them, and re-layouts  34.7 us (19%)
  other arithmetic  15.5 us (9%)
  matrix products  9.26 us (5%)
    ppermute x8, waiting for transfers between devices, _ag_stage(): cur = lax.ppermute(cur, 'blk', _perm(axis, 1, size))  35.5 us
    ppermute x16, waiting for transfers between devices, _rs_stage(): recv = lax.ppermute(buf, 'blk', _perm(axis, 1, size))  31.7 us
    concatenate x3, local copies, waits for them, and re-layouts, _ag_stage(): return jnp.concatenate(got, axis=0)  24.2 us
    ppermute x8, starting transfers between devices, _rs_stage(): recv = lax.ppermute(buf, 'blk', _perm(axis, -1, size))  24 us
    ppermute x4, starting transfers between devices, _ag_stage(): cur = lax.ppermute(cur, 'blk', _perm(axis, -1, size))  12.5 us
    mul x3, other arithmetic, mask_blocks(): return (shaped * cols[:, None, :]).reshape(height, width)  9.32 us
    ppermute x16, starting transfers between devices, _rs_stage(): recv = lax.ppermute(buf, 'blk', _perm(axis, 1, size))  8.18 us
    unnamed x26, local copies, waits for them, and re-layouts  6.78 us
  transfers between devices with their start and end apart: 36, of which 19 were waited for; matrix products, arithmetic and copies ran while one was open for 10% of the time, Pallas kernels for 0%

commit v1 on v0

--- a/solution.py
+++ b/solution.py
@@ -95,10 +95,21 @@
 
     base = tuple(reversed(AG_ORDER))
     piece = normed
-    for axis in AG_ORDER:
+    for i, axis in enumerate(AG_ORDER[:-1]):
         piece = _ag_stage(piece, axis, size)
-    gate = jnp.dot(piece, gate_kept, preferred_element_type=jnp.float32)
-    up_val = jnp.dot(piece, up_kept, preferred_element_type=jnp.float32)
+        if i == 0:
+            piece, gate_kept, up_kept, down_kept = lax.optimization_barrier(
+                (piece, gate_kept, up_kept, down_kept))
+        else:
+            piece = lax.optimization_barrier(piece)
+    last = AG_ORDER[-1]
+    _, n_last = BLK_AXES[last]
+    assert n_last == 2
+    blocks = [piece, lax.ppermute(piece, "blk", _perm(last, 1, size))]
+    gate = jnp.concatenate(
+        [jnp.dot(b, gate_kept, preferred_element_type=jnp.float32) for b in blocks], axis=0)
+    up_val = jnp.concatenate(
+        [jnp.dot(b, up_kept, preferred_element_type=jnp.float32) for b in blocks], axis=0)
     hidden = (jax.nn.silu(gate) * up_val).astype(jnp.bfloat16)
 
     outs = []

time: 180 us -> 146 us (0.81)
  local copies, waits for them, and re-layouts: 34.7 us -> 5.31 us
  matrix products: 9.26 us -> 6.08 us
    concatenate x3 -> x1, local copies, waits for them, and re-layouts: 24.2 us -> 0.02 us  [_ag_stage(): return jnp.concatenate(got, axis=0)]
    ppermute x8 -> x7, waiting for transfers between devices: 35.5 us -> 25.7 us  [_ag_stage(): cur = lax.ppermute(cur, 'blk', _perm(axis, 1, size))]
    ppermute x4, waiting for transfers between devices: 0.01 us -> 8.58 us  [_ag_stage(): cur = lax.ppermute(cur, 'blk', _perm(axis, -1, size))]
    unnamed x26 -> x17, local copies, waits for them, and re-layouts: 6.78 us -> 2.43 us
    ppermute x16, starting transfers between devices: 8.18 us -> 4.62 us  [_rs_stage(): recv = lax.ppermute(buf, 'blk', _perm(axis, 1, size))]
    dot_general x2 -> x4, matrix products: 6.09 us -> 3.03 us  [the longest x2 1.52 us: local(): jnp.dot(b, up_kept, preferred_element_type=jnp.float32)]
    ppermute x0 -> x1, waiting for transfers between devices: none -> 2.61 us  [local(): blocks = [piece, lax.ppermute(piece, 'blk', _perm(last, 1, size))]]
    ppermute x4, starting transfers between devices: 12.5 us -> 15 us  [_ag_stage(): cur = lax.ppermute(cur, 'blk', _perm(axis, -1, size))]
  transfers between devices with their start and end apart: 36 -> 36, of which waited for: 19 -> 21; matrix products, arithmetic and copies ran while one was open for 10% -> 12% of each run, Pallas kernels for 0% -> 0%
where the time goes in v1:
time: 146 us; the launch traced here: 145 us
  waiting for transfers between devices  69.1 us (47%)
  starting transfers between devices  50 us (34%)
  other arithmetic  14.3 us (10%)
  matrix products  6.08 us (4%)
  local copies, waits for them, and re-layouts  5.31 us (4%)
    ppermute x16, waiting for transfers between devices, _rs_stage(): recv = lax.ppermute(buf, 'blk', _perm(axis, 1, size))  32.3 us
    ppermute x8, starting transfers between devices, _rs_stage(): recv = lax.ppermute(buf, 'blk', _perm(axis, -1, size))  25.9 us
    ppermute x7, waiting for transfers between devices, _ag_stage(): cur = lax.ppermute(cur, 'blk', _perm(axis, 1, size))  25.7 us
    ppermute x4, starting transfers between devices, _ag_stage(): cur = lax.ppermute(cur, 'blk', _perm(axis, -1, size))  15 us
    ppermute x4, waiting for transfers between devices, _ag_stage(): cur = lax.ppermute(cur, 'blk', _perm(axis, -1, size))  8.58 us
    mul x2, other arithmetic, mask_blocks(): return (shaped * cols[:, None, :]).reshape(height, width)  8.01 us
    ppermute x16, starting transfers between devices, _rs_stage(): recv = lax.ppermute(buf, 'blk', _perm(axis, 1, size))  4.62 us
    ppermute x7, starting transfers between devices, _ag_stage(): cur = lax.ppermute(cur, 'blk', _perm(axis, 1, size))  4.24 us
  transfers between devices with their start and end apart: 36, of which 21 were waited for; matrix products, arithmetic and copies ran while one was open for 12% of the time, Pallas kernels for 0%

profile of v1, /device:TPU:2, one launch (start us, length us, event | category | flops | bytes accessed | tf_op | source)
XLA Modules:
  0.0 145.4 jit_solution(17384618056189416044)
XLA Ops:
  6.8 2.5 %bitcast_multiply_fusion = bf16[256,8192]{1,0:T(8,128)(2,1)S(1)} fusion(bf16[256,8192]{1,0:T(8,128)(2,1)} %param.12, bf16[2,8192]{1,0:T(2,128)(2,1)S(1)} %bitcast.32), kind=kLoop, calls=%fused_computation | loop fusion | flops 2097152 | bytes 8421376 | tf_op jit(solution)/shard_map/mul | solution.py:20
  9.3 5.5 %bitcast_multiply_fusion.1 = (bf16[8192,256]{1,0:T(8,128)(2,1)S(1)}, bf16[8192,256]{1,0:T(8,128)(2,1)S(1)}) fusion(bf16[8192,256]{1,0:T(8,128)(2,1)} %param.11, bf16[64,256]{1,0:T(8,128)(2,1)S(1)} %bitcast.30, bf16[8192,256]{1,0:T(8,128)(2,1)} %param.10, bf16[64,256]{1,0:T(8,128)(2,1)S(1)} %bitcast.31), kind=kLoop, calls=%fused_computation.1 | loop fusion | flops 4194304 | bytes 16842752 | tf_op jit(solution)/shard_map/mul | solution.py:20
  20.8 5.1 %collective-permute-done.3 = bf16[4,8192]{1,0:T(4,128)(2,1)S(1)} collective-permute-done((bf16[4,8192]{1,0:T(4,128)(2,1)S(1)}, bf16[4,8192]{1,0:T(4,128)(2,1)S(1)}, u32[]{:S(2)}, u32[]{:S(2)}) %collective-permute-start.3) | collective-permute-done | bytes 65568 | tf_op jit(solution)/shard_map/ppermute | solution.py:40
  26.1 5.9 %collective-permute-start.4 = (bf16[16,8192]{1,0:T(8,128)(2,1)S(1)}, bf16[16,8192]{1,0:T(8,128)(2,1)S(1)}, u32[]{:S(2)}, u32[]{:S(2)}) collective-permute-start(bf16[16,8192]{1,0:T(8,128)(2,1)S(1)} %pad_maximum_fusion), channel_id=1, source_target_pairs={{0,224},{2,226},{4,228},{6,230},{8,232},{10,234},{12,236},{14,238}... | collective-permute-start | bytes 786440 | tf_op jit(solution)/shard_map/ppermute | solution.py:44
  32.0 3.9 %collective-permute-done.4 = bf16[16,8192]{1,0:T(8,128)(2,1)S(1)} collective-permute-done((bf16[16,8192]{1,0:T(8,128)(2,1)S(1)}, bf16[16,8192]{1,0:T(8,128)(2,1)S(1)}, u32[]{:S(2)}, u32[]{:S(2)}) %collective-permute-start.4) | collective-permute-done | bytes 262176 | tf_op jit(solution)/shard_map/ppermute | solution.py:44
  35.9 3.7 %collective-permute-start.5 = (bf16[16,8192]{1,0:T(8,128)(2,1)S(1)}, bf16[16,8192]{1,0:T(8,128)(2,1)S(1)}, u32[]{:S(2)}, u32[]{:S(2)}) collective-permute-start(bf16[16,8192]{1,0:T(8,128)(2,1)S(1)} %collective-permute-done.4), channel_id=1, source_target_pairs={{0,224},{2,226},{4,228},{6,230},{8,232},{10,234},{12,236},{14,238}... | collective-permute-start | bytes 786440 | tf_op jit(solution)/shard_map/ppermute | solution.py:44
  39.9 4.7 %collective-permute-done.5 = bf16[16,8192]{1,0:T(8,128)(2,1)S(1)} collective-permute-done((bf16[16,8192]{1,0:T(8,128)(2,1)S(1)}, bf16[16,8192]{1,0:T(8,128)(2,1)S(1)}, u32[]{:S(2)}, u32[]{:S(2)}) %collective-permute-start.5) | collective-permute-done | bytes 262176 | tf_op jit(solution)/shard_map/ppermute | solution.py:44
  44.6 3.7 %collective-permute-start.6 = (bf16[16,8192]{1,0:T(8,128)(2,1)S(1)}, bf16[16,8192]{1,0:T(8,128)(2,1)S(1)}, u32[]{:S(2)}, u32[]{:S(2)}) collective-permute-start(bf16[16,8192]{1,0:T(8,128)(2,1)S(1)} %collective-permute-done.5), channel_id=1, source_target_pairs={{0,224},{2,226},{4,228},{6,230},{8,232},{10,234},{12,236},{14,238}... | collective-permute-start | bytes 786440 | tf_op jit(solution)/shard_map/ppermute | solution.py:44
  48.8 10.0 %collective-permute-done.9 = bf16[16,8192]{1,0:T(8,128)(2,1)S(1)} collective-permute-done((bf16[16,8192]{1,0:T(8,128)(2,1)S(1)}, bf16[16,8192]{1,0:T(8,128)(2,1)S(1)}, u32[]{:S(2)}, u32[]{:S(2)}) %collective-permute-start.9) | collective-permute-done | bytes 262176 | tf_op jit(solution)/shard_map/ppermute | solution.py:40
  58.8 7.6 %collective-permute-done.10 = bf16[16,8192]{1,0:T(8,128)(2,1)S(1)} collective-permute-done((bf16[16,8192]{1,0:T(8,128)(2,1)S(1)}, bf16[16,8192]{1,0:T(8,128)(2,1)S(1)}, u32[]{:S(2)}, u32[]{:S(2)}) %collective-permute-start.10) | collective-permute-done | bytes 262176 | tf_op jit(solution)/shard_map/ppermute | solution.py:40
  68.3 2.6 %collective-permute-done.11 = bf16[128,8192]{1,0:T(8,128)(2,1)S(1)} collective-permute-done((bf16[128,8192]{1,0:T(8,128)(2,1)S(1)}, bf16[128,8192]{1,0:T(8,128)(2,1)S(1)}, u32[]{:S(2)}, u32[]{:S(2)}) %collective-permute-start.11) | collective-permute-done | bytes 2097184 | tf_op jit(solution)/shard_map/ppermute | solution.py:108
  76.9 2.3 %fusion = f32[256,4096]{1,0:T(8,128)S(1)} fusion(bf16[256,256]{1,0:T(8,128)(2,1)S(1)} %reshape.27, bf16[256,8192]{1,0:T(8,128)(2,1)} %copy-done), kind=kOutput, calls=%fused_computation.5 | convolution fusion | flops 536870912 | bytes 6422528 | tf_op jit(solution)/shard_map/dot_general | solution.py:120
  84.0 7.5 %collective-permute-done.13 = f32[16,4096]{1,0:T(8,128)S(1)} collective-permute-done((f32[16,4096]{1,0:T(8,128)S(1)}, f32[16,4096]{1,0:T(8,128)S(1)}, u32[]{:S(2)}, u32[]{:S(2)}) %collective-permute-start.13) | collective-permute-done | bytes 262176 | tf_op jit(solution)/shard_map/ppermute | solution.py:61
  91.7 3.2 %collective-permute-start.17 = (f32[16,4096]{1,0:T(8,128)S(1)}, f32[16,4096]{1,0:T(8,128)S(1)}, u32[]{:S(2)}, u32[]{:S(2)}) collective-permute-start(f32[16,4096]{1,0:T(8,128)S(1)} %get-tuple-element.18), channel_id=1, source_target_pairs={{0,224},{2,226},{4,228},{6,230},{8,232},{10,234},{12,236},{14,238}... | collective-permute-start | bytes 786440 | tf_op jit(solution)/shard_map/ppermute | solution.py:69
  94.9 4.5 %collective-permute-done.25 = f32[32,4096]{1,0:T(8,128)S(1)} collective-permute-done((f32[32,4096]{1,0:T(8,128)S(1)}, f32[32,4096]{1,0:T(8,128)S(1)}, u32[]{:S(2)}, u32[]{:S(2)}) %collective-permute-start.25) | collective-permute-done | bytes 524320 | tf_op jit(solution)/shard_map/ppermute | solution.py:61
  99.6 3.2 %collective-permute-start.27 = (f32[32,4096]{1,0:T(8,128)S(1)}, f32[32,4096]{1,0:T(8,128)S(1)}, u32[]{:S(2)}, u32[]{:S(2)}) collective-permute-start(f32[32,4096]{1,0:T(8,128)S(1)} %get-tuple-element.20), channel_id=1, source_target_pairs={{0,12},{2,14},{4,0},{6,2},{8,4},{10,6},{12,8},{14,10},{16,28},{18,... | collective-permute-start | bytes 1572872 | tf_op jit(solution)/shard_map/ppermute | solution.py:69
  103.0 3.2 %collective-permute-start.18 = (f32[16,4096]{1,0:T(8,128)S(1)}, f32[16,4096]{1,0:T(8,128)S(1)}, u32[]{:S(2)}, u32[]{:S(2)}) collective-permute-start(f32[16,4096]{1,0:T(8,128)S(1)} %get-tuple-element.16), channel_id=1, source_target_pairs={{0,224},{2,226},{4,228},{6,230},{8,232},{10,234},{12,236},{14,238}... | collective-permute-start | bytes 786440 | tf_op jit(solution)/shard_map/ppermute | solution.py:69
  106.2 8.0 %collective-permute-done.26 = f32[32,4096]{1,0:T(8,128)S(1)} collective-permute-done((f32[32,4096]{1,0:T(8,128)S(1)}, f32[32,4096]{1,0:T(8,128)S(1)}, u32[]{:S(2)}, u32[]{:S(2)}) %collective-permute-start.26) | collective-permute-done | bytes 524320 | tf_op jit(solution)/shard_map/ppermute | solution.py:61
  114.6 3.3 %collective-permute-start.19 = (f32[16,4096]{1,0:T(8,128)S(1)}, f32[16,4096]{1,0:T(8,128)S(1)}, u32[]{:S(2)}, u32[]{:S(2)}) collective-permute-start(f32[16,4096]{1,0:T(8,128)S(1)} %get-tuple-element.14), channel_id=1, source_target_pairs={{0,224},{2,226},{4,228},{6,230},{8,232},{10,234},{12,236},{14,238}... | collective-permute-start | bytes 786440 | tf_op jit(solution)/shard_map/ppermute | solution.py:69
  117.9 2.8 %collective-permute-done.28 = f32[4,4096]{1,0:T(4,128)S(1)} collective-permute-done((f32[4,4096]{1,0:T(4,128)S(1)}, f32[4,4096]{1,0:T(4,128)S(1)}, u32[]{:S(2)}, u32[]{:S(2)}) %collective-permute-start.28) | collective-permute-done | bytes 65568 | tf_op jit(solution)/shard_map/ppermute | solution.py:61
  120.8 3.2 %collective-permute-start.32 = (f32[4,4096]{1,0:T(4,128)S(1)}, f32[4,4096]{1,0:T(4,128)S(1)}, u32[]{:S(2)}, u32[]{:S(2)}) collective-permute-start(f32[4,4096]{1,0:T(4,128)S(1)} %get-tuple-element.26), channel_id=1, source_target_pairs={{0,224},{2,226},{4,228},{6,230},{8,232},{10,234},{12,236},{14,238}... | collective-permute-start | bytes 196616 | tf_op jit(solution)/shard_map/ppermute | solution.py:69
  126.4 3.3 %collective-permute-start.33 = (f32[4,4096]{1,0:T(4,128)S(1)}, f32[4,4096]{1,0:T(4,128)S(1)}, u32[]{:S(2)}, u32[]{:S(2)}) collective-permute-start(f32[4,4096]{1,0:T(4,128)S(1)} %get-tuple-element.24), channel_id=1, source_target_pairs={{0,224},{2,226},{4,228},{6,230},{8,232},{10,234},{12,236},{14,238}... | collective-permute-start | bytes 196616 | tf_op jit(solution)/shard_map/ppermute | solution.py:69
  130.3 3.2 %collective-permute-start.22 = (f32[4,4096]{1,0:T(4,128)S(1)}, f32[4,4096]{1,0:T(4,128)S(1)}, u32[]{:S(2)}, u32[]{:S(2)}) collective-permute-start(f32[4,4096]{1,0:T(4,128)S(1)} %get-tuple-element.28), channel_id=1, source_target_pairs={{0,12},{2,14},{4,0},{6,2},{8,4},{10,6},{12,8},{14,10},{16,28},{18,... | collective-permute-start | bytes 196616 | tf_op jit(solution)/shard_map/ppermute | solution.py:69
  133.7 3.2 %collective-permute-start.34 = (f32[4,4096]{1,0:T(4,128)S(1)}, f32[4,4096]{1,0:T(4,128)S(1)}, u32[]{:S(2)}, u32[]{:S(2)}) collective-permute-start(f32[4,4096]{1,0:T(4,128)S(1)} %get-tuple-element.22), channel_id=1, source_target_pairs={{0,224},{2,226},{4,228},{6,230},{8,232},{10,234},{12,236},{14,238}... | collective-permute-start | bytes 196616 | tf_op jit(solution)/shard_map/ppermute | solution.py:69
  (118 shorter events, 38.7 us)
Async XLA Ops:
  1.8 13.0 %collective-permute-start = (bf16[2,8192]{1,0:T(2,128)(2,1)S(1)}, bf16[2,8192]{1,0:T(2,128)(2,1)S(1)}, u32[]{:S(2)}, u32[]{:S(2)}) collective-permute-start(bf16[2,8192]{1,0:T(2,128)(2,1)S(1)} %fusion.11), channel_id=1, source_target_pairs={{0,16},{2,18},{4,20},{6,22},{8,24},{10,26},{12,28},{14,30},{16,0},... | collective-permute-start | bytes 98312 | tf_op jit(solution)/shard_map/ppermute | solution.py:40
  26.1 9.8 %collective-permute-start.4 = (bf16[16,8192]{1,0:T(8,128)(2,1)S(1)}, bf16[16,8192]{1,0:T(8,128)(2,1)S(1)}, u32[]{:S(2)}, u32[]{:S(2)}) collective-permute-start(bf16[16,8192]{1,0:T(8,128)(2,1)S(1)} %pad_maximum_fusion), channel_id=1, source_target_pairs={{0,224},{2,226},{4,228},{6,230},{8,232},{10,234},{12,236},{14,238}... | collective-permute-start | bytes 786440 | tf_op jit(solution)/shard_map/ppermute | solution.py:44
  32.0 7.8 %collective-permute-start.7 = (bf16[16,8192]{1,0:T(8,128)(2,1)S(1)}, bf16[16,8192]{1,0:T(8,128)(2,1)S(1)}, u32[]{:S(2)}, u32[]{:S(2)}) collective-permute-start(bf16[16,8192]{1,0:T(8,128)(2,1)S(1)} %pad_maximum_fusion), channel_id=1, source_target_pairs={{0,32},{2,34},{4,36},{6,38},{8,40},{10,42},{12,44},{14,46},{16,48}... | collective-permute-start | bytes 786440 | tf_op jit(solution)/shard_map/ppermute | solution.py:40
  35.9 8.7 %collective-permute-start.5 = (bf16[16,8192]{1,0:T(8,128)(2,1)S(1)}, bf16[16,8192]{1,0:T(8,128)(2,1)S(1)}, u32[]{:S(2)}, u32[]{:S(2)}) collective-permute-start(bf16[16,8192]{1,0:T(8,128)(2,1)S(1)} %collective-permute-done.4), channel_id=1, source_target_pairs={{0,224},{2,226},{4,228},{6,230},{8,232},{10,234},{12,236},{14,238}... | collective-permute-start | bytes 786440 | tf_op jit(solution)/shard_map/ppermute | solution.py:44
  39.8 8.9 %collective-permute-start.8 = (bf16[16,8192]{1,0:T(8,128)(2,1)S(1)}, bf16[16,8192]{1,0:T(8,128)(2,1)S(1)}, u32[]{:S(2)}, u32[]{:S(2)}) collective-permute-start(bf16[16,8192]{1,0:T(8,128)(2,1)S(1)} %collective-permute-done.7), channel_id=1, source_target_pairs={{0,32},{2,34},{4,36},{6,38},{8,40},{10,42},{12,44},{14,46},{16,48}... | collective-permute-start | bytes 786440 | tf_op jit(solution)/shard_map/ppermute | solution.py:40
  44.6 14.2 %collective-permute-start.6 = (bf16[16,8192]{1,0:T(8,128)(2,1)S(1)}, bf16[16,8192]{1,0:T(8,128)(2,1)S(1)}, u32[]{:S(2)}, u32[]{:S(2)}) collective-permute-start(bf16[16,8192]{1,0:T(8,128)(2,1)S(1)} %collective-permute-done.5), channel_id=1, source_target_pairs={{0,224},{2,226},{4,228},{6,230},{8,232},{10,234},{12,236},{14,238}... | collective-permute-start | bytes 786440 | tf_op jit(solution)/shard_map/ppermute | solution.py:44
  48.7 10.1 %collective-permute-start.9 = (bf16[16,8192]{1,0:T(8,128)(2,1)S(1)}, bf16[16,8192]{1,0:T(8,128)(2,1)S(1)}, u32[]{:S(2)}, u32[]{:S(2)}) collective-permute-start(bf16[16,8192]{1,0:T(8,128)(2,1)S(1)} %collective-permute-done.8), channel_id=1, source_target_pairs={{0,32},{2,34},{4,36},{6,38},{8,40},{10,42},{12,44},{14,46},{16,48}... | collective-permute-start | bytes 786440 | tf_op jit(solution)/shard_map/ppermute | solution.py:40
  58.8 7.6 %collective-permute-start.10 = (bf16[16,8192]{1,0:T(8,128)(2,1)S(1)}, bf16[16,8192]{1,0:T(8,128)(2,1)S(1)}, u32[]{:S(2)}, u32[]{:S(2)}) collective-permute-start(bf16[16,8192]{1,0:T(8,128)(2,1)S(1)} %collective-permute-done.9), channel_id=1, source_target_pairs={{0,32},{2,34},{4,36},{6,38},{8,40},{10,42},{12,44},{14,46},{16,48}... | collective-permute-start | bytes 786440 | tf_op jit(solution)/shard_map/ppermute | solution.py:40
  81.6 9.9 %collective-permute-start.13 = (f32[16,4096]{1,0:T(8,128)S(1)}, f32[16,4096]{1,0:T(8,128)S(1)}, u32[]{:S(2)}, u32[]{:S(2)}) collective-permute-start(f32[16,4096]{1,0:T(8,128)S(1)} %slice.139), channel_id=1, source_target_pairs={{0,32},{2,34},{4,36},{6,38},{8,40},{10,42},{12,44},{14,46},{16,48}... | collective-permute-start | bytes 786440 | tf_op jit(solution)/shard_map/ppermute | solution.py:61
  83.9 15.5 %collective-permute-start.25 = (f32[32,4096]{1,0:T(8,128)S(1)}, f32[32,4096]{1,0:T(8,128)S(1)}, u32[]{:S(2)}, u32[]{:S(2)}) collective-permute-start(f32[32,4096]{1,0:T(8,128)S(1)} %slice.155), channel_id=1, source_target_pairs={{0,4},{2,6},{4,8},{6,10},{8,12},{10,14},{12,0},{14,2},{16,20},{18,... | collective-permute-start | bytes 1572872 | tf_op jit(solution)/shard_map/ppermute | solution.py:61
  91.6 11.3 %collective-permute-start.14 = (f32[16,4096]{1,0:T(8,128)S(1)}, f32[16,4096]{1,0:T(8,128)S(1)}, u32[]{:S(2)}, u32[]{:S(2)}) collective-permute-start(f32[16,4096]{1,0:T(8,128)S(1)} %get-tuple-element.17), channel_id=1, source_target_pairs={{0,32},{2,34},{4,36},{6,38},{8,40},{10,42},{12,44},{14,46},{16,48}... | collective-permute-start | bytes 786440 | tf_op jit(solution)/shard_map/ppermute | solution.py:61
  91.7 11.2 %collective-permute-start.17 = (f32[16,4096]{1,0:T(8,128)S(1)}, f32[16,4096]{1,0:T(8,128)S(1)}, u32[]{:S(2)}, u32[]{:S(2)}) collective-permute-start(f32[16,4096]{1,0:T(8,128)S(1)} %get-tuple-element.18), channel_id=1, source_target_pairs={{0,224},{2,226},{4,228},{6,230},{8,232},{10,234},{12,236},{14,238}... | collective-permute-start | bytes 786440 | tf_op jit(solution)/shard_map/ppermute | solution.py:69
  99.5 14.7 %collective-permute-start.26 = (f32[32,4096]{1,0:T(8,128)S(1)}, f32[32,4096]{1,0:T(8,128)S(1)}, u32[]{:S(2)}, u32[]{:S(2)}) collective-permute-start(f32[32,4096]{1,0:T(8,128)S(1)} %get-tuple-element.19), channel_id=1, source_target_pairs={{0,4},{2,6},{4,8},{6,10},{8,12},{10,14},{12,0},{14,2},{16,20},{18,... | collective-permute-start | bytes 1572872 | tf_op jit(solution)/shard_map/ppermute | solution.py:61
  99.6 14.6 %collective-permute-start.27 = (f32[32,4096]{1,0:T(8,128)S(1)}, f32[32,4096]{1,0:T(8,128)S(1)}, u32[]{:S(2)}, u32[]{:S(2)}) collective-permute-start(f32[32,4096]{1,0:T(8,128)S(1)} %get-tuple-element.20), channel_id=1, source_target_pairs={{0,12},{2,14},{4,0},{6,2},{8,4},{10,6},{12,8},{14,10},{16,28},{18,... | collective-permute-start | bytes 1572872 | tf_op jit(solution)/shard_map/ppermute | solution.py:69
  102.9 11.5 %collective-permute-start.15 = (f32[16,4096]{1,0:T(8,128)S(1)}, f32[16,4096]{1,0:T(8,128)S(1)}, u32[]{:S(2)}, u32[]{:S(2)}) collective-permute-start(f32[16,4096]{1,0:T(8,128)S(1)} %get-tuple-element.15), channel_id=1, source_target_pairs={{0,32},{2,34},{4,36},{6,38},{8,40},{10,42},{12,44},{14,46},{16,48}... | collective-permute-start | bytes 786440 | tf_op jit(solution)/shard_map/ppermute | solution.py:61
  103.0 11.4 %collective-permute-start.18 = (f32[16,4096]{1,0:T(8,128)S(1)}, f32[16,4096]{1,0:T(8,128)S(1)}, u32[]{:S(2)}, u32[]{:S(2)}) collective-permute-start(f32[16,4096]{1,0:T(8,128)S(1)} %get-tuple-element.16), channel_id=1, source_target_pairs={{0,224},{2,226},{4,228},{6,230},{8,232},{10,234},{12,236},{14,238}... | collective-permute-start | bytes 786440 | tf_op jit(solution)/shard_map/ppermute | solution.py:69
  114.3 6.3 %collective-permute-start.28 = (f32[4,4096]{1,0:T(4,128)S(1)}, f32[4,4096]{1,0:T(4,128)S(1)}, u32[]{:S(2)}, u32[]{:S(2)}) collective-permute-start(f32[4,4096]{1,0:T(4,128)S(1)} %slice.159), channel_id=1, source_target_pairs={{0,32},{2,34},{4,36},{6,38},{8,40},{10,42},{12,44},{14,46},{16,48}... | collective-permute-start | bytes 196616 | tf_op jit(solution)/shard_map/ppermute | solution.py:61
  114.5 10.1 %collective-permute-start.16 = (f32[16,4096]{1,0:T(8,128)S(1)}, f32[16,4096]{1,0:T(8,128)S(1)}, u32[]{:S(2)}, u32[]{:S(2)}) collective-permute-start(f32[16,4096]{1,0:T(8,128)S(1)} %get-tuple-element.13), channel_id=1, source_target_pairs={{0,32},{2,34},{4,36},{6,38},{8,40},{10,42},{12,44},{14,46},{16,48}... | collective-permute-start | bytes 786440 | tf_op jit(solution)/shard_map/ppermute | solution.py:61
  114.6 10.0 %collective-permute-start.19 = (f32[16,4096]{1,0:T(8,128)S(1)}, f32[16,4096]{1,0:T(8,128)S(1)}, u32[]{:S(2)}, u32[]{:S(2)}) collective-permute-start(f32[16,4096]{1,0:T(8,128)S(1)} %get-tuple-element.14), channel_id=1, source_target_pairs={{0,224},{2,226},{4,228},{6,230},{8,232},{10,234},{12,236},{14,238}... | collective-permute-start | bytes 786440 | tf_op jit(solution)/shard_map/ppermute | solution.py:69
  120.7 5.6 %collective-permute-start.29 = (f32[4,4096]{1,0:T(4,128)S(1)}, f32[4,4096]{1,0:T(4,128)S(1)}, u32[]{:S(2)}, u32[]{:S(2)}) collective-permute-start(f32[4,4096]{1,0:T(4,128)S(1)} %get-tuple-element.25), channel_id=1, source_target_pairs={{0,32},{2,34},{4,36},{6,38},{8,40},{10,42},{12,44},{14,46},{16,48}... | collective-permute-start | bytes 196616 | tf_op jit(solution)/shard_map/ppermute | solution.py:61
  126.3 7.3 %collective-permute-start.30 = (f32[4,4096]{1,0:T(4,128)S(1)}, f32[4,4096]{1,0:T(4,128)S(1)}, u32[]{:S(2)}, u32[]{:S(2)}) collective-permute-start(f32[4,4096]{1,0:T(4,128)S(1)} %get-tuple-element.23), channel_id=1, source_target_pairs={{0,32},{2,34},{4,36},{6,38},{8,40},{10,42},{12,44},{14,46},{16,48}... | collective-permute-start | bytes 196616 | tf_op jit(solution)/shard_map/ppermute | solution.py:61
  126.4 7.2 %collective-permute-start.33 = (f32[4,4096]{1,0:T(4,128)S(1)}, f32[4,4096]{1,0:T(4,128)S(1)}, u32[]{:S(2)}, u32[]{:S(2)}) collective-permute-start(f32[4,4096]{1,0:T(4,128)S(1)} %get-tuple-element.24), channel_id=1, source_target_pairs={{0,224},{2,226},{4,228},{6,230},{8,232},{10,234},{12,236},{14,238}... | collective-permute-start | bytes 196616 | tf_op jit(solution)/shard_map/ppermute | solution.py:69
  130.2 6.7 %collective-permute-start.21 = (f32[4,4096]{1,0:T(4,128)S(1)}, f32[4,4096]{1,0:T(4,128)S(1)}, u32[]{:S(2)}, u32[]{:S(2)}) collective-permute-start(f32[4,4096]{1,0:T(4,128)S(1)} %get-tuple-element.27), channel_id=1, source_target_pairs={{0,4},{2,6},{4,8},{6,10},{8,12},{10,14},{12,0},{14,2},{16,20},{18,... | collective-permute-start | bytes 196616 | tf_op jit(solution)/shard_map/ppermute | solution.py:61
  130.3 6.6 %collective-permute-start.22 = (f32[4,4096]{1,0:T(4,128)S(1)}, f32[4,4096]{1,0:T(4,128)S(1)}, u32[]{:S(2)}, u32[]{:S(2)}) collective-permute-start(f32[4,4096]{1,0:T(4,128)S(1)} %get-tuple-element.28), channel_id=1, source_target_pairs={{0,12},{2,14},{4,0},{6,2},{8,4},{10,6},{12,8},{14,10},{16,28},{18,... | collective-permute-start | bytes 196616 | tf_op jit(solution)/shard_map/ppermute | solution.py:69
  (15 other events, 129.4 us)

commit v2 on v1

--- a/solution.py
+++ b/solution.py
@@ -22,10 +22,12 @@
 
 def _perm(axis, k, size):
     stride, n = BLK_AXES[axis]
+    cstride = BLK_AXES["c"][0]
     pairs = []
     for i in range(size):
+        kk = k if (i // cstride) % 2 == 0 else -k
         coord = (i // stride) % n
-        pairs.append((i, i + ((coord + k) % n - coord) * stride))
+        pairs.append((i, i + ((coord + kk) % n - coord) * stride))
     return pairs
 
 

time: 146 us -> 141 us (0.966)
  waiting for transfers between devices: 69.1 us -> 63.6 us
    ppermute x16, waiting for transfers between devices: 32.3 us -> 27.6 us  [_rs_stage(): recv = lax.ppermute(buf, 'blk', _perm(axis, 1, size))]
    ppermute x4, waiting for transfers between devices: 8.58 us -> 5.8 us  [_ag_stage(): cur = lax.ppermute(cur, 'blk', _perm(axis, -1, size))]
    ppermute x7, waiting for transfers between devices: 25.7 us -> 27.6 us  [_ag_stage(): cur = lax.ppermute(cur, 'blk', _perm(axis, 1, size))]
  transfers between devices with their start and end apart: 36 -> 36, of which waited for: 21 -> 22; matrix products, arithmetic and copies ran while one was open for 12% -> 12% of each run, Pallas kernels for 0% -> 0%
where the time goes in v2:
time: 141 us
  waiting for transfers between devices  63.6 us (45%)
  starting transfers between devices  51.1 us (36%)
  other arithmetic  14.3 us (10%)
  matrix products  6.07 us (4%)
  local copies, waits for them, and re-layouts  5.31 us (4%)
    ppermute x16, waiting for transfers between devices, _rs_stage(): recv = lax.ppermute(buf, 'blk', _perm(axis, 1, size))  27.6 us
    ppermute x7, waiting for transfers between devices, _ag_stage(): cur = lax.ppermute(cur, 'blk', _perm(axis, 1, size))  27.6 us
    ppermute x8, starting transfers between devices, _rs_stage(): recv = lax.ppermute(buf, 'blk', _perm(axis, -1, size))  25.9 us
    ppermute x4, starting transfers between devices, _ag_stage(): cur = lax.ppermute(cur, 'blk', _perm(axis, -1, size))  15 us
    mul x2, other arithmetic, mask_blocks(): return (shaped * cols[:, None, :]).reshape(height, width)  8.01 us
    ppermute x4, waiting for transfers between devices, _ag_stage(): cur = lax.ppermute(cur, 'blk', _perm(axis, -1, size))  5.8 us
    ppermute x16, starting transfers between devices, _rs_stage(): recv = lax.ppermute(buf, 'blk', _perm(axis, 1, size))  5.04 us
    ppermute x7, starting transfers between devices, _ag_stage(): cur = lax.ppermute(cur, 'blk', _perm(axis, 1, size))  4.92 us
  transfers between devices with their start and end apart: 36, of which 22 were waited for; matrix products, arithmetic and copies ran while one was open for 12% of the time, Pallas kernels for 0%

profile of v2, /device:TPU:2, one launch (start us, length us, event | category | flops | bytes accessed | tf_op | source)
XLA Modules:
  0.0 141.0 jit_solution(7672346577267383119)
XLA Ops:
  6.8 2.5 %bitcast_multiply_fusion = bf16[256,8192]{1,0:T(8,128)(2,1)S(1)} fusion(bf16[256,8192]{1,0:T(8,128)(2,1)} %param.12, bf16[2,8192]{1,0:T(2,128)(2,1)S(1)} %bitcast.32), kind=kLoop, calls=%fused_computation | loop fusion | flops 2097152 | bytes 8421376 | tf_op jit(solution)/shard_map/mul | solution.py:20
  9.3 5.5 %bitcast_multiply_fusion.1 = (bf16[8192,256]{1,0:T(8,128)(2,1)S(1)}, bf16[8192,256]{1,0:T(8,128)(2,1)S(1)}) fusion(bf16[8192,256]{1,0:T(8,128)(2,1)} %param.11, bf16[64,256]{1,0:T(8,128)(2,1)S(1)} %bitcast.30, bf16[8192,256]{1,0:T(8,128)(2,1)} %param.10, bf16[64,256]{1,0:T(8,128)(2,1)S(1)} %bitcast.31), kind=kLoop, calls=%fused_computation.1 | loop fusion | flops 4194304 | bytes 16842752 | tf_op jit(solution)/shard_map/mul | solution.py:20
  18.2 2.2 %collective-permute-done.2 = bf16[4,8192]{1,0:T(4,128)(2,1)S(1)} collective-permute-done((bf16[4,8192]{1,0:T(4,128)(2,1)S(1)}, bf16[4,8192]{1,0:T(4,128)(2,1)S(1)}, u32[]{:S(2)}, u32[]{:S(2)}) %collective-permute-start.2) | collective-permute-done | bytes 65568 | tf_op jit(solution)/shard_map/ppermute | solution.py:42
  21.5 4.4 %collective-permute-done.3 = bf16[4,8192]{1,0:T(4,128)(2,1)S(1)} collective-permute-done((bf16[4,8192]{1,0:T(4,128)(2,1)S(1)}, bf16[4,8192]{1,0:T(4,128)(2,1)S(1)}, u32[]{:S(2)}, u32[]{:S(2)}) %collective-permute-start.3) | collective-permute-done | bytes 65568 | tf_op jit(solution)/shard_map/ppermute | solution.py:42
  26.1 5.9 %collective-permute-start.4 = (bf16[16,8192]{1,0:T(8,128)(2,1)S(1)}, bf16[16,8192]{1,0:T(8,128)(2,1)S(1)}, u32[]{:S(2)}, u32[]{:S(2)}) collective-permute-start(bf16[16,8192]{1,0:T(8,128)(2,1)S(1)} %pad_maximum_fusion), channel_id=1, source_target_pairs={{0,224},{2,34},{4,228},{6,38},{8,232},{10,42},{12,236},{14,46},{16... | collective-permute-start | bytes 786440 | tf_op jit(solution)/shard_map/ppermute | solution.py:46
  32.0 4.1 %collective-permute-done.4 = bf16[16,8192]{1,0:T(8,128)(2,1)S(1)} collective-permute-done((bf16[16,8192]{1,0:T(8,128)(2,1)S(1)}, bf16[16,8192]{1,0:T(8,128)(2,1)S(1)}, u32[]{:S(2)}, u32[]{:S(2)}) %collective-permute-start.4) | collective-permute-done | bytes 262176 | tf_op jit(solution)/shard_map/ppermute | solution.py:46
  36.1 3.7 %collective-permute-start.5 = (bf16[16,8192]{1,0:T(8,128)(2,1)S(1)}, bf16[16,8192]{1,0:T(8,128)(2,1)S(1)}, u32[]{:S(2)}, u32[]{:S(2)}) collective-permute-start(bf16[16,8192]{1,0:T(8,128)(2,1)S(1)} %collective-permute-done.4), channel_id=1, source_target_pairs={{0,224},{2,34},{4,228},{6,38},{8,232},{10,42},{12,236},{14,46},{16... | collective-permute-start | bytes 786440 | tf_op jit(solution)/shard_map/ppermute | solution.py:46
  43.7 3.7 %collective-permute-start.6 = (bf16[16,8192]{1,0:T(8,128)(2,1)S(1)}, bf16[16,8192]{1,0:T(8,128)(2,1)S(1)}, u32[]{:S(2)}, u32[]{:S(2)}) collective-permute-start(bf16[16,8192]{1,0:T(8,128)(2,1)S(1)} %collective-permute-done.5), channel_id=1, source_target_pairs={{0,224},{2,34},{4,228},{6,38},{8,232},{10,42},{12,236},{14,46},{16... | collective-permute-start | bytes 786440 | tf_op jit(solution)/shard_map/ppermute | solution.py:46
  47.4 3.7 %collective-permute-done.8 = bf16[16,8192]{1,0:T(8,128)(2,1)S(1)} collective-permute-done((bf16[16,8192]{1,0:T(8,128)(2,1)S(1)}, bf16[16,8192]{1,0:T(8,128)(2,1)S(1)}, u32[]{:S(2)}, u32[]{:S(2)}) %collective-permute-start.8) | collective-permute-done | bytes 262176 | tf_op jit(solution)/shard_map/ppermute | solution.py:42
  51.1 7.6 %collective-permute-done.9 = bf16[16,8192]{1,0:T(8,128)(2,1)S(1)} collective-permute-done((bf16[16,8192]{1,0:T(8,128)(2,1)S(1)}, bf16[16,8192]{1,0:T(8,128)(2,1)S(1)}, u32[]{:S(2)}, u32[]{:S(2)}) %collective-permute-start.9) | collective-permute-done | bytes 262176 | tf_op jit(solution)/shard_map/ppermute | solution.py:42
  58.6 7.6 %collective-permute-done.10 = bf16[16,8192]{1,0:T(8,128)(2,1)S(1)} collective-permute-done((bf16[16,8192]{1,0:T(8,128)(2,1)S(1)}, bf16[16,8192]{1,0:T(8,128)(2,1)S(1)}, u32[]{:S(2)}, u32[]{:S(2)}) %collective-permute-start.10) | collective-permute-done | bytes 262176 | tf_op jit(solution)/shard_map/ppermute | solution.py:42
  68.1 2.6 %collective-permute-done.11 = bf16[128,8192]{1,0:T(8,128)(2,1)S(1)} collective-permute-done((bf16[128,8192]{1,0:T(8,128)(2,1)S(1)}, bf16[128,8192]{1,0:T(8,128)(2,1)S(1)}, u32[]{:S(2)}, u32[]{:S(2)}) %collective-permute-start.11) | collective-permute-done | bytes 2097184 | tf_op jit(solution)/shard_map/ppermute | solution.py:110
  76.7 2.3 %fusion = f32[256,4096]{1,0:T(8,128)S(1)} fusion(bf16[256,256]{1,0:T(8,128)(2,1)S(1)} %reshape.27, bf16[256,8192]{1,0:T(8,128)(2,1)} %copy-done), kind=kOutput, calls=%fused_computation.5 | convolution fusion | flops 536870912 | bytes 6422528 | tf_op jit(solution)/shard_map/dot_general | solution.py:122
  84.2 4.9 %collective-permute-done.13 = f32[16,4096]{1,0:T(8,128)S(1)} collective-permute-done((f32[16,4096]{1,0:T(8,128)S(1)}, f32[16,4096]{1,0:T(8,128)S(1)}, u32[]{:S(2)}, u32[]{:S(2)}) %collective-permute-start.13) | collective-permute-done | bytes 262176 | tf_op jit(solution)/shard_map/ppermute | solution.py:63
  89.3 3.2 %collective-permute-start.17 = (f32[16,4096]{1,0:T(8,128)S(1)}, f32[16,4096]{1,0:T(8,128)S(1)}, u32[]{:S(2)}, u32[]{:S(2)}) collective-permute-start(f32[16,4096]{1,0:T(8,128)S(1)} %get-tuple-element.18), channel_id=1, source_target_pairs={{0,224},{2,34},{4,228},{6,38},{8,232},{10,42},{12,236},{14,46},{16... | collective-permute-start | bytes 786440 | tf_op jit(solution)/shard_map/ppermute | solution.py:71
  94.4 3.2 %collective-permute-start.27 = (f32[32,4096]{1,0:T(8,128)S(1)}, f32[32,4096]{1,0:T(8,128)S(1)}, u32[]{:S(2)}, u32[]{:S(2)}) collective-permute-start(f32[32,4096]{1,0:T(8,128)S(1)} %get-tuple-element.20), channel_id=1, source_target_pairs={{0,12},{2,6},{4,0},{6,10},{8,4},{10,14},{12,8},{14,2},{16,28},{18,... | collective-permute-start | bytes 1572872 | tf_op jit(solution)/shard_map/ppermute | solution.py:71
  98.1 3.2 %collective-permute-start.18 = (f32[16,4096]{1,0:T(8,128)S(1)}, f32[16,4096]{1,0:T(8,128)S(1)}, u32[]{:S(2)}, u32[]{:S(2)}) collective-permute-start(f32[16,4096]{1,0:T(8,128)S(1)} %get-tuple-element.16), channel_id=1, source_target_pairs={{0,224},{2,34},{4,228},{6,38},{8,232},{10,42},{12,236},{14,46},{16... | collective-permute-start | bytes 786440 | tf_op jit(solution)/shard_map/ppermute | solution.py:71
  101.3 8.2 %collective-permute-done.26 = f32[32,4096]{1,0:T(8,128)S(1)} collective-permute-done((f32[32,4096]{1,0:T(8,128)S(1)}, f32[32,4096]{1,0:T(8,128)S(1)}, u32[]{:S(2)}, u32[]{:S(2)}) %collective-permute-start.26) | collective-permute-done | bytes 524320 | tf_op jit(solution)/shard_map/ppermute | solution.py:63
  109.9 3.3 %collective-permute-start.19 = (f32[16,4096]{1,0:T(8,128)S(1)}, f32[16,4096]{1,0:T(8,128)S(1)}, u32[]{:S(2)}, u32[]{:S(2)}) collective-permute-start(f32[16,4096]{1,0:T(8,128)S(1)} %get-tuple-element.14), channel_id=1, source_target_pairs={{0,224},{2,34},{4,228},{6,38},{8,232},{10,42},{12,236},{14,46},{16... | collective-permute-start | bytes 786440 | tf_op jit(solution)/shard_map/ppermute | solution.py:71
  113.2 2.8 %collective-permute-done.28 = f32[4,4096]{1,0:T(4,128)S(1)} collective-permute-done((f32[4,4096]{1,0:T(4,128)S(1)}, f32[4,4096]{1,0:T(4,128)S(1)}, u32[]{:S(2)}, u32[]{:S(2)}) %collective-permute-start.28) | collective-permute-done | bytes 65568 | tf_op jit(solution)/shard_map/ppermute | solution.py:63
  116.1 3.2 %collective-permute-start.32 = (f32[4,4096]{1,0:T(4,128)S(1)}, f32[4,4096]{1,0:T(4,128)S(1)}, u32[]{:S(2)}, u32[]{:S(2)}) collective-permute-start(f32[4,4096]{1,0:T(4,128)S(1)} %get-tuple-element.26), channel_id=1, source_target_pairs={{0,224},{2,34},{4,228},{6,38},{8,232},{10,42},{12,236},{14,46},{16... | collective-permute-start | bytes 196616 | tf_op jit(solution)/shard_map/ppermute | solution.py:71
  121.7 3.3 %collective-permute-start.33 = (f32[4,4096]{1,0:T(4,128)S(1)}, f32[4,4096]{1,0:T(4,128)S(1)}, u32[]{:S(2)}, u32[]{:S(2)}) collective-permute-start(f32[4,4096]{1,0:T(4,128)S(1)} %get-tuple-element.24), channel_id=1, source_target_pairs={{0,224},{2,34},{4,228},{6,38},{8,232},{10,42},{12,236},{14,46},{16... | collective-permute-start | bytes 196616 | tf_op jit(solution)/shard_map/ppermute | solution.py:71
  125.9 3.2 %collective-permute-start.22 = (f32[4,4096]{1,0:T(4,128)S(1)}, f32[4,4096]{1,0:T(4,128)S(1)}, u32[]{:S(2)}, u32[]{:S(2)}) collective-permute-start(f32[4,4096]{1,0:T(4,128)S(1)} %get-tuple-element.28), channel_id=1, source_target_pairs={{0,12},{2,6},{4,0},{6,10},{8,4},{10,14},{12,8},{14,2},{16,28},{18,... | collective-permute-start | bytes 196616 | tf_op jit(solution)/shard_map/ppermute | solution.py:71
  129.3 3.2 %collective-permute-start.34 = (f32[4,4096]{1,0:T(4,128)S(1)}, f32[4,4096]{1,0:T(4,128)S(1)}, u32[]{:S(2)}, u32[]{:S(2)}) collective-permute-start(f32[4,4096]{1,0:T(4,128)S(1)} %get-tuple-element.22), channel_id=1, source_target_pairs={{0,224},{2,34},{4,228},{6,38},{8,232},{10,42},{12,236},{14,46},{16... | collective-permute-start | bytes 196616 | tf_op jit(solution)/shard_map/ppermute | solution.py:71
  (118 shorter events, 43.0 us)
Async XLA Ops:
  1.8 13.0 %collective-permute-start = (bf16[2,8192]{1,0:T(2,128)(2,1)S(1)}, bf16[2,8192]{1,0:T(2,128)(2,1)S(1)}, u32[]{:S(2)}, u32[]{:S(2)}) collective-permute-start(bf16[2,8192]{1,0:T(2,128)(2,1)S(1)} %fusion.11), channel_id=1, source_target_pairs={{0,16},{2,18},{4,20},{6,22},{8,24},{10,26},{12,28},{14,30},{16,0},... | collective-permute-start | bytes 98312 | tf_op jit(solution)/shard_map/ppermute | solution.py:42
  26.1 10.0 %collective-permute-start.4 = (bf16[16,8192]{1,0:T(8,128)(2,1)S(1)}, bf16[16,8192]{1,0:T(8,128)(2,1)S(1)}, u32[]{:S(2)}, u32[]{:S(2)}) collective-permute-start(bf16[16,8192]{1,0:T(8,128)(2,1)S(1)} %pad_maximum_fusion), channel_id=1, source_target_pairs={{0,224},{2,34},{4,228},{6,38},{8,232},{10,42},{12,236},{14,46},{16... | collective-permute-start | bytes 786440 | tf_op jit(solution)/shard_map/ppermute | solution.py:46
  32.0 9.9 %collective-permute-start.7 = (bf16[16,8192]{1,0:T(8,128)(2,1)S(1)}, bf16[16,8192]{1,0:T(8,128)(2,1)S(1)}, u32[]{:S(2)}, u32[]{:S(2)}) collective-permute-start(bf16[16,8192]{1,0:T(8,128)(2,1)S(1)} %pad_maximum_fusion), channel_id=1, source_target_pairs={{0,32},{2,226},{4,36},{6,230},{8,40},{10,234},{12,44},{14,238},{16... | collective-permute-start | bytes 786440 | tf_op jit(solution)/shard_map/ppermute | solution.py:42
  36.1 7.6 %collective-permute-start.5 = (bf16[16,8192]{1,0:T(8,128)(2,1)S(1)}, bf16[16,8192]{1,0:T(8,128)(2,1)S(1)}, u32[]{:S(2)}, u32[]{:S(2)}) collective-permute-start(bf16[16,8192]{1,0:T(8,128)(2,1)S(1)} %collective-permute-done.4), channel_id=1, source_target_pairs={{0,224},{2,34},{4,228},{6,38},{8,232},{10,42},{12,236},{14,46},{16... | collective-permute-start | bytes 786440 | tf_op jit(solution)/shard_map/ppermute | solution.py:46
  41.9 9.1 %collective-permute-start.8 = (bf16[16,8192]{1,0:T(8,128)(2,1)S(1)}, bf16[16,8192]{1,0:T(8,128)(2,1)S(1)}, u32[]{:S(2)}, u32[]{:S(2)}) collective-permute-start(bf16[16,8192]{1,0:T(8,128)(2,1)S(1)} %collective-permute-done.7), channel_id=1, source_target_pairs={{0,32},{2,226},{4,36},{6,230},{8,40},{10,234},{12,44},{14,238},{16... | collective-permute-start | bytes 786440 | tf_op jit(solution)/shard_map/ppermute | solution.py:42
  43.7 14.9 %collective-permute-start.6 = (bf16[16,8192]{1,0:T(8,128)(2,1)S(1)}, bf16[16,8192]{1,0:T(8,128)(2,1)S(1)}, u32[]{:S(2)}, u32[]{:S(2)}) collective-permute-start(bf16[16,8192]{1,0:T(8,128)(2,1)S(1)} %collective-permute-done.5), channel_id=1, source_target_pairs={{0,224},{2,34},{4,228},{6,38},{8,232},{10,42},{12,236},{14,46},{16... | collective-permute-start | bytes 786440 | tf_op jit(solution)/shard_map/ppermute | solution.py:46
  51.0 7.6 %collective-permute-start.9 = (bf16[16,8192]{1,0:T(8,128)(2,1)S(1)}, bf16[16,8192]{1,0:T(8,128)(2,1)S(1)}, u32[]{:S(2)}, u32[]{:S(2)}) collective-permute-start(bf16[16,8192]{1,0:T(8,128)(2,1)S(1)} %collective-permute-done.8), channel_id=1, source_target_pairs={{0,32},{2,226},{4,36},{6,230},{8,40},{10,234},{12,44},{14,238},{16... | collective-permute-start | bytes 786440 | tf_op jit(solution)/shard_map/ppermute | solution.py:42
  58.6 7.6 %collective-permute-start.10 = (bf16[16,8192]{1,0:T(8,128)(2,1)S(1)}, bf16[16,8192]{1,0:T(8,128)(2,1)S(1)}, u32[]{:S(2)}, u32[]{:S(2)}) collective-permute-start(bf16[16,8192]{1,0:T(8,128)(2,1)S(1)} %collective-permute-done.9), channel_id=1, source_target_pairs={{0,32},{2,226},{4,36},{6,230},{8,40},{10,234},{12,44},{14,238},{16... | collective-permute-start | bytes 786440 | tf_op jit(solution)/shard_map/ppermute | solution.py:42
  81.5 7.7 %collective-permute-start.13 = (f32[16,4096]{1,0:T(8,128)S(1)}, f32[16,4096]{1,0:T(8,128)S(1)}, u32[]{:S(2)}, u32[]{:S(2)}) collective-permute-start(f32[16,4096]{1,0:T(8,128)S(1)} %slice.139), channel_id=1, source_target_pairs={{0,32},{2,226},{4,36},{6,230},{8,40},{10,234},{12,44},{14,238},{16... | collective-permute-start | bytes 786440 | tf_op jit(solution)/shard_map/ppermute | solution.py:63
  83.7 10.5 %collective-permute-start.25 = (f32[32,4096]{1,0:T(8,128)S(1)}, f32[32,4096]{1,0:T(8,128)S(1)}, u32[]{:S(2)}, u32[]{:S(2)}) collective-permute-start(f32[32,4096]{1,0:T(8,128)S(1)} %slice.155), channel_id=1, source_target_pairs={{0,4},{2,14},{4,8},{6,2},{8,12},{10,6},{12,0},{14,10},{16,20},{18,... | collective-permute-start | bytes 1572872 | tf_op jit(solution)/shard_map/ppermute | solution.py:63
  89.2 8.7 %collective-permute-start.14 = (f32[16,4096]{1,0:T(8,128)S(1)}, f32[16,4096]{1,0:T(8,128)S(1)}, u32[]{:S(2)}, u32[]{:S(2)}) collective-permute-start(f32[16,4096]{1,0:T(8,128)S(1)} %get-tuple-element.17), channel_id=1, source_target_pairs={{0,32},{2,226},{4,36},{6,230},{8,40},{10,234},{12,44},{14,238},{16... | collective-permute-start | bytes 786440 | tf_op jit(solution)/shard_map/ppermute | solution.py:63
  89.3 8.6 %collective-permute-start.17 = (f32[16,4096]{1,0:T(8,128)S(1)}, f32[16,4096]{1,0:T(8,128)S(1)}, u32[]{:S(2)}, u32[]{:S(2)}) collective-permute-start(f32[16,4096]{1,0:T(8,128)S(1)} %get-tuple-element.18), channel_id=1, source_target_pairs={{0,224},{2,34},{4,228},{6,38},{8,232},{10,42},{12,236},{14,46},{16... | collective-permute-start | bytes 786440 | tf_op jit(solution)/shard_map/ppermute | solution.py:71
  94.3 15.2 %collective-permute-start.26 = (f32[32,4096]{1,0:T(8,128)S(1)}, f32[32,4096]{1,0:T(8,128)S(1)}, u32[]{:S(2)}, u32[]{:S(2)}) collective-permute-start(f32[32,4096]{1,0:T(8,128)S(1)} %get-tuple-element.19), channel_id=1, source_target_pairs={{0,4},{2,14},{4,8},{6,2},{8,12},{10,6},{12,0},{14,10},{16,20},{18,... | collective-permute-start | bytes 1572872 | tf_op jit(solution)/shard_map/ppermute | solution.py:63
  94.4 15.1 %collective-permute-start.27 = (f32[32,4096]{1,0:T(8,128)S(1)}, f32[32,4096]{1,0:T(8,128)S(1)}, u32[]{:S(2)}, u32[]{:S(2)}) collective-permute-start(f32[32,4096]{1,0:T(8,128)S(1)} %get-tuple-element.20), channel_id=1, source_target_pairs={{0,12},{2,6},{4,0},{6,10},{8,4},{10,14},{12,8},{14,2},{16,28},{18,... | collective-permute-start | bytes 1572872 | tf_op jit(solution)/shard_map/ppermute | solution.py:71
  98.0 11.7 %collective-permute-start.15 = (f32[16,4096]{1,0:T(8,128)S(1)}, f32[16,4096]{1,0:T(8,128)S(1)}, u32[]{:S(2)}, u32[]{:S(2)}) collective-permute-start(f32[16,4096]{1,0:T(8,128)S(1)} %get-tuple-element.15), channel_id=1, source_target_pairs={{0,32},{2,226},{4,36},{6,230},{8,40},{10,234},{12,44},{14,238},{16... | collective-permute-start | bytes 786440 | tf_op jit(solution)/shard_map/ppermute | solution.py:63
  98.1 11.7 %collective-permute-start.18 = (f32[16,4096]{1,0:T(8,128)S(1)}, f32[16,4096]{1,0:T(8,128)S(1)}, u32[]{:S(2)}, u32[]{:S(2)}) collective-permute-start(f32[16,4096]{1,0:T(8,128)S(1)} %get-tuple-element.16), channel_id=1, source_target_pairs={{0,224},{2,34},{4,228},{6,38},{8,232},{10,42},{12,236},{14,46},{16... | collective-permute-start | bytes 786440 | tf_op jit(solution)/shard_map/ppermute | solution.py:71
  109.6 6.3 %collective-permute-start.28 = (f32[4,4096]{1,0:T(4,128)S(1)}, f32[4,4096]{1,0:T(4,128)S(1)}, u32[]{:S(2)}, u32[]{:S(2)}) collective-permute-start(f32[4,4096]{1,0:T(4,128)S(1)} %slice.159), channel_id=1, source_target_pairs={{0,32},{2,226},{4,36},{6,230},{8,40},{10,234},{12,44},{14,238},{16... | collective-permute-start | bytes 196616 | tf_op jit(solution)/shard_map/ppermute | solution.py:63
  109.8 10.2 %collective-permute-start.16 = (f32[16,4096]{1,0:T(8,128)S(1)}, f32[16,4096]{1,0:T(8,128)S(1)}, u32[]{:S(2)}, u32[]{:S(2)}) collective-permute-start(f32[16,4096]{1,0:T(8,128)S(1)} %get-tuple-element.13), channel_id=1, source_target_pairs={{0,32},{2,226},{4,36},{6,230},{8,40},{10,234},{12,44},{14,238},{16... | collective-permute-start | bytes 786440 | tf_op jit(solution)/shard_map/ppermute | solution.py:63
  109.9 10.1 %collective-permute-start.19 = (f32[16,4096]{1,0:T(8,128)S(1)}, f32[16,4096]{1,0:T(8,128)S(1)}, u32[]{:S(2)}, u32[]{:S(2)}) collective-permute-start(f32[16,4096]{1,0:T(8,128)S(1)} %get-tuple-element.14), channel_id=1, source_target_pairs={{0,224},{2,34},{4,228},{6,38},{8,232},{10,42},{12,236},{14,46},{16... | collective-permute-start | bytes 786440 | tf_op jit(solution)/shard_map/ppermute | solution.py:71
  120.1 5.7 %collective-permute-start.20 = (f32[4,4096]{1,0:T(4,128)S(1)}, f32[4,4096]{1,0:T(4,128)S(1)}, u32[]{:S(2)}, u32[]{:S(2)}) collective-permute-start(f32[4,4096]{1,0:T(4,128)S(1)} %slice.147), channel_id=1, source_target_pairs={{0,4},{2,14},{4,8},{6,2},{8,12},{10,6},{12,0},{14,10},{16,20},{18,... | collective-permute-start | bytes 196616 | tf_op jit(solution)/shard_map/ppermute | solution.py:63
  121.6 7.5 %collective-permute-start.30 = (f32[4,4096]{1,0:T(4,128)S(1)}, f32[4,4096]{1,0:T(4,128)S(1)}, u32[]{:S(2)}, u32[]{:S(2)}) collective-permute-start(f32[4,4096]{1,0:T(4,128)S(1)} %get-tuple-element.23), channel_id=1, source_target_pairs={{0,32},{2,226},{4,36},{6,230},{8,40},{10,234},{12,44},{14,238},{16... | collective-permute-start | bytes 196616 | tf_op jit(solution)/shard_map/ppermute | solution.py:63
  121.7 7.4 %collective-permute-start.33 = (f32[4,4096]{1,0:T(4,128)S(1)}, f32[4,4096]{1,0:T(4,128)S(1)}, u32[]{:S(2)}, u32[]{:S(2)}) collective-permute-start(f32[4,4096]{1,0:T(4,128)S(1)} %get-tuple-element.24), channel_id=1, source_target_pairs={{0,224},{2,34},{4,228},{6,38},{8,232},{10,42},{12,236},{14,46},{16... | collective-permute-start | bytes 196616 | tf_op jit(solution)/shard_map/ppermute | solution.py:71
  125.8 6.7 %collective-permute-start.21 = (f32[4,4096]{1,0:T(4,128)S(1)}, f32[4,4096]{1,0:T(4,128)S(1)}, u32[]{:S(2)}, u32[]{:S(2)}) collective-permute-start(f32[4,4096]{1,0:T(4,128)S(1)} %get-tuple-element.27), channel_id=1, source_target_pairs={{0,4},{2,14},{4,8},{6,2},{8,12},{10,6},{12,0},{14,10},{16,20},{18,... | collective-permute-start | bytes 196616 | tf_op jit(solution)/shard_map/ppermute | solution.py:63
  125.9 6.6 %collective-permute-start.22 = (f32[4,4096]{1,0:T(4,128)S(1)}, f32[4,4096]{1,0:T(4,128)S(1)}, u32[]{:S(2)}, u32[]{:S(2)}) collective-permute-start(f32[4,4096]{1,0:T(4,128)S(1)} %get-tuple-element.28), channel_id=1, source_target_pairs={{0,12},{2,6},{4,0},{6,10},{8,4},{10,14},{12,8},{14,2},{16,28},{18,... | collective-permute-start | bytes 196616 | tf_op jit(solution)/shard_map/ppermute | solution.py:71
  (15 other events, 129.9 us)

commit v3 on v2

--- a/solution.py
+++ b/solution.py
@@ -97,13 +97,11 @@
 
     base = tuple(reversed(AG_ORDER))
     piece = normed
+    kept = [gate_kept, up_kept, down_kept]
     for i, axis in enumerate(AG_ORDER[:-1]):
         piece = _ag_stage(piece, axis, size)
-        if i == 0:
-            piece, gate_kept, up_kept, down_kept = lax.optimization_barrier(
-                (piece, gate_kept, up_kept, down_kept))
-        else:
-            piece = lax.optimization_barrier(piece)
+        piece, kept[i] = lax.optimization_barrier((piece, kept[i]))
+    gate_kept, up_kept, down_kept = kept
     last = AG_ORDER[-1]
     _, n_last = BLK_AXES[last]
     assert n_last == 2

time: 141 us -> 138 us (0.979)
  waiting for transfers between devices: 63.6 us -> 61.4 us
  other arithmetic: 14.3 us -> 12.3 us
    ppermute x7, waiting for transfers between devices: 27.6 us -> 19.3 us  [_ag_stage(): cur = lax.ppermute(cur, 'blk', _perm(axis, 1, size))]
    ppermute x4, waiting for transfers between devices: 5.8 us -> 10.5 us  [_ag_stage(): cur = lax.ppermute(cur, 'blk', _perm(axis, -1, size))]
    unnamed x17 -> x25, local copies, waits for them, and re-layouts: 2.43 us -> 3.27 us
    mul x2 -> x3, other arithmetic: 8.01 us -> 7.42 us  [mask_blocks(): return (shaped * cols[:, None, :]).reshape(height, width)]
  transfers between devices with their start and end apart: 36 -> 36, of which waited for: 22 -> 21; matrix products, arithmetic and copies ran while one was open for 12% -> 11% of each run, Pallas kernels for 0% -> 0%
where the time goes in v3:
time: 138 us
  waiting for transfers between devices  61.4 us (44%)
  starting transfers between devices  51.4 us (37%)
  other arithmetic  12.3 us (9%)
  local copies, waits for them, and re-layouts  6.15 us (4%)
  matrix products  6.06 us (4%)
    ppermute x16, waiting for transfers between devices, _rs_stage(): recv = lax.ppermute(buf, 'blk', _perm(axis, 1, size))  28.9 us
    ppermute x8, starting transfers between devices, _rs_stage(): recv = lax.ppermute(buf, 'blk', _perm(axis, -1, size))  25.9 us
    ppermute x7, waiting for transfers between devices, _ag_stage(): cur = lax.ppermute(cur, 'blk', _perm(axis, 1, size))  19.3 us
    ppermute x4, starting transfers between devices, _ag_stage(): cur = lax.ppermute(cur, 'blk', _perm(axis, -1, size))  15 us
    ppermute x4, waiting for transfers between devices, _ag_stage(): cur = lax.ppermute(cur, 'blk', _perm(axis, -1, size))  10.5 us
    mul x3, other arithmetic, mask_blocks(): return (shaped * cols[:, None, :]).reshape(height, width)  7.42 us
    ppermute x16, starting transfers between devices, _rs_stage(): recv = lax.ppermute(buf, 'blk', _perm(axis, 1, size))  5.29 us
    ppermute x7, starting transfers between devices, _ag_stage(): cur = lax.ppermute(cur, 'blk', _perm(axis, 1, size))  4.91 us
  transfers between devices with their start and end apart: 36, of which 21 were waited for; matrix products, arithmetic and copies ran while one was open for 11% of the time, Pallas kernels for 0%

profile of v3, /device:TPU:2, one launch (start us, length us, event | category | flops | bytes accessed | tf_op | source)
XLA Modules:
  0.0 137.8 jit_solution(17875623209898512782)
XLA Ops:
  5.0 4.5 %bitcast_multiply_fusion.2 = bf16[8192,256]{1,0:T(8,128)(2,1)} fusion(bf16[8192,256]{1,0:T(8,128)(2,1)} %param.10, bf16[64,256]{1,0:T(8,128)(2,1)S(1)} %bitcast.32), kind=kLoop, calls=%fused_computation.2 | loop fusion | flops 2097152 | bytes 8421376 | tf_op jit(solution)/shard_map/mul | solution.py:20
  12.9 2.2 %collective-permute-done.2 = bf16[4,8192]{1,0:T(4,128)(2,1)S(1)} collective-permute-done((bf16[4,8192]{1,0:T(4,128)(2,1)S(1)}, bf16[4,8192]{1,0:T(4,128)(2,1)S(1)}, u32[]{:S(2)}, u32[]{:S(2)}) %collective-permute-start.2) | collective-permute-done | bytes 65568 | tf_op jit(solution)/shard_map/ppermute | solution.py:42
  16.6 2.6 %bitcast_multiply_fusion.1 = bf16[8192,256]{1,0:T(8,128)(2,1)S(1)} fusion(bf16[8192,256]{1,0:T(8,128)(2,1)} %param.11, bf16[64,256]{1,0:T(8,128)(2,1)S(1)} %bitcast.30), kind=kLoop, calls=%fused_computation.1 | loop fusion | flops 2097152 | bytes 8421376 | tf_op jit(solution)/shard_map/mul | solution.py:20
  20.8 5.9 %collective-permute-start.4 = (bf16[16,8192]{1,0:T(8,128)(2,1)S(1)}, bf16[16,8192]{1,0:T(8,128)(2,1)S(1)}, u32[]{:S(2)}, u32[]{:S(2)}) collective-permute-start(bf16[16,8192]{1,0:T(8,128)(2,1)S(1)} %pad_maximum_fusion), channel_id=1, source_target_pairs={{0,224},{2,34},{4,228},{6,38},{8,232},{10,42},{12,236},{14,46},{16... | collective-permute-start | bytes 786440 | tf_op jit(solution)/shard_map/ppermute | solution.py:46
  26.8 5.7 %collective-permute-done.4 = bf16[16,8192]{1,0:T(8,128)(2,1)S(1)} collective-permute-done((bf16[16,8192]{1,0:T(8,128)(2,1)S(1)}, bf16[16,8192]{1,0:T(8,128)(2,1)S(1)}, u32[]{:S(2)}, u32[]{:S(2)}) %collective-permute-start.4) | collective-permute-done | bytes 262176 | tf_op jit(solution)/shard_map/ppermute | solution.py:46
  32.4 3.7 %collective-permute-start.5 = (bf16[16,8192]{1,0:T(8,128)(2,1)S(1)}, bf16[16,8192]{1,0:T(8,128)(2,1)S(1)}, u32[]{:S(2)}, u32[]{:S(2)}) collective-permute-start(bf16[16,8192]{1,0:T(8,128)(2,1)S(1)} %collective-permute-done.4), channel_id=1, source_target_pairs={{0,224},{2,34},{4,228},{6,38},{8,232},{10,42},{12,236},{14,46},{16... | collective-permute-start | bytes 786440 | tf_op jit(solution)/shard_map/ppermute | solution.py:46
  36.1 4.8 %collective-permute-done.5 = bf16[16,8192]{1,0:T(8,128)(2,1)S(1)} collective-permute-done((bf16[16,8192]{1,0:T(8,128)(2,1)S(1)}, bf16[16,8192]{1,0:T(8,128)(2,1)S(1)}, u32[]{:S(2)}, u32[]{:S(2)}) %collective-permute-start.5) | collective-permute-done | bytes 262176 | tf_op jit(solution)/shard_map/ppermute | solution.py:46
  41.0 3.7 %collective-permute-start.6 = (bf16[16,8192]{1,0:T(8,128)(2,1)S(1)}, bf16[16,8192]{1,0:T(8,128)(2,1)S(1)}, u32[]{:S(2)}, u32[]{:S(2)}) collective-permute-start(bf16[16,8192]{1,0:T(8,128)(2,1)S(1)} %collective-permute-done.5), channel_id=1, source_target_pairs={{0,224},{2,34},{4,228},{6,38},{8,232},{10,42},{12,236},{14,46},{16... | collective-permute-start | bytes 786440 | tf_op jit(solution)/shard_map/ppermute | solution.py:46
  46.4 7.6 %collective-permute-done.9 = bf16[16,8192]{1,0:T(8,128)(2,1)S(1)} collective-permute-done((bf16[16,8192]{1,0:T(8,128)(2,1)S(1)}, bf16[16,8192]{1,0:T(8,128)(2,1)S(1)}, u32[]{:S(2)}, u32[]{:S(2)}) %collective-permute-start.9) | collective-permute-done | bytes 262176 | tf_op jit(solution)/shard_map/ppermute | solution.py:42
  54.0 7.6 %collective-permute-done.10 = bf16[16,8192]{1,0:T(8,128)(2,1)S(1)} collective-permute-done((bf16[16,8192]{1,0:T(8,128)(2,1)S(1)}, bf16[16,8192]{1,0:T(8,128)(2,1)S(1)}, u32[]{:S(2)}, u32[]{:S(2)}) %collective-permute-start.10) | collective-permute-done | bytes 262176 | tf_op jit(solution)/shard_map/ppermute | solution.py:42
  63.5 2.6 %collective-permute-done.11 = bf16[128,8192]{1,0:T(8,128)(2,1)S(1)} collective-permute-done((bf16[128,8192]{1,0:T(8,128)(2,1)S(1)}, bf16[128,8192]{1,0:T(8,128)(2,1)S(1)}, u32[]{:S(2)}, u32[]{:S(2)}) %collective-permute-start.11) | collective-permute-done | bytes 2097184 | tf_op jit(solution)/shard_map/ppermute | solution.py:108
  72.0 2.3 %fusion = f32[256,4096]{1,0:T(8,128)S(1)} fusion(bf16[256,256]{1,0:T(8,128)(2,1)S(1)} %reshape.27, bf16[256,8192]{1,0:T(8,128)(2,1)} %copy-done.1), kind=kOutput, calls=%fused_computation.5 | convolution fusion | flops 536870912 | bytes 6422528 | tf_op jit(solution)/shard_map/dot_general | solution.py:120
  79.8 4.6 %collective-permute-done.13 = f32[16,4096]{1,0:T(8,128)S(1)} collective-permute-done((f32[16,4096]{1,0:T(8,128)S(1)}, f32[16,4096]{1,0:T(8,128)S(1)}, u32[]{:S(2)}, u32[]{:S(2)}) %collective-permute-start.13) | collective-permute-done | bytes 262176 | tf_op jit(solution)/shard_map/ppermute | solution.py:63
  84.6 3.2 %collective-permute-start.17 = (f32[16,4096]{1,0:T(8,128)S(1)}, f32[16,4096]{1,0:T(8,128)S(1)}, u32[]{:S(2)}, u32[]{:S(2)}) collective-permute-start(f32[16,4096]{1,0:T(8,128)S(1)} %get-tuple-element.22), channel_id=1, source_target_pairs={{0,224},{2,34},{4,228},{6,38},{8,232},{10,42},{12,236},{14,46},{16... | collective-permute-start | bytes 786440 | tf_op jit(solution)/shard_map/ppermute | solution.py:71
  89.7 3.2 %collective-permute-start.27 = (f32[32,4096]{1,0:T(8,128)S(1)}, f32[32,4096]{1,0:T(8,128)S(1)}, u32[]{:S(2)}, u32[]{:S(2)}) collective-permute-start(f32[32,4096]{1,0:T(8,128)S(1)} %get-tuple-element.24), channel_id=1, source_target_pairs={{0,12},{2,6},{4,0},{6,10},{8,4},{10,14},{12,8},{14,2},{16,28},{18,... | collective-permute-start | bytes 1572872 | tf_op jit(solution)/shard_map/ppermute | solution.py:71
  93.4 3.2 %collective-permute-start.18 = (f32[16,4096]{1,0:T(8,128)S(1)}, f32[16,4096]{1,0:T(8,128)S(1)}, u32[]{:S(2)}, u32[]{:S(2)}) collective-permute-start(f32[16,4096]{1,0:T(8,128)S(1)} %get-tuple-element.20), channel_id=1, source_target_pairs={{0,224},{2,34},{4,228},{6,38},{8,232},{10,42},{12,236},{14,46},{16... | collective-permute-start | bytes 786440 | tf_op jit(solution)/shard_map/ppermute | solution.py:71
  96.6 9.0 %collective-permute-done.26 = f32[32,4096]{1,0:T(8,128)S(1)} collective-permute-done((f32[32,4096]{1,0:T(8,128)S(1)}, f32[32,4096]{1,0:T(8,128)S(1)}, u32[]{:S(2)}, u32[]{:S(2)}) %collective-permute-start.26) | collective-permute-done | bytes 524320 | tf_op jit(solution)/shard_map/ppermute | solution.py:63
  106.0 3.3 %collective-permute-start.19 = (f32[16,4096]{1,0:T(8,128)S(1)}, f32[16,4096]{1,0:T(8,128)S(1)}, u32[]{:S(2)}, u32[]{:S(2)}) collective-permute-start(f32[16,4096]{1,0:T(8,128)S(1)} %get-tuple-element.18), channel_id=1, source_target_pairs={{0,224},{2,34},{4,228},{6,38},{8,232},{10,42},{12,236},{14,46},{16... | collective-permute-start | bytes 786440 | tf_op jit(solution)/shard_map/ppermute | solution.py:71
  109.3 2.6 %collective-permute-done.28 = f32[4,4096]{1,0:T(4,128)S(1)} collective-permute-done((f32[4,4096]{1,0:T(4,128)S(1)}, f32[4,4096]{1,0:T(4,128)S(1)}, u32[]{:S(2)}, u32[]{:S(2)}) %collective-permute-start.28) | collective-permute-done | bytes 65568 | tf_op jit(solution)/shard_map/ppermute | solution.py:63
  112.1 3.2 %collective-permute-start.32 = (f32[4,4096]{1,0:T(4,128)S(1)}, f32[4,4096]{1,0:T(4,128)S(1)}, u32[]{:S(2)}, u32[]{:S(2)}) collective-permute-start(f32[4,4096]{1,0:T(4,128)S(1)} %get-tuple-element.30), channel_id=1, source_target_pairs={{0,224},{2,34},{4,228},{6,38},{8,232},{10,42},{12,236},{14,46},{16... | collective-permute-start | bytes 196616 | tf_op jit(solution)/shard_map/ppermute | solution.py:71
  117.8 3.3 %collective-permute-start.33 = (f32[4,4096]{1,0:T(4,128)S(1)}, f32[4,4096]{1,0:T(4,128)S(1)}, u32[]{:S(2)}, u32[]{:S(2)}) collective-permute-start(f32[4,4096]{1,0:T(4,128)S(1)} %get-tuple-element.28), channel_id=1, source_target_pairs={{0,224},{2,34},{4,228},{6,38},{8,232},{10,42},{12,236},{14,46},{16... | collective-permute-start | bytes 196616 | tf_op jit(solution)/shard_map/ppermute | solution.py:71
  122.8 3.2 %collective-permute-start.22 = (f32[4,4096]{1,0:T(4,128)S(1)}, f32[4,4096]{1,0:T(4,128)S(1)}, u32[]{:S(2)}, u32[]{:S(2)}) collective-permute-start(f32[4,4096]{1,0:T(4,128)S(1)} %get-tuple-element.32), channel_id=1, source_target_pairs={{0,12},{2,6},{4,0},{6,10},{8,4},{10,14},{12,8},{14,2},{16,28},{18,... | collective-permute-start | bytes 196616 | tf_op jit(solution)/shard_map/ppermute | solution.py:71
  126.1 3.2 %collective-permute-start.34 = (f32[4,4096]{1,0:T(4,128)S(1)}, f32[4,4096]{1,0:T(4,128)S(1)}, u32[]{:S(2)}, u32[]{:S(2)}) collective-permute-start(f32[4,4096]{1,0:T(4,128)S(1)} %get-tuple-element.26), channel_id=1, source_target_pairs={{0,224},{2,34},{4,228},{6,38},{8,232},{10,42},{12,236},{14,46},{16... | collective-permute-start | bytes 196616 | tf_op jit(solution)/shard_map/ppermute | solution.py:71
  134.9 2.2 %collective-permute-done.35 = f32[2,4096]{1,0:T(2,128)S(1)} collective-permute-done((f32[2,4096]{1,0:T(2,128)S(1)}, f32[2,4096]{1,0:T(2,128)S(1)}, u32[]{:S(2)}, u32[]{:S(2)}) %collective-permute-start.35) | collective-permute-done | bytes 32800 | tf_op jit(solution)/shard_map/ppermute | solution.py:63
  (127 shorter events, 39.7 us)
Async XLA Ops:
  1.8 7.7 %collective-permute-start = (bf16[2,8192]{1,0:T(2,128)(2,1)S(1)}, bf16[2,8192]{1,0:T(2,128)(2,1)S(1)}, u32[]{:S(2)}, u32[]{:S(2)}) collective-permute-start(bf16[2,8192]{1,0:T(2,128)(2,1)S(1)} %fusion.11), channel_id=1, source_target_pairs={{0,16},{2,18},{4,20},{6,22},{8,24},{10,26},{12,28},{14,30},{16,0},... | collective-permute-start | bytes 98312 | tf_op jit(solution)/shard_map/ppermute | solution.py:42
  11.3 9.1 %collective-permute-start.1 = (bf16[4,8192]{1,0:T(4,128)(2,1)S(1)}, bf16[4,8192]{1,0:T(4,128)(2,1)S(1)}, u32[]{:S(2)}, u32[]{:S(2)}) collective-permute-start(bf16[4,8192]{1,0:T(4,128)(2,1)S(1)} %pad_maximum_fusion.3), channel_id=1, source_target_pairs={{0,12},{2,6},{4,0},{6,10},{8,4},{10,14},{12,8},{14,2},{16,28},{18,... | collective-permute-start | bytes 196616 | tf_op jit(solution)/shard_map/ppermute | solution.py:46
  20.8 11.6 %collective-permute-start.4 = (bf16[16,8192]{1,0:T(8,128)(2,1)S(1)}, bf16[16,8192]{1,0:T(8,128)(2,1)S(1)}, u32[]{:S(2)}, u32[]{:S(2)}) collective-permute-start(bf16[16,8192]{1,0:T(8,128)(2,1)S(1)} %pad_maximum_fusion), channel_id=1, source_target_pairs={{0,224},{2,34},{4,228},{6,38},{8,232},{10,42},{12,236},{14,46},{16... | collective-permute-start | bytes 786440 | tf_op jit(solution)/shard_map/ppermute | solution.py:46
  26.7 9.4 %collective-permute-start.7 = (bf16[16,8192]{1,0:T(8,128)(2,1)S(1)}, bf16[16,8192]{1,0:T(8,128)(2,1)S(1)}, u32[]{:S(2)}, u32[]{:S(2)}) collective-permute-start(bf16[16,8192]{1,0:T(8,128)(2,1)S(1)} %pad_maximum_fusion), channel_id=1, source_target_pairs={{0,32},{2,226},{4,36},{6,230},{8,40},{10,234},{12,44},{14,238},{16... | collective-permute-start | bytes 786440 | tf_op jit(solution)/shard_map/ppermute | solution.py:42
  32.4 8.5 %collective-permute-start.5 = (bf16[16,8192]{1,0:T(8,128)(2,1)S(1)}, bf16[16,8192]{1,0:T(8,128)(2,1)S(1)}, u32[]{:S(2)}, u32[]{:S(2)}) collective-permute-start(bf16[16,8192]{1,0:T(8,128)(2,1)S(1)} %collective-permute-done.4), channel_id=1, source_target_pairs={{0,224},{2,34},{4,228},{6,38},{8,232},{10,42},{12,236},{14,46},{16... | collective-permute-start | bytes 786440 | tf_op jit(solution)/shard_map/ppermute | solution.py:46
  36.1 10.2 %collective-permute-start.8 = (bf16[16,8192]{1,0:T(8,128)(2,1)S(1)}, bf16[16,8192]{1,0:T(8,128)(2,1)S(1)}, u32[]{:S(2)}, u32[]{:S(2)}) collective-permute-start(bf16[16,8192]{1,0:T(8,128)(2,1)S(1)} %collective-permute-done.7), channel_id=1, source_target_pairs={{0,32},{2,226},{4,36},{6,230},{8,40},{10,234},{12,44},{14,238},{16... | collective-permute-start | bytes 786440 | tf_op jit(solution)/shard_map/ppermute | solution.py:42
  41.0 13.0 %collective-permute-start.6 = (bf16[16,8192]{1,0:T(8,128)(2,1)S(1)}, bf16[16,8192]{1,0:T(8,128)(2,1)S(1)}, u32[]{:S(2)}, u32[]{:S(2)}) collective-permute-start(bf16[16,8192]{1,0:T(8,128)(2,1)S(1)} %collective-permute-done.5), channel_id=1, source_target_pairs={{0,224},{2,34},{4,228},{6,38},{8,232},{10,42},{12,236},{14,46},{16... | collective-permute-start | bytes 786440 | tf_op jit(solution)/shard_map/ppermute | solution.py:46
  46.4 7.6 %collective-permute-start.9 = (bf16[16,8192]{1,0:T(8,128)(2,1)S(1)}, bf16[16,8192]{1,0:T(8,128)(2,1)S(1)}, u32[]{:S(2)}, u32[]{:S(2)}) collective-permute-start(bf16[16,8192]{1,0:T(8,128)(2,1)S(1)} %collective-permute-done.8), channel_id=1, source_target_pairs={{0,32},{2,226},{4,36},{6,230},{8,40},{10,234},{12,44},{14,238},{16... | collective-permute-start | bytes 786440 | tf_op jit(solution)/shard_map/ppermute | solution.py:42
  53.9 7.6 %collective-permute-start.10 = (bf16[16,8192]{1,0:T(8,128)(2,1)S(1)}, bf16[16,8192]{1,0:T(8,128)(2,1)S(1)}, u32[]{:S(2)}, u32[]{:S(2)}) collective-permute-start(bf16[16,8192]{1,0:T(8,128)(2,1)S(1)} %collective-permute-done.9), channel_id=1, source_target_pairs={{0,32},{2,226},{4,36},{6,230},{8,40},{10,234},{12,44},{14,238},{16... | collective-permute-start | bytes 786440 | tf_op jit(solution)/shard_map/ppermute | solution.py:42
  76.8 7.7 %collective-permute-start.13 = (f32[16,4096]{1,0:T(8,128)S(1)}, f32[16,4096]{1,0:T(8,128)S(1)}, u32[]{:S(2)}, u32[]{:S(2)}) collective-permute-start(f32[16,4096]{1,0:T(8,128)S(1)} %slice.139), channel_id=1, source_target_pairs={{0,32},{2,226},{4,36},{6,230},{8,40},{10,234},{12,44},{14,238},{16... | collective-permute-start | bytes 786440 | tf_op jit(solution)/shard_map/ppermute | solution.py:63
  79.1 10.5 %collective-permute-start.25 = (f32[32,4096]{1,0:T(8,128)S(1)}, f32[32,4096]{1,0:T(8,128)S(1)}, u32[]{:S(2)}, u32[]{:S(2)}) collective-permute-start(f32[32,4096]{1,0:T(8,128)S(1)} %slice.155), channel_id=1, source_target_pairs={{0,4},{2,14},{4,8},{6,2},{8,12},{10,6},{12,0},{14,10},{16,20},{18,... | collective-permute-start | bytes 1572872 | tf_op jit(solution)/shard_map/ppermute | solution.py:63
  84.5 8.7 %collective-permute-start.14 = (f32[16,4096]{1,0:T(8,128)S(1)}, f32[16,4096]{1,0:T(8,128)S(1)}, u32[]{:S(2)}, u32[]{:S(2)}) collective-permute-start(f32[16,4096]{1,0:T(8,128)S(1)} %get-tuple-element.21), channel_id=1, source_target_pairs={{0,32},{2,226},{4,36},{6,230},{8,40},{10,234},{12,44},{14,238},{16... | collective-permute-start | bytes 786440 | tf_op jit(solution)/shard_map/ppermute | solution.py:63
  84.6 8.6 %collective-permute-start.17 = (f32[16,4096]{1,0:T(8,128)S(1)}, f32[16,4096]{1,0:T(8,128)S(1)}, u32[]{:S(2)}, u32[]{:S(2)}) collective-permute-start(f32[16,4096]{1,0:T(8,128)S(1)} %get-tuple-element.22), channel_id=1, source_target_pairs={{0,224},{2,34},{4,228},{6,38},{8,232},{10,42},{12,236},{14,46},{16... | collective-permute-start | bytes 786440 | tf_op jit(solution)/shard_map/ppermute | solution.py:71
  89.6 16.0 %collective-permute-start.26 = (f32[32,4096]{1,0:T(8,128)S(1)}, f32[32,4096]{1,0:T(8,128)S(1)}, u32[]{:S(2)}, u32[]{:S(2)}) collective-permute-start(f32[32,4096]{1,0:T(8,128)S(1)} %get-tuple-element.23), channel_id=1, source_target_pairs={{0,4},{2,14},{4,8},{6,2},{8,12},{10,6},{12,0},{14,10},{16,20},{18,... | collective-permute-start | bytes 1572872 | tf_op jit(solution)/shard_map/ppermute | solution.py:63
  89.7 15.9 %collective-permute-start.27 = (f32[32,4096]{1,0:T(8,128)S(1)}, f32[32,4096]{1,0:T(8,128)S(1)}, u32[]{:S(2)}, u32[]{:S(2)}) collective-permute-start(f32[32,4096]{1,0:T(8,128)S(1)} %get-tuple-element.24), channel_id=1, source_target_pairs={{0,12},{2,6},{4,0},{6,10},{8,4},{10,14},{12,8},{14,2},{16,28},{18,... | collective-permute-start | bytes 1572872 | tf_op jit(solution)/shard_map/ppermute | solution.py:71
  93.3 12.6 %collective-permute-start.15 = (f32[16,4096]{1,0:T(8,128)S(1)}, f32[16,4096]{1,0:T(8,128)S(1)}, u32[]{:S(2)}, u32[]{:S(2)}) collective-permute-start(f32[16,4096]{1,0:T(8,128)S(1)} %get-tuple-element.19), channel_id=1, source_target_pairs={{0,32},{2,226},{4,36},{6,230},{8,40},{10,234},{12,44},{14,238},{16... | collective-permute-start | bytes 786440 | tf_op jit(solution)/shard_map/ppermute | solution.py:63
  93.4 12.5 %collective-permute-start.18 = (f32[16,4096]{1,0:T(8,128)S(1)}, f32[16,4096]{1,0:T(8,128)S(1)}, u32[]{:S(2)}, u32[]{:S(2)}) collective-permute-start(f32[16,4096]{1,0:T(8,128)S(1)} %get-tuple-element.20), channel_id=1, source_target_pairs={{0,224},{2,34},{4,228},{6,38},{8,232},{10,42},{12,236},{14,46},{16... | collective-permute-start | bytes 786440 | tf_op jit(solution)/shard_map/ppermute | solution.py:71
  105.8 6.2 %collective-permute-start.28 = (f32[4,4096]{1,0:T(4,128)S(1)}, f32[4,4096]{1,0:T(4,128)S(1)}, u32[]{:S(2)}, u32[]{:S(2)}) collective-permute-start(f32[4,4096]{1,0:T(4,128)S(1)} %slice.159), channel_id=1, source_target_pairs={{0,32},{2,226},{4,36},{6,230},{8,40},{10,234},{12,44},{14,238},{16... | collective-permute-start | bytes 196616 | tf_op jit(solution)/shard_map/ppermute | solution.py:63
  106.0 11.0 %collective-permute-start.16 = (f32[16,4096]{1,0:T(8,128)S(1)}, f32[16,4096]{1,0:T(8,128)S(1)}, u32[]{:S(2)}, u32[]{:S(2)}) collective-permute-start(f32[16,4096]{1,0:T(8,128)S(1)} %get-tuple-element.17), channel_id=1, source_target_pairs={{0,32},{2,226},{4,36},{6,230},{8,40},{10,234},{12,44},{14,238},{16... | collective-permute-start | bytes 786440 | tf_op jit(solution)/shard_map/ppermute | solution.py:63
  106.0 11.0 %collective-permute-start.19 = (f32[16,4096]{1,0:T(8,128)S(1)}, f32[16,4096]{1,0:T(8,128)S(1)}, u32[]{:S(2)}, u32[]{:S(2)}) collective-permute-start(f32[16,4096]{1,0:T(8,128)S(1)} %get-tuple-element.18), channel_id=1, source_target_pairs={{0,224},{2,34},{4,228},{6,38},{8,232},{10,42},{12,236},{14,46},{16... | collective-permute-start | bytes 786440 | tf_op jit(solution)/shard_map/ppermute | solution.py:71
  117.7 8.2 %collective-permute-start.30 = (f32[4,4096]{1,0:T(4,128)S(1)}, f32[4,4096]{1,0:T(4,128)S(1)}, u32[]{:S(2)}, u32[]{:S(2)}) collective-permute-start(f32[4,4096]{1,0:T(4,128)S(1)} %get-tuple-element.27), channel_id=1, source_target_pairs={{0,32},{2,226},{4,36},{6,230},{8,40},{10,234},{12,44},{14,238},{16... | collective-permute-start | bytes 196616 | tf_op jit(solution)/shard_map/ppermute | solution.py:63
  117.8 8.1 %collective-permute-start.33 = (f32[4,4096]{1,0:T(4,128)S(1)}, f32[4,4096]{1,0:T(4,128)S(1)}, u32[]{:S(2)}, u32[]{:S(2)}) collective-permute-start(f32[4,4096]{1,0:T(4,128)S(1)} %get-tuple-element.28), channel_id=1, source_target_pairs={{0,224},{2,34},{4,228},{6,38},{8,232},{10,42},{12,236},{14,46},{16... | collective-permute-start | bytes 196616 | tf_op jit(solution)/shard_map/ppermute | solution.py:71
  122.7 6.7 %collective-permute-start.21 = (f32[4,4096]{1,0:T(4,128)S(1)}, f32[4,4096]{1,0:T(4,128)S(1)}, u32[]{:S(2)}, u32[]{:S(2)}) collective-permute-start(f32[4,4096]{1,0:T(4,128)S(1)} %get-tuple-element.31), channel_id=1, source_target_pairs={{0,4},{2,14},{4,8},{6,2},{8,12},{10,6},{12,0},{14,10},{16,20},{18,... | collective-permute-start | bytes 196616 | tf_op jit(solution)/shard_map/ppermute | solution.py:63
  122.8 6.6 %collective-permute-start.22 = (f32[4,4096]{1,0:T(4,128)S(1)}, f32[4,4096]{1,0:T(4,128)S(1)}, u32[]{:S(2)}, u32[]{:S(2)}) collective-permute-start(f32[4,4096]{1,0:T(4,128)S(1)} %get-tuple-element.32), channel_id=1, source_target_pairs={{0,12},{2,6},{4,0},{6,10},{8,4},{10,14},{12,8},{14,2},{16,28},{18,... | collective-permute-start | bytes 196616 | tf_op jit(solution)/shard_map/ppermute | solution.py:71
  (19 other events, 177.3 us)

commit v4 on v0

--- a/solution.py
+++ b/solution.py
@@ -4,10 +4,10 @@
 from jax.sharding import PartitionSpec as P
 
 BLK_AXES = {"z": (16, 8), "xh": (8, 2), "y": (2, 4), "c": (1, 2)}
-AG_ORDER = ("xh", "y", "z", "c")
+AG_ORDER = ("xh", "y", "z")
 PARTS = (
-    (32, ("c", "z", "y", "xh")),
-    (32, ("c", "y", "z", "xh")),
+    (32, ("z", "y", "xh")),
+    (32, ("y", "z", "xh")),
 )
 
 
@@ -22,10 +22,12 @@
 
 def _perm(axis, k, size):
     stride, n = BLK_AXES[axis]
+    cstride = BLK_AXES["c"][0]
     pairs = []
     for i in range(size):
+        kk = k if (i // cstride) % 2 == 0 else -k
         coord = (i // stride) % n
-        pairs.append((i, i + ((coord + k) % n - coord) * stride))
+        pairs.append((i, i + ((coord + kk) % n - coord) * stride))
     return pairs
 
 
@@ -95,18 +97,29 @@
 
     base = tuple(reversed(AG_ORDER))
     piece = normed
-    for axis in AG_ORDER:
+    tied = [(gate_kept,), (up_kept, down_kept), ()]
+    kept = []
+    for i, axis in enumerate(AG_ORDER):
         piece = _ag_stage(piece, axis, size)
-    gate = jnp.dot(piece, gate_kept, preferred_element_type=jnp.float32)
-    up_val = jnp.dot(piece, up_kept, preferred_element_type=jnp.float32)
-    hidden = (jax.nn.silu(gate) * up_val).astype(jnp.bfloat16)
+        piece, done = lax.optimization_barrier((piece, tied[i]))
+        kept.extend(done)
+    swap = _perm("c", 1, size)
+    weights = [(w, lax.ppermute(w, "blk", swap)) for w in kept]
+    hidden = []
+    for g_w, u_w in zip(weights[0], weights[1]):
+        gate = jnp.dot(piece, g_w, preferred_element_type=jnp.float32)
+        up_val = jnp.dot(piece, u_w, preferred_element_type=jnp.float32)
+        hidden.append((jax.nn.silu(gate) * up_val).astype(jnp.bfloat16))
 
     outs = []
     lo = 0
     for groups, rs_order in PARTS:
         hi = lo + groups * 128
-        h = hidden if rs_order == base else _reorder_rows(hidden, base, rs_order, t)
-        x = jnp.dot(h, down_kept[:, lo:hi], preferred_element_type=jnp.float32)
+        x = None
+        for h, d_w in zip(hidden, weights[2]):
+            h = h if rs_order == base else _reorder_rows(h, base, rs_order, t)
+            y = jnp.dot(h, d_w[:, lo:hi], preferred_element_type=jnp.float32)
+            x = y if x is None else x + y
         for axis in rs_order:
             x = _rs_stage(x, axis, size)
         outs.append(x)

time: 180 us -> 145 us (0.81)
  local copies, waits for them, and re-layouts: 34.7 us -> 1.13 us
  waiting for transfers between devices: 67.7 us -> 49.4 us
  matrix products: 9.26 us -> 23.8 us
  starting transfers between devices: 51.2 us -> 54.4 us
    concatenate x3 -> x1, local copies, waits for them, and re-layouts: 24.2 us -> 0.02 us  [_ag_stage(): return jnp.concatenate(got, axis=0)]
    ppermute x8 -> x7, waiting for transfers between devices: 35.5 us -> 18.3 us  [_ag_stage(): cur = lax.ppermute(cur, 'blk', _perm(axis, 1, size))]
    dot_general x4 -> x8, matrix products: 9.26 us -> 23.8 us  [the longest x4 12.2 us: local(): y = jnp.dot(h, d_w[:, lo:hi], preferred_element_type=jnp.float32)]
    ppermute x16 -> x14, waiting for transfers between devices: 31.7 us -> 17.6 us  [_rs_stage(): recv = lax.ppermute(buf, 'blk', _perm(axis, 1, size))]
    ppermute x4, waiting for transfers between devices: 0.01 us -> 11 us  [_ag_stage(): cur = lax.ppermute(cur, 'blk', _perm(axis, -1, size))]
    unnamed x26 -> x17, local copies, waits for them, and re-layouts: 6.78 us -> 0.28 us
    ppermute x8, starting transfers between devices: 24 us -> 27.2 us  [_rs_stage(): recv = lax.ppermute(buf, 'blk', _perm(axis, -1, size))]
    ppermute x4, starting transfers between devices: 12.5 us -> 15 us  [_ag_stage(): cur = lax.ppermute(cur, 'blk', _perm(axis, -1, size))]
  transfers between devices with their start and end apart: 36 -> 36, of which waited for: 19 -> 18; matrix products, arithmetic and copies ran while one was open for 10% -> 24% of each run, Pallas kernels for 0% -> 0%
where the time goes in v4:
time: 145 us
  starting transfers between devices  54.4 us (38%)
  waiting for transfers between devices  49.4 us (34%)
  matrix products  23.8 us (16%)
  other arithmetic  15.4 us (11%)
    ppermute x8, starting transfers between devices, _rs_stage(): recv = lax.ppermute(buf, 'blk', _perm(axis, -1, size))  27.2 us
    ppermute x7, waiting for transfers between devices, _ag_stage(): cur = lax.ppermute(cur, 'blk', _perm(axis, 1, size))  18.3 us
    ppermute x14, waiting for transfers between devices, _rs_stage(): recv = lax.ppermute(buf, 'blk', _perm(axis, 1, size))  17.6 us
    ppermute x4, starting transfers between devices, _ag_stage(): cur = lax.ppermute(cur, 'blk', _perm(axis, -1, size))  15 us
    dot_general x4, matrix products, local(): y = jnp.dot(h, d_w[:, lo:hi], preferred_element_type=jnp.float32)  12.2 us
    mul x3, other arithmetic, mask_blocks(): return (shaped * cols[:, None, :]).reshape(height, width)  11.3 us
    ppermute x4, waiting for transfers between devices, _ag_stage(): cur = lax.ppermute(cur, 'blk', _perm(axis, -1, size))  11 us
    ppermute x14, starting transfers between devices, _rs_stage(): recv = lax.ppermute(buf, 'blk', _perm(axis, 1, size))  6.64 us
  transfers between devices with their start and end apart: 36, of which 18 were waited for; matrix products, arithmetic and copies ran while one was open for 24% of the time, Pallas kernels for 0%

profile of v4, /device:TPU:2, one launch (start us, length us, event | category | flops | bytes accessed | tf_op | source)
XLA Modules:
  0.0 144.6 jit_solution(3042465873079956379)
XLA Ops:
  5.0 4.4 %bitcast_multiply_fusion.2 = bf16[8192,256]{1,0:T(8,128)(2,1)} fusion(bf16[8192,256]{1,0:T(8,128)(2,1)} %param.10, bf16[64,256]{1,0:T(8,128)(2,1)S(1)} %bitcast.41), kind=kLoop, calls=%fused_computation.4 | loop fusion | flops 2097152 | bytes 8421376 | tf_op jit(solution)/shard_map/mul | solution.py:20
  16.5 4.7 %bitcast_multiply_fusion.1 = bf16[8192,256]{1,0:T(8,128)(2,1)} fusion(bf16[8192,256]{1,0:T(8,128)(2,1)} %param.11, bf16[64,256]{1,0:T(8,128)(2,1)S(1)} %bitcast.39), kind=kLoop, calls=%fused_computation.3 | loop fusion | flops 2097152 | bytes 8421376 | tf_op jit(solution)/shard_map/mul | solution.py:20
  23.7 5.9 %collective-permute-start.4 = (bf16[16,8192]{1,0:T(8,128)(2,1)S(1)}, bf16[16,8192]{1,0:T(8,128)(2,1)S(1)}, u32[]{:S(2)}, u32[]{:S(2)}) collective-permute-start(bf16[16,8192]{1,0:T(8,128)(2,1)S(1)} %pad_maximum_fusion), channel_id=1, source_target_pairs={{0,224},{2,34},{4,228},{6,38},{8,232},{10,42},{12,236},{14,46},{16... | collective-permute-start | bytes 786440 | tf_op jit(solution)/shard_map/ppermute | solution.py:46
  30.3 5.6 %collective-permute-done.4 = bf16[16,8192]{1,0:T(8,128)(2,1)S(1)} collective-permute-done((bf16[16,8192]{1,0:T(8,128)(2,1)S(1)}, bf16[16,8192]{1,0:T(8,128)(2,1)S(1)}, u32[]{:S(2)}, u32[]{:S(2)}) %collective-permute-start.4) | collective-permute-done | bytes 262176 | tf_op jit(solution)/shard_map/ppermute | solution.py:46
  35.9 3.7 %collective-permute-start.5 = (bf16[16,8192]{1,0:T(8,128)(2,1)S(1)}, bf16[16,8192]{1,0:T(8,128)(2,1)S(1)}, u32[]{:S(2)}, u32[]{:S(2)}) collective-permute-start(bf16[16,8192]{1,0:T(8,128)(2,1)S(1)} %collective-permute-done.4), channel_id=1, source_target_pairs={{0,224},{2,34},{4,228},{6,38},{8,232},{10,42},{12,236},{14,46},{16... | collective-permute-start | bytes 786440 | tf_op jit(solution)/shard_map/ppermute | solution.py:46
  39.6 5.4 %collective-permute-done.5 = bf16[16,8192]{1,0:T(8,128)(2,1)S(1)} collective-permute-done((bf16[16,8192]{1,0:T(8,128)(2,1)S(1)}, bf16[16,8192]{1,0:T(8,128)(2,1)S(1)}, u32[]{:S(2)}, u32[]{:S(2)}) %collective-permute-start.5) | collective-permute-done | bytes 262176 | tf_op jit(solution)/shard_map/ppermute | solution.py:46
  45.0 3.7 %collective-permute-start.6 = (bf16[16,8192]{1,0:T(8,128)(2,1)S(1)}, bf16[16,8192]{1,0:T(8,128)(2,1)S(1)}, u32[]{:S(2)}, u32[]{:S(2)}) collective-permute-start(bf16[16,8192]{1,0:T(8,128)(2,1)S(1)} %collective-permute-done.5), channel_id=1, source_target_pairs={{0,224},{2,34},{4,228},{6,38},{8,232},{10,42},{12,236},{14,46},{16... | collective-permute-start | bytes 786440 | tf_op jit(solution)/shard_map/ppermute | solution.py:46
  49.7 7.6 %collective-permute-done.9 = bf16[16,8192]{1,0:T(8,128)(2,1)S(1)} collective-permute-done((bf16[16,8192]{1,0:T(8,128)(2,1)S(1)}, bf16[16,8192]{1,0:T(8,128)(2,1)S(1)}, u32[]{:S(2)}, u32[]{:S(2)}) %collective-permute-start.9) | collective-permute-done | bytes 262176 | tf_op jit(solution)/shard_map/ppermute | solution.py:42
  57.2 7.6 %collective-permute-done.10 = bf16[16,8192]{1,0:T(8,128)(2,1)S(1)} collective-permute-done((bf16[16,8192]{1,0:T(8,128)(2,1)S(1)}, bf16[16,8192]{1,0:T(8,128)(2,1)S(1)}, u32[]{:S(2)}, u32[]{:S(2)}) %collective-permute-start.10) | collective-permute-done | bytes 262176 | tf_op jit(solution)/shard_map/ppermute | solution.py:42
  64.9 2.9 %fusion.15 = f32[128,256]{1,0:T(8,128)S(1)} fusion(bf16[128,8192]{1,0:T(8,128)(2,1)S(1)} %constant_dynamic-update-slice_fusion, bf16[8192,256]{1,0:T(8,128)(2,1)} %bitcast_multiply_fusion.2), kind=kOutput, calls=%fused_computation.60 | convolution fusion | flops 536870912 | bytes 6422528 | tf_op jit(solution)/shard_map/dot_general | solution.py:110
  67.8 2.9 %multiply_convert_fusion.1 = bf16[128,256]{1,0:T(8,128)(2,1)S(1)} fusion(f32[128,256]{1,0:T(8,128)S(1)} %fusion.15, bf16[128,8192]{1,0:T(8,128)(2,1)S(1)} %constant_dynamic-update-slice_fusion, bf16[8192,256]{1,0:T(8,128)(2,1)} %bitcast_multiply_fusion.1), kind=kOutput, calls=%fused_computation.23 | convolution fusion | flops 537067520 | bytes 6488064 | tf_op jit(solution)/shard_map/dot_general | solution.py:111
  70.9 3.4 %fusion.4 = f32[128,4096]{1,0:T(8,128)} fusion(bf16[128,256]{1,0:T(8,128)(2,1)S(1)} %multiply_convert_fusion.1, bf16[256,8192]{1,0:T(8,128)(2,1)} %bitcast_multiply_fusion), kind=kOutput, calls=%fused_computation.9 | convolution fusion | flops 268435456 | bytes 4259840 | tf_op jit(solution)/shard_map/dot_general | solution.py:121
  74.3 3.4 %fusion.2 = f32[128,4096]{1,0:T(8,128)} fusion(bf16[128,256]{1,0:T(8,128)(2,1)S(1)} %reshape.34, bf16[256,8192]{1,0:T(8,128)(2,1)} %bitcast_multiply_fusion), kind=kOutput, calls=%fused_computation.7 | convolution fusion | flops 268435456 | bytes 4259840 | tf_op jit(solution)/shard_map/dot_general | solution.py:121
  77.7 2.9 %fusion.16 = f32[128,256]{1,0:T(8,128)S(1)} fusion(bf16[128,8192]{1,0:T(8,128)(2,1)S(1)} %constant_dynamic-update-slice_fusion, bf16[8192,256]{1,0:T(8,128)(2,1)} %collective-permute-done.11), kind=kOutput, calls=%fused_computation.61 | convolution fusion | flops 536870912 | bytes 6422528 | tf_op jit(solution)/shard_map/dot_general | solution.py:110
  80.6 2.9 %multiply_convert_fusion = bf16[128,256]{1,0:T(8,128)(2,1)S(1)} fusion(f32[128,256]{1,0:T(8,128)S(1)} %fusion.16, bf16[128,8192]{1,0:T(8,128)(2,1)S(1)} %constant_dynamic-update-slice_fusion, bf16[8192,256]{1,0:T(8,128)(2,1)} %collective-permute-done.12), kind=kOutput, calls=%fused_computation.22 | convolution fusion | flops 537067520 | bytes 6488064 | tf_op jit(solution)/shard_map/dot_general | solution.py:111
  90.3 4.6 %collective-permute-done.14 = f32[16,4096]{1,0:T(8,128)S(1)} collective-permute-done((f32[16,4096]{1,0:T(8,128)S(1)}, f32[16,4096]{1,0:T(8,128)S(1)}, u32[]{:S(2)}, u32[]{:S(2)}) %collective-permute-start.14) | collective-permute-done | bytes 262176 | tf_op jit(solution)/shard_map/ppermute | solution.py:63
  95.0 3.2 %collective-permute-start.18 = (f32[16,4096]{1,0:T(8,128)S(1)}, f32[16,4096]{1,0:T(8,128)S(1)}, u32[]{:S(2)}, u32[]{:S(2)}) collective-permute-start(f32[16,4096]{1,0:T(8,128)S(1)} %get-tuple-element.20), channel_id=1, source_target_pairs={{0,224},{2,34},{4,228},{6,38},{8,232},{10,42},{12,236},{14,46},{16... | collective-permute-start | bytes 786440 | tf_op jit(solution)/shard_map/ppermute | solution.py:71
  99.8 3.2 %collective-permute-start.27 = (f32[32,4096]{1,0:T(8,128)S(1)}, f32[32,4096]{1,0:T(8,128)S(1)}, u32[]{:S(2)}, u32[]{:S(2)}) collective-permute-start(f32[32,4096]{1,0:T(8,128)S(1)} %get-tuple-element.22), channel_id=1, source_target_pairs={{0,12},{2,6},{4,0},{6,10},{8,4},{10,14},{12,8},{14,2},{16,28},{18,... | collective-permute-start | bytes 1572872 | tf_op jit(solution)/shard_map/ppermute | solution.py:71
  104.1 4.0 %collective-permute-start.19 = (f32[16,4096]{1,0:T(8,128)S(1)}, f32[16,4096]{1,0:T(8,128)S(1)}, u32[]{:S(2)}, u32[]{:S(2)}) collective-permute-start(f32[16,4096]{1,0:T(8,128)S(1)} %get-tuple-element.18), channel_id=1, source_target_pairs={{0,224},{2,34},{4,228},{6,38},{8,232},{10,42},{12,236},{14,46},{16... | collective-permute-start | bytes 786440 | tf_op jit(solution)/shard_map/ppermute | solution.py:71
  108.1 4.1 %collective-permute-done.26 = f32[32,4096]{1,0:T(8,128)S(1)} collective-permute-done((f32[32,4096]{1,0:T(8,128)S(1)}, f32[32,4096]{1,0:T(8,128)S(1)}, u32[]{:S(2)}, u32[]{:S(2)}) %collective-permute-start.26) | collective-permute-done | bytes 524320 | tf_op jit(solution)/shard_map/ppermute | solution.py:63
  115.1 3.8 %collective-permute-start.20 = (f32[16,4096]{1,0:T(8,128)S(1)}, f32[16,4096]{1,0:T(8,128)S(1)}, u32[]{:S(2)}, u32[]{:S(2)}) collective-permute-start(f32[16,4096]{1,0:T(8,128)S(1)} %get-tuple-element.16), channel_id=1, source_target_pairs={{0,224},{2,34},{4,228},{6,38},{8,232},{10,42},{12,236},{14,46},{16... | collective-permute-start | bytes 786440 | tf_op jit(solution)/shard_map/ppermute | solution.py:71
  119.0 3.2 %collective-permute-start.32 = (f32[4,4096]{1,0:T(4,128)S(1)}, f32[4,4096]{1,0:T(4,128)S(1)}, u32[]{:S(2)}, u32[]{:S(2)}) collective-permute-start(f32[4,4096]{1,0:T(4,128)S(1)} %get-tuple-element.28), channel_id=1, source_target_pairs={{0,224},{2,34},{4,228},{6,38},{8,232},{10,42},{12,236},{14,46},{16... | collective-permute-start | bytes 196616 | tf_op jit(solution)/shard_map/ppermute | solution.py:71
  124.6 3.5 %collective-permute-start.33 = (f32[4,4096]{1,0:T(4,128)S(1)}, f32[4,4096]{1,0:T(4,128)S(1)}, u32[]{:S(2)}, u32[]{:S(2)}) collective-permute-start(f32[4,4096]{1,0:T(4,128)S(1)} %get-tuple-element.26), channel_id=1, source_target_pairs={{0,224},{2,34},{4,228},{6,38},{8,232},{10,42},{12,236},{14,46},{16... | collective-permute-start | bytes 196616 | tf_op jit(solution)/shard_map/ppermute | solution.py:71
  132.4 3.7 %collective-permute-start.34 = (f32[4,4096]{1,0:T(4,128)S(1)}, f32[4,4096]{1,0:T(4,128)S(1)}, u32[]{:S(2)}, u32[]{:S(2)}) collective-permute-start(f32[4,4096]{1,0:T(4,128)S(1)} %get-tuple-element.24), channel_id=1, source_target_pairs={{0,224},{2,34},{4,228},{6,38},{8,232},{10,42},{12,236},{14,46},{16... | collective-permute-start | bytes 196616 | tf_op jit(solution)/shard_map/ppermute | solution.py:71
  (116 shorter events, 43.9 us)
Async XLA Ops:
  1.8 7.6 %collective-permute-start = (bf16[2,8192]{1,0:T(2,128)(2,1)S(1)}, bf16[2,8192]{1,0:T(2,128)(2,1)S(1)}, u32[]{:S(2)}, u32[]{:S(2)}) collective-permute-start(bf16[2,8192]{1,0:T(2,128)(2,1)S(1)} %fusion.10), channel_id=1, source_target_pairs={{0,16},{2,18},{4,20},{6,22},{8,24},{10,26},{12,28},{14,30},{16,0},... | collective-permute-start | bytes 98312 | tf_op jit(solution)/shard_map/ppermute | solution.py:42
  11.2 12.4 %collective-permute-start.1 = (bf16[4,8192]{1,0:T(4,128)(2,1)S(1)}, bf16[4,8192]{1,0:T(4,128)(2,1)S(1)}, u32[]{:S(2)}, u32[]{:S(2)}) collective-permute-start(bf16[4,8192]{1,0:T(4,128)(2,1)S(1)} %pad_maximum_fusion.1), channel_id=1, source_target_pairs={{0,12},{2,6},{4,0},{6,10},{8,4},{10,14},{12,8},{14,2},{16,28},{18,... | collective-permute-start | bytes 196616 | tf_op jit(solution)/shard_map/ppermute | solution.py:46
  15.1 8.5 %collective-permute-start.3 = (bf16[4,8192]{1,0:T(4,128)(2,1)S(1)}, bf16[4,8192]{1,0:T(4,128)(2,1)S(1)}, u32[]{:S(2)}, u32[]{:S(2)}) collective-permute-start(bf16[4,8192]{1,0:T(4,128)(2,1)S(1)} %collective-permute-done.2), channel_id=1, source_target_pairs={{0,4},{2,14},{4,8},{6,2},{8,12},{10,6},{12,0},{14,10},{16,20},{18,... | collective-permute-start | bytes 196616 | tf_op jit(solution)/shard_map/ppermute | solution.py:42
  23.4 54.2 %collective-permute-start.11 = (bf16[8192,256]{1,0:T(8,128)(2,1)}, bf16[8192,256]{1,0:T(8,128)(2,1)}, u32[]{:S(2)}, u32[]{:S(2)}) collective-permute-start(bf16[8192,256]{1,0:T(8,128)(2,1)} %bitcast_multiply_fusion.2), channel_id=1, source_target_pairs={{0,2},{2,0},{4,6},{6,4},{8,10},{10,8},{12,14},{14,12},{16,18},{18,... | collective-permute-start | bytes 12582920 | tf_op jit(solution)/shard_map/ppermute | solution.py:107
  23.7 12.2 %collective-permute-start.4 = (bf16[16,8192]{1,0:T(8,128)(2,1)S(1)}, bf16[16,8192]{1,0:T(8,128)(2,1)S(1)}, u32[]{:S(2)}, u32[]{:S(2)}) collective-permute-start(bf16[16,8192]{1,0:T(8,128)(2,1)S(1)} %pad_maximum_fusion), channel_id=1, source_target_pairs={{0,224},{2,34},{4,228},{6,38},{8,232},{10,42},{12,236},{14,46},{16... | collective-permute-start | bytes 786440 | tf_op jit(solution)/shard_map/ppermute | solution.py:46
  29.7 9.9 %collective-permute-start.7 = (bf16[16,8192]{1,0:T(8,128)(2,1)S(1)}, bf16[16,8192]{1,0:T(8,128)(2,1)S(1)}, u32[]{:S(2)}, u32[]{:S(2)}) collective-permute-start(bf16[16,8192]{1,0:T(8,128)(2,1)S(1)} %pad_maximum_fusion), channel_id=1, source_target_pairs={{0,32},{2,226},{4,36},{6,230},{8,40},{10,234},{12,44},{14,238},{16... | collective-permute-start | bytes 786440 | tf_op jit(solution)/shard_map/ppermute | solution.py:42
  29.7 50.9 %collective-permute-start.12 = (bf16[8192,256]{1,0:T(8,128)(2,1)}, bf16[8192,256]{1,0:T(8,128)(2,1)}, u32[]{:S(2)}, u32[]{:S(2)}) collective-permute-start(bf16[8192,256]{1,0:T(8,128)(2,1)} %bitcast_multiply_fusion.1), channel_id=1, source_target_pairs={{0,2},{2,0},{4,6},{6,4},{8,10},{10,8},{12,14},{14,12},{16,18},{18,... | collective-permute-start | bytes 12582920 | tf_op jit(solution)/shard_map/ppermute | solution.py:107
  30.0 53.6 %collective-permute-start.13 = (bf16[256,8192]{1,0:T(8,128)(2,1)}, bf16[256,8192]{1,0:T(8,128)(2,1)}, u32[]{:S(2)}, u32[]{:S(2)}) collective-permute-start(bf16[256,8192]{1,0:T(8,128)(2,1)} %bitcast_multiply_fusion), channel_id=1, source_target_pairs={{0,2},{2,0},{4,6},{6,4},{8,10},{10,8},{12,14},{14,12},{16,18},{18,... | collective-permute-start | bytes 12582920 | tf_op jit(solution)/shard_map/ppermute | solution.py:107
  35.9 9.1 %collective-permute-start.5 = (bf16[16,8192]{1,0:T(8,128)(2,1)S(1)}, bf16[16,8192]{1,0:T(8,128)(2,1)S(1)}, u32[]{:S(2)}, u32[]{:S(2)}) collective-permute-start(bf16[16,8192]{1,0:T(8,128)(2,1)S(1)} %collective-permute-done.4), channel_id=1, source_target_pairs={{0,224},{2,34},{4,228},{6,38},{8,232},{10,42},{12,236},{14,46},{16... | collective-permute-start | bytes 786440 | tf_op jit(solution)/shard_map/ppermute | solution.py:46
  39.6 10.1 %collective-permute-start.8 = (bf16[16,8192]{1,0:T(8,128)(2,1)S(1)}, bf16[16,8192]{1,0:T(8,128)(2,1)S(1)}, u32[]{:S(2)}, u32[]{:S(2)}) collective-permute-start(bf16[16,8192]{1,0:T(8,128)(2,1)S(1)} %collective-permute-done.7), channel_id=1, source_target_pairs={{0,32},{2,226},{4,36},{6,230},{8,40},{10,234},{12,44},{14,238},{16... | collective-permute-start | bytes 786440 | tf_op jit(solution)/shard_map/ppermute | solution.py:42
  45.0 12.2 %collective-permute-start.6 = (bf16[16,8192]{1,0:T(8,128)(2,1)S(1)}, bf16[16,8192]{1,0:T(8,128)(2,1)S(1)}, u32[]{:S(2)}, u32[]{:S(2)}) collective-permute-start(bf16[16,8192]{1,0:T(8,128)(2,1)S(1)} %collective-permute-done.5), channel_id=1, source_target_pairs={{0,224},{2,34},{4,228},{6,38},{8,232},{10,42},{12,236},{14,46},{16... | collective-permute-start | bytes 786440 | tf_op jit(solution)/shard_map/ppermute | solution.py:46
  57.2 7.6 %collective-permute-start.10 = (bf16[16,8192]{1,0:T(8,128)(2,1)S(1)}, bf16[16,8192]{1,0:T(8,128)(2,1)S(1)}, u32[]{:S(2)}, u32[]{:S(2)}) collective-permute-start(bf16[16,8192]{1,0:T(8,128)(2,1)S(1)} %collective-permute-done.9), channel_id=1, source_target_pairs={{0,32},{2,226},{4,36},{6,230},{8,40},{10,234},{12,44},{14,238},{16... | collective-permute-start | bytes 786440 | tf_op jit(solution)/shard_map/ppermute | solution.py:42
  86.3 8.6 %collective-permute-start.14 = (f32[16,4096]{1,0:T(8,128)S(1)}, f32[16,4096]{1,0:T(8,128)S(1)}, u32[]{:S(2)}, u32[]{:S(2)}) collective-permute-start(f32[16,4096]{1,0:T(8,128)S(1)} %slice.130), channel_id=1, source_target_pairs={{0,32},{2,226},{4,36},{6,230},{8,40},{10,234},{12,44},{14,238},{16... | collective-permute-start | bytes 786440 | tf_op jit(solution)/shard_map/ppermute | solution.py:63
  89.2 10.5 %collective-permute-start.25 = (f32[32,4096]{1,0:T(8,128)S(1)}, f32[32,4096]{1,0:T(8,128)S(1)}, u32[]{:S(2)}, u32[]{:S(2)}) collective-permute-start(f32[32,4096]{1,0:T(8,128)S(1)} %slice.145), channel_id=1, source_target_pairs={{0,4},{2,14},{4,8},{6,2},{8,12},{10,6},{12,0},{14,10},{16,20},{18,... | collective-permute-start | bytes 1572872 | tf_op jit(solution)/shard_map/ppermute | solution.py:63
  94.9 9.0 %collective-permute-start.15 = (f32[16,4096]{1,0:T(8,128)S(1)}, f32[16,4096]{1,0:T(8,128)S(1)}, u32[]{:S(2)}, u32[]{:S(2)}) collective-permute-start(f32[16,4096]{1,0:T(8,128)S(1)} %get-tuple-element.19), channel_id=1, source_target_pairs={{0,32},{2,226},{4,36},{6,230},{8,40},{10,234},{12,44},{14,238},{16... | collective-permute-start | bytes 786440 | tf_op jit(solution)/shard_map/ppermute | solution.py:63
  95.0 8.9 %collective-permute-start.18 = (f32[16,4096]{1,0:T(8,128)S(1)}, f32[16,4096]{1,0:T(8,128)S(1)}, u32[]{:S(2)}, u32[]{:S(2)}) collective-permute-start(f32[16,4096]{1,0:T(8,128)S(1)} %get-tuple-element.20), channel_id=1, source_target_pairs={{0,224},{2,34},{4,228},{6,38},{8,232},{10,42},{12,236},{14,46},{16... | collective-permute-start | bytes 786440 | tf_op jit(solution)/shard_map/ppermute | solution.py:71
  99.8 12.4 %collective-permute-start.26 = (f32[32,4096]{1,0:T(8,128)S(1)}, f32[32,4096]{1,0:T(8,128)S(1)}, u32[]{:S(2)}, u32[]{:S(2)}) collective-permute-start(f32[32,4096]{1,0:T(8,128)S(1)} %get-tuple-element.21), channel_id=1, source_target_pairs={{0,4},{2,14},{4,8},{6,2},{8,12},{10,6},{12,0},{14,10},{16,20},{18,... | collective-permute-start | bytes 1572872 | tf_op jit(solution)/shard_map/ppermute | solution.py:63
  99.8 12.3 %collective-permute-start.27 = (f32[32,4096]{1,0:T(8,128)S(1)}, f32[32,4096]{1,0:T(8,128)S(1)}, u32[]{:S(2)}, u32[]{:S(2)}) collective-permute-start(f32[32,4096]{1,0:T(8,128)S(1)} %get-tuple-element.22), channel_id=1, source_target_pairs={{0,12},{2,6},{4,0},{6,10},{8,4},{10,14},{12,8},{14,2},{16,28},{18,... | collective-permute-start | bytes 1572872 | tf_op jit(solution)/shard_map/ppermute | solution.py:71
  104.0 8.4 %collective-permute-start.16 = (f32[16,4096]{1,0:T(8,128)S(1)}, f32[16,4096]{1,0:T(8,128)S(1)}, u32[]{:S(2)}, u32[]{:S(2)}) collective-permute-start(f32[16,4096]{1,0:T(8,128)S(1)} %get-tuple-element.17), channel_id=1, source_target_pairs={{0,32},{2,226},{4,36},{6,230},{8,40},{10,234},{12,44},{14,238},{16... | collective-permute-start | bytes 786440 | tf_op jit(solution)/shard_map/ppermute | solution.py:63
  104.1 10.7 %collective-permute-start.19 = (f32[16,4096]{1,0:T(8,128)S(1)}, f32[16,4096]{1,0:T(8,128)S(1)}, u32[]{:S(2)}, u32[]{:S(2)}) collective-permute-start(f32[16,4096]{1,0:T(8,128)S(1)} %get-tuple-element.18), channel_id=1, source_target_pairs={{0,224},{2,34},{4,228},{6,38},{8,232},{10,42},{12,236},{14,46},{16... | collective-permute-start | bytes 786440 | tf_op jit(solution)/shard_map/ppermute | solution.py:71
  114.8 8.3 %collective-permute-start.17 = (f32[16,4096]{1,0:T(8,128)S(1)}, f32[16,4096]{1,0:T(8,128)S(1)}, u32[]{:S(2)}, u32[]{:S(2)}) collective-permute-start(f32[16,4096]{1,0:T(8,128)S(1)} %get-tuple-element.15), channel_id=1, source_target_pairs={{0,32},{2,226},{4,36},{6,230},{8,40},{10,234},{12,44},{14,238},{16... | collective-permute-start | bytes 786440 | tf_op jit(solution)/shard_map/ppermute | solution.py:63
  115.1 8.1 %collective-permute-start.20 = (f32[16,4096]{1,0:T(8,128)S(1)}, f32[16,4096]{1,0:T(8,128)S(1)}, u32[]{:S(2)}, u32[]{:S(2)}) collective-permute-start(f32[16,4096]{1,0:T(8,128)S(1)} %get-tuple-element.16), channel_id=1, source_target_pairs={{0,224},{2,34},{4,228},{6,38},{8,232},{10,42},{12,236},{14,46},{16... | collective-permute-start | bytes 786440 | tf_op jit(solution)/shard_map/ppermute | solution.py:71
  124.6 7.7 %collective-permute-start.30 = (f32[4,4096]{1,0:T(4,128)S(1)}, f32[4,4096]{1,0:T(4,128)S(1)}, u32[]{:S(2)}, u32[]{:S(2)}) collective-permute-start(f32[4,4096]{1,0:T(4,128)S(1)} %get-tuple-element.25), channel_id=1, source_target_pairs={{0,32},{2,226},{4,36},{6,230},{8,40},{10,234},{12,44},{14,238},{16... | collective-permute-start | bytes 196616 | tf_op jit(solution)/shard_map/ppermute | solution.py:63
  124.6 7.6 %collective-permute-start.33 = (f32[4,4096]{1,0:T(4,128)S(1)}, f32[4,4096]{1,0:T(4,128)S(1)}, u32[]{:S(2)}, u32[]{:S(2)}) collective-permute-start(f32[4,4096]{1,0:T(4,128)S(1)} %get-tuple-element.26), channel_id=1, source_target_pairs={{0,224},{2,34},{4,228},{6,38},{8,232},{10,42},{12,236},{14,46},{16... | collective-permute-start | bytes 196616 | tf_op jit(solution)/shard_map/ppermute | solution.py:71
  (15 other events, 95.0 us)

commit v5 on v3

--- a/solution.py
+++ b/solution.py
@@ -6,8 +6,8 @@
 BLK_AXES = {"z": (16, 8), "xh": (8, 2), "y": (2, 4), "c": (1, 2)}
 AG_ORDER = ("xh", "y", "z", "c")
 PARTS = (
-    (32, ("c", "z", "y", "xh")),
-    (32, ("c", "y", "z", "xh")),
+    (36, ("c", "z", "y", "xh")),
+    (28, ("c", "y", "z", "xh")),
 )
 
 

time: 138 us -> 144 us (1.043)
  waiting for transfers between devices: 61.4 us -> 65.4 us
  local copies, waits for them, and re-layouts: 6.15 us -> 2.52 us
  matrix products: 6.06 us -> 8.26 us
  other arithmetic: 12.3 us -> 14.5 us
    ppermute x16, waiting for transfers between devices: 28.9 us -> 33.2 us  [_rs_stage(): recv = lax.ppermute(buf, 'blk', _perm(axis, 1, size))]
    mul x3, other arithmetic: 7.42 us -> 9.62 us  [mask_blocks(): return (shaped * cols[:, None, :]).reshape(height, width)]
    unnamed x25 -> x23, local copies, waits for them, and re-layouts: 3.27 us -> 1.16 us
    dot_general x2, matrix products: 1.6 us -> 3.7 us  [local(): jnp.dot(b, up_kept, preferred_element_type=jnp.float32)]
    slice x8, local copies, waits for them, and re-layouts: 1.91 us -> 0.4 us  [take(): return lax.slice_in_dim(x, j % n * r, (j % n + 1) * r, axis=0)]
  transfers between devices with their start and end apart: 36 -> 36, of which waited for: 21 -> 19; matrix products, arithmetic and copies ran while one was open for 11% -> 10% of each run, Pallas kernels for 0% -> 0%
where the time goes in v5:
time: 144 us; the launch traced here: 143 us
  waiting for transfers between devices  65.4 us (45%)
  starting transfers between devices  51.8 us (36%)
  other arithmetic  14.5 us (10%)
  matrix products  8.26 us (6%)
  local copies, waits for them, and re-layouts  2.52 us (2%)
    ppermute x16, waiting for transfers between devices, _rs_stage(): recv = lax.ppermute(buf, 'blk', _perm(axis, 1, size))  33.2 us
    ppermute x8, starting transfers between devices, _rs_stage(): recv = lax.ppermute(buf, 'blk', _perm(axis, -1, size))  25.4 us
    ppermute x7, waiting for transfers between devices, _ag_stage(): cur = lax.ppermute(cur, 'blk', _perm(axis, 1, size))  18.6 us
    ppermute x4, starting transfers between devices, _ag_stage(): cur = lax.ppermute(cur, 'blk', _perm(axis, -1, size))  15 us
    ppermute x4, waiting for transfers between devices, _ag_stage(): cur = lax.ppermute(cur, 'blk', _perm(axis, -1, size))  11 us
    mul x3, other arithmetic, mask_blocks(): return (shaped * cols[:, None, :]).reshape(height, width)  9.62 us
    ppermute x16, starting transfers between devices, _rs_stage(): recv = lax.ppermute(buf, 'blk', _perm(axis, 1, size))  6.19 us
    ppermute x7, starting transfers between devices, _ag_stage(): cur = lax.ppermute(cur, 'blk', _perm(axis, 1, size))  4.91 us
  transfers between devices with their start and end apart: 36, of which 19 were waited for; matrix products, arithmetic and copies ran while one was open for 10% of the time, Pallas kernels for 0%

profile of v5, /device:TPU:2, one launch (start us, length us, event | category | flops | bytes accessed | tf_op | source)
XLA Modules:
  0.0 143.0 jit_solution(2769495330018765457)
XLA Ops:
  5.0 4.5 %bitcast_multiply_fusion.2 = bf16[8192,256]{1,0:T(8,128)(2,1)} fusion(bf16[8192,256]{1,0:T(8,128)(2,1)} %param.10, bf16[64,256]{1,0:T(8,128)(2,1)S(1)} %bitcast.32), kind=kLoop, calls=%fused_computation.2 | loop fusion | flops 2097152 | bytes 8421376 | tf_op jit(solution)/shard_map/mul | solution.py:20
  16.6 2.6 %bitcast_multiply_fusion.1 = bf16[8192,256]{1,0:T(8,128)(2,1)S(1)} fusion(bf16[8192,256]{1,0:T(8,128)(2,1)} %param.11, bf16[64,256]{1,0:T(8,128)(2,1)S(1)} %bitcast.30), kind=kLoop, calls=%fused_computation.1 | loop fusion | flops 2097152 | bytes 8421376 | tf_op jit(solution)/shard_map/mul | solution.py:20
  20.1 2.5 %bitcast_multiply_fusion = bf16[256,8192]{1,0:T(8,128)(2,1)} fusion(bf16[256,8192]{1,0:T(8,128)(2,1)S(1)} %copy-done.3, bf16[2,8192]{1,0:T(2,128)(2,1)S(1)} %bitcast.31), kind=kLoop, calls=%fused_computation | loop fusion | flops 2097152 | bytes 8421376 | tf_op jit(solution)/shard_map/mul | solution.py:20
  22.7 5.9 %collective-permute-start.4 = (bf16[16,8192]{1,0:T(8,128)(2,1)S(1)}, bf16[16,8192]{1,0:T(8,128)(2,1)S(1)}, u32[]{:S(2)}, u32[]{:S(2)}) collective-permute-start(bf16[16,8192]{1,0:T(8,128)(2,1)S(1)} %pad_maximum_fusion), channel_id=1, source_target_pairs={{0,224},{2,34},{4,228},{6,38},{8,232},{10,42},{12,236},{14,46},{16... | collective-permute-start | bytes 786440 | tf_op jit(solution)/shard_map/ppermute | solution.py:46
  28.7 5.9 %collective-permute-done.4 = bf16[16,8192]{1,0:T(8,128)(2,1)S(1)} collective-permute-done((bf16[16,8192]{1,0:T(8,128)(2,1)S(1)}, bf16[16,8192]{1,0:T(8,128)(2,1)S(1)}, u32[]{:S(2)}, u32[]{:S(2)}) %collective-permute-start.4) | collective-permute-done | bytes 262176 | tf_op jit(solution)/shard_map/ppermute | solution.py:46
  34.6 3.7 %collective-permute-start.5 = (bf16[16,8192]{1,0:T(8,128)(2,1)S(1)}, bf16[16,8192]{1,0:T(8,128)(2,1)S(1)}, u32[]{:S(2)}, u32[]{:S(2)}) collective-permute-start(bf16[16,8192]{1,0:T(8,128)(2,1)S(1)} %collective-permute-done.4), channel_id=1, source_target_pairs={{0,224},{2,34},{4,228},{6,38},{8,232},{10,42},{12,236},{14,46},{16... | collective-permute-start | bytes 786440 | tf_op jit(solution)/shard_map/ppermute | solution.py:46
  38.3 5.1 %collective-permute-done.5 = bf16[16,8192]{1,0:T(8,128)(2,1)S(1)} collective-permute-done((bf16[16,8192]{1,0:T(8,128)(2,1)S(1)}, bf16[16,8192]{1,0:T(8,128)(2,1)S(1)}, u32[]{:S(2)}, u32[]{:S(2)}) %collective-permute-start.5) | collective-permute-done | bytes 262176 | tf_op jit(solution)/shard_map/ppermute | solution.py:46
  43.4 3.7 %collective-permute-start.6 = (bf16[16,8192]{1,0:T(8,128)(2,1)S(1)}, bf16[16,8192]{1,0:T(8,128)(2,1)S(1)}, u32[]{:S(2)}, u32[]{:S(2)}) collective-permute-start(bf16[16,8192]{1,0:T(8,128)(2,1)S(1)} %collective-permute-done.5), channel_id=1, source_target_pairs={{0,224},{2,34},{4,228},{6,38},{8,232},{10,42},{12,236},{14,46},{16... | collective-permute-start | bytes 786440 | tf_op jit(solution)/shard_map/ppermute | solution.py:46
  48.3 7.6 %collective-permute-done.9 = bf16[16,8192]{1,0:T(8,128)(2,1)S(1)} collective-permute-done((bf16[16,8192]{1,0:T(8,128)(2,1)S(1)}, bf16[16,8192]{1,0:T(8,128)(2,1)S(1)}, u32[]{:S(2)}, u32[]{:S(2)}) %collective-permute-start.9) | collective-permute-done | bytes 262176 | tf_op jit(solution)/shard_map/ppermute | solution.py:42
  55.9 7.6 %collective-permute-done.10 = bf16[16,8192]{1,0:T(8,128)(2,1)S(1)} collective-permute-done((bf16[16,8192]{1,0:T(8,128)(2,1)S(1)}, bf16[16,8192]{1,0:T(8,128)(2,1)S(1)}, u32[]{:S(2)}, u32[]{:S(2)}) %collective-permute-start.10) | collective-permute-done | bytes 262176 | tf_op jit(solution)/shard_map/ppermute | solution.py:42
  65.4 2.6 %collective-permute-done.11 = bf16[128,8192]{1,0:T(8,128)(2,1)S(1)} collective-permute-done((bf16[128,8192]{1,0:T(8,128)(2,1)S(1)}, bf16[128,8192]{1,0:T(8,128)(2,1)S(1)}, u32[]{:S(2)}, u32[]{:S(2)}) %collective-permute-start.11) | collective-permute-done | bytes 2097184 | tf_op jit(solution)/shard_map/ppermute | solution.py:108
  68.9 2.9 %fusion.20 = f32[128,256]{1,0:T(8,128)S(1)} fusion(bf16[128,8192]{1,0:T(8,128)(2,1)S(1)} %collective-permute-done.11, bf16[8192,256]{1,0:T(8,128)(2,1)} %copy-done.1), kind=kOutput, calls=%fused_computation.65 | convolution fusion | flops 536870912 | bytes 6422528 | tf_op jit(solution)/shard_map/dot_general | solution.py:112
  82.6 6.3 %collective-permute-done.25 = f32[32,3584]{1,0:T(8,128)S(1)} collective-permute-done((f32[32,3584]{1,0:T(8,128)S(1)}, f32[32,3584]{1,0:T(8,128)S(1)}, u32[]{:S(2)}, u32[]{:S(2)}) %collective-permute-start.25) | collective-permute-done | bytes 458784 | tf_op jit(solution)/shard_map/ppermute | solution.py:63
  89.0 3.2 %collective-permute-start.27 = (f32[32,3584]{1,0:T(8,128)S(1)}, f32[32,3584]{1,0:T(8,128)S(1)}, u32[]{:S(2)}, u32[]{:S(2)}) collective-permute-start(f32[32,3584]{1,0:T(8,128)S(1)} %get-tuple-element.24), channel_id=1, source_target_pairs={{0,12},{2,6},{4,0},{6,10},{8,4},{10,14},{12,8},{14,2},{16,28},{18,... | collective-permute-start | bytes 1376264 | tf_op jit(solution)/shard_map/ppermute | solution.py:71
  92.4 3.2 %collective-permute-start.17 = (f32[16,4608]{1,0:T(8,128)S(1)}, f32[16,4608]{1,0:T(8,128)S(1)}, u32[]{:S(2)}, u32[]{:S(2)}) collective-permute-start(f32[16,4608]{1,0:T(8,128)S(1)} %get-tuple-element.22), channel_id=1, source_target_pairs={{0,224},{2,34},{4,228},{6,38},{8,232},{10,42},{12,236},{14,46},{16... | collective-permute-start | bytes 884744 | tf_op jit(solution)/shard_map/ppermute | solution.py:71
  95.6 7.7 %collective-permute-done.26 = f32[32,3584]{1,0:T(8,128)S(1)} collective-permute-done((f32[32,3584]{1,0:T(8,128)S(1)}, f32[32,3584]{1,0:T(8,128)S(1)}, u32[]{:S(2)}, u32[]{:S(2)}) %collective-permute-start.26) | collective-permute-done | bytes 458784 | tf_op jit(solution)/shard_map/ppermute | solution.py:63
  104.0 3.3 %collective-permute-start.18 = (f32[16,4608]{1,0:T(8,128)S(1)}, f32[16,4608]{1,0:T(8,128)S(1)}, u32[]{:S(2)}, u32[]{:S(2)}) collective-permute-start(f32[16,4608]{1,0:T(8,128)S(1)} %get-tuple-element.20), channel_id=1, source_target_pairs={{0,224},{2,34},{4,228},{6,38},{8,232},{10,42},{12,236},{14,46},{16... | collective-permute-start | bytes 884744 | tf_op jit(solution)/shard_map/ppermute | solution.py:71
  109.8 3.2 %collective-permute-start.32 = (f32[4,3584]{1,0:T(4,128)S(1)}, f32[4,3584]{1,0:T(4,128)S(1)}, u32[]{:S(2)}, u32[]{:S(2)}) collective-permute-start(f32[4,3584]{1,0:T(4,128)S(1)} %get-tuple-element.30), channel_id=1, source_target_pairs={{0,224},{2,34},{4,228},{6,38},{8,232},{10,42},{12,236},{14,46},{16... | collective-permute-start | bytes 172040 | tf_op jit(solution)/shard_map/ppermute | solution.py:71
  113.1 2.5 %collective-permute-done.15 = f32[16,4608]{1,0:T(8,128)S(1)} collective-permute-done((f32[16,4608]{1,0:T(8,128)S(1)}, f32[16,4608]{1,0:T(8,128)S(1)}, u32[]{:S(2)}, u32[]{:S(2)}) %collective-permute-start.15) | collective-permute-done | bytes 294944 | tf_op jit(solution)/shard_map/ppermute | solution.py:63
  115.7 3.2 %collective-permute-start.19 = (f32[16,4608]{1,0:T(8,128)S(1)}, f32[16,4608]{1,0:T(8,128)S(1)}, u32[]{:S(2)}, u32[]{:S(2)}) collective-permute-start(f32[16,4608]{1,0:T(8,128)S(1)} %get-tuple-element.18), channel_id=1, source_target_pairs={{0,224},{2,34},{4,228},{6,38},{8,232},{10,42},{12,236},{14,46},{16... | collective-permute-start | bytes 884744 | tf_op jit(solution)/shard_map/ppermute | solution.py:71
  119.1 3.2 %collective-permute-start.33 = (f32[4,3584]{1,0:T(4,128)S(1)}, f32[4,3584]{1,0:T(4,128)S(1)}, u32[]{:S(2)}, u32[]{:S(2)}) collective-permute-start(f32[4,3584]{1,0:T(4,128)S(1)} %get-tuple-element.28), channel_id=1, source_target_pairs={{0,224},{2,34},{4,228},{6,38},{8,232},{10,42},{12,236},{14,46},{16... | collective-permute-start | bytes 172040 | tf_op jit(solution)/shard_map/ppermute | solution.py:71
  122.3 2.6 %collective-permute-done.16 = f32[16,4608]{1,0:T(8,128)S(1)} collective-permute-done((f32[16,4608]{1,0:T(8,128)S(1)}, f32[16,4608]{1,0:T(8,128)S(1)}, u32[]{:S(2)}, u32[]{:S(2)}) %collective-permute-start.16) | collective-permute-done | bytes 294944 | tf_op jit(solution)/shard_map/ppermute | solution.py:63
  126.1 2.8 %collective-permute-start.34 = (f32[4,3584]{1,0:T(4,128)S(1)}, f32[4,3584]{1,0:T(4,128)S(1)}, u32[]{:S(2)}, u32[]{:S(2)}) collective-permute-start(f32[4,3584]{1,0:T(4,128)S(1)} %get-tuple-element.26), channel_id=1, source_target_pairs={{0,224},{2,34},{4,228},{6,38},{8,232},{10,42},{12,236},{14,46},{16... | collective-permute-start | bytes 172040 | tf_op jit(solution)/shard_map/ppermute | solution.py:71
  131.1 3.2 %collective-permute-start.22 = (f32[4,4608]{1,0:T(4,128)S(1)}, f32[4,4608]{1,0:T(4,128)S(1)}, u32[]{:S(2)}, u32[]{:S(2)}) collective-permute-start(f32[4,4608]{1,0:T(4,128)S(1)} %get-tuple-element.32), channel_id=1, source_target_pairs={{0,12},{2,6},{4,0},{6,10},{8,4},{10,14},{12,8},{14,2},{16,28},{18,... | collective-permute-start | bytes 221192 | tf_op jit(solution)/shard_map/ppermute | solution.py:71
  (125 shorter events, 43.4 us)
Async XLA Ops:
  1.8 7.7 %collective-permute-start = (bf16[2,8192]{1,0:T(2,128)(2,1)S(1)}, bf16[2,8192]{1,0:T(2,128)(2,1)S(1)}, u32[]{:S(2)}, u32[]{:S(2)}) collective-permute-start(bf16[2,8192]{1,0:T(2,128)(2,1)S(1)} %fusion.12), channel_id=1, source_target_pairs={{0,16},{2,18},{4,20},{6,22},{8,24},{10,26},{12,28},{14,30},{16,0},... | collective-permute-start | bytes 98312 | tf_op jit(solution)/shard_map/ppermute | solution.py:42
  11.3 11.3 %collective-permute-start.1 = (bf16[4,8192]{1,0:T(4,128)(2,1)S(1)}, bf16[4,8192]{1,0:T(4,128)(2,1)S(1)}, u32[]{:S(2)}, u32[]{:S(2)}) collective-permute-start(bf16[4,8192]{1,0:T(4,128)(2,1)S(1)} %pad_maximum_fusion.3), channel_id=1, source_target_pairs={{0,12},{2,6},{4,0},{6,10},{8,4},{10,14},{12,8},{14,2},{16,28},{18,... | collective-permute-start | bytes 196616 | tf_op jit(solution)/shard_map/ppermute | solution.py:46
  15.2 7.4 %collective-permute-start.3 = (bf16[4,8192]{1,0:T(4,128)(2,1)S(1)}, bf16[4,8192]{1,0:T(4,128)(2,1)S(1)}, u32[]{:S(2)}, u32[]{:S(2)}) collective-permute-start(bf16[4,8192]{1,0:T(4,128)(2,1)S(1)} %collective-permute-done.2), channel_id=1, source_target_pairs={{0,4},{2,14},{4,8},{6,2},{8,12},{10,6},{12,0},{14,10},{16,20},{18,... | collective-permute-start | bytes 196616 | tf_op jit(solution)/shard_map/ppermute | solution.py:42
  22.7 11.9 %collective-permute-start.4 = (bf16[16,8192]{1,0:T(8,128)(2,1)S(1)}, bf16[16,8192]{1,0:T(8,128)(2,1)S(1)}, u32[]{:S(2)}, u32[]{:S(2)}) collective-permute-start(bf16[16,8192]{1,0:T(8,128)(2,1)S(1)} %pad_maximum_fusion), channel_id=1, source_target_pairs={{0,224},{2,34},{4,228},{6,38},{8,232},{10,42},{12,236},{14,46},{16... | collective-permute-start | bytes 786440 | tf_op jit(solution)/shard_map/ppermute | solution.py:46
  28.7 9.6 %collective-permute-start.7 = (bf16[16,8192]{1,0:T(8,128)(2,1)S(1)}, bf16[16,8192]{1,0:T(8,128)(2,1)S(1)}, u32[]{:S(2)}, u32[]{:S(2)}) collective-permute-start(bf16[16,8192]{1,0:T(8,128)(2,1)S(1)} %pad_maximum_fusion), channel_id=1, source_target_pairs={{0,32},{2,226},{4,36},{6,230},{8,40},{10,234},{12,44},{14,238},{16... | collective-permute-start | bytes 786440 | tf_op jit(solution)/shard_map/ppermute | solution.py:42
  34.6 8.8 %collective-permute-start.5 = (bf16[16,8192]{1,0:T(8,128)(2,1)S(1)}, bf16[16,8192]{1,0:T(8,128)(2,1)S(1)}, u32[]{:S(2)}, u32[]{:S(2)}) collective-permute-start(bf16[16,8192]{1,0:T(8,128)(2,1)S(1)} %collective-permute-done.4), channel_id=1, source_target_pairs={{0,224},{2,34},{4,228},{6,38},{8,232},{10,42},{12,236},{14,46},{16... | collective-permute-start | bytes 786440 | tf_op jit(solution)/shard_map/ppermute | solution.py:46
  38.3 10.0 %collective-permute-start.8 = (bf16[16,8192]{1,0:T(8,128)(2,1)S(1)}, bf16[16,8192]{1,0:T(8,128)(2,1)S(1)}, u32[]{:S(2)}, u32[]{:S(2)}) collective-permute-start(bf16[16,8192]{1,0:T(8,128)(2,1)S(1)} %collective-permute-done.7), channel_id=1, source_target_pairs={{0,32},{2,226},{4,36},{6,230},{8,40},{10,234},{12,44},{14,238},{16... | collective-permute-start | bytes 786440 | tf_op jit(solution)/shard_map/ppermute | solution.py:42
  43.4 12.5 %collective-permute-start.6 = (bf16[16,8192]{1,0:T(8,128)(2,1)S(1)}, bf16[16,8192]{1,0:T(8,128)(2,1)S(1)}, u32[]{:S(2)}, u32[]{:S(2)}) collective-permute-start(bf16[16,8192]{1,0:T(8,128)(2,1)S(1)} %collective-permute-done.5), channel_id=1, source_target_pairs={{0,224},{2,34},{4,228},{6,38},{8,232},{10,42},{12,236},{14,46},{16... | collective-permute-start | bytes 786440 | tf_op jit(solution)/shard_map/ppermute | solution.py:46
  48.3 7.6 %collective-permute-start.9 = (bf16[16,8192]{1,0:T(8,128)(2,1)S(1)}, bf16[16,8192]{1,0:T(8,128)(2,1)S(1)}, u32[]{:S(2)}, u32[]{:S(2)}) collective-permute-start(bf16[16,8192]{1,0:T(8,128)(2,1)S(1)} %collective-permute-done.8), channel_id=1, source_target_pairs={{0,32},{2,226},{4,36},{6,230},{8,40},{10,234},{12,44},{14,238},{16... | collective-permute-start | bytes 786440 | tf_op jit(solution)/shard_map/ppermute | solution.py:42
  55.9 7.6 %collective-permute-start.10 = (bf16[16,8192]{1,0:T(8,128)(2,1)S(1)}, bf16[16,8192]{1,0:T(8,128)(2,1)S(1)}, u32[]{:S(2)}, u32[]{:S(2)}) collective-permute-start(bf16[16,8192]{1,0:T(8,128)(2,1)S(1)} %collective-permute-done.9), channel_id=1, source_target_pairs={{0,32},{2,226},{4,36},{6,230},{8,40},{10,234},{12,44},{14,238},{16... | collective-permute-start | bytes 786440 | tf_op jit(solution)/shard_map/ppermute | solution.py:42
  79.1 9.8 %collective-permute-start.25 = (f32[32,3584]{1,0:T(8,128)S(1)}, f32[32,3584]{1,0:T(8,128)S(1)}, u32[]{:S(2)}, u32[]{:S(2)}) collective-permute-start(f32[32,3584]{1,0:T(8,128)S(1)} %slice.155), channel_id=1, source_target_pairs={{0,4},{2,14},{4,8},{6,2},{8,12},{10,6},{12,0},{14,10},{16,20},{18,... | collective-permute-start | bytes 1376264 | tf_op jit(solution)/shard_map/ppermute | solution.py:63
  82.5 9.8 %collective-permute-start.13 = (f32[16,4608]{1,0:T(8,128)S(1)}, f32[16,4608]{1,0:T(8,128)S(1)}, u32[]{:S(2)}, u32[]{:S(2)}) collective-permute-start(f32[16,4608]{1,0:T(8,128)S(1)} %slice.139), channel_id=1, source_target_pairs={{0,32},{2,226},{4,36},{6,230},{8,40},{10,234},{12,44},{14,238},{16... | collective-permute-start | bytes 884744 | tf_op jit(solution)/shard_map/ppermute | solution.py:63
  88.9 14.4 %collective-permute-start.26 = (f32[32,3584]{1,0:T(8,128)S(1)}, f32[32,3584]{1,0:T(8,128)S(1)}, u32[]{:S(2)}, u32[]{:S(2)}) collective-permute-start(f32[32,3584]{1,0:T(8,128)S(1)} %get-tuple-element.23), channel_id=1, source_target_pairs={{0,4},{2,14},{4,8},{6,2},{8,12},{10,6},{12,0},{14,10},{16,20},{18,... | collective-permute-start | bytes 1376264 | tf_op jit(solution)/shard_map/ppermute | solution.py:63
  89.0 14.3 %collective-permute-start.27 = (f32[32,3584]{1,0:T(8,128)S(1)}, f32[32,3584]{1,0:T(8,128)S(1)}, u32[]{:S(2)}, u32[]{:S(2)}) collective-permute-start(f32[32,3584]{1,0:T(8,128)S(1)} %get-tuple-element.24), channel_id=1, source_target_pairs={{0,12},{2,6},{4,0},{6,10},{8,4},{10,14},{12,8},{14,2},{16,28},{18,... | collective-permute-start | bytes 1376264 | tf_op jit(solution)/shard_map/ppermute | solution.py:71
  92.3 11.5 %collective-permute-start.14 = (f32[16,4608]{1,0:T(8,128)S(1)}, f32[16,4608]{1,0:T(8,128)S(1)}, u32[]{:S(2)}, u32[]{:S(2)}) collective-permute-start(f32[16,4608]{1,0:T(8,128)S(1)} %get-tuple-element.21), channel_id=1, source_target_pairs={{0,32},{2,226},{4,36},{6,230},{8,40},{10,234},{12,44},{14,238},{16... | collective-permute-start | bytes 884744 | tf_op jit(solution)/shard_map/ppermute | solution.py:63
  92.4 11.4 %collective-permute-start.17 = (f32[16,4608]{1,0:T(8,128)S(1)}, f32[16,4608]{1,0:T(8,128)S(1)}, u32[]{:S(2)}, u32[]{:S(2)}) collective-permute-start(f32[16,4608]{1,0:T(8,128)S(1)} %get-tuple-element.22), channel_id=1, source_target_pairs={{0,224},{2,34},{4,228},{6,38},{8,232},{10,42},{12,236},{14,46},{16... | collective-permute-start | bytes 884744 | tf_op jit(solution)/shard_map/ppermute | solution.py:71
  103.9 11.7 %collective-permute-start.15 = (f32[16,4608]{1,0:T(8,128)S(1)}, f32[16,4608]{1,0:T(8,128)S(1)}, u32[]{:S(2)}, u32[]{:S(2)}) collective-permute-start(f32[16,4608]{1,0:T(8,128)S(1)} %get-tuple-element.19), channel_id=1, source_target_pairs={{0,32},{2,226},{4,36},{6,230},{8,40},{10,234},{12,44},{14,238},{16... | collective-permute-start | bytes 884744 | tf_op jit(solution)/shard_map/ppermute | solution.py:63
  104.0 11.6 %collective-permute-start.18 = (f32[16,4608]{1,0:T(8,128)S(1)}, f32[16,4608]{1,0:T(8,128)S(1)}, u32[]{:S(2)}, u32[]{:S(2)}) collective-permute-start(f32[16,4608]{1,0:T(8,128)S(1)} %get-tuple-element.20), channel_id=1, source_target_pairs={{0,224},{2,34},{4,228},{6,38},{8,232},{10,42},{12,236},{14,46},{16... | collective-permute-start | bytes 884744 | tf_op jit(solution)/shard_map/ppermute | solution.py:71
  109.7 9.2 %collective-permute-start.29 = (f32[4,3584]{1,0:T(4,128)S(1)}, f32[4,3584]{1,0:T(4,128)S(1)}, u32[]{:S(2)}, u32[]{:S(2)}) collective-permute-start(f32[4,3584]{1,0:T(4,128)S(1)} %get-tuple-element.29), channel_id=1, source_target_pairs={{0,32},{2,226},{4,36},{6,230},{8,40},{10,234},{12,44},{14,238},{16... | collective-permute-start | bytes 172040 | tf_op jit(solution)/shard_map/ppermute | solution.py:63
  109.8 9.1 %collective-permute-start.32 = (f32[4,3584]{1,0:T(4,128)S(1)}, f32[4,3584]{1,0:T(4,128)S(1)}, u32[]{:S(2)}, u32[]{:S(2)}) collective-permute-start(f32[4,3584]{1,0:T(4,128)S(1)} %get-tuple-element.30), channel_id=1, source_target_pairs={{0,224},{2,34},{4,228},{6,38},{8,232},{10,42},{12,236},{14,46},{16... | collective-permute-start | bytes 172040 | tf_op jit(solution)/shard_map/ppermute | solution.py:71
  115.6 9.3 %collective-permute-start.16 = (f32[16,4608]{1,0:T(8,128)S(1)}, f32[16,4608]{1,0:T(8,128)S(1)}, u32[]{:S(2)}, u32[]{:S(2)}) collective-permute-start(f32[16,4608]{1,0:T(8,128)S(1)} %get-tuple-element.17), channel_id=1, source_target_pairs={{0,32},{2,226},{4,36},{6,230},{8,40},{10,234},{12,44},{14,238},{16... | collective-permute-start | bytes 884744 | tf_op jit(solution)/shard_map/ppermute | solution.py:63
  115.7 9.2 %collective-permute-start.19 = (f32[16,4608]{1,0:T(8,128)S(1)}, f32[16,4608]{1,0:T(8,128)S(1)}, u32[]{:S(2)}, u32[]{:S(2)}) collective-permute-start(f32[16,4608]{1,0:T(8,128)S(1)} %get-tuple-element.18), channel_id=1, source_target_pairs={{0,224},{2,34},{4,228},{6,38},{8,232},{10,42},{12,236},{14,46},{16... | collective-permute-start | bytes 884744 | tf_op jit(solution)/shard_map/ppermute | solution.py:71
  125.6 8.7 %collective-permute-start.31 = (f32[4,3584]{1,0:T(4,128)S(1)}, f32[4,3584]{1,0:T(4,128)S(1)}, u32[]{:S(2)}, u32[]{:S(2)}) collective-permute-start(f32[4,3584]{1,0:T(4,128)S(1)} %get-tuple-element.25), channel_id=1, source_target_pairs={{0,32},{2,226},{4,36},{6,230},{8,40},{10,234},{12,44},{14,238},{16... | collective-permute-start | bytes 172040 | tf_op jit(solution)/shard_map/ppermute | solution.py:63
  126.1 8.2 %collective-permute-start.34 = (f32[4,3584]{1,0:T(4,128)S(1)}, f32[4,3584]{1,0:T(4,128)S(1)}, u32[]{:S(2)}, u32[]{:S(2)}) collective-permute-start(f32[4,3584]{1,0:T(4,128)S(1)} %get-tuple-element.26), channel_id=1, source_target_pairs={{0,224},{2,34},{4,228},{6,38},{8,232},{10,42},{12,236},{14,46},{16... | collective-permute-start | bytes 172040 | tf_op jit(solution)/shard_map/ppermute | solution.py:71
  (18 other events, 177.6 us)

commit v6 on v5

--- a/solution.py
+++ b/solution.py
@@ -5,9 +5,10 @@
 
 BLK_AXES = {"z": (16, 8), "xh": (8, 2), "y": (2, 4), "c": (1, 2)}
 AG_ORDER = ("xh", "y", "z", "c")
+AG_DIRECT = ("y",)
 PARTS = (
-    (36, ("c", "z", "y", "xh")),
-    (28, ("c", "y", "z", "xh")),
+    (32, ("c", "z", "y", "xh"), ("y",)),
+    (32, ("c", "y", "z", "xh"), ()),
 )
 
 
@@ -46,6 +47,22 @@
         cur = lax.ppermute(cur, "blk", _perm(axis, -1, size))
         got[s + 1] = cur
     return jnp.concatenate(got, axis=0)
+
+
+def _ag_direct(block, axis, size):
+    _, n = BLK_AXES[axis]
+    got = [block] + [lax.ppermute(block, "blk", _perm(axis, -o, size)) for o in range(1, n)]
+    return jnp.concatenate(got, axis=0)
+
+
+def _rs_direct(x, axis, size):
+    _, n = BLK_AXES[axis]
+    r = x.shape[0] // n
+    total = lax.slice_in_dim(x, 0, r, axis=0)
+    for o in range(1, n):
+        part = lax.slice_in_dim(x, o * r, (o + 1) * r, axis=0)
+        total = total + lax.ppermute(part, "blk", _perm(axis, o, size))
+    return total
 
 
 def _rs_stage(x, axis, size):
@@ -99,7 +116,10 @@
     piece = normed
     kept = [gate_kept, up_kept, down_kept]
     for i, axis in enumerate(AG_ORDER[:-1]):
-        piece = _ag_stage(piece, axis, size)
+        if axis in AG_DIRECT:
+            piece = _ag_direct(piece, axis, size)
+        else:
+            piece = _ag_stage(piece, axis, size)
         piece, kept[i] = lax.optimization_barrier((piece, kept[i]))
     gate_kept, up_kept, down_kept = kept
     last = AG_ORDER[-1]
@@ -114,12 +134,15 @@
 
     outs = []
     lo = 0
-    for groups, rs_order in PARTS:
+    for groups, rs_order, direct in PARTS:
         hi = lo + groups * 128
         h = hidden if rs_order == base else _reorder_rows(hidden, base, rs_order, t)
         x = jnp.dot(h, down_kept[:, lo:hi], preferred_element_type=jnp.float32)
         for axis in rs_order:
-            x = _rs_stage(x, axis, size)
+            if axis in direct:
+                x = _rs_direct(x, axis, size)
+            else:
+                x = _rs_stage(x, axis, size)
         outs.append(x)
         lo = hi
     summed = jnp.concatenate(outs, axis=1) if len(outs) > 1 else outs[0]

time: 144 us -> 136 us (0.944)
  waiting for transfers between devices: 65.4 us -> 55.6 us
  local copies, waits for them, and re-layouts: 2.52 us -> 6.16 us
  matrix products: 8.26 us -> 6.06 us
  starting transfers between devices: 51.8 us -> 53.7 us
  other arithmetic: 14.5 us -> 13 us
    ppermute x0 -> x6, starting transfers between devices: none -> 8 us  [the longest x3 4.69 us: _ag_direct(): lax.ppermute(block, 'blk', _perm(axis, -o, size))]
    ppermute x16 -> x14, waiting for transfers between devices: 33.2 us -> 25.3 us  [_rs_stage(): recv = lax.ppermute(buf, 'blk', _perm(axis, 1, size))]
    ppermute x8 -> x7, starting transfers between devices: 25.4 us -> 22.6 us  [_rs_stage(): recv = lax.ppermute(buf, 'blk', _perm(axis, -1, size))]
    ppermute x7 -> x5, starting transfers between devices: 4.91 us -> 2.22 us  [_ag_stage(): cur = lax.ppermute(cur, 'blk', _perm(axis, 1, size))]
    mul x3, other arithmetic: 9.62 us -> 7.43 us  [mask_blocks(): return (shaped * cols[:, None, :]).reshape(height, width)]
    dot_general x2, matrix products: 3.7 us -> 1.6 us  [local(): jnp.dot(b, up_kept, preferred_element_type=jnp.float32)]
    unnamed x23, local copies, waits for them, and re-layouts: 1.16 us -> 3.24 us
    ppermute x4 -> x3, waiting for transfers between devices: 11 us -> 9.27 us  [_ag_stage(): cur = lax.ppermute(cur, 'blk', _perm(axis, -1, size))]
  transfers between devices with their start and end apart: 36 -> 36, of which waited for: 19 -> 21; matrix products, arithmetic and copies ran while one was open for 10% -> 12% of each run, Pallas kernels for 0% -> 0%
where the time goes in v6:
time: 136 us; the launch traced here: 135 us
  waiting for transfers between devices  55.6 us (41%)
  starting transfers between devices  53.7 us (39%)
  other arithmetic  13 us (10%)
  local copies, waits for them, and re-layouts  6.16 us (5%)
  matrix products  6.06 us (4%)
    ppermute x14, waiting for transfers between devices, _rs_stage(): recv = lax.ppermute(buf, 'blk', _perm(axis, 1, size))  25.3 us
    ppermute x7, starting transfers between devices, _rs_stage(): recv = lax.ppermute(buf, 'blk', _perm(axis, -1, size))  22.6 us
    ppermute x5, waiting for transfers between devices, _ag_stage(): cur = lax.ppermute(cur, 'blk', _perm(axis, 1, size))  17.3 us
    ppermute x3, starting transfers between devices, _ag_stage(): cur = lax.ppermute(cur, 'blk', _perm(axis, -1, size))  13.3 us
    ppermute x3, waiting for transfers between devices, _ag_stage(): cur = lax.ppermute(cur, 'blk', _perm(axis, -1, size))  9.27 us
    mul x3, other arithmetic, mask_blocks(): return (shaped * cols[:, None, :]).reshape(height, width)  7.43 us
    ppermute x14, starting transfers between devices, _rs_stage(): recv = lax.ppermute(buf, 'blk', _perm(axis, 1, size))  7.25 us
    ppermute x3, starting transfers between devices, _ag_direct(): lax.ppermute(block, 'blk', _perm(axis, -o, size))  4.69 us
  transfers between devices with their start and end apart: 36, of which 21 were waited for; matrix products, arithmetic and copies ran while one was open for 12% of the time, Pallas kernels for 0%

profile of v6, /device:TPU:2, one launch (start us, length us, event | category | flops | bytes accessed | tf_op | source)
XLA Modules:
  0.0 135.0 jit_solution(452424212809979792)
XLA Ops:
  1.8 2.2 %collective-permute-start = (bf16[2,8192]{1,0:T(2,128)(2,1)S(1)}, bf16[2,8192]{1,0:T(2,128)(2,1)S(1)}, u32[]{:S(2)}, u32[]{:S(2)}) collective-permute-start(bf16[2,8192]{1,0:T(2,128)(2,1)S(1)} %fusion.11), channel_id=1, source_target_pairs={{0,16},{2,18},{4,20},{6,22},{8,24},{10,26},{12,28},{14,30},{16,0},... | collective-permute-start | bytes 98312 | tf_op jit(solution)/shard_map/ppermute | solution.py:43
  5.7 4.5 %bitcast_multiply_fusion.2 = bf16[8192,256]{1,0:T(8,128)(2,1)} fusion(bf16[8192,256]{1,0:T(8,128)(2,1)} %param.10, bf16[64,256]{1,0:T(8,128)(2,1)S(1)} %bitcast.32), kind=kLoop, calls=%fused_computation.2 | loop fusion | flops 2097152 | bytes 8421376 | tf_op jit(solution)/shard_map/mul | solution.py:21
  10.3 3.1 %collective-permute-start.1 = (bf16[4,8192]{1,0:T(4,128)(2,1)S(1)}, bf16[4,8192]{1,0:T(4,128)(2,1)S(1)}, u32[]{:S(2)}, u32[]{:S(2)}) collective-permute-start(bf16[4,8192]{1,0:T(4,128)(2,1)S(1)} %pad_maximum_fusion.3), channel_id=1, source_target_pairs={{0,12},{2,6},{4,0},{6,10},{8,4},{10,14},{12,8},{14,2},{16,28},{18,... | collective-permute-start | bytes 196616 | tf_op jit(solution)/shard_map/ppermute | solution.py:54
  15.4 2.6 %bitcast_multiply_fusion.1 = bf16[8192,256]{1,0:T(8,128)(2,1)S(1)} fusion(bf16[8192,256]{1,0:T(8,128)(2,1)} %param.11, bf16[64,256]{1,0:T(8,128)(2,1)S(1)} %bitcast.30), kind=kLoop, calls=%fused_computation.1 | loop fusion | flops 2097152 | bytes 8421376 | tf_op jit(solution)/shard_map/mul | solution.py:21
  20.0 5.9 %collective-permute-start.4 = (bf16[16,8192]{1,0:T(8,128)(2,1)S(1)}, bf16[16,8192]{1,0:T(8,128)(2,1)S(1)}, u32[]{:S(2)}, u32[]{:S(2)}) collective-permute-start(bf16[16,8192]{1,0:T(8,128)(2,1)S(1)} %pad_maximum_fusion), channel_id=1, source_target_pairs={{0,224},{2,34},{4,228},{6,38},{8,232},{10,42},{12,236},{14,46},{16... | collective-permute-start | bytes 786440 | tf_op jit(solution)/shard_map/ppermute | solution.py:47
  26.0 5.1 %collective-permute-done.4 = bf16[16,8192]{1,0:T(8,128)(2,1)S(1)} collective-permute-done((bf16[16,8192]{1,0:T(8,128)(2,1)S(1)}, bf16[16,8192]{1,0:T(8,128)(2,1)S(1)}, u32[]{:S(2)}, u32[]{:S(2)}) %collective-permute-start.4) | collective-permute-done | bytes 262176 | tf_op jit(solution)/shard_map/ppermute | solution.py:47
  31.1 3.7 %collective-permute-start.5 = (bf16[16,8192]{1,0:T(8,128)(2,1)S(1)}, bf16[16,8192]{1,0:T(8,128)(2,1)S(1)}, u32[]{:S(2)}, u32[]{:S(2)}) collective-permute-start(bf16[16,8192]{1,0:T(8,128)(2,1)S(1)} %collective-permute-done.4), channel_id=1, source_target_pairs={{0,224},{2,34},{4,228},{6,38},{8,232},{10,42},{12,236},{14,46},{16... | collective-permute-start | bytes 786440 | tf_op jit(solution)/shard_map/ppermute | solution.py:47
  34.8 4.2 %collective-permute-done.5 = bf16[16,8192]{1,0:T(8,128)(2,1)S(1)} collective-permute-done((bf16[16,8192]{1,0:T(8,128)(2,1)S(1)}, bf16[16,8192]{1,0:T(8,128)(2,1)S(1)}, u32[]{:S(2)}, u32[]{:S(2)}) %collective-permute-start.5) | collective-permute-done | bytes 262176 | tf_op jit(solution)/shard_map/ppermute | solution.py:47
  39.0 3.7 %collective-permute-start.6 = (bf16[16,8192]{1,0:T(8,128)(2,1)S(1)}, bf16[16,8192]{1,0:T(8,128)(2,1)S(1)}, u32[]{:S(2)}, u32[]{:S(2)}) collective-permute-start(bf16[16,8192]{1,0:T(8,128)(2,1)S(1)} %collective-permute-done.5), channel_id=1, source_target_pairs={{0,224},{2,34},{4,228},{6,38},{8,232},{10,42},{12,236},{14,46},{16... | collective-permute-start | bytes 786440 | tf_op jit(solution)/shard_map/ppermute | solution.py:47
  42.6 2.2 %collective-permute-done.8 = bf16[16,8192]{1,0:T(8,128)(2,1)S(1)} collective-permute-done((bf16[16,8192]{1,0:T(8,128)(2,1)S(1)}, bf16[16,8192]{1,0:T(8,128)(2,1)S(1)}, u32[]{:S(2)}, u32[]{:S(2)}) %collective-permute-start.8) | collective-permute-done | bytes 262176 | tf_op jit(solution)/shard_map/ppermute | solution.py:43
  44.8 7.6 %collective-permute-done.9 = bf16[16,8192]{1,0:T(8,128)(2,1)S(1)} collective-permute-done((bf16[16,8192]{1,0:T(8,128)(2,1)S(1)}, bf16[16,8192]{1,0:T(8,128)(2,1)S(1)}, u32[]{:S(2)}, u32[]{:S(2)}) %collective-permute-start.9) | collective-permute-done | bytes 262176 | tf_op jit(solution)/shard_map/ppermute | solution.py:43
  52.4 7.6 %collective-permute-done.10 = bf16[16,8192]{1,0:T(8,128)(2,1)S(1)} collective-permute-done((bf16[16,8192]{1,0:T(8,128)(2,1)S(1)}, bf16[16,8192]{1,0:T(8,128)(2,1)S(1)}, u32[]{:S(2)}, u32[]{:S(2)}) %collective-permute-start.10) | collective-permute-done | bytes 262176 | tf_op jit(solution)/shard_map/ppermute | solution.py:43
  61.9 2.6 %collective-permute-done.11 = bf16[128,8192]{1,0:T(8,128)(2,1)S(1)} collective-permute-done((bf16[128,8192]{1,0:T(8,128)(2,1)S(1)}, bf16[128,8192]{1,0:T(8,128)(2,1)S(1)}, u32[]{:S(2)}, u32[]{:S(2)}) %collective-permute-start.11) | collective-permute-done | bytes 2097184 | tf_op jit(solution)/shard_map/ppermute | solution.py:128
  70.4 2.3 %fusion = f32[256,4096]{1,0:T(8,128)S(1)} fusion(bf16[256,256]{1,0:T(8,128)(2,1)S(1)} %reshape.27, bf16[256,8192]{1,0:T(8,128)(2,1)} %copy-done.1), kind=kOutput, calls=%fused_computation.5 | convolution fusion | flops 536870912 | bytes 6422528 | tf_op jit(solution)/shard_map/dot_general | solution.py:140
  79.4 3.5 %collective-permute-done.13 = f32[16,4096]{1,0:T(8,128)S(1)} collective-permute-done((f32[16,4096]{1,0:T(8,128)S(1)}, f32[16,4096]{1,0:T(8,128)S(1)}, u32[]{:S(2)}, u32[]{:S(2)}) %collective-permute-start.13) | collective-permute-done | bytes 262176 | tf_op jit(solution)/shard_map/ppermute | solution.py:80
  83.0 3.2 %collective-permute-start.17 = (f32[16,4096]{1,0:T(8,128)S(1)}, f32[16,4096]{1,0:T(8,128)S(1)}, u32[]{:S(2)}, u32[]{:S(2)}) collective-permute-start(f32[16,4096]{1,0:T(8,128)S(1)} %get-tuple-element.22), channel_id=1, source_target_pairs={{0,224},{2,34},{4,228},{6,38},{8,232},{10,42},{12,236},{14,46},{16... | collective-permute-start | bytes 786440 | tf_op jit(solution)/shard_map/ppermute | solution.py:88
  88.7 2.7 %collective-permute-start.27 = (f32[32,4096]{1,0:T(8,128)S(1)}, f32[32,4096]{1,0:T(8,128)S(1)}, u32[]{:S(2)}, u32[]{:S(2)}) collective-permute-start(f32[32,4096]{1,0:T(8,128)S(1)} %get-tuple-element.24), channel_id=1, source_target_pairs={{0,12},{2,6},{4,0},{6,10},{8,4},{10,14},{12,8},{14,2},{16,28},{18,... | collective-permute-start | bytes 1572872 | tf_op jit(solution)/shard_map/ppermute | solution.py:88
  91.8 3.2 %collective-permute-start.18 = (f32[16,4096]{1,0:T(8,128)S(1)}, f32[16,4096]{1,0:T(8,128)S(1)}, u32[]{:S(2)}, u32[]{:S(2)}) collective-permute-start(f32[16,4096]{1,0:T(8,128)S(1)} %get-tuple-element.20), channel_id=1, source_target_pairs={{0,224},{2,34},{4,228},{6,38},{8,232},{10,42},{12,236},{14,46},{16... | collective-permute-start | bytes 786440 | tf_op jit(solution)/shard_map/ppermute | solution.py:88
  95.1 8.8 %collective-permute-done.26 = f32[32,4096]{1,0:T(8,128)S(1)} collective-permute-done((f32[32,4096]{1,0:T(8,128)S(1)}, f32[32,4096]{1,0:T(8,128)S(1)}, u32[]{:S(2)}, u32[]{:S(2)}) %collective-permute-start.26) | collective-permute-done | bytes 524320 | tf_op jit(solution)/shard_map/ppermute | solution.py:80
  104.3 3.3 %collective-permute-start.19 = (f32[16,4096]{1,0:T(8,128)S(1)}, f32[16,4096]{1,0:T(8,128)S(1)}, u32[]{:S(2)}, u32[]{:S(2)}) collective-permute-start(f32[16,4096]{1,0:T(8,128)S(1)} %get-tuple-element.18), channel_id=1, source_target_pairs={{0,224},{2,34},{4,228},{6,38},{8,232},{10,42},{12,236},{14,46},{16... | collective-permute-start | bytes 786440 | tf_op jit(solution)/shard_map/ppermute | solution.py:88
  107.5 2.7 %collective-permute-done.28 = f32[4,4096]{1,0:T(4,128)S(1)} collective-permute-done((f32[4,4096]{1,0:T(4,128)S(1)}, f32[4,4096]{1,0:T(4,128)S(1)}, u32[]{:S(2)}, u32[]{:S(2)}) %collective-permute-start.28) | collective-permute-done | bytes 65568 | tf_op jit(solution)/shard_map/ppermute | solution.py:80
  110.4 3.2 %collective-permute-start.32 = (f32[4,4096]{1,0:T(4,128)S(1)}, f32[4,4096]{1,0:T(4,128)S(1)}, u32[]{:S(2)}, u32[]{:S(2)}) collective-permute-start(f32[4,4096]{1,0:T(4,128)S(1)} %get-tuple-element.30), channel_id=1, source_target_pairs={{0,224},{2,34},{4,228},{6,38},{8,232},{10,42},{12,236},{14,46},{16... | collective-permute-start | bytes 196616 | tf_op jit(solution)/shard_map/ppermute | solution.py:88
  116.0 3.8 %collective-permute-start.33 = (f32[4,4096]{1,0:T(4,128)S(1)}, f32[4,4096]{1,0:T(4,128)S(1)}, u32[]{:S(2)}, u32[]{:S(2)}) collective-permute-start(f32[4,4096]{1,0:T(4,128)S(1)} %get-tuple-element.28), channel_id=1, source_target_pairs={{0,224},{2,34},{4,228},{6,38},{8,232},{10,42},{12,236},{14,46},{16... | collective-permute-start | bytes 196616 | tf_op jit(solution)/shard_map/ppermute | solution.py:88
  123.3 3.2 %collective-permute-start.34 = (f32[4,4096]{1,0:T(4,128)S(1)}, f32[4,4096]{1,0:T(4,128)S(1)}, u32[]{:S(2)}, u32[]{:S(2)}) collective-permute-start(f32[4,4096]{1,0:T(4,128)S(1)} %get-tuple-element.26), channel_id=1, source_target_pairs={{0,224},{2,34},{4,228},{6,38},{8,232},{10,42},{12,236},{14,46},{16... | collective-permute-start | bytes 196616 | tf_op jit(solution)/shard_map/ppermute | solution.py:88
  (124 shorter events, 39.7 us)
Async XLA Ops:
  1.8 8.4 %collective-permute-start = (bf16[2,8192]{1,0:T(2,128)(2,1)S(1)}, bf16[2,8192]{1,0:T(2,128)(2,1)S(1)}, u32[]{:S(2)}, u32[]{:S(2)}) collective-permute-start(bf16[2,8192]{1,0:T(2,128)(2,1)S(1)} %fusion.11), channel_id=1, source_target_pairs={{0,16},{2,18},{4,20},{6,22},{8,24},{10,26},{12,28},{14,30},{16,0},... | collective-permute-start | bytes 98312 | tf_op jit(solution)/shard_map/ppermute | solution.py:43
  10.3 8.9 %collective-permute-start.1 = (bf16[4,8192]{1,0:T(4,128)(2,1)S(1)}, bf16[4,8192]{1,0:T(4,128)(2,1)S(1)}, u32[]{:S(2)}, u32[]{:S(2)}) collective-permute-start(bf16[4,8192]{1,0:T(4,128)(2,1)S(1)} %pad_maximum_fusion.3), channel_id=1, source_target_pairs={{0,12},{2,6},{4,0},{6,10},{8,4},{10,14},{12,8},{14,2},{16,28},{18,... | collective-permute-start | bytes 196616 | tf_op jit(solution)/shard_map/ppermute | solution.py:54
  20.0 11.1 %collective-permute-start.4 = (bf16[16,8192]{1,0:T(8,128)(2,1)S(1)}, bf16[16,8192]{1,0:T(8,128)(2,1)S(1)}, u32[]{:S(2)}, u32[]{:S(2)}) collective-permute-start(bf16[16,8192]{1,0:T(8,128)(2,1)S(1)} %pad_maximum_fusion), channel_id=1, source_target_pairs={{0,224},{2,34},{4,228},{6,38},{8,232},{10,42},{12,236},{14,46},{16... | collective-permute-start | bytes 786440 | tf_op jit(solution)/shard_map/ppermute | solution.py:47
  25.9 8.8 %collective-permute-start.7 = (bf16[16,8192]{1,0:T(8,128)(2,1)S(1)}, bf16[16,8192]{1,0:T(8,128)(2,1)S(1)}, u32[]{:S(2)}, u32[]{:S(2)}) collective-permute-start(bf16[16,8192]{1,0:T(8,128)(2,1)S(1)} %pad_maximum_fusion), channel_id=1, source_target_pairs={{0,32},{2,226},{4,36},{6,230},{8,40},{10,234},{12,44},{14,238},{16... | collective-permute-start | bytes 786440 | tf_op jit(solution)/shard_map/ppermute | solution.py:43
  31.1 7.9 %collective-permute-start.5 = (bf16[16,8192]{1,0:T(8,128)(2,1)S(1)}, bf16[16,8192]{1,0:T(8,128)(2,1)S(1)}, u32[]{:S(2)}, u32[]{:S(2)}) collective-permute-start(bf16[16,8192]{1,0:T(8,128)(2,1)S(1)} %collective-permute-done.4), channel_id=1, source_target_pairs={{0,224},{2,34},{4,228},{6,38},{8,232},{10,42},{12,236},{14,46},{16... | collective-permute-start | bytes 786440 | tf_op jit(solution)/shard_map/ppermute | solution.py:47
  34.8 10.0 %collective-permute-start.8 = (bf16[16,8192]{1,0:T(8,128)(2,1)S(1)}, bf16[16,8192]{1,0:T(8,128)(2,1)S(1)}, u32[]{:S(2)}, u32[]{:S(2)}) collective-permute-start(bf16[16,8192]{1,0:T(8,128)(2,1)S(1)} %collective-permute-done.7), channel_id=1, source_target_pairs={{0,32},{2,226},{4,36},{6,230},{8,40},{10,234},{12,44},{14,238},{16... | collective-permute-start | bytes 786440 | tf_op jit(solution)/shard_map/ppermute | solution.py:43
  39.0 13.4 %collective-permute-start.6 = (bf16[16,8192]{1,0:T(8,128)(2,1)S(1)}, bf16[16,8192]{1,0:T(8,128)(2,1)S(1)}, u32[]{:S(2)}, u32[]{:S(2)}) collective-permute-start(bf16[16,8192]{1,0:T(8,128)(2,1)S(1)} %collective-permute-done.5), channel_id=1, source_target_pairs={{0,224},{2,34},{4,228},{6,38},{8,232},{10,42},{12,236},{14,46},{16... | collective-permute-start | bytes 786440 | tf_op jit(solution)/shard_map/ppermute | solution.py:47
  44.8 7.6 %collective-permute-start.9 = (bf16[16,8192]{1,0:T(8,128)(2,1)S(1)}, bf16[16,8192]{1,0:T(8,128)(2,1)S(1)}, u32[]{:S(2)}, u32[]{:S(2)}) collective-permute-start(bf16[16,8192]{1,0:T(8,128)(2,1)S(1)} %collective-permute-done.8), channel_id=1, source_target_pairs={{0,32},{2,226},{4,36},{6,230},{8,40},{10,234},{12,44},{14,238},{16... | collective-permute-start | bytes 786440 | tf_op jit(solution)/shard_map/ppermute | solution.py:43
  52.4 7.6 %collective-permute-start.10 = (bf16[16,8192]{1,0:T(8,128)(2,1)S(1)}, bf16[16,8192]{1,0:T(8,128)(2,1)S(1)}, u32[]{:S(2)}, u32[]{:S(2)}) collective-permute-start(bf16[16,8192]{1,0:T(8,128)(2,1)S(1)} %collective-permute-done.9), channel_id=1, source_target_pairs={{0,32},{2,226},{4,36},{6,230},{8,40},{10,234},{12,44},{14,238},{16... | collective-permute-start | bytes 786440 | tf_op jit(solution)/shard_map/ppermute | solution.py:43
  75.2 7.7 %collective-permute-start.13 = (f32[16,4096]{1,0:T(8,128)S(1)}, f32[16,4096]{1,0:T(8,128)S(1)}, u32[]{:S(2)}, u32[]{:S(2)}) collective-permute-start(f32[16,4096]{1,0:T(8,128)S(1)} %slice.139), channel_id=1, source_target_pairs={{0,32},{2,226},{4,36},{6,230},{8,40},{10,234},{12,44},{14,238},{16... | collective-permute-start | bytes 786440 | tf_op jit(solution)/shard_map/ppermute | solution.py:80
  77.5 10.5 %collective-permute-start.25 = (f32[32,4096]{1,0:T(8,128)S(1)}, f32[32,4096]{1,0:T(8,128)S(1)}, u32[]{:S(2)}, u32[]{:S(2)}) collective-permute-start(f32[32,4096]{1,0:T(8,128)S(1)} %slice.155), channel_id=1, source_target_pairs={{0,4},{2,14},{4,8},{6,2},{8,12},{10,6},{12,0},{14,10},{16,20},{18,... | collective-permute-start | bytes 1572872 | tf_op jit(solution)/shard_map/ppermute | solution.py:80
  82.9 8.7 %collective-permute-start.14 = (f32[16,4096]{1,0:T(8,128)S(1)}, f32[16,4096]{1,0:T(8,128)S(1)}, u32[]{:S(2)}, u32[]{:S(2)}) collective-permute-start(f32[16,4096]{1,0:T(8,128)S(1)} %get-tuple-element.21), channel_id=1, source_target_pairs={{0,32},{2,226},{4,36},{6,230},{8,40},{10,234},{12,44},{14,238},{16... | collective-permute-start | bytes 786440 | tf_op jit(solution)/shard_map/ppermute | solution.py:80
  83.0 8.6 %collective-permute-start.17 = (f32[16,4096]{1,0:T(8,128)S(1)}, f32[16,4096]{1,0:T(8,128)S(1)}, u32[]{:S(2)}, u32[]{:S(2)}) collective-permute-start(f32[16,4096]{1,0:T(8,128)S(1)} %get-tuple-element.22), channel_id=1, source_target_pairs={{0,224},{2,34},{4,228},{6,38},{8,232},{10,42},{12,236},{14,46},{16... | collective-permute-start | bytes 786440 | tf_op jit(solution)/shard_map/ppermute | solution.py:88
  88.1 15.8 %collective-permute-start.26 = (f32[32,4096]{1,0:T(8,128)S(1)}, f32[32,4096]{1,0:T(8,128)S(1)}, u32[]{:S(2)}, u32[]{:S(2)}) collective-permute-start(f32[32,4096]{1,0:T(8,128)S(1)} %get-tuple-element.23), channel_id=1, source_target_pairs={{0,4},{2,14},{4,8},{6,2},{8,12},{10,6},{12,0},{14,10},{16,20},{18,... | collective-permute-start | bytes 1572872 | tf_op jit(solution)/shard_map/ppermute | solution.py:80
  88.7 15.2 %collective-permute-start.27 = (f32[32,4096]{1,0:T(8,128)S(1)}, f32[32,4096]{1,0:T(8,128)S(1)}, u32[]{:S(2)}, u32[]{:S(2)}) collective-permute-start(f32[32,4096]{1,0:T(8,128)S(1)} %get-tuple-element.24), channel_id=1, source_target_pairs={{0,12},{2,6},{4,0},{6,10},{8,4},{10,14},{12,8},{14,2},{16,28},{18,... | collective-permute-start | bytes 1572872 | tf_op jit(solution)/shard_map/ppermute | solution.py:88
  91.7 12.3 %collective-permute-start.15 = (f32[16,4096]{1,0:T(8,128)S(1)}, f32[16,4096]{1,0:T(8,128)S(1)}, u32[]{:S(2)}, u32[]{:S(2)}) collective-permute-start(f32[16,4096]{1,0:T(8,128)S(1)} %get-tuple-element.19), channel_id=1, source_target_pairs={{0,32},{2,226},{4,36},{6,230},{8,40},{10,234},{12,44},{14,238},{16... | collective-permute-start | bytes 786440 | tf_op jit(solution)/shard_map/ppermute | solution.py:80
  91.8 12.3 %collective-permute-start.18 = (f32[16,4096]{1,0:T(8,128)S(1)}, f32[16,4096]{1,0:T(8,128)S(1)}, u32[]{:S(2)}, u32[]{:S(2)}) collective-permute-start(f32[16,4096]{1,0:T(8,128)S(1)} %get-tuple-element.20), channel_id=1, source_target_pairs={{0,224},{2,34},{4,228},{6,38},{8,232},{10,42},{12,236},{14,46},{16... | collective-permute-start | bytes 786440 | tf_op jit(solution)/shard_map/ppermute | solution.py:88
  104.0 6.2 %collective-permute-start.28 = (f32[4,4096]{1,0:T(4,128)S(1)}, f32[4,4096]{1,0:T(4,128)S(1)}, u32[]{:S(2)}, u32[]{:S(2)}) collective-permute-start(f32[4,4096]{1,0:T(4,128)S(1)} %slice.159), channel_id=1, source_target_pairs={{0,32},{2,226},{4,36},{6,230},{8,40},{10,234},{12,44},{14,238},{16... | collective-permute-start | bytes 196616 | tf_op jit(solution)/shard_map/ppermute | solution.py:80
  104.2 10.8 %collective-permute-start.16 = (f32[16,4096]{1,0:T(8,128)S(1)}, f32[16,4096]{1,0:T(8,128)S(1)}, u32[]{:S(2)}, u32[]{:S(2)}) collective-permute-start(f32[16,4096]{1,0:T(8,128)S(1)} %get-tuple-element.17), channel_id=1, source_target_pairs={{0,32},{2,226},{4,36},{6,230},{8,40},{10,234},{12,44},{14,238},{16... | collective-permute-start | bytes 786440 | tf_op jit(solution)/shard_map/ppermute | solution.py:80
  104.3 10.7 %collective-permute-start.19 = (f32[16,4096]{1,0:T(8,128)S(1)}, f32[16,4096]{1,0:T(8,128)S(1)}, u32[]{:S(2)}, u32[]{:S(2)}) collective-permute-start(f32[16,4096]{1,0:T(8,128)S(1)} %get-tuple-element.18), channel_id=1, source_target_pairs={{0,224},{2,34},{4,228},{6,38},{8,232},{10,42},{12,236},{14,46},{16... | collective-permute-start | bytes 786440 | tf_op jit(solution)/shard_map/ppermute | solution.py:88
  116.0 7.2 %collective-permute-start.30 = (f32[4,4096]{1,0:T(4,128)S(1)}, f32[4,4096]{1,0:T(4,128)S(1)}, u32[]{:S(2)}, u32[]{:S(2)}) collective-permute-start(f32[4,4096]{1,0:T(4,128)S(1)} %get-tuple-element.27), channel_id=1, source_target_pairs={{0,32},{2,226},{4,36},{6,230},{8,40},{10,234},{12,44},{14,238},{16... | collective-permute-start | bytes 196616 | tf_op jit(solution)/shard_map/ppermute | solution.py:80
  116.0 7.1 %collective-permute-start.33 = (f32[4,4096]{1,0:T(4,128)S(1)}, f32[4,4096]{1,0:T(4,128)S(1)}, u32[]{:S(2)}, u32[]{:S(2)}) collective-permute-start(f32[4,4096]{1,0:T(4,128)S(1)} %get-tuple-element.28), channel_id=1, source_target_pairs={{0,224},{2,34},{4,228},{6,38},{8,232},{10,42},{12,236},{14,46},{16... | collective-permute-start | bytes 196616 | tf_op jit(solution)/shard_map/ppermute | solution.py:88
  119.9 6.7 %collective-permute-start.20 = (f32[4,4096]{1,0:T(4,128)S(1)}, f32[4,4096]{1,0:T(4,128)S(1)}, u32[]{:S(2)}, u32[]{:S(2)}) collective-permute-start(f32[4,4096]{1,0:T(4,128)S(1)} %get-tuple-element.31), channel_id=1, source_target_pairs={{0,4},{2,14},{4,8},{6,2},{8,12},{10,6},{12,0},{14,10},{16,20},{18,... | collective-permute-start | bytes 196616 | tf_op jit(solution)/shard_map/ppermute | solution.py:64
  119.9 6.6 %collective-permute-start.21 = (f32[4,4096]{1,0:T(4,128)S(1)}, f32[4,4096]{1,0:T(4,128)S(1)}, u32[]{:S(2)}, u32[]{:S(2)}) collective-permute-start(f32[4,4096]{1,0:T(4,128)S(1)} %get-tuple-element.33), channel_id=1, source_target_pairs={{0,8},{2,10},{4,12},{6,14},{8,0},{10,2},{12,4},{14,6},{16,24},{18,... | collective-permute-start | bytes 196616 | tf_op jit(solution)/shard_map/ppermute | solution.py:64
  (18 other events, 168.7 us)

commit v7 on v6

--- a/solution.py
+++ b/solution.py
@@ -8,7 +8,7 @@
 AG_DIRECT = ("y",)
 PARTS = (
     (32, ("c", "z", "y", "xh"), ("y",)),
-    (32, ("c", "y", "z", "xh"), ()),
+    (32, ("c", "y", "z", "xh"), ("z",)),
 )
 
 

time: 136 us -> 139 us (1.022)
  starting transfers between devices: 53.7 us -> 57.3 us
    ppermute x3 -> x10, starting transfers between devices: 3.31 us -> 17.7 us  [_rs_direct(): total = total + lax.ppermute(part, 'blk', _perm(axis, o, size))]
    ppermute x7 -> x4, starting transfers between devices: 22.6 us -> 12 us  [_rs_stage(): recv = lax.ppermute(buf, 'blk', _perm(axis, -1, size))]
    ppermute x14 -> x10, waiting for transfers between devices: 25.3 us -> 22.1 us  [_rs_stage(): recv = lax.ppermute(buf, 'blk', _perm(axis, 1, size))]
    ppermute x3 -> x10, waiting for transfers between devices: 0.42 us -> 2.28 us  [_rs_direct(): total = total + lax.ppermute(part, 'blk', _perm(axis, o, size))]
    ppermute x14 -> x10, starting transfers between devices: 7.25 us -> 7.09 us  [_rs_stage(): recv = lax.ppermute(buf, 'blk', _perm(axis, 1, size))]
  transfers between devices with their start and end apart: 36 -> 36, of which waited for: 21 -> 17; matrix products, arithmetic and copies ran while one was open for 12% -> 11% of each run, Pallas kernels for 0% -> 0%
where the time goes in v7:
time: 139 us; the launch traced here: 137 us
  starting transfers between devices  57.3 us (41%)
  waiting for transfers between devices  54.3 us (39%)
  other arithmetic  12.9 us (9%)
  local copies, waits for them, and re-layouts  6.23 us (4%)
  matrix products  6.06 us (4%)
    ppermute x10, waiting for transfers between devices, _rs_stage(): recv = lax.ppermute(buf, 'blk', _perm(axis, 1, size))  22.1 us
    ppermute x10, starting transfers between devices, _rs_direct(): total = total + lax.ppermute(part, 'blk', _perm(axis, o, size))  17.7 us
    ppermute x5, waiting for transfers between devices, _ag_stage(): cur = lax.ppermute(cur, 'blk', _perm(axis, 1, size))  17.3 us
    ppermute x3, starting transfers between devices, _ag_stage(): cur = lax.ppermute(cur, 'blk', _perm(axis, -1, size))  13.3 us
    ppermute x4, starting transfers between devices, _rs_stage(): recv = lax.ppermute(buf, 'blk', _perm(axis, -1, size))  12 us
    ppermute x3, waiting for transfers between devices, _ag_stage(): cur = lax.ppermute(cur, 'blk', _perm(axis, -1, size))  9.27 us
    mul x3, other arithmetic, mask_blocks(): return (shaped * cols[:, None, :]).reshape(height, width)  7.42 us
    ppermute x10, starting transfers between devices, _rs_stage(): recv = lax.ppermute(buf, 'blk', _perm(axis, 1, size))  7.09 us
  transfers between devices with their start and end apart: 36, of which 17 were waited for; matrix products, arithmetic and copies ran while one was open for 11% of the time, Pallas kernels for 0%

profile of v7, /device:TPU:2, one launch (start us, length us, event | category | flops | bytes accessed | tf_op | source)
XLA Modules:
  0.0 137.2 jit_solution(2237922446949591809)
XLA Ops:
  1.8 2.2 %collective-permute-start = (bf16[2,8192]{1,0:T(2,128)(2,1)S(1)}, bf16[2,8192]{1,0:T(2,128)(2,1)S(1)}, u32[]{:S(2)}, u32[]{:S(2)}) collective-permute-start(bf16[2,8192]{1,0:T(2,128)(2,1)S(1)} %fusion.11), channel_id=1, source_target_pairs={{0,16},{2,18},{4,20},{6,22},{8,24},{10,26},{12,28},{14,30},{16,0},... | collective-permute-start | bytes 98312 | tf_op jit(solution)/shard_map/ppermute | solution.py:43
  5.7 4.5 %bitcast_multiply_fusion.2 = bf16[8192,256]{1,0:T(8,128)(2,1)} fusion(bf16[8192,256]{1,0:T(8,128)(2,1)} %param.10, bf16[64,256]{1,0:T(8,128)(2,1)S(1)} %bitcast.32), kind=kLoop, calls=%fused_computation.2 | loop fusion | flops 2097152 | bytes 8421376 | tf_op jit(solution)/shard_map/mul | solution.py:21
  10.3 3.1 %collective-permute-start.1 = (bf16[4,8192]{1,0:T(4,128)(2,1)S(1)}, bf16[4,8192]{1,0:T(4,128)(2,1)S(1)}, u32[]{:S(2)}, u32[]{:S(2)}) collective-permute-start(bf16[4,8192]{1,0:T(4,128)(2,1)S(1)} %pad_maximum_fusion.3), channel_id=1, source_target_pairs={{0,12},{2,6},{4,0},{6,10},{8,4},{10,14},{12,8},{14,2},{16,28},{18,... | collective-permute-start | bytes 196616 | tf_op jit(solution)/shard_map/ppermute | solution.py:54
  15.4 2.6 %bitcast_multiply_fusion.1 = bf16[8192,256]{1,0:T(8,128)(2,1)S(1)} fusion(bf16[8192,256]{1,0:T(8,128)(2,1)} %param.11, bf16[64,256]{1,0:T(8,128)(2,1)S(1)} %bitcast.30), kind=kLoop, calls=%fused_computation.1 | loop fusion | flops 2097152 | bytes 8421376 | tf_op jit(solution)/shard_map/mul | solution.py:21
  20.0 5.9 %collective-permute-start.4 = (bf16[16,8192]{1,0:T(8,128)(2,1)S(1)}, bf16[16,8192]{1,0:T(8,128)(2,1)S(1)}, u32[]{:S(2)}, u32[]{:S(2)}) collective-permute-start(bf16[16,8192]{1,0:T(8,128)(2,1)S(1)} %pad_maximum_fusion), channel_id=1, source_target_pairs={{0,224},{2,34},{4,228},{6,38},{8,232},{10,42},{12,236},{14,46},{16... | collective-permute-start | bytes 786440 | tf_op jit(solution)/shard_map/ppermute | solution.py:47
  26.0 5.1 %collective-permute-done.4 = bf16[16,8192]{1,0:T(8,128)(2,1)S(1)} collective-permute-done((bf16[16,8192]{1,0:T(8,128)(2,1)S(1)}, bf16[16,8192]{1,0:T(8,128)(2,1)S(1)}, u32[]{:S(2)}, u32[]{:S(2)}) %collective-permute-start.4) | collective-permute-done | bytes 262176 | tf_op jit(solution)/shard_map/ppermute | solution.py:47
  31.1 3.7 %collective-permute-start.5 = (bf16[16,8192]{1,0:T(8,128)(2,1)S(1)}, bf16[16,8192]{1,0:T(8,128)(2,1)S(1)}, u32[]{:S(2)}, u32[]{:S(2)}) collective-permute-start(bf16[16,8192]{1,0:T(8,128)(2,1)S(1)} %collective-permute-done.4), channel_id=1, source_target_pairs={{0,224},{2,34},{4,228},{6,38},{8,232},{10,42},{12,236},{14,46},{16... | collective-permute-start | bytes 786440 | tf_op jit(solution)/shard_map/ppermute | solution.py:47
  34.8 4.2 %collective-permute-done.5 = bf16[16,8192]{1,0:T(8,128)(2,1)S(1)} collective-permute-done((bf16[16,8192]{1,0:T(8,128)(2,1)S(1)}, bf16[16,8192]{1,0:T(8,128)(2,1)S(1)}, u32[]{:S(2)}, u32[]{:S(2)}) %collective-permute-start.5) | collective-permute-done | bytes 262176 | tf_op jit(solution)/shard_map/ppermute | solution.py:47
  38.9 3.7 %collective-permute-start.6 = (bf16[16,8192]{1,0:T(8,128)(2,1)S(1)}, bf16[16,8192]{1,0:T(8,128)(2,1)S(1)}, u32[]{:S(2)}, u32[]{:S(2)}) collective-permute-start(bf16[16,8192]{1,0:T(8,128)(2,1)S(1)} %collective-permute-done.5), channel_id=1, source_target_pairs={{0,224},{2,34},{4,228},{6,38},{8,232},{10,42},{12,236},{14,46},{16... | collective-permute-start | bytes 786440 | tf_op jit(solution)/shard_map/ppermute | solution.py:47
  42.6 2.2 %collective-permute-done.8 = bf16[16,8192]{1,0:T(8,128)(2,1)S(1)} collective-permute-done((bf16[16,8192]{1,0:T(8,128)(2,1)S(1)}, bf16[16,8192]{1,0:T(8,128)(2,1)S(1)}, u32[]{:S(2)}, u32[]{:S(2)}) %collective-permute-start.8) | collective-permute-done | bytes 262176 | tf_op jit(solution)/shard_map/ppermute | solution.py:43
  44.8 7.6 %collective-permute-done.9 = bf16[16,8192]{1,0:T(8,128)(2,1)S(1)} collective-permute-done((bf16[16,8192]{1,0:T(8,128)(2,1)S(1)}, bf16[16,8192]{1,0:T(8,128)(2,1)S(1)}, u32[]{:S(2)}, u32[]{:S(2)}) %collective-permute-start.9) | collective-permute-done | bytes 262176 | tf_op jit(solution)/shard_map/ppermute | solution.py:43
  52.4 7.6 %collective-permute-done.10 = bf16[16,8192]{1,0:T(8,128)(2,1)S(1)} collective-permute-done((bf16[16,8192]{1,0:T(8,128)(2,1)S(1)}, bf16[16,8192]{1,0:T(8,128)(2,1)S(1)}, u32[]{:S(2)}, u32[]{:S(2)}) %collective-permute-start.10) | collective-permute-done | bytes 262176 | tf_op jit(solution)/shard_map/ppermute | solution.py:43
  61.9 2.6 %collective-permute-done.11 = bf16[128,8192]{1,0:T(8,128)(2,1)S(1)} collective-permute-done((bf16[128,8192]{1,0:T(8,128)(2,1)S(1)}, bf16[128,8192]{1,0:T(8,128)(2,1)S(1)}, u32[]{:S(2)}, u32[]{:S(2)}) %collective-permute-start.11) | collective-permute-done | bytes 2097184 | tf_op jit(solution)/shard_map/ppermute | solution.py:128
  70.4 2.3 %fusion = f32[256,4096]{1,0:T(8,128)S(1)} fusion(bf16[256,256]{1,0:T(8,128)(2,1)S(1)} %reshape.27, bf16[256,8192]{1,0:T(8,128)(2,1)} %copy-done.1), kind=kOutput, calls=%fused_computation.5 | convolution fusion | flops 536870912 | bytes 6422528 | tf_op jit(solution)/shard_map/dot_general | solution.py:140
  75.3 7.6 %collective-permute-done.13 = f32[16,4096]{1,0:T(8,128)S(1)} collective-permute-done((f32[16,4096]{1,0:T(8,128)S(1)}, f32[16,4096]{1,0:T(8,128)S(1)}, u32[]{:S(2)}, u32[]{:S(2)}) %collective-permute-start.13) | collective-permute-done | bytes 262176 | tf_op jit(solution)/shard_map/ppermute | solution.py:80
  83.0 3.2 %collective-permute-start.17 = (f32[16,4096]{1,0:T(8,128)S(1)}, f32[16,4096]{1,0:T(8,128)S(1)}, u32[]{:S(2)}, u32[]{:S(2)}) collective-permute-start(f32[16,4096]{1,0:T(8,128)S(1)} %get-tuple-element.22), channel_id=1, source_target_pairs={{0,224},{2,34},{4,228},{6,38},{8,232},{10,42},{12,236},{14,46},{16... | collective-permute-start | bytes 786440 | tf_op jit(solution)/shard_map/ppermute | solution.py:88
  88.4 3.2 %collective-permute-done.14 = f32[16,4096]{1,0:T(8,128)S(1)} collective-permute-done((f32[16,4096]{1,0:T(8,128)S(1)}, f32[16,4096]{1,0:T(8,128)S(1)}, u32[]{:S(2)}, u32[]{:S(2)}) %collective-permute-start.14) | collective-permute-done | bytes 262176 | tf_op jit(solution)/shard_map/ppermute | solution.py:80
  91.8 3.2 %collective-permute-start.18 = (f32[16,4096]{1,0:T(8,128)S(1)}, f32[16,4096]{1,0:T(8,128)S(1)}, u32[]{:S(2)}, u32[]{:S(2)}) collective-permute-start(f32[16,4096]{1,0:T(8,128)S(1)} %get-tuple-element.20), channel_id=1, source_target_pairs={{0,224},{2,34},{4,228},{6,38},{8,232},{10,42},{12,236},{14,46},{16... | collective-permute-start | bytes 786440 | tf_op jit(solution)/shard_map/ppermute | solution.py:88
  100.6 3.5 %collective-permute-start.19 = (f32[16,4096]{1,0:T(8,128)S(1)}, f32[16,4096]{1,0:T(8,128)S(1)}, u32[]{:S(2)}, u32[]{:S(2)}) collective-permute-start(f32[16,4096]{1,0:T(8,128)S(1)} %get-tuple-element.18), channel_id=1, source_target_pairs={{0,224},{2,34},{4,228},{6,38},{8,232},{10,42},{12,236},{14,46},{16... | collective-permute-start | bytes 786440 | tf_op jit(solution)/shard_map/ppermute | solution.py:88
  104.1 5.0 %collective-permute-done.26 = f32[32,4096]{1,0:T(8,128)S(1)} collective-permute-done((f32[32,4096]{1,0:T(8,128)S(1)}, f32[32,4096]{1,0:T(8,128)S(1)}, u32[]{:S(2)}, u32[]{:S(2)}) %collective-permute-start.26) | collective-permute-done | bytes 524320 | tf_op jit(solution)/shard_map/ppermute | solution.py:80
  109.6 2.1 %collective-permute-start.29 = (f32[4,4096]{1,0:T(4,128)S(1)}, f32[4,4096]{1,0:T(4,128)S(1)}, u32[]{:S(2)}, u32[]{:S(2)}) collective-permute-start(f32[4,4096]{1,0:T(4,128)S(1)} %get-tuple-element.31), channel_id=1, source_target_pairs={{0,64},{2,194},{4,68},{6,198},{8,72},{10,202},{12,76},{14,206},{16... | collective-permute-start | bytes 196616 | tf_op jit(solution)/shard_map/ppermute | solution.py:64
  113.3 2.6 %collective-permute-start.31 = (f32[4,4096]{1,0:T(4,128)S(1)}, f32[4,4096]{1,0:T(4,128)S(1)}, u32[]{:S(2)}, u32[]{:S(2)}) collective-permute-start(f32[4,4096]{1,0:T(4,128)S(1)} %get-tuple-element.29), channel_id=1, source_target_pairs={{0,128},{2,130},{4,132},{6,134},{8,136},{10,138},{12,140},{14,142}... | collective-permute-start | bytes 196616 | tf_op jit(solution)/shard_map/ppermute | solution.py:64
  115.9 4.8 %collective-permute-start.32 = (f32[4,4096]{1,0:T(4,128)S(1)}, f32[4,4096]{1,0:T(4,128)S(1)}, u32[]{:S(2)}, u32[]{:S(2)}) collective-permute-start(f32[4,4096]{1,0:T(4,128)S(1)} %get-tuple-element.28), channel_id=1, source_target_pairs={{0,160},{2,98},{4,164},{6,102},{8,168},{10,106},{12,172},{14,110},... | collective-permute-start | bytes 196616 | tf_op jit(solution)/shard_map/ppermute | solution.py:64
  133.5 3.0 %collective-permute-done.23 = f32[2,4096]{1,0:T(2,128)S(1)} collective-permute-done((f32[2,4096]{1,0:T(2,128)S(1)}, f32[2,4096]{1,0:T(2,128)S(1)}, u32[]{:S(2)}, u32[]{:S(2)}) %collective-permute-start.23) | collective-permute-done | bytes 32800 | tf_op jit(solution)/shard_map/ppermute | solution.py:80
  (121 shorter events, 41.3 us)
Async XLA Ops:
  1.8 8.4 %collective-permute-start = (bf16[2,8192]{1,0:T(2,128)(2,1)S(1)}, bf16[2,8192]{1,0:T(2,128)(2,1)S(1)}, u32[]{:S(2)}, u32[]{:S(2)}) collective-permute-start(bf16[2,8192]{1,0:T(2,128)(2,1)S(1)} %fusion.11), channel_id=1, source_target_pairs={{0,16},{2,18},{4,20},{6,22},{8,24},{10,26},{12,28},{14,30},{16,0},... | collective-permute-start | bytes 98312 | tf_op jit(solution)/shard_map/ppermute | solution.py:43
  10.3 8.9 %collective-permute-start.1 = (bf16[4,8192]{1,0:T(4,128)(2,1)S(1)}, bf16[4,8192]{1,0:T(4,128)(2,1)S(1)}, u32[]{:S(2)}, u32[]{:S(2)}) collective-permute-start(bf16[4,8192]{1,0:T(4,128)(2,1)S(1)} %pad_maximum_fusion.3), channel_id=1, source_target_pairs={{0,12},{2,6},{4,0},{6,10},{8,4},{10,14},{12,8},{14,2},{16,28},{18,... | collective-permute-start | bytes 196616 | tf_op jit(solution)/shard_map/ppermute | solution.py:54
  20.0 11.1 %collective-permute-start.4 = (bf16[16,8192]{1,0:T(8,128)(2,1)S(1)}, bf16[16,8192]{1,0:T(8,128)(2,1)S(1)}, u32[]{:S(2)}, u32[]{:S(2)}) collective-permute-start(bf16[16,8192]{1,0:T(8,128)(2,1)S(1)} %pad_maximum_fusion), channel_id=1, source_target_pairs={{0,224},{2,34},{4,228},{6,38},{8,232},{10,42},{12,236},{14,46},{16... | collective-permute-start | bytes 786440 | tf_op jit(solution)/shard_map/ppermute | solution.py:47
  25.9 8.8 %collective-permute-start.7 = (bf16[16,8192]{1,0:T(8,128)(2,1)S(1)}, bf16[16,8192]{1,0:T(8,128)(2,1)S(1)}, u32[]{:S(2)}, u32[]{:S(2)}) collective-permute-start(bf16[16,8192]{1,0:T(8,128)(2,1)S(1)} %pad_maximum_fusion), channel_id=1, source_target_pairs={{0,32},{2,226},{4,36},{6,230},{8,40},{10,234},{12,44},{14,238},{16... | collective-permute-start | bytes 786440 | tf_op jit(solution)/shard_map/ppermute | solution.py:43
  31.1 7.9 %collective-permute-start.5 = (bf16[16,8192]{1,0:T(8,128)(2,1)S(1)}, bf16[16,8192]{1,0:T(8,128)(2,1)S(1)}, u32[]{:S(2)}, u32[]{:S(2)}) collective-permute-start(bf16[16,8192]{1,0:T(8,128)(2,1)S(1)} %collective-permute-done.4), channel_id=1, source_target_pairs={{0,224},{2,34},{4,228},{6,38},{8,232},{10,42},{12,236},{14,46},{16... | collective-permute-start | bytes 786440 | tf_op jit(solution)/shard_map/ppermute | solution.py:47
  34.7 10.0 %collective-permute-start.8 = (bf16[16,8192]{1,0:T(8,128)(2,1)S(1)}, bf16[16,8192]{1,0:T(8,128)(2,1)S(1)}, u32[]{:S(2)}, u32[]{:S(2)}) collective-permute-start(bf16[16,8192]{1,0:T(8,128)(2,1)S(1)} %collective-permute-done.7), channel_id=1, source_target_pairs={{0,32},{2,226},{4,36},{6,230},{8,40},{10,234},{12,44},{14,238},{16... | collective-permute-start | bytes 786440 | tf_op jit(solution)/shard_map/ppermute | solution.py:43
  38.9 13.4 %collective-permute-start.6 = (bf16[16,8192]{1,0:T(8,128)(2,1)S(1)}, bf16[16,8192]{1,0:T(8,128)(2,1)S(1)}, u32[]{:S(2)}, u32[]{:S(2)}) collective-permute-start(bf16[16,8192]{1,0:T(8,128)(2,1)S(1)} %collective-permute-done.5), channel_id=1, source_target_pairs={{0,224},{2,34},{4,228},{6,38},{8,232},{10,42},{12,236},{14,46},{16... | collective-permute-start | bytes 786440 | tf_op jit(solution)/shard_map/ppermute | solution.py:47
  44.8 7.6 %collective-permute-start.9 = (bf16[16,8192]{1,0:T(8,128)(2,1)S(1)}, bf16[16,8192]{1,0:T(8,128)(2,1)S(1)}, u32[]{:S(2)}, u32[]{:S(2)}) collective-permute-start(bf16[16,8192]{1,0:T(8,128)(2,1)S(1)} %collective-permute-done.8), channel_id=1, source_target_pairs={{0,32},{2,226},{4,36},{6,230},{8,40},{10,234},{12,44},{14,238},{16... | collective-permute-start | bytes 786440 | tf_op jit(solution)/shard_map/ppermute | solution.py:43
  72.9 13.3 %collective-permute-start.24 = (f32[128,4096]{1,0:T(8,128)S(1)}, f32[128,4096]{1,0:T(8,128)S(1)}, u32[]{:S(2)}, u32[]{:S(2)}) collective-permute-start(f32[128,4096]{1,0:T(8,128)S(1)} %slice.153), channel_id=1, source_target_pairs={{0,2},{2,0},{4,6},{6,4},{8,10},{10,8},{12,14},{14,12},{16,18},{18,... | collective-permute-start | bytes 6291464 | tf_op jit(solution)/shard_map/ppermute | solution.py:80
  75.2 7.7 %collective-permute-start.13 = (f32[16,4096]{1,0:T(8,128)S(1)}, f32[16,4096]{1,0:T(8,128)S(1)}, u32[]{:S(2)}, u32[]{:S(2)}) collective-permute-start(f32[16,4096]{1,0:T(8,128)S(1)} %slice.139), channel_id=1, source_target_pairs={{0,32},{2,226},{4,36},{6,230},{8,40},{10,234},{12,44},{14,238},{16... | collective-permute-start | bytes 786440 | tf_op jit(solution)/shard_map/ppermute | solution.py:80
  82.9 8.7 %collective-permute-start.14 = (f32[16,4096]{1,0:T(8,128)S(1)}, f32[16,4096]{1,0:T(8,128)S(1)}, u32[]{:S(2)}, u32[]{:S(2)}) collective-permute-start(f32[16,4096]{1,0:T(8,128)S(1)} %get-tuple-element.21), channel_id=1, source_target_pairs={{0,32},{2,226},{4,36},{6,230},{8,40},{10,234},{12,44},{14,238},{16... | collective-permute-start | bytes 786440 | tf_op jit(solution)/shard_map/ppermute | solution.py:80
  83.0 8.6 %collective-permute-start.17 = (f32[16,4096]{1,0:T(8,128)S(1)}, f32[16,4096]{1,0:T(8,128)S(1)}, u32[]{:S(2)}, u32[]{:S(2)}) collective-permute-start(f32[16,4096]{1,0:T(8,128)S(1)} %get-tuple-element.22), channel_id=1, source_target_pairs={{0,224},{2,34},{4,228},{6,38},{8,232},{10,42},{12,236},{14,46},{16... | collective-permute-start | bytes 786440 | tf_op jit(solution)/shard_map/ppermute | solution.py:88
  86.6 10.5 %collective-permute-start.25 = (f32[32,4096]{1,0:T(8,128)S(1)}, f32[32,4096]{1,0:T(8,128)S(1)}, u32[]{:S(2)}, u32[]{:S(2)}) collective-permute-start(f32[32,4096]{1,0:T(8,128)S(1)} %slice.155), channel_id=1, source_target_pairs={{0,4},{2,14},{4,8},{6,2},{8,12},{10,6},{12,0},{14,10},{16,20},{18,... | collective-permute-start | bytes 1572872 | tf_op jit(solution)/shard_map/ppermute | solution.py:80
  91.7 8.7 %collective-permute-start.15 = (f32[16,4096]{1,0:T(8,128)S(1)}, f32[16,4096]{1,0:T(8,128)S(1)}, u32[]{:S(2)}, u32[]{:S(2)}) collective-permute-start(f32[16,4096]{1,0:T(8,128)S(1)} %get-tuple-element.19), channel_id=1, source_target_pairs={{0,32},{2,226},{4,36},{6,230},{8,40},{10,234},{12,44},{14,238},{16... | collective-permute-start | bytes 786440 | tf_op jit(solution)/shard_map/ppermute | solution.py:80
  91.8 8.6 %collective-permute-start.18 = (f32[16,4096]{1,0:T(8,128)S(1)}, f32[16,4096]{1,0:T(8,128)S(1)}, u32[]{:S(2)}, u32[]{:S(2)}) collective-permute-start(f32[16,4096]{1,0:T(8,128)S(1)} %get-tuple-element.20), channel_id=1, source_target_pairs={{0,224},{2,34},{4,228},{6,38},{8,232},{10,42},{12,236},{14,46},{16... | collective-permute-start | bytes 786440 | tf_op jit(solution)/shard_map/ppermute | solution.py:88
  97.1 12.0 %collective-permute-start.26 = (f32[32,4096]{1,0:T(8,128)S(1)}, f32[32,4096]{1,0:T(8,128)S(1)}, u32[]{:S(2)}, u32[]{:S(2)}) collective-permute-start(f32[32,4096]{1,0:T(8,128)S(1)} %get-tuple-element.23), channel_id=1, source_target_pairs={{0,4},{2,14},{4,8},{6,2},{8,12},{10,6},{12,0},{14,10},{16,20},{18,... | collective-permute-start | bytes 1572872 | tf_op jit(solution)/shard_map/ppermute | solution.py:80
  98.4 10.7 %collective-permute-start.27 = (f32[32,4096]{1,0:T(8,128)S(1)}, f32[32,4096]{1,0:T(8,128)S(1)}, u32[]{:S(2)}, u32[]{:S(2)}) collective-permute-start(f32[32,4096]{1,0:T(8,128)S(1)} %get-tuple-element.24), channel_id=1, source_target_pairs={{0,12},{2,6},{4,0},{6,10},{8,4},{10,14},{12,8},{14,2},{16,28},{18,... | collective-permute-start | bytes 1572872 | tf_op jit(solution)/shard_map/ppermute | solution.py:88
  100.5 12.8 %collective-permute-start.16 = (f32[16,4096]{1,0:T(8,128)S(1)}, f32[16,4096]{1,0:T(8,128)S(1)}, u32[]{:S(2)}, u32[]{:S(2)}) collective-permute-start(f32[16,4096]{1,0:T(8,128)S(1)} %get-tuple-element.17), channel_id=1, source_target_pairs={{0,32},{2,226},{4,36},{6,230},{8,40},{10,234},{12,44},{14,238},{16... | collective-permute-start | bytes 786440 | tf_op jit(solution)/shard_map/ppermute | solution.py:80
  100.6 15.2 %collective-permute-start.19 = (f32[16,4096]{1,0:T(8,128)S(1)}, f32[16,4096]{1,0:T(8,128)S(1)}, u32[]{:S(2)}, u32[]{:S(2)}) collective-permute-start(f32[16,4096]{1,0:T(8,128)S(1)} %get-tuple-element.18), channel_id=1, source_target_pairs={{0,224},{2,34},{4,228},{6,38},{8,232},{10,42},{12,236},{14,46},{16... | collective-permute-start | bytes 786440 | tf_op jit(solution)/shard_map/ppermute | solution.py:88
  109.3 11.4 %collective-permute-start.28 = (f32[4,4096]{1,0:T(4,128)S(1)}, f32[4,4096]{1,0:T(4,128)S(1)}, u32[]{:S(2)}, u32[]{:S(2)}) collective-permute-start(f32[4,4096]{1,0:T(4,128)S(1)} %get-tuple-element.25), channel_id=1, source_target_pairs={{0,32},{2,226},{4,36},{6,230},{8,40},{10,234},{12,44},{14,238},{16... | collective-permute-start | bytes 196616 | tf_op jit(solution)/shard_map/ppermute | solution.py:64
  109.6 11.4 %collective-permute-start.29 = (f32[4,4096]{1,0:T(4,128)S(1)}, f32[4,4096]{1,0:T(4,128)S(1)}, u32[]{:S(2)}, u32[]{:S(2)}) collective-permute-start(f32[4,4096]{1,0:T(4,128)S(1)} %get-tuple-element.31), channel_id=1, source_target_pairs={{0,64},{2,194},{4,68},{6,198},{8,72},{10,202},{12,76},{14,206},{16... | collective-permute-start | bytes 196616 | tf_op jit(solution)/shard_map/ppermute | solution.py:64
  111.7 11.8 %collective-permute-start.30 = (f32[4,4096]{1,0:T(4,128)S(1)}, f32[4,4096]{1,0:T(4,128)S(1)}, u32[]{:S(2)}, u32[]{:S(2)}) collective-permute-start(f32[4,4096]{1,0:T(4,128)S(1)} %get-tuple-element.30), channel_id=1, source_target_pairs={{0,96},{2,162},{4,100},{6,166},{8,104},{10,170},{12,108},{14,174},... | collective-permute-start | bytes 196616 | tf_op jit(solution)/shard_map/ppermute | solution.py:64
  113.3 11.9 %collective-permute-start.31 = (f32[4,4096]{1,0:T(4,128)S(1)}, f32[4,4096]{1,0:T(4,128)S(1)}, u32[]{:S(2)}, u32[]{:S(2)}) collective-permute-start(f32[4,4096]{1,0:T(4,128)S(1)} %get-tuple-element.29), channel_id=1, source_target_pairs={{0,128},{2,130},{4,132},{6,134},{8,136},{10,138},{12,140},{14,142}... | collective-permute-start | bytes 196616 | tf_op jit(solution)/shard_map/ppermute | solution.py:64
  115.9 10.7 %collective-permute-start.32 = (f32[4,4096]{1,0:T(4,128)S(1)}, f32[4,4096]{1,0:T(4,128)S(1)}, u32[]{:S(2)}, u32[]{:S(2)}) collective-permute-start(f32[4,4096]{1,0:T(4,128)S(1)} %get-tuple-element.28), channel_id=1, source_target_pairs={{0,160},{2,98},{4,164},{6,102},{8,168},{10,106},{12,172},{14,110},... | collective-permute-start | bytes 196616 | tf_op jit(solution)/shard_map/ppermute | solution.py:64
  (18 other events, 174.2 us)

commit v8 on v6

--- a/solution.py
+++ b/solution.py
@@ -137,8 +137,13 @@
     for groups, rs_order, direct in PARTS:
         hi = lo + groups * 128
         h = hidden if rs_order == base else _reorder_rows(hidden, base, rs_order, t)
-        x = jnp.dot(h, down_kept[:, lo:hi], preferred_element_type=jnp.float32)
-        for axis in rs_order:
+        first = rs_order[0]
+        assert first == base[0] and BLK_AXES[first][1] == 2
+        half = h.shape[0] // 2
+        sent = jnp.dot(h[half:], down_kept[:, lo:hi], preferred_element_type=jnp.float32)
+        recv = lax.ppermute(sent, "blk", _perm(first, 1, size))
+        x = jnp.dot(h[:half], down_kept[:, lo:hi], preferred_element_type=jnp.float32) + recv
+        for axis in rs_order[1:]:
             if axis in direct:
                 x = _rs_direct(x, axis, size)
             else:

time: 136 us -> 137 us (level)
  matrix products: 6.06 us -> 12.6 us
  local copies, waits for them, and re-layouts: 6.16 us -> 2.22 us
    dot_general x2 -> x4, matrix products: 3.04 us -> 9.53 us  [the longest x2 5.22 us: local(): jnp.dot(h[half:], down_kept[:, lo:hi], preferred_element_type=jnp.float32)]
    unnamed x23 -> x21, local copies, waits for them, and re-layouts: 3.24 us -> 1.09 us
    ppermute x14 -> x12, waiting for transfers between devices: 25.3 us -> 23.4 us  [_rs_stage(): recv = lax.ppermute(buf, 'blk', _perm(axis, 1, size))]
    slice x7 -> x5, local copies, waits for them, and re-layouts: 1.92 us -> 0.11 us  [take(): return lax.slice_in_dim(x, j % n * r, (j % n + 1) * r, axis=0)]
    ppermute x0 -> x2, waiting for transfers between devices: none -> 1.69 us  [local(): recv = lax.ppermute(sent, 'blk', _perm(first, 1, size))]
    ppermute x14 -> x12, starting transfers between devices: 7.25 us -> 6.63 us  [_rs_stage(): recv = lax.ppermute(buf, 'blk', _perm(axis, 1, size))]
  transfers between devices with their start and end apart: 36 -> 36, of which waited for: 21 -> 18; matrix products, arithmetic and copies ran while one was open for 12% -> 15% of each run, Pallas kernels for 0% -> 0%
where the time goes in v8:
time: 137 us; the launch traced here: 136 us
  waiting for transfers between devices  55.4 us (40%)
  starting transfers between devices  53 us (39%)
  other arithmetic  12.6 us (9%)
  matrix products  12.6 us (9%)
  local copies, waits for them, and re-layouts  2.22 us (2%)
    ppermute x12, waiting for transfers between devices, _rs_stage(): recv = lax.ppermute(buf, 'blk', _perm(axis, 1, size))  23.4 us
    ppermute x7, starting transfers between devices, _rs_stage(): recv = lax.ppermute(buf, 'blk', _perm(axis, -1, size))  22.1 us
    ppermute x5, waiting for transfers between devices, _ag_stage(): cur = lax.ppermute(cur, 'blk', _perm(axis, 1, size))  17.3 us
    ppermute x3, starting transfers between devices, _ag_stage(): cur = lax.ppermute(cur, 'blk', _perm(axis, -1, size))  13.3 us
    ppermute x3, waiting for transfers between devices, _ag_stage(): cur = lax.ppermute(cur, 'blk', _perm(axis, -1, size))  9.27 us
    mul x3, other arithmetic, mask_blocks(): return (shaped * cols[:, None, :]).reshape(height, width)  7.43 us
    ppermute x12, starting transfers between devices, _rs_stage(): recv = lax.ppermute(buf, 'blk', _perm(axis, 1, size))  6.63 us
    dot_general x2, matrix products, local(): jnp.dot(h[half:], down_kept[:, lo:hi], preferred_element_type=jnp.float32)  5.22 us
  transfers between devices with their start and end apart: 36, of which 18 were waited for; matrix products, arithmetic and copies ran while one was open for 15% of the time, Pallas kernels for 0%

profile of v8, /device:TPU:2, one launch (start us, length us, event | category | flops | bytes accessed | tf_op | source)
XLA Modules:
  0.0 136.3 jit_solution(5425690133961243127)
XLA Ops:
  1.8 2.2 %collective-permute-start = (bf16[2,8192]{1,0:T(2,128)(2,1)S(1)}, bf16[2,8192]{1,0:T(2,128)(2,1)S(1)}, u32[]{:S(2)}, u32[]{:S(2)}) collective-permute-start(bf16[2,8192]{1,0:T(2,128)(2,1)S(1)} %fusion.12), channel_id=1, source_target_pairs={{0,16},{2,18},{4,20},{6,22},{8,24},{10,26},{12,28},{14,30},{16,0},... | collective-permute-start | bytes 98312 | tf_op jit(solution)/shard_map/ppermute | solution.py:43
  5.7 4.5 %bitcast_multiply_fusion.2 = bf16[8192,256]{1,0:T(8,128)(2,1)} fusion(bf16[8192,256]{1,0:T(8,128)(2,1)} %param.10, bf16[64,256]{1,0:T(8,128)(2,1)S(1)} %bitcast.33), kind=kLoop, calls=%fused_computation.4 | loop fusion | flops 2097152 | bytes 8421376 | tf_op jit(solution)/shard_map/mul | solution.py:21
  10.3 3.1 %collective-permute-start.1 = (bf16[4,8192]{1,0:T(4,128)(2,1)S(1)}, bf16[4,8192]{1,0:T(4,128)(2,1)S(1)}, u32[]{:S(2)}, u32[]{:S(2)}) collective-permute-start(bf16[4,8192]{1,0:T(4,128)(2,1)S(1)} %pad_maximum_fusion.3), channel_id=1, source_target_pairs={{0,12},{2,6},{4,0},{6,10},{8,4},{10,14},{12,8},{14,2},{16,28},{18,... | collective-permute-start | bytes 196616 | tf_op jit(solution)/shard_map/ppermute | solution.py:54
  15.4 2.6 %bitcast_multiply_fusion.1 = bf16[8192,256]{1,0:T(8,128)(2,1)S(1)} fusion(bf16[8192,256]{1,0:T(8,128)(2,1)} %param.11, bf16[64,256]{1,0:T(8,128)(2,1)S(1)} %bitcast.31), kind=kLoop, calls=%fused_computation.3 | loop fusion | flops 2097152 | bytes 8421376 | tf_op jit(solution)/shard_map/mul | solution.py:21
  20.0 5.9 %collective-permute-start.4 = (bf16[16,8192]{1,0:T(8,128)(2,1)S(1)}, bf16[16,8192]{1,0:T(8,128)(2,1)S(1)}, u32[]{:S(2)}, u32[]{:S(2)}) collective-permute-start(bf16[16,8192]{1,0:T(8,128)(2,1)S(1)} %pad_maximum_fusion), channel_id=1, source_target_pairs={{0,224},{2,34},{4,228},{6,38},{8,232},{10,42},{12,236},{14,46},{16... | collective-permute-start | bytes 786440 | tf_op jit(solution)/shard_map/ppermute | solution.py:47
  26.0 5.1 %collective-permute-done.4 = bf16[16,8192]{1,0:T(8,128)(2,1)S(1)} collective-permute-done((bf16[16,8192]{1,0:T(8,128)(2,1)S(1)}, bf16[16,8192]{1,0:T(8,128)(2,1)S(1)}, u32[]{:S(2)}, u32[]{:S(2)}) %collective-permute-start.4) | collective-permute-done | bytes 262176 | tf_op jit(solution)/shard_map/ppermute | solution.py:47
  31.1 3.7 %collective-permute-start.5 = (bf16[16,8192]{1,0:T(8,128)(2,1)S(1)}, bf16[16,8192]{1,0:T(8,128)(2,1)S(1)}, u32[]{:S(2)}, u32[]{:S(2)}) collective-permute-start(bf16[16,8192]{1,0:T(8,128)(2,1)S(1)} %collective-permute-done.4), channel_id=1, source_target_pairs={{0,224},{2,34},{4,228},{6,38},{8,232},{10,42},{12,236},{14,46},{16... | collective-permute-start | bytes 786440 | tf_op jit(solution)/shard_map/ppermute | solution.py:47
  34.8 4.2 %collective-permute-done.5 = bf16[16,8192]{1,0:T(8,128)(2,1)S(1)} collective-permute-done((bf16[16,8192]{1,0:T(8,128)(2,1)S(1)}, bf16[16,8192]{1,0:T(8,128)(2,1)S(1)}, u32[]{:S(2)}, u32[]{:S(2)}) %collective-permute-start.5) | collective-permute-done | bytes 262176 | tf_op jit(solution)/shard_map/ppermute | solution.py:47
  38.9 3.7 %collective-permute-start.6 = (bf16[16,8192]{1,0:T(8,128)(2,1)S(1)}, bf16[16,8192]{1,0:T(8,128)(2,1)S(1)}, u32[]{:S(2)}, u32[]{:S(2)}) collective-permute-start(bf16[16,8192]{1,0:T(8,128)(2,1)S(1)} %collective-permute-done.5), channel_id=1, source_target_pairs={{0,224},{2,34},{4,228},{6,38},{8,232},{10,42},{12,236},{14,46},{16... | collective-permute-start | bytes 786440 | tf_op jit(solution)/shard_map/ppermute | solution.py:47
  44.8 7.6 %collective-permute-done.9 = bf16[16,8192]{1,0:T(8,128)(2,1)S(1)} collective-permute-done((bf16[16,8192]{1,0:T(8,128)(2,1)S(1)}, bf16[16,8192]{1,0:T(8,128)(2,1)S(1)}, u32[]{:S(2)}, u32[]{:S(2)}) %collective-permute-start.9) | collective-permute-done | bytes 262176 | tf_op jit(solution)/shard_map/ppermute | solution.py:43
  52.4 7.6 %collective-permute-done.10 = bf16[16,8192]{1,0:T(8,128)(2,1)S(1)} collective-permute-done((bf16[16,8192]{1,0:T(8,128)(2,1)S(1)}, bf16[16,8192]{1,0:T(8,128)(2,1)S(1)}, u32[]{:S(2)}, u32[]{:S(2)}) %collective-permute-start.10) | collective-permute-done | bytes 262176 | tf_op jit(solution)/shard_map/ppermute | solution.py:43
  61.9 2.6 %collective-permute-done.11 = bf16[128,8192]{1,0:T(8,128)(2,1)S(1)} collective-permute-done((bf16[128,8192]{1,0:T(8,128)(2,1)S(1)}, bf16[128,8192]{1,0:T(8,128)(2,1)S(1)}, u32[]{:S(2)}, u32[]{:S(2)}) %collective-permute-start.11) | collective-permute-done | bytes 2097184 | tf_op jit(solution)/shard_map/ppermute | solution.py:128
  68.8 3.4 %fusion = f32[128,4096]{1,0:T(8,128)} fusion(bf16[128,256]{1,0:T(8,128)(2,1)S(1)} %slice.131, bf16[256,8192]{1,0:T(8,128)(2,1)} %copy-done), kind=kOutput, calls=%fused_computation.5 | convolution fusion | flops 268435456 | bytes 4259840 | tf_op jit(solution)/shard_map/dot_general | solution.py:143
  72.7 2.2 %convolution_add_fusion.1 = f32[128,4096]{1,0:T(8,128)S(1)} fusion(f32[128,4096]{1,0:T(8,128)S(1)} %collective-permute-done.12, bf16[256,8192]{1,0:T(8,128)(2,1)} %copy-done, bf16[256,256]{1,0:T(8,128)(2,1)S(1)} %get-tuple-element.34), kind=kOutput, calls=%fused_computation.1 | convolution fusion | flops 268959744 | bytes 6356992 | tf_op jit(solution)/shard_map/dot_general | solution.py:145
  82.8 3.2 %collective-permute-start.17 = (f32[16,4096]{1,0:T(8,128)S(1)}, f32[16,4096]{1,0:T(8,128)S(1)}, u32[]{:S(2)}, u32[]{:S(2)}) collective-permute-start(f32[16,4096]{1,0:T(8,128)S(1)} %get-tuple-element.22), channel_id=1, source_target_pairs={{0,224},{2,34},{4,228},{6,38},{8,232},{10,42},{12,236},{14,46},{16... | collective-permute-start | bytes 786440 | tf_op jit(solution)/shard_map/ppermute | solution.py:88
  86.0 3.4 %collective-permute-done.25 = f32[32,4096]{1,0:T(8,128)S(1)} collective-permute-done((f32[32,4096]{1,0:T(8,128)S(1)}, f32[32,4096]{1,0:T(8,128)S(1)}, u32[]{:S(2)}, u32[]{:S(2)}) %collective-permute-start.25) | collective-permute-done | bytes 524320 | tf_op jit(solution)/shard_map/ppermute | solution.py:80
  90.1 2.7 %collective-permute-start.27 = (f32[32,4096]{1,0:T(8,128)S(1)}, f32[32,4096]{1,0:T(8,128)S(1)}, u32[]{:S(2)}, u32[]{:S(2)}) collective-permute-start(f32[32,4096]{1,0:T(8,128)S(1)} %get-tuple-element.24), channel_id=1, source_target_pairs={{0,12},{2,6},{4,0},{6,10},{8,4},{10,14},{12,8},{14,2},{16,28},{18,... | collective-permute-start | bytes 1572872 | tf_op jit(solution)/shard_map/ppermute | solution.py:88
  93.0 3.2 %collective-permute-start.18 = (f32[16,4096]{1,0:T(8,128)S(1)}, f32[16,4096]{1,0:T(8,128)S(1)}, u32[]{:S(2)}, u32[]{:S(2)}) collective-permute-start(f32[16,4096]{1,0:T(8,128)S(1)} %get-tuple-element.20), channel_id=1, source_target_pairs={{0,224},{2,34},{4,228},{6,38},{8,232},{10,42},{12,236},{14,46},{16... | collective-permute-start | bytes 786440 | tf_op jit(solution)/shard_map/ppermute | solution.py:88
  96.2 9.3 %collective-permute-done.26 = f32[32,4096]{1,0:T(8,128)S(1)} collective-permute-done((f32[32,4096]{1,0:T(8,128)S(1)}, f32[32,4096]{1,0:T(8,128)S(1)}, u32[]{:S(2)}, u32[]{:S(2)}) %collective-permute-start.26) | collective-permute-done | bytes 524320 | tf_op jit(solution)/shard_map/ppermute | solution.py:80
  106.0 3.3 %collective-permute-start.19 = (f32[16,4096]{1,0:T(8,128)S(1)}, f32[16,4096]{1,0:T(8,128)S(1)}, u32[]{:S(2)}, u32[]{:S(2)}) collective-permute-start(f32[16,4096]{1,0:T(8,128)S(1)} %get-tuple-element.18), channel_id=1, source_target_pairs={{0,224},{2,34},{4,228},{6,38},{8,232},{10,42},{12,236},{14,46},{16... | collective-permute-start | bytes 786440 | tf_op jit(solution)/shard_map/ppermute | solution.py:88
  109.3 2.6 %collective-permute-done.28 = f32[4,4096]{1,0:T(4,128)S(1)} collective-permute-done((f32[4,4096]{1,0:T(4,128)S(1)}, f32[4,4096]{1,0:T(4,128)S(1)}, u32[]{:S(2)}, u32[]{:S(2)}) %collective-permute-start.28) | collective-permute-done | bytes 65568 | tf_op jit(solution)/shard_map/ppermute | solution.py:80
  112.0 3.2 %collective-permute-start.32 = (f32[4,4096]{1,0:T(4,128)S(1)}, f32[4,4096]{1,0:T(4,128)S(1)}, u32[]{:S(2)}, u32[]{:S(2)}) collective-permute-start(f32[4,4096]{1,0:T(4,128)S(1)} %get-tuple-element.30), channel_id=1, source_target_pairs={{0,224},{2,34},{4,228},{6,38},{8,232},{10,42},{12,236},{14,46},{16... | collective-permute-start | bytes 196616 | tf_op jit(solution)/shard_map/ppermute | solution.py:88
  117.9 3.2 %collective-permute-start.33 = (f32[4,4096]{1,0:T(4,128)S(1)}, f32[4,4096]{1,0:T(4,128)S(1)}, u32[]{:S(2)}, u32[]{:S(2)}) collective-permute-start(f32[4,4096]{1,0:T(4,128)S(1)} %get-tuple-element.28), channel_id=1, source_target_pairs={{0,224},{2,34},{4,228},{6,38},{8,232},{10,42},{12,236},{14,46},{16... | collective-permute-start | bytes 196616 | tf_op jit(solution)/shard_map/ppermute | solution.py:88
  124.6 3.2 %collective-permute-start.34 = (f32[4,4096]{1,0:T(4,128)S(1)}, f32[4,4096]{1,0:T(4,128)S(1)}, u32[]{:S(2)}, u32[]{:S(2)}) collective-permute-start(f32[4,4096]{1,0:T(4,128)S(1)} %get-tuple-element.26), channel_id=1, source_target_pairs={{0,224},{2,34},{4,228},{6,38},{8,232},{10,42},{12,236},{14,46},{16... | collective-permute-start | bytes 196616 | tf_op jit(solution)/shard_map/ppermute | solution.py:88
  (122 shorter events, 40.0 us)
Async XLA Ops:
  1.8 8.4 %collective-permute-start = (bf16[2,8192]{1,0:T(2,128)(2,1)S(1)}, bf16[2,8192]{1,0:T(2,128)(2,1)S(1)}, u32[]{:S(2)}, u32[]{:S(2)}) collective-permute-start(bf16[2,8192]{1,0:T(2,128)(2,1)S(1)} %fusion.12), channel_id=1, source_target_pairs={{0,16},{2,18},{4,20},{6,22},{8,24},{10,26},{12,28},{14,30},{16,0},... | collective-permute-start | bytes 98312 | tf_op jit(solution)/shard_map/ppermute | solution.py:43
  10.3 8.9 %collective-permute-start.1 = (bf16[4,8192]{1,0:T(4,128)(2,1)S(1)}, bf16[4,8192]{1,0:T(4,128)(2,1)S(1)}, u32[]{:S(2)}, u32[]{:S(2)}) collective-permute-start(bf16[4,8192]{1,0:T(4,128)(2,1)S(1)} %pad_maximum_fusion.3), channel_id=1, source_target_pairs={{0,12},{2,6},{4,0},{6,10},{8,4},{10,14},{12,8},{14,2},{16,28},{18,... | collective-permute-start | bytes 196616 | tf_op jit(solution)/shard_map/ppermute | solution.py:54
  20.0 11.1 %collective-permute-start.4 = (bf16[16,8192]{1,0:T(8,128)(2,1)S(1)}, bf16[16,8192]{1,0:T(8,128)(2,1)S(1)}, u32[]{:S(2)}, u32[]{:S(2)}) collective-permute-start(bf16[16,8192]{1,0:T(8,128)(2,1)S(1)} %pad_maximum_fusion), channel_id=1, source_target_pairs={{0,224},{2,34},{4,228},{6,38},{8,232},{10,42},{12,236},{14,46},{16... | collective-permute-start | bytes 786440 | tf_op jit(solution)/shard_map/ppermute | solution.py:47
  25.9 8.8 %collective-permute-start.7 = (bf16[16,8192]{1,0:T(8,128)(2,1)S(1)}, bf16[16,8192]{1,0:T(8,128)(2,1)S(1)}, u32[]{:S(2)}, u32[]{:S(2)}) collective-permute-start(bf16[16,8192]{1,0:T(8,128)(2,1)S(1)} %pad_maximum_fusion), channel_id=1, source_target_pairs={{0,32},{2,226},{4,36},{6,230},{8,40},{10,234},{12,44},{14,238},{16... | collective-permute-start | bytes 786440 | tf_op jit(solution)/shard_map/ppermute | solution.py:43
  31.1 7.9 %collective-permute-start.5 = (bf16[16,8192]{1,0:T(8,128)(2,1)S(1)}, bf16[16,8192]{1,0:T(8,128)(2,1)S(1)}, u32[]{:S(2)}, u32[]{:S(2)}) collective-permute-start(bf16[16,8192]{1,0:T(8,128)(2,1)S(1)} %collective-permute-done.4), channel_id=1, source_target_pairs={{0,224},{2,34},{4,228},{6,38},{8,232},{10,42},{12,236},{14,46},{16... | collective-permute-start | bytes 786440 | tf_op jit(solution)/shard_map/ppermute | solution.py:47
  34.7 10.0 %collective-permute-start.8 = (bf16[16,8192]{1,0:T(8,128)(2,1)S(1)}, bf16[16,8192]{1,0:T(8,128)(2,1)S(1)}, u32[]{:S(2)}, u32[]{:S(2)}) collective-permute-start(bf16[16,8192]{1,0:T(8,128)(2,1)S(1)} %collective-permute-done.7), channel_id=1, source_target_pairs={{0,32},{2,226},{4,36},{6,230},{8,40},{10,234},{12,44},{14,238},{16... | collective-permute-start | bytes 786440 | tf_op jit(solution)/shard_map/ppermute | solution.py:43
  38.9 13.4 %collective-permute-start.6 = (bf16[16,8192]{1,0:T(8,128)(2,1)S(1)}, bf16[16,8192]{1,0:T(8,128)(2,1)S(1)}, u32[]{:S(2)}, u32[]{:S(2)}) collective-permute-start(bf16[16,8192]{1,0:T(8,128)(2,1)S(1)} %collective-permute-done.5), channel_id=1, source_target_pairs={{0,224},{2,34},{4,228},{6,38},{8,232},{10,42},{12,236},{14,46},{16... | collective-permute-start | bytes 786440 | tf_op jit(solution)/shard_map/ppermute | solution.py:47
  44.8 7.6 %collective-permute-start.9 = (bf16[16,8192]{1,0:T(8,128)(2,1)S(1)}, bf16[16,8192]{1,0:T(8,128)(2,1)S(1)}, u32[]{:S(2)}, u32[]{:S(2)}) collective-permute-start(bf16[16,8192]{1,0:T(8,128)(2,1)S(1)} %collective-permute-done.8), channel_id=1, source_target_pairs={{0,32},{2,226},{4,36},{6,230},{8,40},{10,234},{12,44},{14,238},{16... | collective-permute-start | bytes 786440 | tf_op jit(solution)/shard_map/ppermute | solution.py:43
  52.4 7.6 %collective-permute-start.10 = (bf16[16,8192]{1,0:T(8,128)(2,1)S(1)}, bf16[16,8192]{1,0:T(8,128)(2,1)S(1)}, u32[]{:S(2)}, u32[]{:S(2)}) collective-permute-start(bf16[16,8192]{1,0:T(8,128)(2,1)S(1)} %collective-permute-done.9), channel_id=1, source_target_pairs={{0,32},{2,226},{4,36},{6,230},{8,40},{10,234},{12,44},{14,238},{16... | collective-permute-start | bytes 786440 | tf_op jit(solution)/shard_map/ppermute | solution.py:43
  75.0 7.7 %collective-permute-start.13 = (f32[16,4096]{1,0:T(8,128)S(1)}, f32[16,4096]{1,0:T(8,128)S(1)}, u32[]{:S(2)}, u32[]{:S(2)}) collective-permute-start(f32[16,4096]{1,0:T(8,128)S(1)} %slice.149), channel_id=1, source_target_pairs={{0,32},{2,226},{4,36},{6,230},{8,40},{10,234},{12,44},{14,238},{16... | collective-permute-start | bytes 786440 | tf_op jit(solution)/shard_map/ppermute | solution.py:80
  78.9 10.5 %collective-permute-start.25 = (f32[32,4096]{1,0:T(8,128)S(1)}, f32[32,4096]{1,0:T(8,128)S(1)}, u32[]{:S(2)}, u32[]{:S(2)}) collective-permute-start(f32[32,4096]{1,0:T(8,128)S(1)} %slice.165), channel_id=1, source_target_pairs={{0,4},{2,14},{4,8},{6,2},{8,12},{10,6},{12,0},{14,10},{16,20},{18,... | collective-permute-start | bytes 1572872 | tf_op jit(solution)/shard_map/ppermute | solution.py:80
  82.7 10.1 %collective-permute-start.14 = (f32[16,4096]{1,0:T(8,128)S(1)}, f32[16,4096]{1,0:T(8,128)S(1)}, u32[]{:S(2)}, u32[]{:S(2)}) collective-permute-start(f32[16,4096]{1,0:T(8,128)S(1)} %get-tuple-element.21), channel_id=1, source_target_pairs={{0,32},{2,226},{4,36},{6,230},{8,40},{10,234},{12,44},{14,238},{16... | collective-permute-start | bytes 786440 | tf_op jit(solution)/shard_map/ppermute | solution.py:80
  82.8 10.0 %collective-permute-start.17 = (f32[16,4096]{1,0:T(8,128)S(1)}, f32[16,4096]{1,0:T(8,128)S(1)}, u32[]{:S(2)}, u32[]{:S(2)}) collective-permute-start(f32[16,4096]{1,0:T(8,128)S(1)} %get-tuple-element.22), channel_id=1, source_target_pairs={{0,224},{2,34},{4,228},{6,38},{8,232},{10,42},{12,236},{14,46},{16... | collective-permute-start | bytes 786440 | tf_op jit(solution)/shard_map/ppermute | solution.py:88
  89.5 16.1 %collective-permute-start.26 = (f32[32,4096]{1,0:T(8,128)S(1)}, f32[32,4096]{1,0:T(8,128)S(1)}, u32[]{:S(2)}, u32[]{:S(2)}) collective-permute-start(f32[32,4096]{1,0:T(8,128)S(1)} %get-tuple-element.23), channel_id=1, source_target_pairs={{0,4},{2,14},{4,8},{6,2},{8,12},{10,6},{12,0},{14,10},{16,20},{18,... | collective-permute-start | bytes 1572872 | tf_op jit(solution)/shard_map/ppermute | solution.py:80
  90.1 15.4 %collective-permute-start.27 = (f32[32,4096]{1,0:T(8,128)S(1)}, f32[32,4096]{1,0:T(8,128)S(1)}, u32[]{:S(2)}, u32[]{:S(2)}) collective-permute-start(f32[32,4096]{1,0:T(8,128)S(1)} %get-tuple-element.24), channel_id=1, source_target_pairs={{0,12},{2,6},{4,0},{6,10},{8,4},{10,14},{12,8},{14,2},{16,28},{18,... | collective-permute-start | bytes 1572872 | tf_op jit(solution)/shard_map/ppermute | solution.py:88
  92.9 12.9 %collective-permute-start.15 = (f32[16,4096]{1,0:T(8,128)S(1)}, f32[16,4096]{1,0:T(8,128)S(1)}, u32[]{:S(2)}, u32[]{:S(2)}) collective-permute-start(f32[16,4096]{1,0:T(8,128)S(1)} %get-tuple-element.19), channel_id=1, source_target_pairs={{0,32},{2,226},{4,36},{6,230},{8,40},{10,234},{12,44},{14,238},{16... | collective-permute-start | bytes 786440 | tf_op jit(solution)/shard_map/ppermute | solution.py:80
  93.0 12.8 %collective-permute-start.18 = (f32[16,4096]{1,0:T(8,128)S(1)}, f32[16,4096]{1,0:T(8,128)S(1)}, u32[]{:S(2)}, u32[]{:S(2)}) collective-permute-start(f32[16,4096]{1,0:T(8,128)S(1)} %get-tuple-element.20), channel_id=1, source_target_pairs={{0,224},{2,34},{4,228},{6,38},{8,232},{10,42},{12,236},{14,46},{16... | collective-permute-start | bytes 786440 | tf_op jit(solution)/shard_map/ppermute | solution.py:88
  105.7 6.2 %collective-permute-start.28 = (f32[4,4096]{1,0:T(4,128)S(1)}, f32[4,4096]{1,0:T(4,128)S(1)}, u32[]{:S(2)}, u32[]{:S(2)}) collective-permute-start(f32[4,4096]{1,0:T(4,128)S(1)} %slice.169), channel_id=1, source_target_pairs={{0,32},{2,226},{4,36},{6,230},{8,40},{10,234},{12,44},{14,238},{16... | collective-permute-start | bytes 196616 | tf_op jit(solution)/shard_map/ppermute | solution.py:80
  105.9 11.1 %collective-permute-start.16 = (f32[16,4096]{1,0:T(8,128)S(1)}, f32[16,4096]{1,0:T(8,128)S(1)}, u32[]{:S(2)}, u32[]{:S(2)}) collective-permute-start(f32[16,4096]{1,0:T(8,128)S(1)} %get-tuple-element.17), channel_id=1, source_target_pairs={{0,32},{2,226},{4,36},{6,230},{8,40},{10,234},{12,44},{14,238},{16... | collective-permute-start | bytes 786440 | tf_op jit(solution)/shard_map/ppermute | solution.py:80
  106.0 11.0 %collective-permute-start.19 = (f32[16,4096]{1,0:T(8,128)S(1)}, f32[16,4096]{1,0:T(8,128)S(1)}, u32[]{:S(2)}, u32[]{:S(2)}) collective-permute-start(f32[16,4096]{1,0:T(8,128)S(1)} %get-tuple-element.18), channel_id=1, source_target_pairs={{0,224},{2,34},{4,228},{6,38},{8,232},{10,42},{12,236},{14,46},{16... | collective-permute-start | bytes 786440 | tf_op jit(solution)/shard_map/ppermute | solution.py:88
  117.8 6.7 %collective-permute-start.30 = (f32[4,4096]{1,0:T(4,128)S(1)}, f32[4,4096]{1,0:T(4,128)S(1)}, u32[]{:S(2)}, u32[]{:S(2)}) collective-permute-start(f32[4,4096]{1,0:T(4,128)S(1)} %get-tuple-element.27), channel_id=1, source_target_pairs={{0,32},{2,226},{4,36},{6,230},{8,40},{10,234},{12,44},{14,238},{16... | collective-permute-start | bytes 196616 | tf_op jit(solution)/shard_map/ppermute | solution.py:80
  117.9 6.6 %collective-permute-start.33 = (f32[4,4096]{1,0:T(4,128)S(1)}, f32[4,4096]{1,0:T(4,128)S(1)}, u32[]{:S(2)}, u32[]{:S(2)}) collective-permute-start(f32[4,4096]{1,0:T(4,128)S(1)} %get-tuple-element.28), channel_id=1, source_target_pairs={{0,224},{2,34},{4,228},{6,38},{8,232},{10,42},{12,236},{14,46},{16... | collective-permute-start | bytes 196616 | tf_op jit(solution)/shard_map/ppermute | solution.py:88
  121.1 6.7 %collective-permute-start.20 = (f32[4,4096]{1,0:T(4,128)S(1)}, f32[4,4096]{1,0:T(4,128)S(1)}, u32[]{:S(2)}, u32[]{:S(2)}) collective-permute-start(f32[4,4096]{1,0:T(4,128)S(1)} %get-tuple-element.31), channel_id=1, source_target_pairs={{0,4},{2,14},{4,8},{6,2},{8,12},{10,6},{12,0},{14,10},{16,20},{18,... | collective-permute-start | bytes 196616 | tf_op jit(solution)/shard_map/ppermute | solution.py:64
  121.2 6.6 %collective-permute-start.21 = (f32[4,4096]{1,0:T(4,128)S(1)}, f32[4,4096]{1,0:T(4,128)S(1)}, u32[]{:S(2)}, u32[]{:S(2)}) collective-permute-start(f32[4,4096]{1,0:T(4,128)S(1)} %get-tuple-element.33), channel_id=1, source_target_pairs={{0,8},{2,10},{4,12},{6,14},{8,0},{10,2},{12,4},{14,6},{16,24},{18,... | collective-permute-start | bytes 196616 | tf_op jit(solution)/shard_map/ppermute | solution.py:64
  (17 other events, 168.6 us)

commit v9 on v7

--- a/solution.py
+++ b/solution.py
@@ -7,8 +7,8 @@
 AG_ORDER = ("xh", "y", "z", "c")
 AG_DIRECT = ("y",)
 PARTS = (
-    (32, ("c", "z", "y", "xh"), ("y",)),
-    (32, ("c", "y", "z", "xh"), ("z",)),
+    (34, ("c", "z", "y", "xh"), ("y",)),
+    (30, ("c", "y", "z", "xh"), ()),
 )
 
 

time: 139 us -> 147 us (1.058)
  waiting for transfers between devices: 54.3 us -> 67 us
  starting transfers between devices: 57.3 us -> 52.8 us
  local copies, waits for them, and re-layouts: 6.23 us -> 2.49 us
  matrix products: 6.06 us -> 8.34 us
  other arithmetic: 12.9 us -> 15.1 us
    ppermute x10 -> x3, starting transfers between devices: 17.7 us -> 3.31 us  [_rs_direct(): total = total + lax.ppermute(part, 'blk', _perm(axis, o, size))]
    ppermute x10 -> x14, waiting for transfers between devices: 22.1 us -> 34.8 us  [_rs_stage(): recv = lax.ppermute(buf, 'blk', _perm(axis, 1, size))]
    ppermute x4 -> x7, starting transfers between devices: 12 us -> 22 us  [_rs_stage(): recv = lax.ppermute(buf, 'blk', _perm(axis, -1, size))]
    mul x3, other arithmetic: 7.42 us -> 9.61 us  [mask_blocks(): return (shaped * cols[:, None, :]).reshape(height, width)]
    unnamed x23 -> x21, local copies, waits for them, and re-layouts: 3.25 us -> 1.1 us
    dot_general x2, matrix products: 1.6 us -> 3.7 us  [local(): jnp.dot(b, up_kept, preferred_element_type=jnp.float32)]
    slice x6 -> x7, local copies, waits for them, and re-layouts: 1.9 us -> 0.38 us  [take(): return lax.slice_in_dim(x, j % n * r, (j % n + 1) * r, axis=0)]
    ppermute x10 -> x14, starting transfers between devices: 7.09 us -> 7.02 us  [_rs_stage(): recv = lax.ppermute(buf, 'blk', _perm(axis, 1, size))]
  transfers between devices with their start and end apart: 36 -> 36, of which waited for: 17 -> 17; matrix products, arithmetic and copies ran while one was open for 11% -> 10% of each run, Pallas kernels for 0% -> 0%
where the time goes in v9:
time: 147 us; the launch traced here: 146 us
  waiting for transfers between devices  67 us (46%)
  starting transfers between devices  52.8 us (36%)
  other arithmetic  15.1 us (10%)
  matrix products  8.34 us (6%)
  local copies, waits for them, and re-layouts  2.49 us (2%)
    ppermute x14, waiting for transfers between devices, _rs_stage(): recv = lax.ppermute(buf, 'blk', _perm(axis, 1, size))  34.8 us
    ppermute x7, starting transfers between devices, _rs_stage(): recv = lax.ppermute(buf, 'blk', _perm(axis, -1, size))  22 us
    ppermute x5, waiting for transfers between devices, _ag_stage(): cur = lax.ppermute(cur, 'blk', _perm(axis, 1, size))  16.7 us
    ppermute x3, starting transfers between devices, _ag_stage(): cur = lax.ppermute(cur, 'blk', _perm(axis, -1, size))  13.3 us
    ppermute x3, waiting for transfers between devices, _ag_stage(): cur = lax.ppermute(cur, 'blk', _perm(axis, -1, size))  10.7 us
    mul x3, other arithmetic, mask_blocks(): return (shaped * cols[:, None, :]).reshape(height, width)  9.61 us
    ppermute x14, starting transfers between devices, _rs_stage(): recv = lax.ppermute(buf, 'blk', _perm(axis, 1, size))  7.02 us
    ppermute x3, starting transfers between devices, _ag_direct(): lax.ppermute(block, 'blk', _perm(axis, -o, size))  4.69 us
  transfers between devices with their start and end apart: 36, of which 17 were waited for; matrix products, arithmetic and copies ran while one was open for 10% of the time, Pallas kernels for 0%

profile of v9, /device:TPU:2, one launch (start us, length us, event | category | flops | bytes accessed | tf_op | source)
XLA Modules:
  0.0 146.3 jit_solution(436407521446815137)
XLA Ops:
  5.7 4.5 %bitcast_multiply_fusion.2 = bf16[8192,256]{1,0:T(8,128)(2,1)} fusion(bf16[8192,256]{1,0:T(8,128)(2,1)} %param.10, bf16[64,256]{1,0:T(8,128)(2,1)S(1)} %bitcast.32), kind=kLoop, calls=%fused_computation.2 | loop fusion | flops 2097152 | bytes 8421376 | tf_op jit(solution)/shard_map/mul | solution.py:21
  10.3 3.1 %collective-permute-start.1 = (bf16[4,8192]{1,0:T(4,128)(2,1)S(1)}, bf16[4,8192]{1,0:T(4,128)(2,1)S(1)}, u32[]{:S(2)}, u32[]{:S(2)}) collective-permute-start(bf16[4,8192]{1,0:T(4,128)(2,1)S(1)} %pad_maximum_fusion.3), channel_id=1, source_target_pairs={{0,12},{2,6},{4,0},{6,10},{8,4},{10,14},{12,8},{14,2},{16,28},{18,... | collective-permute-start | bytes 196616 | tf_op jit(solution)/shard_map/ppermute | solution.py:54
  15.4 2.6 %bitcast_multiply_fusion.1 = bf16[8192,256]{1,0:T(8,128)(2,1)S(1)} fusion(bf16[8192,256]{1,0:T(8,128)(2,1)} %param.11, bf16[64,256]{1,0:T(8,128)(2,1)S(1)} %bitcast.30), kind=kLoop, calls=%fused_computation.1 | loop fusion | flops 2097152 | bytes 8421376 | tf_op jit(solution)/shard_map/mul | solution.py:21
  18.8 2.5 %bitcast_multiply_fusion = bf16[256,8192]{1,0:T(8,128)(2,1)} fusion(bf16[256,8192]{1,0:T(8,128)(2,1)S(1)} %copy-done.3, bf16[2,8192]{1,0:T(2,128)(2,1)S(1)} %bitcast.31), kind=kLoop, calls=%fused_computation | loop fusion | flops 2097152 | bytes 8421376 | tf_op jit(solution)/shard_map/mul | solution.py:21
  21.5 5.9 %collective-permute-start.4 = (bf16[16,8192]{1,0:T(8,128)(2,1)S(1)}, bf16[16,8192]{1,0:T(8,128)(2,1)S(1)}, u32[]{:S(2)}, u32[]{:S(2)}) collective-permute-start(bf16[16,8192]{1,0:T(8,128)(2,1)S(1)} %pad_maximum_fusion), channel_id=1, source_target_pairs={{0,224},{2,34},{4,228},{6,38},{8,232},{10,42},{12,236},{14,46},{16... | collective-permute-start | bytes 786440 | tf_op jit(solution)/shard_map/ppermute | solution.py:47
  27.5 5.7 %collective-permute-done.4 = bf16[16,8192]{1,0:T(8,128)(2,1)S(1)} collective-permute-done((bf16[16,8192]{1,0:T(8,128)(2,1)S(1)}, bf16[16,8192]{1,0:T(8,128)(2,1)S(1)}, u32[]{:S(2)}, u32[]{:S(2)}) %collective-permute-start.4) | collective-permute-done | bytes 262176 | tf_op jit(solution)/shard_map/ppermute | solution.py:47
  33.2 3.7 %collective-permute-start.5 = (bf16[16,8192]{1,0:T(8,128)(2,1)S(1)}, bf16[16,8192]{1,0:T(8,128)(2,1)S(1)}, u32[]{:S(2)}, u32[]{:S(2)}) collective-permute-start(bf16[16,8192]{1,0:T(8,128)(2,1)S(1)} %collective-permute-done.4), channel_id=1, source_target_pairs={{0,224},{2,34},{4,228},{6,38},{8,232},{10,42},{12,236},{14,46},{16... | collective-permute-start | bytes 786440 | tf_op jit(solution)/shard_map/ppermute | solution.py:47
  36.9 4.9 %collective-permute-done.5 = bf16[16,8192]{1,0:T(8,128)(2,1)S(1)} collective-permute-done((bf16[16,8192]{1,0:T(8,128)(2,1)S(1)}, bf16[16,8192]{1,0:T(8,128)(2,1)S(1)}, u32[]{:S(2)}, u32[]{:S(2)}) %collective-permute-start.5) | collective-permute-done | bytes 262176 | tf_op jit(solution)/shard_map/ppermute | solution.py:47
  41.8 3.7 %collective-permute-start.6 = (bf16[16,8192]{1,0:T(8,128)(2,1)S(1)}, bf16[16,8192]{1,0:T(8,128)(2,1)S(1)}, u32[]{:S(2)}, u32[]{:S(2)}) collective-permute-start(bf16[16,8192]{1,0:T(8,128)(2,1)S(1)} %collective-permute-done.5), channel_id=1, source_target_pairs={{0,224},{2,34},{4,228},{6,38},{8,232},{10,42},{12,236},{14,46},{16... | collective-permute-start | bytes 786440 | tf_op jit(solution)/shard_map/ppermute | solution.py:47
  47.1 7.6 %collective-permute-done.9 = bf16[16,8192]{1,0:T(8,128)(2,1)S(1)} collective-permute-done((bf16[16,8192]{1,0:T(8,128)(2,1)S(1)}, bf16[16,8192]{1,0:T(8,128)(2,1)S(1)}, u32[]{:S(2)}, u32[]{:S(2)}) %collective-permute-start.9) | collective-permute-done | bytes 262176 | tf_op jit(solution)/shard_map/ppermute | solution.py:43
  54.7 7.6 %collective-permute-done.10 = bf16[16,8192]{1,0:T(8,128)(2,1)S(1)} collective-permute-done((bf16[16,8192]{1,0:T(8,128)(2,1)S(1)}, bf16[16,8192]{1,0:T(8,128)(2,1)S(1)}, u32[]{:S(2)}, u32[]{:S(2)}) %collective-permute-start.10) | collective-permute-done | bytes 262176 | tf_op jit(solution)/shard_map/ppermute | solution.py:43
  64.2 2.6 %collective-permute-done.11 = bf16[128,8192]{1,0:T(8,128)(2,1)S(1)} collective-permute-done((bf16[128,8192]{1,0:T(8,128)(2,1)S(1)}, bf16[128,8192]{1,0:T(8,128)(2,1)S(1)}, u32[]{:S(2)}, u32[]{:S(2)}) %collective-permute-start.11) | collective-permute-done | bytes 2097184 | tf_op jit(solution)/shard_map/ppermute | solution.py:128
  67.7 2.9 %fusion.22 = f32[128,256]{1,0:T(8,128)S(1)} fusion(bf16[128,8192]{1,0:T(8,128)(2,1)S(1)} %collective-permute-done.11, bf16[8192,256]{1,0:T(8,128)(2,1)} %copy-done.1), kind=kOutput, calls=%fused_computation.66 | convolution fusion | flops 536870912 | bytes 6422528 | tf_op jit(solution)/shard_map/dot_general | solution.py:132
  79.9 8.4 %collective-permute-done.25 = f32[32,3840]{1,0:T(8,128)S(1)} collective-permute-done((f32[32,3840]{1,0:T(8,128)S(1)}, f32[32,3840]{1,0:T(8,128)S(1)}, u32[]{:S(2)}, u32[]{:S(2)}) %collective-permute-start.25) | collective-permute-done | bytes 491552 | tf_op jit(solution)/shard_map/ppermute | solution.py:80
  88.9 2.8 %collective-permute-start.27 = (f32[32,3840]{1,0:T(8,128)S(1)}, f32[32,3840]{1,0:T(8,128)S(1)}, u32[]{:S(2)}, u32[]{:S(2)}) collective-permute-start(f32[32,3840]{1,0:T(8,128)S(1)} %get-tuple-element.24), channel_id=1, source_target_pairs={{0,12},{2,6},{4,0},{6,10},{8,4},{10,14},{12,8},{14,2},{16,28},{18,... | collective-permute-start | bytes 1474568 | tf_op jit(solution)/shard_map/ppermute | solution.py:88
  92.0 11.7 %collective-permute-done.26 = f32[32,3840]{1,0:T(8,128)S(1)} collective-permute-done((f32[32,3840]{1,0:T(8,128)S(1)}, f32[32,3840]{1,0:T(8,128)S(1)}, u32[]{:S(2)}, u32[]{:S(2)}) %collective-permute-start.26) | collective-permute-done | bytes 491552 | tf_op jit(solution)/shard_map/ppermute | solution.py:80
  104.1 3.5 %collective-permute-start.17 = (f32[16,4352]{1,0:T(8,128)S(1)}, f32[16,4352]{1,0:T(8,128)S(1)}, u32[]{:S(2)}, u32[]{:S(2)}) collective-permute-start(f32[16,4352]{1,0:T(8,128)S(1)} %get-tuple-element.22), channel_id=1, source_target_pairs={{0,224},{2,34},{4,228},{6,38},{8,232},{10,42},{12,236},{14,46},{16... | collective-permute-start | bytes 835592 | tf_op jit(solution)/shard_map/ppermute | solution.py:88
  110.0 3.2 %collective-permute-start.32 = (f32[4,3840]{1,0:T(4,128)S(1)}, f32[4,3840]{1,0:T(4,128)S(1)}, u32[]{:S(2)}, u32[]{:S(2)}) collective-permute-start(f32[4,3840]{1,0:T(4,128)S(1)} %get-tuple-element.30), channel_id=1, source_target_pairs={{0,224},{2,34},{4,228},{6,38},{8,232},{10,42},{12,236},{14,46},{16... | collective-permute-start | bytes 184328 | tf_op jit(solution)/shard_map/ppermute | solution.py:88
  115.7 3.2 %collective-permute-start.18 = (f32[16,4352]{1,0:T(8,128)S(1)}, f32[16,4352]{1,0:T(8,128)S(1)}, u32[]{:S(2)}, u32[]{:S(2)}) collective-permute-start(f32[16,4352]{1,0:T(8,128)S(1)} %get-tuple-element.20), channel_id=1, source_target_pairs={{0,224},{2,34},{4,228},{6,38},{8,232},{10,42},{12,236},{14,46},{16... | collective-permute-start | bytes 835592 | tf_op jit(solution)/shard_map/ppermute | solution.py:88
  119.1 3.2 %collective-permute-start.33 = (f32[4,3840]{1,0:T(4,128)S(1)}, f32[4,3840]{1,0:T(4,128)S(1)}, u32[]{:S(2)}, u32[]{:S(2)}) collective-permute-start(f32[4,3840]{1,0:T(4,128)S(1)} %get-tuple-element.28), channel_id=1, source_target_pairs={{0,224},{2,34},{4,228},{6,38},{8,232},{10,42},{12,236},{14,46},{16... | collective-permute-start | bytes 184328 | tf_op jit(solution)/shard_map/ppermute | solution.py:88
  122.3 2.4 %collective-permute-done.15 = f32[16,4352]{1,0:T(8,128)S(1)} collective-permute-done((f32[16,4352]{1,0:T(8,128)S(1)}, f32[16,4352]{1,0:T(8,128)S(1)}, u32[]{:S(2)}, u32[]{:S(2)}) %collective-permute-start.15) | collective-permute-done | bytes 278560 | tf_op jit(solution)/shard_map/ppermute | solution.py:80
  125.4 2.8 %collective-permute-start.19 = (f32[16,4352]{1,0:T(8,128)S(1)}, f32[16,4352]{1,0:T(8,128)S(1)}, u32[]{:S(2)}, u32[]{:S(2)}) collective-permute-start(f32[16,4352]{1,0:T(8,128)S(1)} %get-tuple-element.18), channel_id=1, source_target_pairs={{0,224},{2,34},{4,228},{6,38},{8,232},{10,42},{12,236},{14,46},{16... | collective-permute-start | bytes 835592 | tf_op jit(solution)/shard_map/ppermute | solution.py:88
  128.3 3.2 %collective-permute-start.34 = (f32[4,3840]{1,0:T(4,128)S(1)}, f32[4,3840]{1,0:T(4,128)S(1)}, u32[]{:S(2)}, u32[]{:S(2)}) collective-permute-start(f32[4,3840]{1,0:T(4,128)S(1)} %get-tuple-element.26), channel_id=1, source_target_pairs={{0,224},{2,34},{4,228},{6,38},{8,232},{10,42},{12,236},{14,46},{16... | collective-permute-start | bytes 184328 | tf_op jit(solution)/shard_map/ppermute | solution.py:88
  141.7 3.9 %collective-permute-done.23 = f32[2,4352]{1,0:T(2,128)S(1)} collective-permute-done((f32[2,4352]{1,0:T(2,128)S(1)}, f32[2,4352]{1,0:T(2,128)S(1)}, u32[]{:S(2)}, u32[]{:S(2)}) %collective-permute-start.23) | collective-permute-done | bytes 34848 | tf_op jit(solution)/shard_map/ppermute | solution.py:80
  (122 shorter events, 40.1 us)
Async XLA Ops:
  1.8 8.4 %collective-permute-start = (bf16[2,8192]{1,0:T(2,128)(2,1)S(1)}, bf16[2,8192]{1,0:T(2,128)(2,1)S(1)}, u32[]{:S(2)}, u32[]{:S(2)}) collective-permute-start(bf16[2,8192]{1,0:T(2,128)(2,1)S(1)} %fusion.13), channel_id=1, source_target_pairs={{0,16},{2,18},{4,20},{6,22},{8,24},{10,26},{12,28},{14,30},{16,0},... | collective-permute-start | bytes 98312 | tf_op jit(solution)/shard_map/ppermute | solution.py:43
  10.3 11.1 %collective-permute-start.1 = (bf16[4,8192]{1,0:T(4,128)(2,1)S(1)}, bf16[4,8192]{1,0:T(4,128)(2,1)S(1)}, u32[]{:S(2)}, u32[]{:S(2)}) collective-permute-start(bf16[4,8192]{1,0:T(4,128)(2,1)S(1)} %pad_maximum_fusion.3), channel_id=1, source_target_pairs={{0,12},{2,6},{4,0},{6,10},{8,4},{10,14},{12,8},{14,2},{16,28},{18,... | collective-permute-start | bytes 196616 | tf_op jit(solution)/shard_map/ppermute | solution.py:54
  13.4 8.0 %collective-permute-start.2 = (bf16[4,8192]{1,0:T(4,128)(2,1)S(1)}, bf16[4,8192]{1,0:T(4,128)(2,1)S(1)}, u32[]{:S(2)}, u32[]{:S(2)}) collective-permute-start(bf16[4,8192]{1,0:T(4,128)(2,1)S(1)} %pad_maximum_fusion.3), channel_id=1, source_target_pairs={{0,8},{2,10},{4,12},{6,14},{8,0},{10,2},{12,4},{14,6},{16,24},{18,... | collective-permute-start | bytes 196616 | tf_op jit(solution)/shard_map/ppermute | solution.py:54
  21.5 11.7 %collective-permute-start.4 = (bf16[16,8192]{1,0:T(8,128)(2,1)S(1)}, bf16[16,8192]{1,0:T(8,128)(2,1)S(1)}, u32[]{:S(2)}, u32[]{:S(2)}) collective-permute-start(bf16[16,8192]{1,0:T(8,128)(2,1)S(1)} %pad_maximum_fusion), channel_id=1, source_target_pairs={{0,224},{2,34},{4,228},{6,38},{8,232},{10,42},{12,236},{14,46},{16... | collective-permute-start | bytes 786440 | tf_op jit(solution)/shard_map/ppermute | solution.py:47
  27.4 9.5 %collective-permute-start.7 = (bf16[16,8192]{1,0:T(8,128)(2,1)S(1)}, bf16[16,8192]{1,0:T(8,128)(2,1)S(1)}, u32[]{:S(2)}, u32[]{:S(2)}) collective-permute-start(bf16[16,8192]{1,0:T(8,128)(2,1)S(1)} %pad_maximum_fusion), channel_id=1, source_target_pairs={{0,32},{2,226},{4,36},{6,230},{8,40},{10,234},{12,44},{14,238},{16... | collective-permute-start | bytes 786440 | tf_op jit(solution)/shard_map/ppermute | solution.py:43
  33.2 8.6 %collective-permute-start.5 = (bf16[16,8192]{1,0:T(8,128)(2,1)S(1)}, bf16[16,8192]{1,0:T(8,128)(2,1)S(1)}, u32[]{:S(2)}, u32[]{:S(2)}) collective-permute-start(bf16[16,8192]{1,0:T(8,128)(2,1)S(1)} %collective-permute-done.4), channel_id=1, source_target_pairs={{0,224},{2,34},{4,228},{6,38},{8,232},{10,42},{12,236},{14,46},{16... | collective-permute-start | bytes 786440 | tf_op jit(solution)/shard_map/ppermute | solution.py:47
  36.9 10.2 %collective-permute-start.8 = (bf16[16,8192]{1,0:T(8,128)(2,1)S(1)}, bf16[16,8192]{1,0:T(8,128)(2,1)S(1)}, u32[]{:S(2)}, u32[]{:S(2)}) collective-permute-start(bf16[16,8192]{1,0:T(8,128)(2,1)S(1)} %collective-permute-done.7), channel_id=1, source_target_pairs={{0,32},{2,226},{4,36},{6,230},{8,40},{10,234},{12,44},{14,238},{16... | collective-permute-start | bytes 786440 | tf_op jit(solution)/shard_map/ppermute | solution.py:43
  41.8 12.8 %collective-permute-start.6 = (bf16[16,8192]{1,0:T(8,128)(2,1)S(1)}, bf16[16,8192]{1,0:T(8,128)(2,1)S(1)}, u32[]{:S(2)}, u32[]{:S(2)}) collective-permute-start(bf16[16,8192]{1,0:T(8,128)(2,1)S(1)} %collective-permute-done.5), channel_id=1, source_target_pairs={{0,224},{2,34},{4,228},{6,38},{8,232},{10,42},{12,236},{14,46},{16... | collective-permute-start | bytes 786440 | tf_op jit(solution)/shard_map/ppermute | solution.py:47
  75.0 16.6 %collective-permute-start.12 = (f32[128,4352]{1,0:T(8,128)S(1)}, f32[128,4352]{1,0:T(8,128)S(1)}, u32[]{:S(2)}, u32[]{:S(2)}) collective-permute-start(f32[128,4352]{1,0:T(8,128)S(1)} %slice.137), channel_id=1, source_target_pairs={{0,2},{2,0},{4,6},{6,4},{8,10},{10,8},{12,14},{14,12},{16,18},{18,... | collective-permute-start | bytes 6684680 | tf_op jit(solution)/shard_map/ppermute | solution.py:80
  78.1 10.1 %collective-permute-start.25 = (f32[32,3840]{1,0:T(8,128)S(1)}, f32[32,3840]{1,0:T(8,128)S(1)}, u32[]{:S(2)}, u32[]{:S(2)}) collective-permute-start(f32[32,3840]{1,0:T(8,128)S(1)} %slice.155), channel_id=1, source_target_pairs={{0,4},{2,14},{4,8},{6,2},{8,12},{10,6},{12,0},{14,10},{16,20},{18,... | collective-permute-start | bytes 1474568 | tf_op jit(solution)/shard_map/ppermute | solution.py:80
  88.3 15.4 %collective-permute-start.26 = (f32[32,3840]{1,0:T(8,128)S(1)}, f32[32,3840]{1,0:T(8,128)S(1)}, u32[]{:S(2)}, u32[]{:S(2)}) collective-permute-start(f32[32,3840]{1,0:T(8,128)S(1)} %get-tuple-element.23), channel_id=1, source_target_pairs={{0,4},{2,14},{4,8},{6,2},{8,12},{10,6},{12,0},{14,10},{16,20},{18,... | collective-permute-start | bytes 1474568 | tf_op jit(solution)/shard_map/ppermute | solution.py:80
  88.9 14.8 %collective-permute-start.27 = (f32[32,3840]{1,0:T(8,128)S(1)}, f32[32,3840]{1,0:T(8,128)S(1)}, u32[]{:S(2)}, u32[]{:S(2)}) collective-permute-start(f32[32,3840]{1,0:T(8,128)S(1)} %get-tuple-element.24), channel_id=1, source_target_pairs={{0,12},{2,6},{4,0},{6,10},{8,4},{10,14},{12,8},{14,2},{16,28},{18,... | collective-permute-start | bytes 1474568 | tf_op jit(solution)/shard_map/ppermute | solution.py:88
  91.9 12.0 %collective-permute-start.13 = (f32[16,4352]{1,0:T(8,128)S(1)}, f32[16,4352]{1,0:T(8,128)S(1)}, u32[]{:S(2)}, u32[]{:S(2)}) collective-permute-start(f32[16,4352]{1,0:T(8,128)S(1)} %slice.139), channel_id=1, source_target_pairs={{0,32},{2,226},{4,36},{6,230},{8,40},{10,234},{12,44},{14,238},{16... | collective-permute-start | bytes 835592 | tf_op jit(solution)/shard_map/ppermute | solution.py:80
  104.0 11.6 %collective-permute-start.14 = (f32[16,4352]{1,0:T(8,128)S(1)}, f32[16,4352]{1,0:T(8,128)S(1)}, u32[]{:S(2)}, u32[]{:S(2)}) collective-permute-start(f32[16,4352]{1,0:T(8,128)S(1)} %get-tuple-element.21), channel_id=1, source_target_pairs={{0,32},{2,226},{4,36},{6,230},{8,40},{10,234},{12,44},{14,238},{16... | collective-permute-start | bytes 835592 | tf_op jit(solution)/shard_map/ppermute | solution.py:80
  104.1 11.5 %collective-permute-start.17 = (f32[16,4352]{1,0:T(8,128)S(1)}, f32[16,4352]{1,0:T(8,128)S(1)}, u32[]{:S(2)}, u32[]{:S(2)}) collective-permute-start(f32[16,4352]{1,0:T(8,128)S(1)} %get-tuple-element.22), channel_id=1, source_target_pairs={{0,224},{2,34},{4,228},{6,38},{8,232},{10,42},{12,236},{14,46},{16... | collective-permute-start | bytes 835592 | tf_op jit(solution)/shard_map/ppermute | solution.py:88
  109.9 9.0 %collective-permute-start.29 = (f32[4,3840]{1,0:T(4,128)S(1)}, f32[4,3840]{1,0:T(4,128)S(1)}, u32[]{:S(2)}, u32[]{:S(2)}) collective-permute-start(f32[4,3840]{1,0:T(4,128)S(1)} %get-tuple-element.29), channel_id=1, source_target_pairs={{0,32},{2,226},{4,36},{6,230},{8,40},{10,234},{12,44},{14,238},{16... | collective-permute-start | bytes 184328 | tf_op jit(solution)/shard_map/ppermute | solution.py:80
  110.0 9.0 %collective-permute-start.32 = (f32[4,3840]{1,0:T(4,128)S(1)}, f32[4,3840]{1,0:T(4,128)S(1)}, u32[]{:S(2)}, u32[]{:S(2)}) collective-permute-start(f32[4,3840]{1,0:T(4,128)S(1)} %get-tuple-element.30), channel_id=1, source_target_pairs={{0,224},{2,34},{4,228},{6,38},{8,232},{10,42},{12,236},{14,46},{16... | collective-permute-start | bytes 184328 | tf_op jit(solution)/shard_map/ppermute | solution.py:88
  115.7 9.1 %collective-permute-start.15 = (f32[16,4352]{1,0:T(8,128)S(1)}, f32[16,4352]{1,0:T(8,128)S(1)}, u32[]{:S(2)}, u32[]{:S(2)}) collective-permute-start(f32[16,4352]{1,0:T(8,128)S(1)} %get-tuple-element.19), channel_id=1, source_target_pairs={{0,32},{2,226},{4,36},{6,230},{8,40},{10,234},{12,44},{14,238},{16... | collective-permute-start | bytes 835592 | tf_op jit(solution)/shard_map/ppermute | solution.py:80
  115.7 9.0 %collective-permute-start.18 = (f32[16,4352]{1,0:T(8,128)S(1)}, f32[16,4352]{1,0:T(8,128)S(1)}, u32[]{:S(2)}, u32[]{:S(2)}) collective-permute-start(f32[16,4352]{1,0:T(8,128)S(1)} %get-tuple-element.20), channel_id=1, source_target_pairs={{0,224},{2,34},{4,228},{6,38},{8,232},{10,42},{12,236},{14,46},{16... | collective-permute-start | bytes 835592 | tf_op jit(solution)/shard_map/ppermute | solution.py:88
  119.0 9.1 %collective-permute-start.30 = (f32[4,3840]{1,0:T(4,128)S(1)}, f32[4,3840]{1,0:T(4,128)S(1)}, u32[]{:S(2)}, u32[]{:S(2)}) collective-permute-start(f32[4,3840]{1,0:T(4,128)S(1)} %get-tuple-element.27), channel_id=1, source_target_pairs={{0,32},{2,226},{4,36},{6,230},{8,40},{10,234},{12,44},{14,238},{16... | collective-permute-start | bytes 184328 | tf_op jit(solution)/shard_map/ppermute | solution.py:80
  119.1 9.1 %collective-permute-start.33 = (f32[4,3840]{1,0:T(4,128)S(1)}, f32[4,3840]{1,0:T(4,128)S(1)}, u32[]{:S(2)}, u32[]{:S(2)}) collective-permute-start(f32[4,3840]{1,0:T(4,128)S(1)} %get-tuple-element.28), channel_id=1, source_target_pairs={{0,224},{2,34},{4,228},{6,38},{8,232},{10,42},{12,236},{14,46},{16... | collective-permute-start | bytes 184328 | tf_op jit(solution)/shard_map/ppermute | solution.py:88
  124.8 7.8 %collective-permute-start.16 = (f32[16,4352]{1,0:T(8,128)S(1)}, f32[16,4352]{1,0:T(8,128)S(1)}, u32[]{:S(2)}, u32[]{:S(2)}) collective-permute-start(f32[16,4352]{1,0:T(8,128)S(1)} %get-tuple-element.17), channel_id=1, source_target_pairs={{0,32},{2,226},{4,36},{6,230},{8,40},{10,234},{12,44},{14,238},{16... | collective-permute-start | bytes 835592 | tf_op jit(solution)/shard_map/ppermute | solution.py:80
  128.2 7.9 %collective-permute-start.31 = (f32[4,3840]{1,0:T(4,128)S(1)}, f32[4,3840]{1,0:T(4,128)S(1)}, u32[]{:S(2)}, u32[]{:S(2)}) collective-permute-start(f32[4,3840]{1,0:T(4,128)S(1)} %get-tuple-element.25), channel_id=1, source_target_pairs={{0,32},{2,226},{4,36},{6,230},{8,40},{10,234},{12,44},{14,238},{16... | collective-permute-start | bytes 184328 | tf_op jit(solution)/shard_map/ppermute | solution.py:80
  128.3 7.8 %collective-permute-start.34 = (f32[4,3840]{1,0:T(4,128)S(1)}, f32[4,3840]{1,0:T(4,128)S(1)}, u32[]{:S(2)}, u32[]{:S(2)}) collective-permute-start(f32[4,3840]{1,0:T(4,128)S(1)} %get-tuple-element.26), channel_id=1, source_target_pairs={{0,224},{2,34},{4,228},{6,38},{8,232},{10,42},{12,236},{14,46},{16... | collective-permute-start | bytes 184328 | tf_op jit(solution)/shard_map/ppermute | solution.py:88
  (17 other events, 175.8 us)

commit v10 on v7

--- a/solution.py
+++ b/solution.py
@@ -8,7 +8,7 @@
 AG_DIRECT = ("y",)
 PARTS = (
     (32, ("c", "z", "y", "xh"), ("y",)),
-    (32, ("c", "y", "z", "xh"), ("z",)),
+    (32, ("c", "y", "z", "xh"), ("y",)),
 )
 
 

time: 139 us -> 148 us (1.065)
  waiting for transfers between devices: 54.3 us -> 66.4 us
  starting transfers between devices: 57.3 us -> 52.6 us
  other arithmetic: 12.9 us -> 15.1 us
  matrix products: 6.06 us -> 8.21 us
  local copies, waits for them, and re-layouts: 6.23 us -> 4.4 us
    ppermute x10 -> x6, waiting for transfers between devices: 2.28 us -> 24.2 us  [_rs_direct(): total = total + lax.ppermute(part, 'blk', _perm(axis, o, size))]
    ppermute x10 -> x12, waiting for transfers between devices: 22.1 us -> 12.2 us  [_rs_stage(): recv = lax.ppermute(buf, 'blk', _perm(axis, 1, size))]
    ppermute x10 -> x6, starting transfers between devices: 17.7 us -> 8.29 us  [_rs_direct(): total = total + lax.ppermute(part, 'blk', _perm(axis, o, size))]
    ppermute x4 -> x6, starting transfers between devices: 12 us -> 19.1 us  [_rs_stage(): recv = lax.ppermute(buf, 'blk', _perm(axis, -1, size))]
    ppermute x10 -> x12, starting transfers between devices: 7.09 us -> 4.76 us  [_rs_stage(): recv = lax.ppermute(buf, 'blk', _perm(axis, 1, size))]
    mul x3, other arithmetic: 7.42 us -> 9.61 us  [mask_blocks(): return (shaped * cols[:, None, :]).reshape(height, width)]
    dot_general x2, matrix products: 1.6 us -> 3.7 us  [local(): jnp.dot(b, up_kept, preferred_element_type=jnp.float32)]
    unnamed x23 -> x21, local copies, waits for them, and re-layouts: 3.25 us -> 2.84 us
  transfers between devices with their start and end apart: 36 -> 36, of which waited for: 17 -> 18; matrix products, arithmetic and copies ran while one was open for 11% -> 10% of each run, Pallas kernels for 0% -> 0%
where the time goes in v10:
time: 148 us; the launch traced here: 147 us
  waiting for transfers between devices  66.4 us (45%)
  starting transfers between devices  52.6 us (36%)
  other arithmetic  15.1 us (10%)
  matrix products  8.21 us (6%)
  local copies, waits for them, and re-layouts  4.4 us (3%)
    ppermute x6, waiting for transfers between devices, _rs_direct(): total = total + lax.ppermute(part, 'blk', _perm(axis, o, size))  24.2 us
    ppermute x6, starting transfers between devices, _rs_stage(): recv = lax.ppermute(buf, 'blk', _perm(axis, -1, size))  19.1 us
    ppermute x5, waiting for transfers between devices, _ag_stage(): cur = lax.ppermute(cur, 'blk', _perm(axis, 1, size))  16.7 us
    ppermute x3, starting transfers between devices, _ag_stage(): cur = lax.ppermute(cur, 'blk', _perm(axis, -1, size))  13.3 us
    ppermute x12, waiting for transfers between devices, _rs_stage(): recv = lax.ppermute(buf, 'blk', _perm(axis, 1, size))  12.2 us
    ppermute x3, waiting for transfers between devices, _ag_stage(): cur = lax.ppermute(cur, 'blk', _perm(axis, -1, size))  10.7 us
    mul x3, other arithmetic, mask_blocks(): return (shaped * cols[:, None, :]).reshape(height, width)  9.61 us
    ppermute x6, starting transfers between devices, _rs_direct(): total = total + lax.ppermute(part, 'blk', _perm(axis, o, size))  8.29 us
  transfers between devices with their start and end apart: 36, of which 18 were waited for; matrix products, arithmetic and copies ran while one was open for 10% of the time, Pallas kernels for 0%

profile of v10, /device:TPU:2, one launch (start us, length us, event | category | flops | bytes accessed | tf_op | source)
XLA Modules:
  0.0 147.3 jit_solution(10427676358029080153)
XLA Ops:
  5.7 4.5 %bitcast_multiply_fusion.2 = bf16[8192,256]{1,0:T(8,128)(2,1)} fusion(bf16[8192,256]{1,0:T(8,128)(2,1)} %param.10, bf16[64,256]{1,0:T(8,128)(2,1)S(1)} %bitcast.32), kind=kLoop, calls=%fused_computation.2 | loop fusion | flops 2097152 | bytes 8421376 | tf_op jit(solution)/shard_map/mul | solution.py:21
  10.3 3.1 %collective-permute-start.1 = (bf16[4,8192]{1,0:T(4,128)(2,1)S(1)}, bf16[4,8192]{1,0:T(4,128)(2,1)S(1)}, u32[]{:S(2)}, u32[]{:S(2)}) collective-permute-start(bf16[4,8192]{1,0:T(4,128)(2,1)S(1)} %pad_maximum_fusion.3), channel_id=1, source_target_pairs={{0,12},{2,6},{4,0},{6,10},{8,4},{10,14},{12,8},{14,2},{16,28},{18,... | collective-permute-start | bytes 196616 | tf_op jit(solution)/shard_map/ppermute | solution.py:54
  15.4 2.6 %bitcast_multiply_fusion.1 = bf16[8192,256]{1,0:T(8,128)(2,1)S(1)} fusion(bf16[8192,256]{1,0:T(8,128)(2,1)} %param.11, bf16[64,256]{1,0:T(8,128)(2,1)S(1)} %bitcast.30), kind=kLoop, calls=%fused_computation.1 | loop fusion | flops 2097152 | bytes 8421376 | tf_op jit(solution)/shard_map/mul | solution.py:21
  18.8 2.5 %bitcast_multiply_fusion = bf16[256,8192]{1,0:T(8,128)(2,1)} fusion(bf16[256,8192]{1,0:T(8,128)(2,1)S(1)} %copy-done.3, bf16[2,8192]{1,0:T(2,128)(2,1)S(1)} %bitcast.31), kind=kLoop, calls=%fused_computation | loop fusion | flops 2097152 | bytes 8421376 | tf_op jit(solution)/shard_map/mul | solution.py:21
  21.5 5.9 %collective-permute-start.4 = (bf16[16,8192]{1,0:T(8,128)(2,1)S(1)}, bf16[16,8192]{1,0:T(8,128)(2,1)S(1)}, u32[]{:S(2)}, u32[]{:S(2)}) collective-permute-start(bf16[16,8192]{1,0:T(8,128)(2,1)S(1)} %pad_maximum_fusion), channel_id=1, source_target_pairs={{0,224},{2,34},{4,228},{6,38},{8,232},{10,42},{12,236},{14,46},{16... | collective-permute-start | bytes 786440 | tf_op jit(solution)/shard_map/ppermute | solution.py:47
  27.5 5.7 %collective-permute-done.4 = bf16[16,8192]{1,0:T(8,128)(2,1)S(1)} collective-permute-done((bf16[16,8192]{1,0:T(8,128)(2,1)S(1)}, bf16[16,8192]{1,0:T(8,128)(2,1)S(1)}, u32[]{:S(2)}, u32[]{:S(2)}) %collective-permute-start.4) | collective-permute-done | bytes 262176 | tf_op jit(solution)/shard_map/ppermute | solution.py:47
  33.2 3.7 %collective-permute-start.5 = (bf16[16,8192]{1,0:T(8,128)(2,1)S(1)}, bf16[16,8192]{1,0:T(8,128)(2,1)S(1)}, u32[]{:S(2)}, u32[]{:S(2)}) collective-permute-start(bf16[16,8192]{1,0:T(8,128)(2,1)S(1)} %collective-permute-done.4), channel_id=1, source_target_pairs={{0,224},{2,34},{4,228},{6,38},{8,232},{10,42},{12,236},{14,46},{16... | collective-permute-start | bytes 786440 | tf_op jit(solution)/shard_map/ppermute | solution.py:47
  36.9 4.9 %collective-permute-done.5 = bf16[16,8192]{1,0:T(8,128)(2,1)S(1)} collective-permute-done((bf16[16,8192]{1,0:T(8,128)(2,1)S(1)}, bf16[16,8192]{1,0:T(8,128)(2,1)S(1)}, u32[]{:S(2)}, u32[]{:S(2)}) %collective-permute-start.5) | collective-permute-done | bytes 262176 | tf_op jit(solution)/shard_map/ppermute | solution.py:47
  41.8 3.7 %collective-permute-start.6 = (bf16[16,8192]{1,0:T(8,128)(2,1)S(1)}, bf16[16,8192]{1,0:T(8,128)(2,1)S(1)}, u32[]{:S(2)}, u32[]{:S(2)}) collective-permute-start(bf16[16,8192]{1,0:T(8,128)(2,1)S(1)} %collective-permute-done.5), channel_id=1, source_target_pairs={{0,224},{2,34},{4,228},{6,38},{8,232},{10,42},{12,236},{14,46},{16... | collective-permute-start | bytes 786440 | tf_op jit(solution)/shard_map/ppermute | solution.py:47
  47.1 7.6 %collective-permute-done.9 = bf16[16,8192]{1,0:T(8,128)(2,1)S(1)} collective-permute-done((bf16[16,8192]{1,0:T(8,128)(2,1)S(1)}, bf16[16,8192]{1,0:T(8,128)(2,1)S(1)}, u32[]{:S(2)}, u32[]{:S(2)}) %collective-permute-start.9) | collective-permute-done | bytes 262176 | tf_op jit(solution)/shard_map/ppermute | solution.py:43
  54.7 7.6 %collective-permute-done.10 = bf16[16,8192]{1,0:T(8,128)(2,1)S(1)} collective-permute-done((bf16[16,8192]{1,0:T(8,128)(2,1)S(1)}, bf16[16,8192]{1,0:T(8,128)(2,1)S(1)}, u32[]{:S(2)}, u32[]{:S(2)}) %collective-permute-start.10) | collective-permute-done | bytes 262176 | tf_op jit(solution)/shard_map/ppermute | solution.py:43
  64.2 2.6 %collective-permute-done.11 = bf16[128,8192]{1,0:T(8,128)(2,1)S(1)} collective-permute-done((bf16[128,8192]{1,0:T(8,128)(2,1)S(1)}, bf16[128,8192]{1,0:T(8,128)(2,1)S(1)}, u32[]{:S(2)}, u32[]{:S(2)}) %collective-permute-start.11) | collective-permute-done | bytes 2097184 | tf_op jit(solution)/shard_map/ppermute | solution.py:128
  67.7 2.9 %fusion.24 = f32[128,256]{1,0:T(8,128)S(1)} fusion(bf16[128,8192]{1,0:T(8,128)(2,1)S(1)} %collective-permute-done.11, bf16[8192,256]{1,0:T(8,128)(2,1)} %copy-done.1), kind=kOutput, calls=%fused_computation.67 | convolution fusion | flops 536870912 | bytes 6422528 | tf_op jit(solution)/shard_map/dot_general | solution.py:132
  83.5 18.9 %collective-permute-done.25 = f32[32,4096]{1,0:T(8,128)S(1)} collective-permute-done((f32[32,4096]{1,0:T(8,128)S(1)}, f32[32,4096]{1,0:T(8,128)S(1)}, u32[]{:S(2)}, u32[]{:S(2)}) %collective-permute-start.25) | collective-permute-done | bytes 524320 | tf_op jit(solution)/shard_map/ppermute | solution.py:64
  102.3 3.0 %collective-permute-done.26 = f32[32,4096]{1,0:T(8,128)S(1)} collective-permute-done((f32[32,4096]{1,0:T(8,128)S(1)}, f32[32,4096]{1,0:T(8,128)S(1)}, u32[]{:S(2)}, u32[]{:S(2)}) %collective-permute-start.26) | collective-permute-done | bytes 524320 | tf_op jit(solution)/shard_map/ppermute | solution.py:64
  105.7 3.3 %collective-permute-start.17 = (f32[16,4096]{1,0:T(8,128)S(1)}, f32[16,4096]{1,0:T(8,128)S(1)}, u32[]{:S(2)}, u32[]{:S(2)}) collective-permute-start(f32[16,4096]{1,0:T(8,128)S(1)} %get-tuple-element.22), channel_id=1, source_target_pairs={{0,224},{2,34},{4,228},{6,38},{8,232},{10,42},{12,236},{14,46},{16... | collective-permute-start | bytes 786440 | tf_op jit(solution)/shard_map/ppermute | solution.py:88
  109.0 2.6 %collective-permute-done.28 = f32[4,4096]{1,0:T(4,128)S(1)} collective-permute-done((f32[4,4096]{1,0:T(4,128)S(1)}, f32[4,4096]{1,0:T(4,128)S(1)}, u32[]{:S(2)}, u32[]{:S(2)}) %collective-permute-start.28) | collective-permute-done | bytes 65568 | tf_op jit(solution)/shard_map/ppermute | solution.py:80
  112.0 3.2 %collective-permute-start.32 = (f32[4,4096]{1,0:T(4,128)S(1)}, f32[4,4096]{1,0:T(4,128)S(1)}, u32[]{:S(2)}, u32[]{:S(2)}) collective-permute-start(f32[4,4096]{1,0:T(4,128)S(1)} %get-tuple-element.31), channel_id=1, source_target_pairs={{0,224},{2,34},{4,228},{6,38},{8,232},{10,42},{12,236},{14,46},{16... | collective-permute-start | bytes 196616 | tf_op jit(solution)/shard_map/ppermute | solution.py:88
  117.1 3.2 %collective-permute-start.18 = (f32[16,4096]{1,0:T(8,128)S(1)}, f32[16,4096]{1,0:T(8,128)S(1)}, u32[]{:S(2)}, u32[]{:S(2)}) collective-permute-start(f32[16,4096]{1,0:T(8,128)S(1)} %get-tuple-element.20), channel_id=1, source_target_pairs={{0,224},{2,34},{4,228},{6,38},{8,232},{10,42},{12,236},{14,46},{16... | collective-permute-start | bytes 786440 | tf_op jit(solution)/shard_map/ppermute | solution.py:88
  120.4 3.2 %collective-permute-start.33 = (f32[4,4096]{1,0:T(4,128)S(1)}, f32[4,4096]{1,0:T(4,128)S(1)}, u32[]{:S(2)}, u32[]{:S(2)}) collective-permute-start(f32[4,4096]{1,0:T(4,128)S(1)} %get-tuple-element.29), channel_id=1, source_target_pairs={{0,224},{2,34},{4,228},{6,38},{8,232},{10,42},{12,236},{14,46},{16... | collective-permute-start | bytes 196616 | tf_op jit(solution)/shard_map/ppermute | solution.py:88
  126.2 2.9 %collective-permute-start.19 = (f32[16,4096]{1,0:T(8,128)S(1)}, f32[16,4096]{1,0:T(8,128)S(1)}, u32[]{:S(2)}, u32[]{:S(2)}) collective-permute-start(f32[16,4096]{1,0:T(8,128)S(1)} %get-tuple-element.18), channel_id=1, source_target_pairs={{0,224},{2,34},{4,228},{6,38},{8,232},{10,42},{12,236},{14,46},{16... | collective-permute-start | bytes 786440 | tf_op jit(solution)/shard_map/ppermute | solution.py:88
  129.3 3.2 %collective-permute-start.34 = (f32[4,4096]{1,0:T(4,128)S(1)}, f32[4,4096]{1,0:T(4,128)S(1)}, u32[]{:S(2)}, u32[]{:S(2)}) collective-permute-start(f32[4,4096]{1,0:T(4,128)S(1)} %get-tuple-element.27), channel_id=1, source_target_pairs={{0,224},{2,34},{4,228},{6,38},{8,232},{10,42},{12,236},{14,46},{16... | collective-permute-start | bytes 196616 | tf_op jit(solution)/shard_map/ppermute | solution.py:88
  134.4 2.4 %collective-permute-start.21 = (f32[4,4096]{1,0:T(4,128)S(1)}, f32[4,4096]{1,0:T(4,128)S(1)}, u32[]{:S(2)}, u32[]{:S(2)}) collective-permute-start(f32[4,4096]{1,0:T(4,128)S(1)} %get-tuple-element.34), channel_id=1, source_target_pairs={{0,8},{2,10},{4,12},{6,14},{8,0},{10,2},{12,4},{14,6},{16,24},{18,... | collective-permute-start | bytes 196616 | tf_op jit(solution)/shard_map/ppermute | solution.py:64
  142.7 3.9 %collective-permute-done.23 = f32[2,4096]{1,0:T(2,128)S(1)} collective-permute-done((f32[2,4096]{1,0:T(2,128)S(1)}, f32[2,4096]{1,0:T(2,128)S(1)}, u32[]{:S(2)}, u32[]{:S(2)}) %collective-permute-start.23) | collective-permute-done | bytes 32800 | tf_op jit(solution)/shard_map/ppermute | solution.py:80
  (121 shorter events, 39.7 us)
Async XLA Ops:
  1.8 8.4 %collective-permute-start = (bf16[2,8192]{1,0:T(2,128)(2,1)S(1)}, bf16[2,8192]{1,0:T(2,128)(2,1)S(1)}, u32[]{:S(2)}, u32[]{:S(2)}) collective-permute-start(bf16[2,8192]{1,0:T(2,128)(2,1)S(1)} %fusion.12), channel_id=1, source_target_pairs={{0,16},{2,18},{4,20},{6,22},{8,24},{10,26},{12,28},{14,30},{16,0},... | collective-permute-start | bytes 98312 | tf_op jit(solution)/shard_map/ppermute | solution.py:43
  10.3 11.1 %collective-permute-start.1 = (bf16[4,8192]{1,0:T(4,128)(2,1)S(1)}, bf16[4,8192]{1,0:T(4,128)(2,1)S(1)}, u32[]{:S(2)}, u32[]{:S(2)}) collective-permute-start(bf16[4,8192]{1,0:T(4,128)(2,1)S(1)} %pad_maximum_fusion.3), channel_id=1, source_target_pairs={{0,12},{2,6},{4,0},{6,10},{8,4},{10,14},{12,8},{14,2},{16,28},{18,... | collective-permute-start | bytes 196616 | tf_op jit(solution)/shard_map/ppermute | solution.py:54
  13.4 8.0 %collective-permute-start.2 = (bf16[4,8192]{1,0:T(4,128)(2,1)S(1)}, bf16[4,8192]{1,0:T(4,128)(2,1)S(1)}, u32[]{:S(2)}, u32[]{:S(2)}) collective-permute-start(bf16[4,8192]{1,0:T(4,128)(2,1)S(1)} %pad_maximum_fusion.3), channel_id=1, source_target_pairs={{0,8},{2,10},{4,12},{6,14},{8,0},{10,2},{12,4},{14,6},{16,24},{18,... | collective-permute-start | bytes 196616 | tf_op jit(solution)/shard_map/ppermute | solution.py:54
  21.5 11.7 %collective-permute-start.4 = (bf16[16,8192]{1,0:T(8,128)(2,1)S(1)}, bf16[16,8192]{1,0:T(8,128)(2,1)S(1)}, u32[]{:S(2)}, u32[]{:S(2)}) collective-permute-start(bf16[16,8192]{1,0:T(8,128)(2,1)S(1)} %pad_maximum_fusion), channel_id=1, source_target_pairs={{0,224},{2,34},{4,228},{6,38},{8,232},{10,42},{12,236},{14,46},{16... | collective-permute-start | bytes 786440 | tf_op jit(solution)/shard_map/ppermute | solution.py:47
  27.4 9.5 %collective-permute-start.7 = (bf16[16,8192]{1,0:T(8,128)(2,1)S(1)}, bf16[16,8192]{1,0:T(8,128)(2,1)S(1)}, u32[]{:S(2)}, u32[]{:S(2)}) collective-permute-start(bf16[16,8192]{1,0:T(8,128)(2,1)S(1)} %pad_maximum_fusion), channel_id=1, source_target_pairs={{0,32},{2,226},{4,36},{6,230},{8,40},{10,234},{12,44},{14,238},{16... | collective-permute-start | bytes 786440 | tf_op jit(solution)/shard_map/ppermute | solution.py:43
  33.2 8.6 %collective-permute-start.5 = (bf16[16,8192]{1,0:T(8,128)(2,1)S(1)}, bf16[16,8192]{1,0:T(8,128)(2,1)S(1)}, u32[]{:S(2)}, u32[]{:S(2)}) collective-permute-start(bf16[16,8192]{1,0:T(8,128)(2,1)S(1)} %collective-permute-done.4), channel_id=1, source_target_pairs={{0,224},{2,34},{4,228},{6,38},{8,232},{10,42},{12,236},{14,46},{16... | collective-permute-start | bytes 786440 | tf_op jit(solution)/shard_map/ppermute | solution.py:47
  36.9 10.2 %collective-permute-start.8 = (bf16[16,8192]{1,0:T(8,128)(2,1)S(1)}, bf16[16,8192]{1,0:T(8,128)(2,1)S(1)}, u32[]{:S(2)}, u32[]{:S(2)}) collective-permute-start(bf16[16,8192]{1,0:T(8,128)(2,1)S(1)} %collective-permute-done.7), channel_id=1, source_target_pairs={{0,32},{2,226},{4,36},{6,230},{8,40},{10,234},{12,44},{14,238},{16... | collective-permute-start | bytes 786440 | tf_op jit(solution)/shard_map/ppermute | solution.py:43
  41.8 12.8 %collective-permute-start.6 = (bf16[16,8192]{1,0:T(8,128)(2,1)S(1)}, bf16[16,8192]{1,0:T(8,128)(2,1)S(1)}, u32[]{:S(2)}, u32[]{:S(2)}) collective-permute-start(bf16[16,8192]{1,0:T(8,128)(2,1)S(1)} %collective-permute-done.5), channel_id=1, source_target_pairs={{0,224},{2,34},{4,228},{6,38},{8,232},{10,42},{12,236},{14,46},{16... | collective-permute-start | bytes 786440 | tf_op jit(solution)/shard_map/ppermute | solution.py:47
  54.7 7.6 %collective-permute-start.10 = (bf16[16,8192]{1,0:T(8,128)(2,1)S(1)}, bf16[16,8192]{1,0:T(8,128)(2,1)S(1)}, u32[]{:S(2)}, u32[]{:S(2)}) collective-permute-start(bf16[16,8192]{1,0:T(8,128)(2,1)S(1)} %collective-permute-done.9), channel_id=1, source_target_pairs={{0,32},{2,226},{4,36},{6,230},{8,40},{10,234},{12,44},{14,238},{16... | collective-permute-start | bytes 786440 | tf_op jit(solution)/shard_map/ppermute | solution.py:43
  78.5 23.9 %collective-permute-start.25 = (f32[32,4096]{1,0:T(8,128)S(1)}, f32[32,4096]{1,0:T(8,128)S(1)}, u32[]{:S(2)}, u32[]{:S(2)}) collective-permute-start(f32[32,4096]{1,0:T(8,128)S(1)} %get-tuple-element.23), channel_id=1, source_target_pairs={{0,4},{2,14},{4,8},{6,2},{8,12},{10,6},{12,0},{14,10},{16,20},{18,... | collective-permute-start | bytes 1572872 | tf_op jit(solution)/shard_map/ppermute | solution.py:64
  80.2 25.1 %collective-permute-start.26 = (f32[32,4096]{1,0:T(8,128)S(1)}, f32[32,4096]{1,0:T(8,128)S(1)}, u32[]{:S(2)}, u32[]{:S(2)}) collective-permute-start(f32[32,4096]{1,0:T(8,128)S(1)} %get-tuple-element.25), channel_id=1, source_target_pairs={{0,8},{2,10},{4,12},{6,14},{8,0},{10,2},{12,4},{14,6},{16,24},{18,... | collective-permute-start | bytes 1572872 | tf_op jit(solution)/shard_map/ppermute | solution.py:64
  82.3 23.1 %collective-permute-start.27 = (f32[32,4096]{1,0:T(8,128)S(1)}, f32[32,4096]{1,0:T(8,128)S(1)}, u32[]{:S(2)}, u32[]{:S(2)}) collective-permute-start(f32[32,4096]{1,0:T(8,128)S(1)} %get-tuple-element.24), channel_id=1, source_target_pairs={{0,12},{2,6},{4,0},{6,10},{8,4},{10,14},{12,8},{14,2},{16,28},{18,... | collective-permute-start | bytes 1572872 | tf_op jit(solution)/shard_map/ppermute | solution.py:64
  83.4 22.2 %collective-permute-start.13 = (f32[16,4096]{1,0:T(8,128)S(1)}, f32[16,4096]{1,0:T(8,128)S(1)}, u32[]{:S(2)}, u32[]{:S(2)}) collective-permute-start(f32[16,4096]{1,0:T(8,128)S(1)} %slice.139), channel_id=1, source_target_pairs={{0,32},{2,226},{4,36},{6,230},{8,40},{10,234},{12,44},{14,238},{16... | collective-permute-start | bytes 786440 | tf_op jit(solution)/shard_map/ppermute | solution.py:80
  105.6 11.3 %collective-permute-start.14 = (f32[16,4096]{1,0:T(8,128)S(1)}, f32[16,4096]{1,0:T(8,128)S(1)}, u32[]{:S(2)}, u32[]{:S(2)}) collective-permute-start(f32[16,4096]{1,0:T(8,128)S(1)} %get-tuple-element.21), channel_id=1, source_target_pairs={{0,32},{2,226},{4,36},{6,230},{8,40},{10,234},{12,44},{14,238},{16... | collective-permute-start | bytes 786440 | tf_op jit(solution)/shard_map/ppermute | solution.py:80
  105.7 11.2 %collective-permute-start.17 = (f32[16,4096]{1,0:T(8,128)S(1)}, f32[16,4096]{1,0:T(8,128)S(1)}, u32[]{:S(2)}, u32[]{:S(2)}) collective-permute-start(f32[16,4096]{1,0:T(8,128)S(1)} %get-tuple-element.22), channel_id=1, source_target_pairs={{0,224},{2,34},{4,228},{6,38},{8,232},{10,42},{12,236},{14,46},{16... | collective-permute-start | bytes 786440 | tf_op jit(solution)/shard_map/ppermute | solution.py:88
  111.7 8.6 %collective-permute-start.29 = (f32[4,4096]{1,0:T(4,128)S(1)}, f32[4,4096]{1,0:T(4,128)S(1)}, u32[]{:S(2)}, u32[]{:S(2)}) collective-permute-start(f32[4,4096]{1,0:T(4,128)S(1)} %get-tuple-element.30), channel_id=1, source_target_pairs={{0,32},{2,226},{4,36},{6,230},{8,40},{10,234},{12,44},{14,238},{16... | collective-permute-start | bytes 196616 | tf_op jit(solution)/shard_map/ppermute | solution.py:80
  112.0 8.3 %collective-permute-start.32 = (f32[4,4096]{1,0:T(4,128)S(1)}, f32[4,4096]{1,0:T(4,128)S(1)}, u32[]{:S(2)}, u32[]{:S(2)}) collective-permute-start(f32[4,4096]{1,0:T(4,128)S(1)} %get-tuple-element.31), channel_id=1, source_target_pairs={{0,224},{2,34},{4,228},{6,38},{8,232},{10,42},{12,236},{14,46},{16... | collective-permute-start | bytes 196616 | tf_op jit(solution)/shard_map/ppermute | solution.py:88
  117.0 8.6 %collective-permute-start.15 = (f32[16,4096]{1,0:T(8,128)S(1)}, f32[16,4096]{1,0:T(8,128)S(1)}, u32[]{:S(2)}, u32[]{:S(2)}) collective-permute-start(f32[16,4096]{1,0:T(8,128)S(1)} %get-tuple-element.19), channel_id=1, source_target_pairs={{0,32},{2,226},{4,36},{6,230},{8,40},{10,234},{12,44},{14,238},{16... | collective-permute-start | bytes 786440 | tf_op jit(solution)/shard_map/ppermute | solution.py:80
  117.1 8.5 %collective-permute-start.18 = (f32[16,4096]{1,0:T(8,128)S(1)}, f32[16,4096]{1,0:T(8,128)S(1)}, u32[]{:S(2)}, u32[]{:S(2)}) collective-permute-start(f32[16,4096]{1,0:T(8,128)S(1)} %get-tuple-element.20), channel_id=1, source_target_pairs={{0,224},{2,34},{4,228},{6,38},{8,232},{10,42},{12,236},{14,46},{16... | collective-permute-start | bytes 786440 | tf_op jit(solution)/shard_map/ppermute | solution.py:88
  120.3 8.8 %collective-permute-start.30 = (f32[4,4096]{1,0:T(4,128)S(1)}, f32[4,4096]{1,0:T(4,128)S(1)}, u32[]{:S(2)}, u32[]{:S(2)}) collective-permute-start(f32[4,4096]{1,0:T(4,128)S(1)} %get-tuple-element.28), channel_id=1, source_target_pairs={{0,32},{2,226},{4,36},{6,230},{8,40},{10,234},{12,44},{14,238},{16... | collective-permute-start | bytes 196616 | tf_op jit(solution)/shard_map/ppermute | solution.py:80
  120.4 8.7 %collective-permute-start.33 = (f32[4,4096]{1,0:T(4,128)S(1)}, f32[4,4096]{1,0:T(4,128)S(1)}, u32[]{:S(2)}, u32[]{:S(2)}) collective-permute-start(f32[4,4096]{1,0:T(4,128)S(1)} %get-tuple-element.29), channel_id=1, source_target_pairs={{0,224},{2,34},{4,228},{6,38},{8,232},{10,42},{12,236},{14,46},{16... | collective-permute-start | bytes 196616 | tf_op jit(solution)/shard_map/ppermute | solution.py:88
  125.7 7.7 %collective-permute-start.16 = (f32[16,4096]{1,0:T(8,128)S(1)}, f32[16,4096]{1,0:T(8,128)S(1)}, u32[]{:S(2)}, u32[]{:S(2)}) collective-permute-start(f32[16,4096]{1,0:T(8,128)S(1)} %get-tuple-element.17), channel_id=1, source_target_pairs={{0,32},{2,226},{4,36},{6,230},{8,40},{10,234},{12,44},{14,238},{16... | collective-permute-start | bytes 786440 | tf_op jit(solution)/shard_map/ppermute | solution.py:80
  129.2 7.9 %collective-permute-start.31 = (f32[4,4096]{1,0:T(4,128)S(1)}, f32[4,4096]{1,0:T(4,128)S(1)}, u32[]{:S(2)}, u32[]{:S(2)}) collective-permute-start(f32[4,4096]{1,0:T(4,128)S(1)} %get-tuple-element.26), channel_id=1, source_target_pairs={{0,32},{2,226},{4,36},{6,230},{8,40},{10,234},{12,44},{14,238},{16... | collective-permute-start | bytes 196616 | tf_op jit(solution)/shard_map/ppermute | solution.py:80
  129.3 7.9 %collective-permute-start.34 = (f32[4,4096]{1,0:T(4,128)S(1)}, f32[4,4096]{1,0:T(4,128)S(1)}, u32[]{:S(2)}, u32[]{:S(2)}) collective-permute-start(f32[4,4096]{1,0:T(4,128)S(1)} %get-tuple-element.27), channel_id=1, source_target_pairs={{0,224},{2,34},{4,228},{6,38},{8,232},{10,42},{12,236},{14,46},{16... | collective-permute-start | bytes 196616 | tf_op jit(solution)/shard_map/ppermute | solution.py:88
  (17 other events, 171.6 us)

commit v11 on v6

--- a/solution.py
+++ b/solution.py
@@ -114,14 +114,14 @@
 
     base = tuple(reversed(AG_ORDER))
     piece = normed
-    kept = [gate_kept, up_kept, down_kept]
+    kept = [down_kept, up_kept, gate_kept]
     for i, axis in enumerate(AG_ORDER[:-1]):
         if axis in AG_DIRECT:
             piece = _ag_direct(piece, axis, size)
         else:
             piece = _ag_stage(piece, axis, size)
         piece, kept[i] = lax.optimization_barrier((piece, kept[i]))
-    gate_kept, up_kept, down_kept = kept
+    down_kept, up_kept, gate_kept = kept
     last = AG_ORDER[-1]
     _, n_last = BLK_AXES[last]
     assert n_last == 2

time: 136 us -> 137 us (level)
  local copies, waits for them, and re-layouts: 6.16 us -> 7.53 us
    unnamed x23, local copies, waits for them, and re-layouts: 3.24 us -> 4.66 us
  transfers between devices with their start and end apart: 36 -> 36, of which waited for: 21 -> 20; matrix products, arithmetic and copies ran while one was open for 12% -> 11% of each run, Pallas kernels for 0% -> 0%
where the time goes in v11:
time: 137 us; the launch traced here: 136 us
  waiting for transfers between devices  55.9 us (41%)
  starting transfers between devices  53.1 us (39%)
  other arithmetic  12.3 us (9%)
  local copies, waits for them, and re-layouts  7.53 us (5%)
  matrix products  6.24 us (5%)
    ppermute x14, waiting for transfers between devices, _rs_stage(): recv = lax.ppermute(buf, 'blk', _perm(axis, 1, size))  25.7 us
    ppermute x7, starting transfers between devices, _rs_stage(): recv = lax.ppermute(buf, 'blk', _perm(axis, -1, size))  22.1 us
    ppermute x5, waiting for transfers between devices, _ag_stage(): cur = lax.ppermute(cur, 'blk', _perm(axis, 1, size))  17.2 us
    ppermute x3, starting transfers between devices, _ag_stage(): cur = lax.ppermute(cur, 'blk', _perm(axis, -1, size))  13.3 us
    ppermute x3, waiting for transfers between devices, _ag_stage(): cur = lax.ppermute(cur, 'blk', _perm(axis, -1, size))  9.52 us
    mul x3, other arithmetic, mask_blocks(): return (shaped * cols[:, None, :]).reshape(height, width)  7.43 us
    ppermute x14, starting transfers between devices, _rs_stage(): recv = lax.ppermute(buf, 'blk', _perm(axis, 1, size))  7.14 us
    ppermute x3, starting transfers between devices, _ag_direct(): lax.ppermute(block, 'blk', _perm(axis, -o, size))  4.69 us
  transfers between devices with their start and end apart: 36, of which 20 were waited for; matrix products, arithmetic and copies ran while one was open for 11% of the time, Pallas kernels for 0%

profile of v11, /device:TPU:2, one launch (start us, length us, event | category | flops | bytes accessed | tf_op | source)
XLA Modules:
  0.0 135.6 jit_solution(5313661855184031765)
XLA Ops:
  1.8 2.2 %collective-permute-start = (bf16[2,8192]{1,0:T(2,128)(2,1)S(1)}, bf16[2,8192]{1,0:T(2,128)(2,1)S(1)}, u32[]{:S(2)}, u32[]{:S(2)}) collective-permute-start(bf16[2,8192]{1,0:T(2,128)(2,1)S(1)} %fusion.11), channel_id=1, source_target_pairs={{0,16},{2,18},{4,20},{6,22},{8,24},{10,26},{12,28},{14,30},{16,0},... | collective-permute-start | bytes 98312 | tf_op jit(solution)/shard_map/ppermute | solution.py:43
  4.9 4.5 %bitcast_multiply_fusion.2 = bf16[256,8192]{1,0:T(8,128)(2,1)} fusion(bf16[256,8192]{1,0:T(8,128)(2,1)} %param.12, bf16[2,8192]{1,0:T(2,128)(2,1)S(1)} %bitcast.32), kind=kLoop, calls=%fused_computation.2 | loop fusion | flops 2097152 | bytes 8421376 | tf_op jit(solution)/shard_map/mul | solution.py:21
  9.5 3.1 %collective-permute-start.1 = (bf16[4,8192]{1,0:T(4,128)(2,1)S(1)}, bf16[4,8192]{1,0:T(4,128)(2,1)S(1)}, u32[]{:S(2)}, u32[]{:S(2)}) collective-permute-start(bf16[4,8192]{1,0:T(4,128)(2,1)S(1)} %pad_maximum_fusion.3), channel_id=1, source_target_pairs={{0,12},{2,6},{4,0},{6,10},{8,4},{10,14},{12,8},{14,2},{16,28},{18,... | collective-permute-start | bytes 196616 | tf_op jit(solution)/shard_map/ppermute | solution.py:54
  14.8 2.6 %bitcast_multiply_fusion.1 = bf16[8192,256]{1,0:T(8,128)(2,1)S(1)} fusion(bf16[8192,256]{1,0:T(8,128)(2,1)} %param.11, bf16[64,256]{1,0:T(8,128)(2,1)S(1)} %bitcast.30), kind=kLoop, calls=%fused_computation.1 | loop fusion | flops 2097152 | bytes 8421376 | tf_op jit(solution)/shard_map/mul | solution.py:21
  19.2 5.9 %collective-permute-start.4 = (bf16[16,8192]{1,0:T(8,128)(2,1)S(1)}, bf16[16,8192]{1,0:T(8,128)(2,1)S(1)}, u32[]{:S(2)}, u32[]{:S(2)}) collective-permute-start(bf16[16,8192]{1,0:T(8,128)(2,1)S(1)} %pad_maximum_fusion), channel_id=1, source_target_pairs={{0,224},{2,34},{4,228},{6,38},{8,232},{10,42},{12,236},{14,46},{16... | collective-permute-start | bytes 786440 | tf_op jit(solution)/shard_map/ppermute | solution.py:47
  25.2 5.2 %collective-permute-done.4 = bf16[16,8192]{1,0:T(8,128)(2,1)S(1)} collective-permute-done((bf16[16,8192]{1,0:T(8,128)(2,1)S(1)}, bf16[16,8192]{1,0:T(8,128)(2,1)S(1)}, u32[]{:S(2)}, u32[]{:S(2)}) %collective-permute-start.4) | collective-permute-done | bytes 262176 | tf_op jit(solution)/shard_map/ppermute | solution.py:47
  30.4 3.7 %collective-permute-start.5 = (bf16[16,8192]{1,0:T(8,128)(2,1)S(1)}, bf16[16,8192]{1,0:T(8,128)(2,1)S(1)}, u32[]{:S(2)}, u32[]{:S(2)}) collective-permute-start(bf16[16,8192]{1,0:T(8,128)(2,1)S(1)} %collective-permute-done.4), channel_id=1, source_target_pairs={{0,224},{2,34},{4,228},{6,38},{8,232},{10,42},{12,236},{14,46},{16... | collective-permute-start | bytes 786440 | tf_op jit(solution)/shard_map/ppermute | solution.py:47
  34.1 4.3 %collective-permute-done.5 = bf16[16,8192]{1,0:T(8,128)(2,1)S(1)} collective-permute-done((bf16[16,8192]{1,0:T(8,128)(2,1)S(1)}, bf16[16,8192]{1,0:T(8,128)(2,1)S(1)}, u32[]{:S(2)}, u32[]{:S(2)}) %collective-permute-start.5) | collective-permute-done | bytes 262176 | tf_op jit(solution)/shard_map/ppermute | solution.py:47
  38.4 3.7 %collective-permute-start.6 = (bf16[16,8192]{1,0:T(8,128)(2,1)S(1)}, bf16[16,8192]{1,0:T(8,128)(2,1)S(1)}, u32[]{:S(2)}, u32[]{:S(2)}) collective-permute-start(bf16[16,8192]{1,0:T(8,128)(2,1)S(1)} %collective-permute-done.5), channel_id=1, source_target_pairs={{0,224},{2,34},{4,228},{6,38},{8,232},{10,42},{12,236},{14,46},{16... | collective-permute-start | bytes 786440 | tf_op jit(solution)/shard_map/ppermute | solution.py:47
  42.1 2.1 %collective-permute-done.8 = bf16[16,8192]{1,0:T(8,128)(2,1)S(1)} collective-permute-done((bf16[16,8192]{1,0:T(8,128)(2,1)S(1)}, bf16[16,8192]{1,0:T(8,128)(2,1)S(1)}, u32[]{:S(2)}, u32[]{:S(2)}) %collective-permute-start.8) | collective-permute-done | bytes 262176 | tf_op jit(solution)/shard_map/ppermute | solution.py:43
  44.2 7.6 %collective-permute-done.9 = bf16[16,8192]{1,0:T(8,128)(2,1)S(1)} collective-permute-done((bf16[16,8192]{1,0:T(8,128)(2,1)S(1)}, bf16[16,8192]{1,0:T(8,128)(2,1)S(1)}, u32[]{:S(2)}, u32[]{:S(2)}) %collective-permute-start.9) | collective-permute-done | bytes 262176 | tf_op jit(solution)/shard_map/ppermute | solution.py:43
  51.8 7.6 %collective-permute-done.10 = bf16[16,8192]{1,0:T(8,128)(2,1)S(1)} collective-permute-done((bf16[16,8192]{1,0:T(8,128)(2,1)S(1)}, bf16[16,8192]{1,0:T(8,128)(2,1)S(1)}, u32[]{:S(2)}, u32[]{:S(2)}) %collective-permute-start.10) | collective-permute-done | bytes 262176 | tf_op jit(solution)/shard_map/ppermute | solution.py:43
  61.3 2.5 %collective-permute-done.11 = bf16[128,8192]{1,0:T(8,128)(2,1)S(1)} collective-permute-done((bf16[128,8192]{1,0:T(8,128)(2,1)S(1)}, bf16[128,8192]{1,0:T(8,128)(2,1)S(1)}, u32[]{:S(2)}, u32[]{:S(2)}) %collective-permute-start.11) | collective-permute-done | bytes 2097184 | tf_op jit(solution)/shard_map/ppermute | solution.py:128
  71.3 2.3 %fusion = f32[256,4096]{1,0:T(8,128)S(1)} fusion(bf16[256,256]{1,0:T(8,128)(2,1)S(1)} %reshape.27, bf16[256,8192]{1,0:T(8,128)(2,1)} %bitcast_multiply_fusion.2), kind=kOutput, calls=%fused_computation.5 | convolution fusion | flops 536870912 | bytes 6422528 | tf_op jit(solution)/shard_map/dot_general | solution.py:140
  80.1 3.6 %collective-permute-done.13 = f32[16,4096]{1,0:T(8,128)S(1)} collective-permute-done((f32[16,4096]{1,0:T(8,128)S(1)}, f32[16,4096]{1,0:T(8,128)S(1)}, u32[]{:S(2)}, u32[]{:S(2)}) %collective-permute-start.13) | collective-permute-done | bytes 262176 | tf_op jit(solution)/shard_map/ppermute | solution.py:80
  83.9 3.2 %collective-permute-start.17 = (f32[16,4096]{1,0:T(8,128)S(1)}, f32[16,4096]{1,0:T(8,128)S(1)}, u32[]{:S(2)}, u32[]{:S(2)}) collective-permute-start(f32[16,4096]{1,0:T(8,128)S(1)} %get-tuple-element.22), channel_id=1, source_target_pairs={{0,224},{2,34},{4,228},{6,38},{8,232},{10,42},{12,236},{14,46},{16... | collective-permute-start | bytes 786440 | tf_op jit(solution)/shard_map/ppermute | solution.py:88
  89.5 2.7 %collective-permute-start.27 = (f32[32,4096]{1,0:T(8,128)S(1)}, f32[32,4096]{1,0:T(8,128)S(1)}, u32[]{:S(2)}, u32[]{:S(2)}) collective-permute-start(f32[32,4096]{1,0:T(8,128)S(1)} %get-tuple-element.24), channel_id=1, source_target_pairs={{0,12},{2,6},{4,0},{6,10},{8,4},{10,14},{12,8},{14,2},{16,28},{18,... | collective-permute-start | bytes 1572872 | tf_op jit(solution)/shard_map/ppermute | solution.py:88
  92.7 3.2 %collective-permute-start.18 = (f32[16,4096]{1,0:T(8,128)S(1)}, f32[16,4096]{1,0:T(8,128)S(1)}, u32[]{:S(2)}, u32[]{:S(2)}) collective-permute-start(f32[16,4096]{1,0:T(8,128)S(1)} %get-tuple-element.20), channel_id=1, source_target_pairs={{0,224},{2,34},{4,228},{6,38},{8,232},{10,42},{12,236},{14,46},{16... | collective-permute-start | bytes 786440 | tf_op jit(solution)/shard_map/ppermute | solution.py:88
  95.9 9.1 %collective-permute-done.26 = f32[32,4096]{1,0:T(8,128)S(1)} collective-permute-done((f32[32,4096]{1,0:T(8,128)S(1)}, f32[32,4096]{1,0:T(8,128)S(1)}, u32[]{:S(2)}, u32[]{:S(2)}) %collective-permute-start.26) | collective-permute-done | bytes 524320 | tf_op jit(solution)/shard_map/ppermute | solution.py:80
  105.3 3.3 %collective-permute-start.19 = (f32[16,4096]{1,0:T(8,128)S(1)}, f32[16,4096]{1,0:T(8,128)S(1)}, u32[]{:S(2)}, u32[]{:S(2)}) collective-permute-start(f32[16,4096]{1,0:T(8,128)S(1)} %get-tuple-element.18), channel_id=1, source_target_pairs={{0,224},{2,34},{4,228},{6,38},{8,232},{10,42},{12,236},{14,46},{16... | collective-permute-start | bytes 786440 | tf_op jit(solution)/shard_map/ppermute | solution.py:88
  108.6 2.6 %collective-permute-done.28 = f32[4,4096]{1,0:T(4,128)S(1)} collective-permute-done((f32[4,4096]{1,0:T(4,128)S(1)}, f32[4,4096]{1,0:T(4,128)S(1)}, u32[]{:S(2)}, u32[]{:S(2)}) %collective-permute-start.28) | collective-permute-done | bytes 65568 | tf_op jit(solution)/shard_map/ppermute | solution.py:80
  111.4 3.2 %collective-permute-start.32 = (f32[4,4096]{1,0:T(4,128)S(1)}, f32[4,4096]{1,0:T(4,128)S(1)}, u32[]{:S(2)}, u32[]{:S(2)}) collective-permute-start(f32[4,4096]{1,0:T(4,128)S(1)} %get-tuple-element.30), channel_id=1, source_target_pairs={{0,224},{2,34},{4,228},{6,38},{8,232},{10,42},{12,236},{14,46},{16... | collective-permute-start | bytes 196616 | tf_op jit(solution)/shard_map/ppermute | solution.py:88
  117.1 3.3 %collective-permute-start.33 = (f32[4,4096]{1,0:T(4,128)S(1)}, f32[4,4096]{1,0:T(4,128)S(1)}, u32[]{:S(2)}, u32[]{:S(2)}) collective-permute-start(f32[4,4096]{1,0:T(4,128)S(1)} %get-tuple-element.28), channel_id=1, source_target_pairs={{0,224},{2,34},{4,228},{6,38},{8,232},{10,42},{12,236},{14,46},{16... | collective-permute-start | bytes 196616 | tf_op jit(solution)/shard_map/ppermute | solution.py:88
  123.9 3.2 %collective-permute-start.34 = (f32[4,4096]{1,0:T(4,128)S(1)}, f32[4,4096]{1,0:T(4,128)S(1)}, u32[]{:S(2)}, u32[]{:S(2)}) collective-permute-start(f32[4,4096]{1,0:T(4,128)S(1)} %get-tuple-element.26), channel_id=1, source_target_pairs={{0,224},{2,34},{4,228},{6,38},{8,232},{10,42},{12,236},{14,46},{16... | collective-permute-start | bytes 196616 | tf_op jit(solution)/shard_map/ppermute | solution.py:88
  (124 shorter events, 40.4 us)
Async XLA Ops:
  1.8 7.6 %collective-permute-start = (bf16[2,8192]{1,0:T(2,128)(2,1)S(1)}, bf16[2,8192]{1,0:T(2,128)(2,1)S(1)}, u32[]{:S(2)}, u32[]{:S(2)}) collective-permute-start(bf16[2,8192]{1,0:T(2,128)(2,1)S(1)} %fusion.11), channel_id=1, source_target_pairs={{0,16},{2,18},{4,20},{6,22},{8,24},{10,26},{12,28},{14,30},{16,0},... | collective-permute-start | bytes 98312 | tf_op jit(solution)/shard_map/ppermute | solution.py:43
  9.5 9.0 %collective-permute-start.1 = (bf16[4,8192]{1,0:T(4,128)(2,1)S(1)}, bf16[4,8192]{1,0:T(4,128)(2,1)S(1)}, u32[]{:S(2)}, u32[]{:S(2)}) collective-permute-start(bf16[4,8192]{1,0:T(4,128)(2,1)S(1)} %pad_maximum_fusion.3), channel_id=1, source_target_pairs={{0,12},{2,6},{4,0},{6,10},{8,4},{10,14},{12,8},{14,2},{16,28},{18,... | collective-permute-start | bytes 196616 | tf_op jit(solution)/shard_map/ppermute | solution.py:54
  19.2 11.2 %collective-permute-start.4 = (bf16[16,8192]{1,0:T(8,128)(2,1)S(1)}, bf16[16,8192]{1,0:T(8,128)(2,1)S(1)}, u32[]{:S(2)}, u32[]{:S(2)}) collective-permute-start(bf16[16,8192]{1,0:T(8,128)(2,1)S(1)} %pad_maximum_fusion), channel_id=1, source_target_pairs={{0,224},{2,34},{4,228},{6,38},{8,232},{10,42},{12,236},{14,46},{16... | collective-permute-start | bytes 786440 | tf_op jit(solution)/shard_map/ppermute | solution.py:47
  25.1 8.9 %collective-permute-start.7 = (bf16[16,8192]{1,0:T(8,128)(2,1)S(1)}, bf16[16,8192]{1,0:T(8,128)(2,1)S(1)}, u32[]{:S(2)}, u32[]{:S(2)}) collective-permute-start(bf16[16,8192]{1,0:T(8,128)(2,1)S(1)} %pad_maximum_fusion), channel_id=1, source_target_pairs={{0,32},{2,226},{4,36},{6,230},{8,40},{10,234},{12,44},{14,238},{16... | collective-permute-start | bytes 786440 | tf_op jit(solution)/shard_map/ppermute | solution.py:43
  30.4 8.0 %collective-permute-start.5 = (bf16[16,8192]{1,0:T(8,128)(2,1)S(1)}, bf16[16,8192]{1,0:T(8,128)(2,1)S(1)}, u32[]{:S(2)}, u32[]{:S(2)}) collective-permute-start(bf16[16,8192]{1,0:T(8,128)(2,1)S(1)} %collective-permute-done.4), channel_id=1, source_target_pairs={{0,224},{2,34},{4,228},{6,38},{8,232},{10,42},{12,236},{14,46},{16... | collective-permute-start | bytes 786440 | tf_op jit(solution)/shard_map/ppermute | solution.py:47
  34.1 10.1 %collective-permute-start.8 = (bf16[16,8192]{1,0:T(8,128)(2,1)S(1)}, bf16[16,8192]{1,0:T(8,128)(2,1)S(1)}, u32[]{:S(2)}, u32[]{:S(2)}) collective-permute-start(bf16[16,8192]{1,0:T(8,128)(2,1)S(1)} %collective-permute-done.7), channel_id=1, source_target_pairs={{0,32},{2,226},{4,36},{6,230},{8,40},{10,234},{12,44},{14,238},{16... | collective-permute-start | bytes 786440 | tf_op jit(solution)/shard_map/ppermute | solution.py:43
  38.4 13.4 %collective-permute-start.6 = (bf16[16,8192]{1,0:T(8,128)(2,1)S(1)}, bf16[16,8192]{1,0:T(8,128)(2,1)S(1)}, u32[]{:S(2)}, u32[]{:S(2)}) collective-permute-start(bf16[16,8192]{1,0:T(8,128)(2,1)S(1)} %collective-permute-done.5), channel_id=1, source_target_pairs={{0,224},{2,34},{4,228},{6,38},{8,232},{10,42},{12,236},{14,46},{16... | collective-permute-start | bytes 786440 | tf_op jit(solution)/shard_map/ppermute | solution.py:47
  44.2 7.6 %collective-permute-start.9 = (bf16[16,8192]{1,0:T(8,128)(2,1)S(1)}, bf16[16,8192]{1,0:T(8,128)(2,1)S(1)}, u32[]{:S(2)}, u32[]{:S(2)}) collective-permute-start(bf16[16,8192]{1,0:T(8,128)(2,1)S(1)} %collective-permute-done.8), channel_id=1, source_target_pairs={{0,32},{2,226},{4,36},{6,230},{8,40},{10,234},{12,44},{14,238},{16... | collective-permute-start | bytes 786440 | tf_op jit(solution)/shard_map/ppermute | solution.py:43
  51.8 7.6 %collective-permute-start.10 = (bf16[16,8192]{1,0:T(8,128)(2,1)S(1)}, bf16[16,8192]{1,0:T(8,128)(2,1)S(1)}, u32[]{:S(2)}, u32[]{:S(2)}) collective-permute-start(bf16[16,8192]{1,0:T(8,128)(2,1)S(1)} %collective-permute-done.9), channel_id=1, source_target_pairs={{0,32},{2,226},{4,36},{6,230},{8,40},{10,234},{12,44},{14,238},{16... | collective-permute-start | bytes 786440 | tf_op jit(solution)/shard_map/ppermute | solution.py:43
  76.1 7.7 %collective-permute-start.13 = (f32[16,4096]{1,0:T(8,128)S(1)}, f32[16,4096]{1,0:T(8,128)S(1)}, u32[]{:S(2)}, u32[]{:S(2)}) collective-permute-start(f32[16,4096]{1,0:T(8,128)S(1)} %slice.139), channel_id=1, source_target_pairs={{0,32},{2,226},{4,36},{6,230},{8,40},{10,234},{12,44},{14,238},{16... | collective-permute-start | bytes 786440 | tf_op jit(solution)/shard_map/ppermute | solution.py:80
  78.3 10.5 %collective-permute-start.25 = (f32[32,4096]{1,0:T(8,128)S(1)}, f32[32,4096]{1,0:T(8,128)S(1)}, u32[]{:S(2)}, u32[]{:S(2)}) collective-permute-start(f32[32,4096]{1,0:T(8,128)S(1)} %slice.155), channel_id=1, source_target_pairs={{0,4},{2,14},{4,8},{6,2},{8,12},{10,6},{12,0},{14,10},{16,20},{18,... | collective-permute-start | bytes 1572872 | tf_op jit(solution)/shard_map/ppermute | solution.py:80
  83.8 8.7 %collective-permute-start.14 = (f32[16,4096]{1,0:T(8,128)S(1)}, f32[16,4096]{1,0:T(8,128)S(1)}, u32[]{:S(2)}, u32[]{:S(2)}) collective-permute-start(f32[16,4096]{1,0:T(8,128)S(1)} %get-tuple-element.21), channel_id=1, source_target_pairs={{0,32},{2,226},{4,36},{6,230},{8,40},{10,234},{12,44},{14,238},{16... | collective-permute-start | bytes 786440 | tf_op jit(solution)/shard_map/ppermute | solution.py:80
  83.9 8.6 %collective-permute-start.17 = (f32[16,4096]{1,0:T(8,128)S(1)}, f32[16,4096]{1,0:T(8,128)S(1)}, u32[]{:S(2)}, u32[]{:S(2)}) collective-permute-start(f32[16,4096]{1,0:T(8,128)S(1)} %get-tuple-element.22), channel_id=1, source_target_pairs={{0,224},{2,34},{4,228},{6,38},{8,232},{10,42},{12,236},{14,46},{16... | collective-permute-start | bytes 786440 | tf_op jit(solution)/shard_map/ppermute | solution.py:88
  88.9 16.0 %collective-permute-start.26 = (f32[32,4096]{1,0:T(8,128)S(1)}, f32[32,4096]{1,0:T(8,128)S(1)}, u32[]{:S(2)}, u32[]{:S(2)}) collective-permute-start(f32[32,4096]{1,0:T(8,128)S(1)} %get-tuple-element.23), channel_id=1, source_target_pairs={{0,4},{2,14},{4,8},{6,2},{8,12},{10,6},{12,0},{14,10},{16,20},{18,... | collective-permute-start | bytes 1572872 | tf_op jit(solution)/shard_map/ppermute | solution.py:80
  89.5 15.4 %collective-permute-start.27 = (f32[32,4096]{1,0:T(8,128)S(1)}, f32[32,4096]{1,0:T(8,128)S(1)}, u32[]{:S(2)}, u32[]{:S(2)}) collective-permute-start(f32[32,4096]{1,0:T(8,128)S(1)} %get-tuple-element.24), channel_id=1, source_target_pairs={{0,12},{2,6},{4,0},{6,10},{8,4},{10,14},{12,8},{14,2},{16,28},{18,... | collective-permute-start | bytes 1572872 | tf_op jit(solution)/shard_map/ppermute | solution.py:88
  92.6 12.6 %collective-permute-start.15 = (f32[16,4096]{1,0:T(8,128)S(1)}, f32[16,4096]{1,0:T(8,128)S(1)}, u32[]{:S(2)}, u32[]{:S(2)}) collective-permute-start(f32[16,4096]{1,0:T(8,128)S(1)} %get-tuple-element.19), channel_id=1, source_target_pairs={{0,32},{2,226},{4,36},{6,230},{8,40},{10,234},{12,44},{14,238},{16... | collective-permute-start | bytes 786440 | tf_op jit(solution)/shard_map/ppermute | solution.py:80
  92.7 12.5 %collective-permute-start.18 = (f32[16,4096]{1,0:T(8,128)S(1)}, f32[16,4096]{1,0:T(8,128)S(1)}, u32[]{:S(2)}, u32[]{:S(2)}) collective-permute-start(f32[16,4096]{1,0:T(8,128)S(1)} %get-tuple-element.20), channel_id=1, source_target_pairs={{0,224},{2,34},{4,228},{6,38},{8,232},{10,42},{12,236},{14,46},{16... | collective-permute-start | bytes 786440 | tf_op jit(solution)/shard_map/ppermute | solution.py:88
  105.0 6.2 %collective-permute-start.28 = (f32[4,4096]{1,0:T(4,128)S(1)}, f32[4,4096]{1,0:T(4,128)S(1)}, u32[]{:S(2)}, u32[]{:S(2)}) collective-permute-start(f32[4,4096]{1,0:T(4,128)S(1)} %slice.159), channel_id=1, source_target_pairs={{0,32},{2,226},{4,36},{6,230},{8,40},{10,234},{12,44},{14,238},{16... | collective-permute-start | bytes 196616 | tf_op jit(solution)/shard_map/ppermute | solution.py:80
  105.2 11.1 %collective-permute-start.16 = (f32[16,4096]{1,0:T(8,128)S(1)}, f32[16,4096]{1,0:T(8,128)S(1)}, u32[]{:S(2)}, u32[]{:S(2)}) collective-permute-start(f32[16,4096]{1,0:T(8,128)S(1)} %get-tuple-element.17), channel_id=1, source_target_pairs={{0,32},{2,226},{4,36},{6,230},{8,40},{10,234},{12,44},{14,238},{16... | collective-permute-start | bytes 786440 | tf_op jit(solution)/shard_map/ppermute | solution.py:80
  105.3 11.0 %collective-permute-start.19 = (f32[16,4096]{1,0:T(8,128)S(1)}, f32[16,4096]{1,0:T(8,128)S(1)}, u32[]{:S(2)}, u32[]{:S(2)}) collective-permute-start(f32[16,4096]{1,0:T(8,128)S(1)} %get-tuple-element.18), channel_id=1, source_target_pairs={{0,224},{2,34},{4,228},{6,38},{8,232},{10,42},{12,236},{14,46},{16... | collective-permute-start | bytes 786440 | tf_op jit(solution)/shard_map/ppermute | solution.py:88
  117.0 6.7 %collective-permute-start.30 = (f32[4,4096]{1,0:T(4,128)S(1)}, f32[4,4096]{1,0:T(4,128)S(1)}, u32[]{:S(2)}, u32[]{:S(2)}) collective-permute-start(f32[4,4096]{1,0:T(4,128)S(1)} %get-tuple-element.27), channel_id=1, source_target_pairs={{0,32},{2,226},{4,36},{6,230},{8,40},{10,234},{12,44},{14,238},{16... | collective-permute-start | bytes 196616 | tf_op jit(solution)/shard_map/ppermute | solution.py:80
  117.1 6.6 %collective-permute-start.33 = (f32[4,4096]{1,0:T(4,128)S(1)}, f32[4,4096]{1,0:T(4,128)S(1)}, u32[]{:S(2)}, u32[]{:S(2)}) collective-permute-start(f32[4,4096]{1,0:T(4,128)S(1)} %get-tuple-element.28), channel_id=1, source_target_pairs={{0,224},{2,34},{4,228},{6,38},{8,232},{10,42},{12,236},{14,46},{16... | collective-permute-start | bytes 196616 | tf_op jit(solution)/shard_map/ppermute | solution.py:88
  120.4 6.7 %collective-permute-start.20 = (f32[4,4096]{1,0:T(4,128)S(1)}, f32[4,4096]{1,0:T(4,128)S(1)}, u32[]{:S(2)}, u32[]{:S(2)}) collective-permute-start(f32[4,4096]{1,0:T(4,128)S(1)} %get-tuple-element.31), channel_id=1, source_target_pairs={{0,4},{2,14},{4,8},{6,2},{8,12},{10,6},{12,0},{14,10},{16,20},{18,... | collective-permute-start | bytes 196616 | tf_op jit(solution)/shard_map/ppermute | solution.py:64
  120.5 6.6 %collective-permute-start.21 = (f32[4,4096]{1,0:T(4,128)S(1)}, f32[4,4096]{1,0:T(4,128)S(1)}, u32[]{:S(2)}, u32[]{:S(2)}) collective-permute-start(f32[4,4096]{1,0:T(4,128)S(1)} %get-tuple-element.33), channel_id=1, source_target_pairs={{0,8},{2,10},{4,12},{6,14},{8,0},{10,2},{12,4},{14,6},{16,24},{18,... | collective-permute-start | bytes 196616 | tf_op jit(solution)/shard_map/ppermute | solution.py:64
  (18 other events, 92.9 us)

commit v12 on v6

--- a/solution.py
+++ b/solution.py
@@ -68,8 +68,8 @@
 def _rs_stage(x, axis, size):
     _, n = BLK_AXES[axis]
     r = x.shape[0] // n
-    m_plus = n // 2
-    m_minus = n - 1 - m_plus
+    m_minus = n // 2
+    m_plus = n - 1 - m_minus
 
     def take(j):
         return lax.slice_in_dim(x, (j % n) * r, (j % n + 1) * r, axis=0)

time: 136 us -> 135 us (level)
  waiting for transfers between devices: 55.6 us -> 54.2 us
    ppermute x14 -> x7, waiting for transfers between devices: 25.3 us -> 11.2 us  [_rs_stage(): recv = lax.ppermute(buf, 'blk', _perm(axis, 1, size))]
    ppermute x7 -> x14, waiting for transfers between devices: 0.13 us -> 12.2 us  [_rs_stage(): recv = lax.ppermute(buf, 'blk', _perm(axis, -1, size))]
    ppermute x14 -> x7, starting transfers between devices: 7.25 us -> 5.77 us  [_rs_stage(): recv = lax.ppermute(buf, 'blk', _perm(axis, 1, size))]
    ppermute x7 -> x14, starting transfers between devices: 22.6 us -> 23.7 us  [_rs_stage(): recv = lax.ppermute(buf, 'blk', _perm(axis, -1, size))]
where the time goes in v12:
time: 135 us; the launch traced here: 133 us
  waiting for transfers between devices  54.2 us (40%)
  starting transfers between devices  53.6 us (40%)
  other arithmetic  13 us (10%)
  local copies, waits for them, and re-layouts  6.16 us (5%)
  matrix products  6.06 us (4%)
    ppermute x14, starting transfers between devices, _rs_stage(): recv = lax.ppermute(buf, 'blk', _perm(axis, -1, size))  23.7 us
    ppermute x5, waiting for transfers between devices, _ag_stage(): cur = lax.ppermute(cur, 'blk', _perm(axis, 1, size))  17.3 us
    ppermute x3, starting transfers between devices, _ag_stage(): cur = lax.ppermute(cur, 'blk', _perm(axis, -1, size))  13.3 us
    ppermute x14, waiting for transfers between devices, _rs_stage(): recv = lax.ppermute(buf, 'blk', _perm(axis, -1, size))  12.2 us
    ppermute x7, waiting for transfers between devices, _rs_stage(): recv = lax.ppermute(buf, 'blk', _perm(axis, 1, size))  11.2 us
    ppermute x3, waiting for transfers between devices, _ag_stage(): cur = lax.ppermute(cur, 'blk', _perm(axis, -1, size))  9.27 us
    mul x3, other arithmetic, mask_blocks(): return (shaped * cols[:, None, :]).reshape(height, width)  7.43 us
    ppermute x7, starting transfers between devices, _rs_stage(): recv = lax.ppermute(buf, 'blk', _perm(axis, 1, size))  5.77 us
  transfers between devices with their start and end apart: 36, of which 21 were waited for; matrix products, arithmetic and copies ran while one was open for 12% of the time, Pallas kernels for 0%

profile of v12, /device:TPU:2, one launch (start us, length us, event | category | flops | bytes accessed | tf_op | source)
XLA Modules:
  0.0 133.4 jit_solution(6468335482119662414)
XLA Ops:
  1.8 2.2 %collective-permute-start = (bf16[2,8192]{1,0:T(2,128)(2,1)S(1)}, bf16[2,8192]{1,0:T(2,128)(2,1)S(1)}, u32[]{:S(2)}, u32[]{:S(2)}) collective-permute-start(bf16[2,8192]{1,0:T(2,128)(2,1)S(1)} %fusion.11), channel_id=1, source_target_pairs={{0,16},{2,18},{4,20},{6,22},{8,24},{10,26},{12,28},{14,30},{16,0},... | collective-permute-start | bytes 98312 | tf_op jit(solution)/shard_map/ppermute | solution.py:43
  5.7 4.5 %bitcast_multiply_fusion.2 = bf16[8192,256]{1,0:T(8,128)(2,1)} fusion(bf16[8192,256]{1,0:T(8,128)(2,1)} %param.10, bf16[64,256]{1,0:T(8,128)(2,1)S(1)} %bitcast.32), kind=kLoop, calls=%fused_computation.2 | loop fusion | flops 2097152 | bytes 8421376 | tf_op jit(solution)/shard_map/mul | solution.py:21
  10.3 3.1 %collective-permute-start.1 = (bf16[4,8192]{1,0:T(4,128)(2,1)S(1)}, bf16[4,8192]{1,0:T(4,128)(2,1)S(1)}, u32[]{:S(2)}, u32[]{:S(2)}) collective-permute-start(bf16[4,8192]{1,0:T(4,128)(2,1)S(1)} %pad_maximum_fusion.3), channel_id=1, source_target_pairs={{0,12},{2,6},{4,0},{6,10},{8,4},{10,14},{12,8},{14,2},{16,28},{18,... | collective-permute-start | bytes 196616 | tf_op jit(solution)/shard_map/ppermute | solution.py:54
  15.4 2.6 %bitcast_multiply_fusion.1 = bf16[8192,256]{1,0:T(8,128)(2,1)S(1)} fusion(bf16[8192,256]{1,0:T(8,128)(2,1)} %param.11, bf16[64,256]{1,0:T(8,128)(2,1)S(1)} %bitcast.30), kind=kLoop, calls=%fused_computation.1 | loop fusion | flops 2097152 | bytes 8421376 | tf_op jit(solution)/shard_map/mul | solution.py:21
  20.0 5.9 %collective-permute-start.4 = (bf16[16,8192]{1,0:T(8,128)(2,1)S(1)}, bf16[16,8192]{1,0:T(8,128)(2,1)S(1)}, u32[]{:S(2)}, u32[]{:S(2)}) collective-permute-start(bf16[16,8192]{1,0:T(8,128)(2,1)S(1)} %pad_maximum_fusion), channel_id=1, source_target_pairs={{0,224},{2,34},{4,228},{6,38},{8,232},{10,42},{12,236},{14,46},{16... | collective-permute-start | bytes 786440 | tf_op jit(solution)/shard_map/ppermute | solution.py:47
  26.0 5.1 %collective-permute-done.4 = bf16[16,8192]{1,0:T(8,128)(2,1)S(1)} collective-permute-done((bf16[16,8192]{1,0:T(8,128)(2,1)S(1)}, bf16[16,8192]{1,0:T(8,128)(2,1)S(1)}, u32[]{:S(2)}, u32[]{:S(2)}) %collective-permute-start.4) | collective-permute-done | bytes 262176 | tf_op jit(solution)/shard_map/ppermute | solution.py:47
  31.1 3.7 %collective-permute-start.5 = (bf16[16,8192]{1,0:T(8,128)(2,1)S(1)}, bf16[16,8192]{1,0:T(8,128)(2,1)S(1)}, u32[]{:S(2)}, u32[]{:S(2)}) collective-permute-start(bf16[16,8192]{1,0:T(8,128)(2,1)S(1)} %collective-permute-done.4), channel_id=1, source_target_pairs={{0,224},{2,34},{4,228},{6,38},{8,232},{10,42},{12,236},{14,46},{16... | collective-permute-start | bytes 786440 | tf_op jit(solution)/shard_map/ppermute | solution.py:47
  34.8 4.2 %collective-permute-done.5 = bf16[16,8192]{1,0:T(8,128)(2,1)S(1)} collective-permute-done((bf16[16,8192]{1,0:T(8,128)(2,1)S(1)}, bf16[16,8192]{1,0:T(8,128)(2,1)S(1)}, u32[]{:S(2)}, u32[]{:S(2)}) %collective-permute-start.5) | collective-permute-done | bytes 262176 | tf_op jit(solution)/shard_map/ppermute | solution.py:47
  39.0 3.7 %collective-permute-start.6 = (bf16[16,8192]{1,0:T(8,128)(2,1)S(1)}, bf16[16,8192]{1,0:T(8,128)(2,1)S(1)}, u32[]{:S(2)}, u32[]{:S(2)}) collective-permute-start(bf16[16,8192]{1,0:T(8,128)(2,1)S(1)} %collective-permute-done.5), channel_id=1, source_target_pairs={{0,224},{2,34},{4,228},{6,38},{8,232},{10,42},{12,236},{14,46},{16... | collective-permute-start | bytes 786440 | tf_op jit(solution)/shard_map/ppermute | solution.py:47
  42.6 2.2 %collective-permute-done.8 = bf16[16,8192]{1,0:T(8,128)(2,1)S(1)} collective-permute-done((bf16[16,8192]{1,0:T(8,128)(2,1)S(1)}, bf16[16,8192]{1,0:T(8,128)(2,1)S(1)}, u32[]{:S(2)}, u32[]{:S(2)}) %collective-permute-start.8) | collective-permute-done | bytes 262176 | tf_op jit(solution)/shard_map/ppermute | solution.py:43
  44.8 7.6 %collective-permute-done.9 = bf16[16,8192]{1,0:T(8,128)(2,1)S(1)} collective-permute-done((bf16[16,8192]{1,0:T(8,128)(2,1)S(1)}, bf16[16,8192]{1,0:T(8,128)(2,1)S(1)}, u32[]{:S(2)}, u32[]{:S(2)}) %collective-permute-start.9) | collective-permute-done | bytes 262176 | tf_op jit(solution)/shard_map/ppermute | solution.py:43
  52.4 7.6 %collective-permute-done.10 = bf16[16,8192]{1,0:T(8,128)(2,1)S(1)} collective-permute-done((bf16[16,8192]{1,0:T(8,128)(2,1)S(1)}, bf16[16,8192]{1,0:T(8,128)(2,1)S(1)}, u32[]{:S(2)}, u32[]{:S(2)}) %collective-permute-start.10) | collective-permute-done | bytes 262176 | tf_op jit(solution)/shard_map/ppermute | solution.py:43
  61.9 2.6 %collective-permute-done.11 = bf16[128,8192]{1,0:T(8,128)(2,1)S(1)} collective-permute-done((bf16[128,8192]{1,0:T(8,128)(2,1)S(1)}, bf16[128,8192]{1,0:T(8,128)(2,1)S(1)}, u32[]{:S(2)}, u32[]{:S(2)}) %collective-permute-start.11) | collective-permute-done | bytes 2097184 | tf_op jit(solution)/shard_map/ppermute | solution.py:128
  70.4 2.3 %fusion = f32[256,4096]{1,0:T(8,128)S(1)} fusion(bf16[256,256]{1,0:T(8,128)(2,1)S(1)} %reshape.27, bf16[256,8192]{1,0:T(8,128)(2,1)} %copy-done.1), kind=kOutput, calls=%fused_computation.5 | convolution fusion | flops 536870912 | bytes 6422528 | tf_op jit(solution)/shard_map/dot_general | solution.py:140
  75.3 1.9 %collective-permute-done.24 = f32[128,4096]{1,0:T(8,128)S(1)} collective-permute-done((f32[128,4096]{1,0:T(8,128)S(1)}, f32[128,4096]{1,0:T(8,128)S(1)}, u32[]{:S(2)}, u32[]{:S(2)}) %collective-permute-start.24) | collective-permute-done | bytes 2097184 | tf_op jit(solution)/shard_map/ppermute | solution.py:88
  79.3 2.3 %collective-permute-done.16 = f32[16,4096]{1,0:T(8,128)S(1)} collective-permute-done((f32[16,4096]{1,0:T(8,128)S(1)}, f32[16,4096]{1,0:T(8,128)S(1)}, u32[]{:S(2)}, u32[]{:S(2)}) %collective-permute-start.16) | collective-permute-done | bytes 262176 | tf_op jit(solution)/shard_map/ppermute | solution.py:88
  81.8 3.2 %collective-permute-start.17 = (f32[16,4096]{1,0:T(8,128)S(1)}, f32[16,4096]{1,0:T(8,128)S(1)}, u32[]{:S(2)}, u32[]{:S(2)}) collective-permute-start(f32[16,4096]{1,0:T(8,128)S(1)} %get-tuple-element.22), channel_id=1, source_target_pairs={{0,224},{2,34},{4,228},{6,38},{8,232},{10,42},{12,236},{14,46},{16... | collective-permute-start | bytes 786440 | tf_op jit(solution)/shard_map/ppermute | solution.py:88
  91.9 3.2 %collective-permute-start.18 = (f32[16,4096]{1,0:T(8,128)S(1)}, f32[16,4096]{1,0:T(8,128)S(1)}, u32[]{:S(2)}, u32[]{:S(2)}) collective-permute-start(f32[16,4096]{1,0:T(8,128)S(1)} %get-tuple-element.20), channel_id=1, source_target_pairs={{0,224},{2,34},{4,228},{6,38},{8,232},{10,42},{12,236},{14,46},{16... | collective-permute-start | bytes 786440 | tf_op jit(solution)/shard_map/ppermute | solution.py:88
  95.1 7.8 %collective-permute-done.25 = f32[32,4096]{1,0:T(8,128)S(1)} collective-permute-done((f32[32,4096]{1,0:T(8,128)S(1)}, f32[32,4096]{1,0:T(8,128)S(1)}, u32[]{:S(2)}, u32[]{:S(2)}) %collective-permute-start.25) | collective-permute-done | bytes 524320 | tf_op jit(solution)/shard_map/ppermute | solution.py:80
  103.2 2.1 %collective-permute-start.15 = (f32[16,4096]{1,0:T(8,128)S(1)}, f32[16,4096]{1,0:T(8,128)S(1)}, u32[]{:S(2)}, u32[]{:S(2)}) collective-permute-start(f32[16,4096]{1,0:T(8,128)S(1)} %get-tuple-element.17), channel_id=1, source_target_pairs={{0,32},{2,226},{4,36},{6,230},{8,40},{10,234},{12,44},{14,238},{16... | collective-permute-start | bytes 786440 | tf_op jit(solution)/shard_map/ppermute | solution.py:80
  108.1 3.2 %collective-permute-start.32 = (f32[4,4096]{1,0:T(4,128)S(1)}, f32[4,4096]{1,0:T(4,128)S(1)}, u32[]{:S(2)}, u32[]{:S(2)}) collective-permute-start(f32[4,4096]{1,0:T(4,128)S(1)} %get-tuple-element.30), channel_id=1, source_target_pairs={{0,224},{2,34},{4,228},{6,38},{8,232},{10,42},{12,236},{14,46},{16... | collective-permute-start | bytes 196616 | tf_op jit(solution)/shard_map/ppermute | solution.py:88
  118.2 3.1 %collective-permute-start.21 = (f32[4,4096]{1,0:T(4,128)S(1)}, f32[4,4096]{1,0:T(4,128)S(1)}, u32[]{:S(2)}, u32[]{:S(2)}) collective-permute-start(f32[4,4096]{1,0:T(4,128)S(1)} %get-tuple-element.33), channel_id=1, source_target_pairs={{0,8},{2,10},{4,12},{6,14},{8,0},{10,2},{12,4},{14,6},{16,24},{18,... | collective-permute-start | bytes 196616 | tf_op jit(solution)/shard_map/ppermute | solution.py:64
  121.5 3.2 %collective-permute-start.34 = (f32[4,4096]{1,0:T(4,128)S(1)}, f32[4,4096]{1,0:T(4,128)S(1)}, u32[]{:S(2)}, u32[]{:S(2)}) collective-permute-start(f32[4,4096]{1,0:T(4,128)S(1)} %get-tuple-element.26), channel_id=1, source_target_pairs={{0,224},{2,34},{4,228},{6,38},{8,232},{10,42},{12,236},{14,46},{16... | collective-permute-start | bytes 196616 | tf_op jit(solution)/shard_map/ppermute | solution.py:88
  127.2 2.2 %collective-permute-start.35 = (f32[2,4096]{1,0:T(2,128)S(1)}, f32[2,4096]{1,0:T(2,128)S(1)}, u32[]{:S(2)}, u32[]{:S(2)}) collective-permute-start(f32[2,4096]{1,0:T(2,128)S(1)} %slice.167), channel_id=1, source_target_pairs={{0,16},{2,18},{4,20},{6,22},{8,24},{10,26},{12,28},{14,30},{16,0},... | collective-permute-start | bytes 98312 | tf_op jit(solution)/shard_map/ppermute | solution.py:88
  (124 shorter events, 43.4 us)
Async XLA Ops:
  1.8 8.4 %collective-permute-start = (bf16[2,8192]{1,0:T(2,128)(2,1)S(1)}, bf16[2,8192]{1,0:T(2,128)(2,1)S(1)}, u32[]{:S(2)}, u32[]{:S(2)}) collective-permute-start(bf16[2,8192]{1,0:T(2,128)(2,1)S(1)} %fusion.11), channel_id=1, source_target_pairs={{0,16},{2,18},{4,20},{6,22},{8,24},{10,26},{12,28},{14,30},{16,0},... | collective-permute-start | bytes 98312 | tf_op jit(solution)/shard_map/ppermute | solution.py:43
  10.3 8.9 %collective-permute-start.1 = (bf16[4,8192]{1,0:T(4,128)(2,1)S(1)}, bf16[4,8192]{1,0:T(4,128)(2,1)S(1)}, u32[]{:S(2)}, u32[]{:S(2)}) collective-permute-start(bf16[4,8192]{1,0:T(4,128)(2,1)S(1)} %pad_maximum_fusion.3), channel_id=1, source_target_pairs={{0,12},{2,6},{4,0},{6,10},{8,4},{10,14},{12,8},{14,2},{16,28},{18,... | collective-permute-start | bytes 196616 | tf_op jit(solution)/shard_map/ppermute | solution.py:54
  20.0 11.1 %collective-permute-start.4 = (bf16[16,8192]{1,0:T(8,128)(2,1)S(1)}, bf16[16,8192]{1,0:T(8,128)(2,1)S(1)}, u32[]{:S(2)}, u32[]{:S(2)}) collective-permute-start(bf16[16,8192]{1,0:T(8,128)(2,1)S(1)} %pad_maximum_fusion), channel_id=1, source_target_pairs={{0,224},{2,34},{4,228},{6,38},{8,232},{10,42},{12,236},{14,46},{16... | collective-permute-start | bytes 786440 | tf_op jit(solution)/shard_map/ppermute | solution.py:47
  25.9 8.8 %collective-permute-start.7 = (bf16[16,8192]{1,0:T(8,128)(2,1)S(1)}, bf16[16,8192]{1,0:T(8,128)(2,1)S(1)}, u32[]{:S(2)}, u32[]{:S(2)}) collective-permute-start(bf16[16,8192]{1,0:T(8,128)(2,1)S(1)} %pad_maximum_fusion), channel_id=1, source_target_pairs={{0,32},{2,226},{4,36},{6,230},{8,40},{10,234},{12,44},{14,238},{16... | collective-permute-start | bytes 786440 | tf_op jit(solution)/shard_map/ppermute | solution.py:43
  31.1 7.9 %collective-permute-start.5 = (bf16[16,8192]{1,0:T(8,128)(2,1)S(1)}, bf16[16,8192]{1,0:T(8,128)(2,1)S(1)}, u32[]{:S(2)}, u32[]{:S(2)}) collective-permute-start(bf16[16,8192]{1,0:T(8,128)(2,1)S(1)} %collective-permute-done.4), channel_id=1, source_target_pairs={{0,224},{2,34},{4,228},{6,38},{8,232},{10,42},{12,236},{14,46},{16... | collective-permute-start | bytes 786440 | tf_op jit(solution)/shard_map/ppermute | solution.py:47
  34.8 10.0 %collective-permute-start.8 = (bf16[16,8192]{1,0:T(8,128)(2,1)S(1)}, bf16[16,8192]{1,0:T(8,128)(2,1)S(1)}, u32[]{:S(2)}, u32[]{:S(2)}) collective-permute-start(bf16[16,8192]{1,0:T(8,128)(2,1)S(1)} %collective-permute-done.7), channel_id=1, source_target_pairs={{0,32},{2,226},{4,36},{6,230},{8,40},{10,234},{12,44},{14,238},{16... | collective-permute-start | bytes 786440 | tf_op jit(solution)/shard_map/ppermute | solution.py:43
  39.0 13.4 %collective-permute-start.6 = (bf16[16,8192]{1,0:T(8,128)(2,1)S(1)}, bf16[16,8192]{1,0:T(8,128)(2,1)S(1)}, u32[]{:S(2)}, u32[]{:S(2)}) collective-permute-start(bf16[16,8192]{1,0:T(8,128)(2,1)S(1)} %collective-permute-done.5), channel_id=1, source_target_pairs={{0,224},{2,34},{4,228},{6,38},{8,232},{10,42},{12,236},{14,46},{16... | collective-permute-start | bytes 786440 | tf_op jit(solution)/shard_map/ppermute | solution.py:47
  44.8 7.6 %collective-permute-start.9 = (bf16[16,8192]{1,0:T(8,128)(2,1)S(1)}, bf16[16,8192]{1,0:T(8,128)(2,1)S(1)}, u32[]{:S(2)}, u32[]{:S(2)}) collective-permute-start(bf16[16,8192]{1,0:T(8,128)(2,1)S(1)} %collective-permute-done.8), channel_id=1, source_target_pairs={{0,32},{2,226},{4,36},{6,230},{8,40},{10,234},{12,44},{14,238},{16... | collective-permute-start | bytes 786440 | tf_op jit(solution)/shard_map/ppermute | solution.py:43
  52.4 7.6 %collective-permute-start.10 = (bf16[16,8192]{1,0:T(8,128)(2,1)S(1)}, bf16[16,8192]{1,0:T(8,128)(2,1)S(1)}, u32[]{:S(2)}, u32[]{:S(2)}) collective-permute-start(bf16[16,8192]{1,0:T(8,128)(2,1)S(1)} %collective-permute-done.9), channel_id=1, source_target_pairs={{0,32},{2,226},{4,36},{6,230},{8,40},{10,234},{12,44},{14,238},{16... | collective-permute-start | bytes 786440 | tf_op jit(solution)/shard_map/ppermute | solution.py:43
  75.2 6.5 %collective-permute-start.16 = (f32[16,4096]{1,0:T(8,128)S(1)}, f32[16,4096]{1,0:T(8,128)S(1)}, u32[]{:S(2)}, u32[]{:S(2)}) collective-permute-start(f32[16,4096]{1,0:T(8,128)S(1)} %slice.142), channel_id=1, source_target_pairs={{0,224},{2,34},{4,228},{6,38},{8,232},{10,42},{12,236},{14,46},{16... | collective-permute-start | bytes 786440 | tf_op jit(solution)/shard_map/ppermute | solution.py:88
  77.5 9.3 %collective-permute-start.26 = (f32[32,4096]{1,0:T(8,128)S(1)}, f32[32,4096]{1,0:T(8,128)S(1)}, u32[]{:S(2)}, u32[]{:S(2)}) collective-permute-start(f32[32,4096]{1,0:T(8,128)S(1)} %slice.156), channel_id=1, source_target_pairs={{0,12},{2,6},{4,0},{6,10},{8,4},{10,14},{12,8},{14,2},{16,28},{18,... | collective-permute-start | bytes 1572872 | tf_op jit(solution)/shard_map/ppermute | solution.py:88
  81.7 10.0 %collective-permute-start.13 = (f32[16,4096]{1,0:T(8,128)S(1)}, f32[16,4096]{1,0:T(8,128)S(1)}, u32[]{:S(2)}, u32[]{:S(2)}) collective-permute-start(f32[16,4096]{1,0:T(8,128)S(1)} %get-tuple-element.21), channel_id=1, source_target_pairs={{0,32},{2,226},{4,36},{6,230},{8,40},{10,234},{12,44},{14,238},{16... | collective-permute-start | bytes 786440 | tf_op jit(solution)/shard_map/ppermute | solution.py:80
  81.8 9.9 %collective-permute-start.17 = (f32[16,4096]{1,0:T(8,128)S(1)}, f32[16,4096]{1,0:T(8,128)S(1)}, u32[]{:S(2)}, u32[]{:S(2)}) collective-permute-start(f32[16,4096]{1,0:T(8,128)S(1)} %get-tuple-element.22), channel_id=1, source_target_pairs={{0,224},{2,34},{4,228},{6,38},{8,232},{10,42},{12,236},{14,46},{16... | collective-permute-start | bytes 786440 | tf_op jit(solution)/shard_map/ppermute | solution.py:88
  86.9 16.1 %collective-permute-start.25 = (f32[32,4096]{1,0:T(8,128)S(1)}, f32[32,4096]{1,0:T(8,128)S(1)}, u32[]{:S(2)}, u32[]{:S(2)}) collective-permute-start(f32[32,4096]{1,0:T(8,128)S(1)} %get-tuple-element.23), channel_id=1, source_target_pairs={{0,4},{2,14},{4,8},{6,2},{8,12},{10,6},{12,0},{14,10},{16,20},{18,... | collective-permute-start | bytes 1572872 | tf_op jit(solution)/shard_map/ppermute | solution.py:80
  88.7 14.2 %collective-permute-start.27 = (f32[32,4096]{1,0:T(8,128)S(1)}, f32[32,4096]{1,0:T(8,128)S(1)}, u32[]{:S(2)}, u32[]{:S(2)}) collective-permute-start(f32[32,4096]{1,0:T(8,128)S(1)} %get-tuple-element.24), channel_id=1, source_target_pairs={{0,12},{2,6},{4,0},{6,10},{8,4},{10,14},{12,8},{14,2},{16,28},{18,... | collective-permute-start | bytes 1572872 | tf_op jit(solution)/shard_map/ppermute | solution.py:88
  91.8 11.3 %collective-permute-start.14 = (f32[16,4096]{1,0:T(8,128)S(1)}, f32[16,4096]{1,0:T(8,128)S(1)}, u32[]{:S(2)}, u32[]{:S(2)}) collective-permute-start(f32[16,4096]{1,0:T(8,128)S(1)} %get-tuple-element.19), channel_id=1, source_target_pairs={{0,32},{2,226},{4,36},{6,230},{8,40},{10,234},{12,44},{14,238},{16... | collective-permute-start | bytes 786440 | tf_op jit(solution)/shard_map/ppermute | solution.py:80
  91.9 11.2 %collective-permute-start.18 = (f32[16,4096]{1,0:T(8,128)S(1)}, f32[16,4096]{1,0:T(8,128)S(1)}, u32[]{:S(2)}, u32[]{:S(2)}) collective-permute-start(f32[16,4096]{1,0:T(8,128)S(1)} %get-tuple-element.20), channel_id=1, source_target_pairs={{0,224},{2,34},{4,228},{6,38},{8,232},{10,42},{12,236},{14,46},{16... | collective-permute-start | bytes 786440 | tf_op jit(solution)/shard_map/ppermute | solution.py:88
  103.2 8.7 %collective-permute-start.15 = (f32[16,4096]{1,0:T(8,128)S(1)}, f32[16,4096]{1,0:T(8,128)S(1)}, u32[]{:S(2)}, u32[]{:S(2)}) collective-permute-start(f32[16,4096]{1,0:T(8,128)S(1)} %get-tuple-element.17), channel_id=1, source_target_pairs={{0,32},{2,226},{4,36},{6,230},{8,40},{10,234},{12,44},{14,238},{16... | collective-permute-start | bytes 786440 | tf_op jit(solution)/shard_map/ppermute | solution.py:80
  105.3 7.7 %collective-permute-start.19 = (f32[16,4096]{1,0:T(8,128)S(1)}, f32[16,4096]{1,0:T(8,128)S(1)}, u32[]{:S(2)}, u32[]{:S(2)}) collective-permute-start(f32[16,4096]{1,0:T(8,128)S(1)} %get-tuple-element.18), channel_id=1, source_target_pairs={{0,224},{2,34},{4,228},{6,38},{8,232},{10,42},{12,236},{14,46},{16... | collective-permute-start | bytes 786440 | tf_op jit(solution)/shard_map/ppermute | solution.py:88
  108.1 6.3 %collective-permute-start.28 = (f32[4,4096]{1,0:T(4,128)S(1)}, f32[4,4096]{1,0:T(4,128)S(1)}, u32[]{:S(2)}, u32[]{:S(2)}) collective-permute-start(f32[4,4096]{1,0:T(4,128)S(1)} %get-tuple-element.29), channel_id=1, source_target_pairs={{0,32},{2,226},{4,36},{6,230},{8,40},{10,234},{12,44},{14,238},{16... | collective-permute-start | bytes 196616 | tf_op jit(solution)/shard_map/ppermute | solution.py:80
  108.1 6.2 %collective-permute-start.32 = (f32[4,4096]{1,0:T(4,128)S(1)}, f32[4,4096]{1,0:T(4,128)S(1)}, u32[]{:S(2)}, u32[]{:S(2)}) collective-permute-start(f32[4,4096]{1,0:T(4,128)S(1)} %get-tuple-element.30), channel_id=1, source_target_pairs={{0,224},{2,34},{4,228},{6,38},{8,232},{10,42},{12,236},{14,46},{16... | collective-permute-start | bytes 196616 | tf_op jit(solution)/shard_map/ppermute | solution.py:88
  114.4 7.0 %collective-permute-start.29 = (f32[4,4096]{1,0:T(4,128)S(1)}, f32[4,4096]{1,0:T(4,128)S(1)}, u32[]{:S(2)}, u32[]{:S(2)}) collective-permute-start(f32[4,4096]{1,0:T(4,128)S(1)} %get-tuple-element.27), channel_id=1, source_target_pairs={{0,32},{2,226},{4,36},{6,230},{8,40},{10,234},{12,44},{14,238},{16... | collective-permute-start | bytes 196616 | tf_op jit(solution)/shard_map/ppermute | solution.py:80
  117.8 7.0 %collective-permute-start.20 = (f32[4,4096]{1,0:T(4,128)S(1)}, f32[4,4096]{1,0:T(4,128)S(1)}, u32[]{:S(2)}, u32[]{:S(2)}) collective-permute-start(f32[4,4096]{1,0:T(4,128)S(1)} %get-tuple-element.31), channel_id=1, source_target_pairs={{0,4},{2,14},{4,8},{6,2},{8,12},{10,6},{12,0},{14,10},{16,20},{18,... | collective-permute-start | bytes 196616 | tf_op jit(solution)/shard_map/ppermute | solution.py:64
  118.2 6.6 %collective-permute-start.21 = (f32[4,4096]{1,0:T(4,128)S(1)}, f32[4,4096]{1,0:T(4,128)S(1)}, u32[]{:S(2)}, u32[]{:S(2)}) collective-permute-start(f32[4,4096]{1,0:T(4,128)S(1)} %get-tuple-element.33), channel_id=1, source_target_pairs={{0,8},{2,10},{4,12},{6,14},{8,0},{10,2},{12,4},{14,6},{16,24},{18,... | collective-permute-start | bytes 196616 | tf_op jit(solution)/shard_map/ppermute | solution.py:64
  (18 other events, 166.9 us)
